TPU v7x, 128 devices: a whole 4x4x4 slice. The times are simulated.
128 devices in a mesh: row: 16 (over z, y), col: 8 (over x, core).
Axes of the slice: x: 4, y: 4, z: 4, core: 2. Of those that a mesh axis runs over, the one named last changes fastest.
Arguments:
- queries: float32 [32768, 256], P(('row', 'col')), may hold values from -1 to 1
- passages: float32 [32768, 256], P(('col', 'row')), may hold values from -1 to 1
- mean_cost: float32 [1], replicated, may hold values from 1 to 3
Outputs:
- row_potential: float32 [32768], P('row')
- col_potential: float32 [32768], P('col')
All inputs are finite; a program needn't handle non-finite values.
Results may differ from a plain program's by a relative error of at most 0.0003.
Values sent between devices are 32-bit elements; how exact they have to be, the bound alone decides.
No kernel may reach another device: no remote copies, remote signals or barrier semaphores. Data moves between devices by JAX's collectives and lax.ppermute only.
A program may use at most 256 MiB of HBM per device.

v0:
```python
import math

import jax
import jax.numpy as jnp
from jax import lax
from jax.sharding import PartitionSpec as P

ITERS = 3


def inner_costs(left, right):
    left_norms = jnp.sum(left * left, axis=1)
    right_norms = jnp.sum(right * right, axis=1)
    inner = lax.dot_general(
        left,
        right,
        (((1,), (1,)), ((), ())),
        precision=lax.Precision.HIGHEST,
        preferred_element_type=jnp.float32,
    )
    return left_norms[:, None] + right_norms[None, :] - 2.0 * inner


def logsum_col(scores):
    peak = lax.pmax(jnp.max(scores, axis=1), "col")
    totals = lax.psum(jnp.sum(jnp.exp(scores - peak[:, None]), axis=1), "col")
    return peak + jnp.log(totals)


def logsum_row(scores):
    peak = lax.pmax(jnp.max(scores, axis=0), "row")
    totals = lax.psum(jnp.sum(jnp.exp(scores - peak[None, :]), axis=0), "row")
    return peak + jnp.log(totals)


def per_device(queries, passages, mean_cost):
    entropy_scale = 0.1 * mean_cost[0]
    row_count = lax.axis_size("row")
    col_count = lax.axis_size("col")
    all_queries = queries.shape[0] * row_count * col_count
    all_passages = passages.shape[0] * row_count * col_count
    query_block = lax.all_gather(queries, "col", axis=0, tiled=True)
    cost_tile = inner_costs(query_block, lax.all_gather(passages, "row", axis=0, tiled=True))
    col_potential = jnp.zeros((cost_tile.shape[1],), jnp.float32)
    row_potential = jnp.zeros((cost_tile.shape[0],), jnp.float32)
    for repeat in range(ITERS):
        scores = (col_potential[None, :] - cost_tile) / entropy_scale
        row_potential = -entropy_scale * math.log(all_queries) - entropy_scale * logsum_col(scores)
        scores = (row_potential[:, None] - cost_tile) / entropy_scale
        col_potential = -entropy_scale * math.log(all_passages) - entropy_scale * logsum_row(scores)
    return (row_potential, col_potential)


def solution(mesh):
    placed = (P(("row", "col"), None), P(("col", "row"), None), P())
    return jax.shard_map(
        per_device, mesh=mesh, in_specs=placed, out_specs=(P("row"), P("col")), check_vma=False
    )
```

profile of v0, /device:TPU:0, one launch (start us, length us, event | category | flops | bytes accessed | tf_op | source)
XLA Modules:
  0.0 790.6 jit_solution(16992387078408955022)
XLA Ops:
  7.2 0.0 all-gather.3.cloned.1.call-start
  7.2 0.7 all-gather.3.cloned.1.call-update
  7.9 0.0 all-gather.5.cloned.1.call-start
  7.9 0.7 all-gather.5.cloned.1.call-update
  9.3 28.2 %all-gather.3.cloned.1.call-done = f32[2048,256]{1,0:T(8,128)} async-done(((f32[256,256]{1,0:T(8,128)}), f32[2048,256]{1,0:T(8,128)}) %all-gather.3.cloned.1.call-update) | async-done | bytes 2097168 | tf_op jit(solution)/shard_map/all_gather | solution.py:42
  37.5 1.9 multiply_reduce_fusion.1
  39.4 52.2 %all-gather.5.cloned.1.call-done = f32[4096,256]{1,0:T(8,128)} async-done(((f32[256,256]{1,0:T(8,128)}), f32[4096,256]{1,0:T(8,128)}) %all-gather.5.cloned.1.call-update) | async-done | bytes 4194320 | tf_op jit(solution)/shard_map/all_gather | solution.py:43
  91.6 2.8 multiply_reduce_fusion
  94.4 38.7 %fusion = (f32[2048]{0:T(1024)S(1)}, f32[2048,4096]{1,0:T(8,128)}) fusion(f32[]{:T(128)} %bitcast, f32[2048,256]{1,0:T(8,128)} %all-gather.3.cloned.1.call-done, f32[4096,256]{1,0:T(8,128)} %all-gather.5.cloned.1.call-done, f32[4096]{0:T(1024)S(1)} %multiply_reduce_fusion, f32[2048]{0:T(1024)S(1)} %multiply_reduce_fusion.1), kind=kOutput, calls=%fused_computation.13 | convolution fusion | flops 25820133376 | bytes 39878660 | tf_op jit(solution)/shard_map/dot_general | solution.py:14
  133.1 14.6 %pmax.42 = f32[2048]{0:T(1024)S(1)} all-reduce(f32[2048]{0:T(1024)S(1)} %get-tuple-element.2), channel_id=1, replica_groups=mesh['row'=16,'col'=8] {'col'}, use_global_device_ids=true, to_apply=%region_3.0 | all-reduce | flops 2048 | bytes 16384 | tf_op jit(solution)/shard_map/pmax | solution.py:25
  147.7 14.5 %exponential_reduce_fusion.5 = f32[2048]{0:T(1024)S(1)} fusion(f32[2048]{0:T(1024)S(1)} %pmax.42, f32[]{:T(128)} %bitcast, f32[2048,4096]{1,0:T(8,128)} %get-tuple-element.3), kind=kLoop, calls=%fused_computation.10 | loop fusion | flops 33552384 | bytes 33570820 | tf_op jit(solution)/shard_map/reduce_sum | solution.py:26
  162.2 12.8 %psum.42 = f32[2048]{0:T(1024)S(1)} all-reduce(f32[2048]{0:T(1024)S(1)} %exponential_reduce_fusion.5), channel_id=1, replica_groups=mesh['row'=16,'col'=8] {'col'}, use_global_device_ids=true, to_apply=%region_5.0 | all-reduce | flops 2048 | bytes 16384 | tf_op jit(solution)/shard_map/psum | solution.py:26
  175.1 13.1 %fusion.3 = f32[4096]{0:T(1024)S(1)} fusion(f32[]{:T(128)} %bitcast, f32[2048,4096]{1,0:T(8,128)} %get-tuple-element.3, f32[2048]{0:T(1024)S(1)} %multiply_subtract_fusion.6), kind=kLoop, calls=%fused_computation.17 | loop fusion | flops 25161728 | bytes 33579012 | tf_op jit(solution)/shard_map/reduce_max | solution.py:31
  188.3 72.4 %pmax.43 = f32[4096]{0:T(1024)S(1)} all-reduce(f32[4096]{0:T(1024)S(1)} %fusion.3), channel_id=1, replica_groups=mesh['row'=16,'col'=8] {'row'}, use_global_device_ids=true, to_apply=%region_7.0 | all-reduce | flops 4096 | bytes 32768 | tf_op jit(solution)/shard_map/pmax | solution.py:31
  260.7 14.4 %exponential_reduce_fusion.4 = f32[4096]{0:T(1024)S(1)} fusion(f32[4096]{0:T(1024)S(1)} %pmax.43, f32[]{:T(128)} %bitcast, f32[2048,4096]{1,0:T(8,128)} %get-tuple-element.3, f32[2048]{0:T(1024)S(1)} %multiply_subtract_fusion.6), kind=kLoop, calls=%fused_computation.8 | loop fusion | flops 33550336 | bytes 33595396 | tf_op jit(solution)/shard_map/reduce_sum | solution.py:32
  275.0 69.5 %psum.43 = f32[4096]{0:T(1024)S(1)} all-reduce(f32[4096]{0:T(1024)S(1)} %exponential_reduce_fusion.4), channel_id=1, replica_groups=mesh['row'=16,'col'=8] {'row'}, use_global_device_ids=true, to_apply=%region_9.0 | all-reduce | flops 4096 | bytes 32768 | tf_op jit(solution)/shard_map/psum | solution.py:32
  344.6 12.8 %fusion.1 = f32[2048]{0:T(1024)S(1)} fusion(f32[]{:T(128)} %bitcast, f32[2048,4096]{1,0:T(8,128)} %get-tuple-element.3, f32[4096]{0:T(1024)S(1)} %multiply_subtract_fusion.3), kind=kLoop, calls=%fused_computation.14 | loop fusion | flops 25163776 | bytes 33579012 | tf_op jit(solution)/shard_map/reduce_max | solution.py:25
  357.4 12.7 %pmax.44 = f32[2048]{0:T(1024)S(1)} all-reduce(f32[2048]{0:T(1024)S(1)} %fusion.1), channel_id=1, replica_groups=mesh['row'=16,'col'=8] {'col'}, use_global_device_ids=true, to_apply=%region_11.0 | all-reduce | flops 2048 | bytes 16384 | tf_op jit(solution)/shard_map/pmax | solution.py:25
  370.0 14.6 %exponential_reduce_fusion.3 = f32[2048]{0:T(1024)S(1)} fusion(f32[2048]{0:T(1024)S(1)} %pmax.44, f32[]{:T(128)} %bitcast, f32[2048,4096]{1,0:T(8,128)} %get-tuple-element.3, f32[4096]{0:T(1024)S(1)} %multiply_subtract_fusion.3), kind=kLoop, calls=%fused_computation.6 | loop fusion | flops 33552384 | bytes 33587204 | tf_op jit(solution)/shard_map/reduce_sum | solution.py:26
  384.6 12.7 %psum.44 = f32[2048]{0:T(1024)S(1)} all-reduce(f32[2048]{0:T(1024)S(1)} %exponential_reduce_fusion.3), channel_id=1, replica_groups=mesh['row'=16,'col'=8] {'col'}, use_global_device_ids=true, to_apply=%region_13.0 | all-reduce | flops 2048 | bytes 16384 | tf_op jit(solution)/shard_map/psum | solution.py:26
  397.3 13.1 %fusion.4 = f32[4096]{0:T(1024)S(1)} fusion(f32[]{:T(128)} %bitcast, f32[2048,4096]{1,0:T(8,128)} %get-tuple-element.3, f32[2048]{0:T(1024)S(1)} %multiply_subtract_fusion.5), kind=kLoop, calls=%fused_computation.18 | loop fusion | flops 25161728 | bytes 33579012 | tf_op jit(solution)/shard_map/reduce_max | solution.py:31
  410.4 69.5 %pmax.45 = f32[4096]{0:T(1024)S(1)} all-reduce(f32[4096]{0:T(1024)S(1)} %fusion.4), channel_id=1, replica_groups=mesh['row'=16,'col'=8] {'row'}, use_global_device_ids=true, to_apply=%region_15.0 | all-reduce | flops 4096 | bytes 32768 | tf_op jit(solution)/shard_map/pmax | solution.py:31
  480.0 14.4 %exponential_reduce_fusion.2 = f32[4096]{0:T(1024)S(1)} fusion(f32[4096]{0:T(1024)S(1)} %pmax.45, f32[]{:T(128)} %bitcast, f32[2048,4096]{1,0:T(8,128)} %get-tuple-element.3, f32[2048]{0:T(1024)S(1)} %multiply_subtract_fusion.5), kind=kLoop, calls=%fused_computation.4 | loop fusion | flops 33550336 | bytes 33595396 | tf_op jit(solution)/shard_map/reduce_sum | solution.py:32
  494.3 69.5 %psum.45 = f32[4096]{0:T(1024)S(1)} all-reduce(f32[4096]{0:T(1024)S(1)} %exponential_reduce_fusion.2), channel_id=1, replica_groups=mesh['row'=16,'col'=8] {'row'}, use_global_device_ids=true, to_apply=%region_17.0 | all-reduce | flops 4096 | bytes 32768 | tf_op jit(solution)/shard_map/psum | solution.py:32
  563.9 12.8 %fusion.2 = f32[2048]{0:T(1024)S(1)} fusion(f32[]{:T(128)} %bitcast, f32[2048,4096]{1,0:T(8,128)} %get-tuple-element.3, f32[4096]{0:T(1024)S(1)} %multiply_subtract_fusion.2), kind=kLoop, calls=%fused_computation.15 | loop fusion | flops 25163776 | bytes 33579012 | tf_op jit(solution)/shard_map/reduce_max | solution.py:25
  576.6 12.7 %pmax.46 = f32[2048]{0:T(1024)S(1)} all-reduce(f32[2048]{0:T(1024)S(1)} %fusion.2), channel_id=1, replica_groups=mesh['row'=16,'col'=8] {'col'}, use_global_device_ids=true, to_apply=%region_19.0 | all-reduce | flops 2048 | bytes 16384 | tf_op jit(solution)/shard_map/pmax | solution.py:25
  589.3 14.6 %exponential_reduce_fusion.1 = f32[2048]{0:T(1024)S(1)} fusion(f32[2048]{0:T(1024)S(1)} %pmax.46, f32[]{:T(128)} %bitcast, f32[2048,4096]{1,0:T(8,128)} %get-tuple-element.3, f32[4096]{0:T(1024)S(1)} %multiply_subtract_fusion.2), kind=kLoop, calls=%fused_computation.2 | loop fusion | flops 33552384 | bytes 33587204 | tf_op jit(solution)/shard_map/reduce_sum | solution.py:26
  603.9 12.7 %psum.46 = f32[2048]{0:T(1024)S(1)} all-reduce(f32[2048]{0:T(1024)S(1)} %exponential_reduce_fusion.1), channel_id=1, replica_groups=mesh['row'=16,'col'=8] {'col'}, use_global_device_ids=true, to_apply=%region_21.0 | all-reduce | flops 2048 | bytes 16384 | tf_op jit(solution)/shard_map/psum | solution.py:26
  616.6 0.0 copy-start
  616.6 13.1 %fusion.5 = f32[4096]{0:T(1024)S(1)} fusion(f32[]{:T(128)} %bitcast, f32[2048,4096]{1,0:T(8,128)} %get-tuple-element.3, f32[2048]{0:T(1024)S(1)} %multiply_subtract_fusion.4), kind=kLoop, calls=%fused_computation.19 | loop fusion | flops 25161728 | bytes 33579012 | tf_op jit(solution)/shard_map/reduce_max | solution.py:31
  629.7 69.5 %pmax.47 = f32[4096]{0:T(1024)S(1)} all-reduce(f32[4096]{0:T(1024)S(1)} %fusion.5), channel_id=1, replica_groups=mesh['row'=16,'col'=8] {'row'}, use_global_device_ids=true, to_apply=%region_23.0 | all-reduce | flops 4096 | bytes 32768 | tf_op jit(solution)/shard_map/pmax | solution.py:31
  699.3 14.4 %exponential_reduce_fusion = f32[4096]{0:T(1024)S(1)} fusion(f32[4096]{0:T(1024)S(1)} %pmax.47, f32[]{:T(128)} %bitcast, f32[2048,4096]{1,0:T(8,128)} %get-tuple-element.3, f32[2048]{0:T(1024)S(1)} %multiply_subtract_fusion.4), kind=kLoop, calls=%fused_computation | loop fusion | flops 33550336 | bytes 33595396 | tf_op jit(solution)/shard_map/reduce_sum | solution.py:32
  713.6 0.0 copy-done
  713.7 69.5 %psum.47 = f32[4096]{0:T(1024)S(1)} all-reduce(f32[4096]{0:T(1024)S(1)} %exponential_reduce_fusion), channel_id=1, replica_groups=mesh['row'=16,'col'=8] {'row'}, use_global_device_ids=true, to_apply=%region_25.0 | all-reduce | flops 4096 | bytes 32768 | tf_op jit(solution)/shard_map/psum | solution.py:32
  783.2 0.6 multiply_subtract_fusion.1
  (5 shorter events, 0.1 us)
Async XLA Ops:
  7.2 30.3 %all-gather.3.cloned.1.call-start = ((), (), s32[]{:S(2)}) async-start(), calls=%async_computation | async-start | bytes 2359296 | tf_op jit(solution)/shard_map/all_gather | solution.py:42
  7.9 83.7 %all-gather.5.cloned.1.call-start = ((), (), s32[]{:S(2)}) async-start(), calls=%async_computation.1 | async-start | bytes 4456448 | tf_op jit(solution)/shard_map/all_gather | solution.py:43
  616.6 97.1 %copy-start = (f32[2048]{0:T(1024)}, f32[2048]{0:T(1024)S(1)}, u32[]{:S(2)}) copy-start(f32[2048]{0:T(1024)S(1)} %multiply_subtract_fusion.4) | copy-start | bytes 24580
Sparse Core Ops, SparseCore 0:
  9.7 27.7 all-gather.2
  39.6 51.9 all-gather.4
where the time goes:
time: 792 us; the launch traced here: 791 us
  blocking collectives  498 us (63%)
  other arithmetic  157 us (20%)
  waiting for transfers between devices  81.7 us (10%)
  matrix products  38.7 us (5%)
  between operations  14.9 us (2%)
    pmax x3, blocking collectives, logsum_row(): peak = lax.pmax(jnp.max(scores, axis=0), 'row')  211 us
    psum x3, blocking collectives, logsum_row(): totals = lax.psum(jnp.sum(jnp.exp(scores - peak[None, :]), axis=0), 'row')  209 us
    all_gather x1, waiting for transfers between devices, per_device(): lax.all_gather(passages, 'row', axis=0, tiled=True)  52.2 us
    reduce_sum x3, other arithmetic, logsum_col(): totals = lax.psum(jnp.sum(jnp.exp(scores - peak[:, None]), axis=1), 'col')  43.7 us
    reduce_sum x3, other arithmetic, logsum_row(): totals = lax.psum(jnp.sum(jnp.exp(scores - peak[None, :]), axis=0), 'row')  43.1 us
    pmax x3, blocking collectives, logsum_col(): peak = lax.pmax(jnp.max(scores, axis=1), 'col')  39.9 us
    reduce_max x3, other arithmetic, logsum_row(): peak = lax.pmax(jnp.max(scores, axis=0), 'row')  39.4 us
    dot_general x1, matrix products, inner_costs(): lax.dot_general(left, right, (((1,), (1,)), ((), ())), precision=lax.Prec...  38.7 us
  transfers between devices with their start and end apart: 2, of which 2 were waited for; matrix products, arithmetic and copies ran while one was open for 0% of the time, Pallas kernels for 0%

commit v1 on v0

--- a/solution.py
+++ b/solution.py
@@ -21,16 +21,30 @@
     return left_norms[:, None] + right_norms[None, :] - 2.0 * inner
 
 
+def combine_over(peak, total, axis):
+    size = lax.axis_size(axis)
+    packed = jnp.stack([peak, total])
+    step = 1
+    while step < size:
+        perm = [(i, i ^ step) for i in range(size)]
+        other = lax.ppermute(packed, axis, perm)
+        new_peak = jnp.maximum(packed[0], other[0])
+        new_total = packed[1] * jnp.exp(packed[0] - new_peak) + other[1] * jnp.exp(other[0] - new_peak)
+        packed = jnp.stack([new_peak, new_total])
+        step *= 2
+    return packed[0] + jnp.log(packed[1])
+
+
 def logsum_col(scores):
-    peak = lax.pmax(jnp.max(scores, axis=1), "col")
-    totals = lax.psum(jnp.sum(jnp.exp(scores - peak[:, None]), axis=1), "col")
-    return peak + jnp.log(totals)
+    peak = jnp.max(scores, axis=1)
+    totals = jnp.sum(jnp.exp(scores - peak[:, None]), axis=1)
+    return combine_over(peak, totals, "col")
 
 
 def logsum_row(scores):
-    peak = lax.pmax(jnp.max(scores, axis=0), "row")
-    totals = lax.psum(jnp.sum(jnp.exp(scores - peak[None, :]), axis=0), "row")
-    return peak + jnp.log(totals)
+    peak = jnp.max(scores, axis=0)
+    totals = jnp.sum(jnp.exp(scores - peak[None, :]), axis=0)
+    return combine_over(peak, totals, "row")
 
 
 def per_device(queries, passages, mean_cost):

time: 792 us -> 328 us (0.41)
  blocking collectives: 498 us -> 0 us
  other arithmetic: 157 us -> 103 us
  waiting for transfers between devices: 81.7 us -> 126 us
  starting transfers between devices: 0.08 us -> 43.8 us
    pmax x6 -> x0, blocking collectives: 251 us -> none  [the longest x3 211 us: logsum_row(): peak = lax.pmax(jnp.max(scores, axis=0), 'row')]
    psum x6 -> x0, blocking collectives: 247 us -> none  [the longest x3 209 us: logsum_row(): totals = lax.psum(jnp.sum(jnp.exp(scores - peak[None, :]), axis=0), 'row')]
    ppermute x0 -> x21, waiting for transfers between devices: none -> 44.8 us  [combine_over(): other = lax.ppermute(packed, axis, perm)]
    ppermute x0 -> x21, starting transfers between devices: none -> 43.8 us  [combine_over(): other = lax.ppermute(packed, axis, perm)]
    reduce_max x5, other arithmetic: 64.9 us -> 33.7 us  [the longest x3 25.7 us: logsum_row(): peak = jnp.max(scores, axis=0)]
    reduce_sum x6, other arithmetic: 86.8 us -> 62.7 us  [the longest x3 31.7 us: logsum_row(): totals = jnp.sum(jnp.exp(scores - peak[None, :]), axis=0)]
  transfers between devices with their start and end apart: 2 -> 23, of which waited for: 2 -> 23; matrix products, arithmetic and copies ran while one was open for 0% -> 1% of each run, Pallas kernels for 0% -> 0%
where the time goes in v1:
time: 328 us
  waiting for transfers between devices  126 us (38%)
  other arithmetic  103 us (31%)
  starting transfers between devices  43.8 us (13%)
  matrix products  38.8 us (12%)
  between operations  15.2 us (5%)
    all_gather x1, waiting for transfers between devices, per_device(): lax.all_gather(passages, 'row', axis=0, tiled=True)  52.2 us
    ppermute x21, waiting for transfers between devices, combine_over(): other = lax.ppermute(packed, axis, perm)  44.8 us
    ppermute x21, starting transfers between devices, combine_over(): other = lax.ppermute(packed, axis, perm)  43.8 us
    dot_general x1, matrix products, inner_costs(): lax.dot_general(left, right, (((1,), (1,)), ((), ())), precision=lax.Prec...  38.8 us
    reduce_sum x3, other arithmetic, logsum_row(): totals = jnp.sum(jnp.exp(scores - peak[None, :]), axis=0)  31.7 us
    reduce_sum x3, other arithmetic, logsum_col(): totals = jnp.sum(jnp.exp(scores - peak[:, None]), axis=1)  30.9 us
    all_gather x1, waiting for transfers between devices, per_device(): query_block = lax.all_gather(queries, 'col', axis=0, tiled=True)  28.2 us
    reduce_max x3, other arithmetic, logsum_row(): peak = jnp.max(scores, axis=0)  25.7 us
  transfers between devices with their start and end apart: 23, of which 23 were waited for; matrix products, arithmetic and copies ran while one was open for 1% of the time, Pallas kernels for 0%

profile of v1, /device:TPU:0, one launch (start us, length us, event | category | flops | bytes accessed | tf_op | source)
XLA Modules:
  0.0 327.8 jit_solution(17510143639253110666)
XLA Ops:
  9.3 28.2 %all-gather.3.cloned.1.call-done = f32[2048,256]{1,0:T(8,128)} async-done(((f32[256,256]{1,0:T(8,128)}), f32[2048,256]{1,0:T(8,128)}) %all-gather.3.cloned.1.call-update) | async-done | bytes 2097168 | tf_op jit(solution)/shard_map/all_gather | solution.py:56
  37.5 1.9 multiply_reduce_fusion.1
  39.4 52.2 %all-gather.5.cloned.1.call-done = f32[4096,256]{1,0:T(8,128)} async-done(((f32[256,256]{1,0:T(8,128)}), f32[4096,256]{1,0:T(8,128)}) %all-gather.5.cloned.1.call-update) | async-done | bytes 4194320 | tf_op jit(solution)/shard_map/all_gather | solution.py:57
  91.6 2.8 multiply_reduce_fusion
  94.4 38.8 %fusion = (f32[2048]{0:T(1024)S(1)}, f32[2048,4096]{1,0:T(8,128)}) fusion(f32[]{:T(128)} %bitcast, f32[2048,256]{1,0:T(8,128)} %all-gather.3.cloned.1.call-done, f32[4096,256]{1,0:T(8,128)} %all-gather.5.cloned.1.call-done, f32[4096]{0:T(1024)S(1)} %multiply_reduce_fusion, f32[2048]{0:T(1024)S(1)} %multiply_reduce_fusion.1), kind=kOutput, calls=%fused_computation.13 | convolution fusion | flops 25820133376 | bytes 39878660 | tf_op jit(solution)/shard_map/dot_general | solution.py:14
  133.1 14.5 %exponential_reduce_fusion.5 = f32[2048]{0:T(1024)S(1)} fusion(f32[2048]{0:T(1024)S(1)} %get-tuple-element.58, f32[]{:T(128)} %bitcast, f32[2048,4096]{1,0:T(8,128)} %get-tuple-element.59), kind=kLoop, calls=%fused_computation.10 | loop fusion | flops 33552384 | bytes 33570820 | tf_op jit(solution)/shard_map/reduce_sum | solution.py:40
  150.6 2.3 collective-permute-done.1
  152.9 3.2 collective-permute-start.2
  156.2 2.3 collective-permute-done.2
  158.5 15.7 %fusion.3 = f32[4096]{0:T(1024)S(1)} fusion(f32[]{:T(128)} %bitcast, f32[2048,4096]{1,0:T(8,128)} %get-tuple-element.59, f32[2048]{0:T(1024)S(1)} %multiply_subtract_fusion.6), kind=kLoop, calls=%fused_computation.17 | loop fusion | flops 25161728 | bytes 33579012 | tf_op jit(solution)/shard_map/reduce_max | solution.py:45
  174.2 16.4 %exponential_reduce_fusion.4 = f32[4096]{0:T(1024)S(1)} fusion(f32[4096]{0:T(1024)S(1)} %fusion.3, f32[]{:T(128)} %bitcast, f32[2048,4096]{1,0:T(8,128)} %get-tuple-element.59, f32[2048]{0:T(1024)S(1)} %multiply_subtract_fusion.6), kind=kLoop, calls=%fused_computation.8 | loop fusion | flops 33550336 | bytes 33595396 | tf_op jit(solution)/shard_map/reduce_sum | solution.py:46
  190.7 1.6 collective-permute-start.3
  192.3 2.4 collective-permute-done.3
  194.8 3.1 collective-permute-start.4
  197.9 2.4 collective-permute-done.4
  202.0 2.4 collective-permute-done.5
  204.5 3.3 %collective-permute-start.6 = (f32[2,4096]{1,0:T(2,128)S(1)}, f32[2,4096]{1,0:T(2,128)S(1)}, u32[]{:S(2)}, u32[]{:S(2)}) collective-permute-start(f32[2,4096]{1,0:T(2,128)S(1)} %pad_maximum_fusion.3), channel_id=1, source_target_pairs={{0,64},{8,72},{16,80},{24,88},{32,96},{40,104},{48,112},{56,120},{... | collective-permute-start | bytes 98312 | tf_op jit(solution)/shard_map/ppermute | solution.py:30
  207.8 2.2 collective-permute-done.6
  210.2 4.0 %fusion.1 = f32[2048]{0:T(1024)S(1)} fusion(f32[]{:T(128)} %bitcast, f32[2048,4096]{1,0:T(8,128)S(1)} %bitcast.44, f32[4096]{0:T(1024)S(1)} %bitcast.57), kind=kLoop, calls=%fused_computation.14 | loop fusion | flops 25163776 | bytes 33579012 | tf_op jit(solution)/shard_map/reduce_max | solution.py:39
  214.2 8.2 %exponential_reduce_fusion.3 = f32[2048]{0:T(1024)S(1)} fusion(f32[2048]{0:T(1024)S(1)} %fusion.1, f32[]{:T(128)} %bitcast, f32[2048,4096]{1,0:T(8,128)S(1)} %bitcast.44, f32[4096]{0:T(1024)S(1)} %bitcast.58), kind=kLoop, calls=%fused_computation.6 | loop fusion | flops 33552384 | bytes 33587204 | tf_op jit(solution)/shard_map/reduce_sum | solution.py:40
  225.3 2.3 collective-permute-done.8
  227.7 3.1 collective-permute-start.9
  230.7 2.3 collective-permute-done.9
  233.0 5.0 %fusion.4 = f32[4096]{0:T(1024)S(1)} fusion(f32[]{:T(128)} %bitcast, f32[2048,4096]{1,0:T(8,128)S(1)} %bitcast.44, f32[2048]{0:T(1024)S(1)} %multiply_subtract_fusion.5), kind=kLoop, calls=%fused_computation.18 | loop fusion | flops 25161728 | bytes 33579012 | tf_op jit(solution)/shard_map/reduce_max | solution.py:45
  238.1 7.6 %exponential_reduce_fusion.2 = f32[4096]{0:T(1024)S(1)} fusion(f32[4096]{0:T(1024)S(1)} %fusion.4, f32[]{:T(128)} %bitcast, f32[2048,4096]{1,0:T(8,128)S(1)} %bitcast.44, f32[2048]{0:T(1024)S(1)} %multiply_subtract_fusion.5), kind=kLoop, calls=%fused_computation.4 | loop fusion | flops 33550336 | bytes 33595396 | tf_op jit(solution)/shard_map/reduce_sum | solution.py:46
  245.8 1.6 collective-permute-start.10
  247.3 2.4 collective-permute-done.10
  249.9 3.1 collective-permute-start.11
  253.0 2.4 collective-permute-done.11
  255.5 1.8 collective-permute-start.12
  257.3 2.2 collective-permute-done.12
  259.6 3.3 %collective-permute-start.13 = (f32[2,4096]{1,0:T(2,128)S(1)}, f32[2,4096]{1,0:T(2,128)S(1)}, u32[]{:S(2)}, u32[]{:S(2)}) collective-permute-start(f32[2,4096]{1,0:T(2,128)S(1)} %pad_maximum_fusion.7), channel_id=1, source_target_pairs={{0,64},{8,72},{16,80},{24,88},{32,96},{40,104},{48,112},{56,120},{... | collective-permute-start | bytes 98312 | tf_op jit(solution)/shard_map/ppermute | solution.py:30
  262.9 2.2 collective-permute-done.13
  265.2 4.0 %fusion.2 = f32[2048]{0:T(1024)S(1)} fusion(f32[]{:T(128)} %bitcast, f32[2048,4096]{1,0:T(8,128)S(1)} %bitcast.44, f32[4096]{0:T(1024)S(1)} %bitcast.59), kind=kLoop, calls=%fused_computation.15 | loop fusion | flops 25163776 | bytes 33579012 | tf_op jit(solution)/shard_map/reduce_max | solution.py:39
  269.2 8.2 %exponential_reduce_fusion.1 = f32[2048]{0:T(1024)S(1)} fusion(f32[2048]{0:T(1024)S(1)} %fusion.2, f32[]{:T(128)} %bitcast, f32[2048,4096]{1,0:T(8,128)S(1)} %bitcast.44, f32[4096]{0:T(1024)S(1)} %bitcast.60), kind=kLoop, calls=%fused_computation.2 | loop fusion | flops 33552384 | bytes 33587204 | tf_op jit(solution)/shard_map/reduce_sum | solution.py:40
  280.3 2.3 collective-permute-done.15
  282.6 3.3 %collective-permute-start.16 = (f32[2,2048]{1,0:T(2,128)S(1)}, f32[2,2048]{1,0:T(2,128)S(1)}, u32[]{:S(2)}, u32[]{:S(2)}) collective-permute-start(f32[2,2048]{1,0:T(2,128)S(1)} %pad_maximum_fusion.20), channel_id=1, source_target_pairs={{0,4},{1,5},{2,6},{3,7},{4,0},{5,1},{6,2},{7,3},{8,12},{9,13},{10,... | collective-permute-start | bytes 49160 | tf_op jit(solution)/shard_map/ppermute | solution.py:30
  285.9 2.3 collective-permute-done.16
  288.2 5.0 %fusion.5 = f32[4096]{0:T(1024)S(1)} fusion(f32[]{:T(128)} %bitcast, f32[2048,4096]{1,0:T(8,128)S(1)} %bitcast.44, f32[2048]{0:T(1024)S(1)} %multiply_subtract_fusion.4), kind=kLoop, calls=%fused_computation.19 | loop fusion | flops 25161728 | bytes 33579012 | tf_op jit(solution)/shard_map/reduce_max | solution.py:45
  293.3 7.6 %exponential_reduce_fusion = f32[4096]{0:T(1024)S(1)} fusion(f32[4096]{0:T(1024)S(1)} %fusion.5, f32[]{:T(128)} %bitcast, f32[2048,4096]{1,0:T(8,128)S(1)} %bitcast.44, f32[2048]{0:T(1024)S(1)} %multiply_subtract_fusion.4), kind=kLoop, calls=%fused_computation | loop fusion | flops 33550336 | bytes 33595396 | tf_op jit(solution)/shard_map/reduce_sum | solution.py:46
  301.0 1.6 collective-permute-start.17
  302.5 2.4 collective-permute-done.17
  305.1 3.1 collective-permute-start.18
  308.2 2.4 collective-permute-done.18
  310.7 2.0 collective-permute-start.19
  312.7 2.0 collective-permute-done.19
  314.8 3.3 %collective-permute-start.20 = (f32[2,4096]{1,0:T(2,128)S(1)}, f32[2,4096]{1,0:T(2,128)S(1)}, u32[]{:S(2)}, u32[]{:S(2)}) collective-permute-start(f32[2,4096]{1,0:T(2,128)S(1)} %pad_maximum_fusion.11), channel_id=1, source_target_pairs={{0,64},{8,72},{16,80},{24,88},{32,96},{40,104},{48,112},{56,120},{... | collective-permute-start | bytes 98312 | tf_op jit(solution)/shard_map/ppermute | solution.py:30
  318.1 2.2 collective-permute-done.20
  (79 shorter events, 13.8 us)
Async XLA Ops:
  7.2 30.3 %all-gather.3.cloned.1.call-start = ((), (), s32[]{:S(2)}) async-start(), calls=%async_computation | async-start | bytes 2359296 | tf_op jit(solution)/shard_map/all_gather | solution.py:56
  7.9 83.7 %all-gather.5.cloned.1.call-start = ((), (), s32[]{:S(2)}) async-start(), calls=%async_computation.1 | async-start | bytes 4456448 | tf_op jit(solution)/shard_map/all_gather | solution.py:57
  147.7 1.3 collective-permute-start
  149.0 3.8 %collective-permute-start.1 = (f32[2,2048]{1,0:T(2,128)S(1)}, f32[2,2048]{1,0:T(2,128)S(1)}, u32[]{:S(2)}, u32[]{:S(2)}) collective-permute-start(f32[2,2048]{1,0:T(2,128)S(1)} %pad_maximum_fusion.13), channel_id=1, source_target_pairs={{0,2},{1,3},{2,0},{3,1},{4,6},{5,7},{6,4},{7,5},{8,10},{9,11},{10,... | collective-permute-start | bytes 49160 | tf_op jit(solution)/shard_map/ppermute | solution.py:30
  152.9 5.5 %collective-permute-start.2 = (f32[2,2048]{1,0:T(2,128)S(1)}, f32[2,2048]{1,0:T(2,128)S(1)}, u32[]{:S(2)}, u32[]{:S(2)}) collective-permute-start(f32[2,2048]{1,0:T(2,128)S(1)} %pad_maximum_fusion.14), channel_id=1, source_target_pairs={{0,4},{1,5},{2,6},{3,7},{4,0},{5,1},{6,2},{7,3},{8,12},{9,13},{10,... | collective-permute-start | bytes 49160 | tf_op jit(solution)/shard_map/ppermute | solution.py:30
  158.5 51.6 %slice-start = ((s8[33554432]{0:T(1024)(128)(4,1)}), s8[4194304]{0:T(1024)(128)(4,1)S(1)}, s32[]{:S(2)}) async-start(s8[33554432]{0:T(1024)(128)(4,1)} %bitcast.43), calls=%async_computation.2 | async-start | bytes 8388608
  158.5 51.6 %slice-start.1 = ((s8[33554432]{0:T(1024)(128)(4,1)}), s8[4194304]{0:T(1024)(128)(4,1)S(1)}, s32[]{:S(2)}) async-start(s8[33554432]{0:T(1024)(128)(4,1)} %bitcast.43), calls=%async_computation.3 | async-start | bytes 8388608
  158.5 51.6 %slice-start.2 = ((s8[33554432]{0:T(1024)(128)(4,1)}), s8[4194304]{0:T(1024)(128)(4,1)S(1)}, s32[]{:S(2)}) async-start(s8[33554432]{0:T(1024)(128)(4,1)} %bitcast.43), calls=%async_computation.4 | async-start | bytes 8388608
  158.5 51.6 %slice-start.3 = ((s8[33554432]{0:T(1024)(128)(4,1)}), s8[4194304]{0:T(1024)(128)(4,1)S(1)}, s32[]{:S(2)}) async-start(s8[33554432]{0:T(1024)(128)(4,1)} %bitcast.43), calls=%async_computation.5 | async-start | bytes 8388608
  174.2 36.0 %slice-start.4 = ((s8[33554432]{0:T(1024)(128)(4,1)}), s8[4194304]{0:T(1024)(128)(4,1)S(1)}, s32[]{:S(2)}) async-start(s8[33554432]{0:T(1024)(128)(4,1)} %bitcast.43), calls=%async_computation.6 | async-start | bytes 8388608
  174.2 36.0 %slice-start.5 = ((s8[33554432]{0:T(1024)(128)(4,1)}), s8[4194304]{0:T(1024)(128)(4,1)S(1)}, s32[]{:S(2)}) async-start(s8[33554432]{0:T(1024)(128)(4,1)} %bitcast.43), calls=%async_computation.7 | async-start | bytes 8388608
  174.2 36.0 %slice-start.6 = ((s8[33554432]{0:T(1024)(128)(4,1)}), s8[4194304]{0:T(1024)(128)(4,1)S(1)}, s32[]{:S(2)}) async-start(s8[33554432]{0:T(1024)(128)(4,1)} %bitcast.43), calls=%async_computation.8 | async-start | bytes 8388608
  174.2 36.0 %slice-start.7 = ((s8[33554432]{0:T(1024)(128)(4,1)}), s8[4194304]{0:T(1024)(128)(4,1)S(1)}, s32[]{:S(2)}) async-start(s8[33554432]{0:T(1024)(128)(4,1)} %bitcast.43), calls=%async_computation.9 | async-start | bytes 8388608
  190.7 4.0 %collective-permute-start.3 = (f32[2,4096]{1,0:T(2,128)S(1)}, f32[2,4096]{1,0:T(2,128)S(1)}, u32[]{:S(2)}, u32[]{:S(2)}) collective-permute-start(f32[2,4096]{1,0:T(2,128)S(1)} %pad_maximum_fusion), channel_id=1, source_target_pairs={{0,8},{8,0},{16,24},{24,16},{32,40},{40,32},{48,56},{56,48},{64,72... | collective-permute-start | bytes 98312 | tf_op jit(solution)/shard_map/ppermute | solution.py:30
  194.8 5.5 %collective-permute-start.4 = (f32[2,4096]{1,0:T(2,128)S(1)}, f32[2,4096]{1,0:T(2,128)S(1)}, u32[]{:S(2)}, u32[]{:S(2)}) collective-permute-start(f32[2,4096]{1,0:T(2,128)S(1)} %pad_maximum_fusion.1), channel_id=1, source_target_pairs={{0,16},{8,24},{16,0},{24,8},{32,48},{40,56},{48,32},{56,40},{64,80... | collective-permute-start | bytes 98312 | tf_op jit(solution)/shard_map/ppermute | solution.py:30
  200.4 4.0 %collective-permute-start.5 = (f32[2,4096]{1,0:T(2,128)S(1)}, f32[2,4096]{1,0:T(2,128)S(1)}, u32[]{:S(2)}, u32[]{:S(2)}) collective-permute-start(f32[2,4096]{1,0:T(2,128)S(1)} %pad_maximum_fusion.2), channel_id=1, source_target_pairs={{0,32},{8,40},{16,48},{24,56},{32,0},{40,8},{48,16},{56,24},{64,96... | collective-permute-start | bytes 98312 | tf_op jit(solution)/shard_map/ppermute | solution.py:30
  204.5 5.5 %collective-permute-start.6 = (f32[2,4096]{1,0:T(2,128)S(1)}, f32[2,4096]{1,0:T(2,128)S(1)}, u32[]{:S(2)}, u32[]{:S(2)}) collective-permute-start(f32[2,4096]{1,0:T(2,128)S(1)} %pad_maximum_fusion.3), channel_id=1, source_target_pairs={{0,64},{8,72},{16,80},{24,88},{32,96},{40,104},{48,112},{56,120},{... | collective-permute-start | bytes 98312 | tf_op jit(solution)/shard_map/ppermute | solution.py:30
  222.4 1.3 collective-permute-start.7
  223.8 3.8 %collective-permute-start.8 = (f32[2,2048]{1,0:T(2,128)S(1)}, f32[2,2048]{1,0:T(2,128)S(1)}, u32[]{:S(2)}, u32[]{:S(2)}) collective-permute-start(f32[2,2048]{1,0:T(2,128)S(1)} %pad_maximum_fusion.16), channel_id=1, source_target_pairs={{0,2},{1,3},{2,0},{3,1},{4,6},{5,7},{6,4},{7,5},{8,10},{9,11},{10,... | collective-permute-start | bytes 49160 | tf_op jit(solution)/shard_map/ppermute | solution.py:30
  227.7 5.3 %collective-permute-start.9 = (f32[2,2048]{1,0:T(2,128)S(1)}, f32[2,2048]{1,0:T(2,128)S(1)}, u32[]{:S(2)}, u32[]{:S(2)}) collective-permute-start(f32[2,2048]{1,0:T(2,128)S(1)} %pad_maximum_fusion.17), channel_id=1, source_target_pairs={{0,4},{1,5},{2,6},{3,7},{4,0},{5,1},{6,2},{7,3},{8,12},{9,13},{10,... | collective-permute-start | bytes 49160 | tf_op jit(solution)/shard_map/ppermute | solution.py:30
  245.8 4.0 %collective-permute-start.10 = (f32[2,4096]{1,0:T(2,128)S(1)}, f32[2,4096]{1,0:T(2,128)S(1)}, u32[]{:S(2)}, u32[]{:S(2)}) collective-permute-start(f32[2,4096]{1,0:T(2,128)S(1)} %pad_maximum_fusion.4), channel_id=1, source_target_pairs={{0,8},{8,0},{16,24},{24,16},{32,40},{40,32},{48,56},{56,48},{64,72... | collective-permute-start | bytes 98312 | tf_op jit(solution)/shard_map/ppermute | solution.py:30
  249.9 5.5 %collective-permute-start.11 = (f32[2,4096]{1,0:T(2,128)S(1)}, f32[2,4096]{1,0:T(2,128)S(1)}, u32[]{:S(2)}, u32[]{:S(2)}) collective-permute-start(f32[2,4096]{1,0:T(2,128)S(1)} %pad_maximum_fusion.5), channel_id=1, source_target_pairs={{0,16},{8,24},{16,0},{24,8},{32,48},{40,56},{48,32},{56,40},{64,80... | collective-permute-start | bytes 98312 | tf_op jit(solution)/shard_map/ppermute | solution.py:30
  255.5 4.0 %collective-permute-start.12 = (f32[2,4096]{1,0:T(2,128)S(1)}, f32[2,4096]{1,0:T(2,128)S(1)}, u32[]{:S(2)}, u32[]{:S(2)}) collective-permute-start(f32[2,4096]{1,0:T(2,128)S(1)} %pad_maximum_fusion.6), channel_id=1, source_target_pairs={{0,32},{8,40},{16,48},{24,56},{32,0},{40,8},{48,16},{56,24},{64,96... | collective-permute-start | bytes 98312 | tf_op jit(solution)/shard_map/ppermute | solution.py:30
  259.6 5.5 %collective-permute-start.13 = (f32[2,4096]{1,0:T(2,128)S(1)}, f32[2,4096]{1,0:T(2,128)S(1)}, u32[]{:S(2)}, u32[]{:S(2)}) collective-permute-start(f32[2,4096]{1,0:T(2,128)S(1)} %pad_maximum_fusion.7), channel_id=1, source_target_pairs={{0,64},{8,72},{16,80},{24,88},{32,96},{40,104},{48,112},{56,120},{... | collective-permute-start | bytes 98312 | tf_op jit(solution)/shard_map/ppermute | solution.py:30
  277.4 1.3 collective-permute-start.14
  278.7 3.8 %collective-permute-start.15 = (f32[2,2048]{1,0:T(2,128)S(1)}, f32[2,2048]{1,0:T(2,128)S(1)}, u32[]{:S(2)}, u32[]{:S(2)}) collective-permute-start(f32[2,2048]{1,0:T(2,128)S(1)} %pad_maximum_fusion.19), channel_id=1, source_target_pairs={{0,2},{1,3},{2,0},{3,1},{4,6},{5,7},{6,4},{7,5},{8,10},{9,11},{10,... | collective-permute-start | bytes 49160 | tf_op jit(solution)/shard_map/ppermute | solution.py:30
  282.6 5.5 %collective-permute-start.16 = (f32[2,2048]{1,0:T(2,128)S(1)}, f32[2,2048]{1,0:T(2,128)S(1)}, u32[]{:S(2)}, u32[]{:S(2)}) collective-permute-start(f32[2,2048]{1,0:T(2,128)S(1)} %pad_maximum_fusion.20), channel_id=1, source_target_pairs={{0,4},{1,5},{2,6},{3,7},{4,0},{5,1},{6,2},{7,3},{8,12},{9,13},{10,... | collective-permute-start | bytes 49160 | tf_op jit(solution)/shard_map/ppermute | solution.py:30
  288.2 12.7 %copy-start = (f32[2048]{0:T(1024)}, f32[2048]{0:T(1024)S(1)}, u32[]{:S(2)}) copy-start(f32[2048]{0:T(1024)S(1)} %multiply_subtract_fusion.4) | copy-start | bytes 24580
  301.0 4.0 %collective-permute-start.17 = (f32[2,4096]{1,0:T(2,128)S(1)}, f32[2,4096]{1,0:T(2,128)S(1)}, u32[]{:S(2)}, u32[]{:S(2)}) collective-permute-start(f32[2,4096]{1,0:T(2,128)S(1)} %pad_maximum_fusion.8), channel_id=1, source_target_pairs={{0,8},{8,0},{16,24},{24,16},{32,40},{40,32},{48,56},{56,48},{64,72... | collective-permute-start | bytes 98312 | tf_op jit(solution)/shard_map/ppermute | solution.py:30
  305.1 5.5 %collective-permute-start.18 = (f32[2,4096]{1,0:T(2,128)S(1)}, f32[2,4096]{1,0:T(2,128)S(1)}, u32[]{:S(2)}, u32[]{:S(2)}) collective-permute-start(f32[2,4096]{1,0:T(2,128)S(1)} %pad_maximum_fusion.9), channel_id=1, source_target_pairs={{0,16},{8,24},{16,0},{24,8},{32,48},{40,56},{48,32},{56,40},{64,80... | collective-permute-start | bytes 98312 | tf_op jit(solution)/shard_map/ppermute | solution.py:30
  310.7 4.0 %collective-permute-start.19 = (f32[2,4096]{1,0:T(2,128)S(1)}, f32[2,4096]{1,0:T(2,128)S(1)}, u32[]{:S(2)}, u32[]{:S(2)}) collective-permute-start(f32[2,4096]{1,0:T(2,128)S(1)} %pad_maximum_fusion.10), channel_id=1, source_target_pairs={{0,32},{8,40},{16,48},{24,56},{32,0},{40,8},{48,16},{56,24},{64,96... | collective-permute-start | bytes 98312 | tf_op jit(solution)/shard_map/ppermute | solution.py:30
  314.8 5.5 %collective-permute-start.20 = (f32[2,4096]{1,0:T(2,128)S(1)}, f32[2,4096]{1,0:T(2,128)S(1)}, u32[]{:S(2)}, u32[]{:S(2)}) collective-permute-start(f32[2,4096]{1,0:T(2,128)S(1)} %pad_maximum_fusion.11), channel_id=1, source_target_pairs={{0,64},{8,72},{16,80},{24,88},{32,96},{40,104},{48,112},{56,120},{... | collective-permute-start | bytes 98312 | tf_op jit(solution)/shard_map/ppermute | solution.py:30
Sparse Core Ops, SparseCore 0:
  9.7 27.7 all-gather.2
  39.6 51.9 all-gather.4

commit v2 on v1

--- a/solution.py
+++ b/solution.py
@@ -21,30 +21,68 @@
     return left_norms[:, None] + right_norms[None, :] - 2.0 * inner
 
 
-def combine_over(peak, total, axis):
+def digit_partners(axis, size, stride, width, shift):
+    perm = []
+    for i in range(size):
+        p = (i // stride) % width
+        perm.append((i, i + (((p + shift) % width) - p) * stride))
+    return perm
+
+
+def exchange(x, axis, stride, width):
     size = lax.axis_size(axis)
+    pos = (lax.axis_index(axis) // stride) % width
+    received = [x] + [lax.ppermute(x, axis, digit_partners(axis, size, stride, width, k)) for k in range(1, width)]
+    stacked = jnp.stack(received)
+    return [lax.dynamic_index_in_dim(stacked, (pos - q) % width, 0, keepdims=False) for q in range(width)]
+
+
+def combine_over(peak, total, axis, digits):
     packed = jnp.stack([peak, total])
-    step = 1
-    while step < size:
-        perm = [(i, i ^ step) for i in range(size)]
-        other = lax.ppermute(packed, axis, perm)
-        new_peak = jnp.maximum(packed[0], other[0])
-        new_total = packed[1] * jnp.exp(packed[0] - new_peak) + other[1] * jnp.exp(other[0] - new_peak)
+    stride = 1
+    for width in digits:
+        parts = exchange(packed, axis, stride, width)
+        new_peak = parts[0][0]
+        for part in parts[1:]:
+            new_peak = jnp.maximum(new_peak, part[0])
+        new_total = parts[0][1] * jnp.exp(parts[0][0] - new_peak)
+        for part in parts[1:]:
+            new_total = new_total + part[1] * jnp.exp(part[0] - new_peak)
         packed = jnp.stack([new_peak, new_total])
-        step *= 2
+        stride *= width
     return packed[0] + jnp.log(packed[1])
+
+
+def radix_digits(size):
+    digits = []
+    while size > 1:
+        width = 4 if size % 4 == 0 else 2
+        digits.append(width)
+        size //= width
+    return tuple(digits)
+
+
+def col_digits(size):
+    if size % 2 == 0:
+        return (2,) + radix_digits(size // 2)
+    return radix_digits(size)
 
 
 def logsum_col(scores):
     peak = jnp.max(scores, axis=1)
     totals = jnp.sum(jnp.exp(scores - peak[:, None]), axis=1)
-    return combine_over(peak, totals, "col")
+    return combine_over(peak, totals, "col", col_digits(lax.axis_size("col")))
 
 
 def logsum_row(scores):
     peak = jnp.max(scores, axis=0)
     totals = jnp.sum(jnp.exp(scores - peak[None, :]), axis=0)
-    return combine_over(peak, totals, "row")
+    return combine_over(peak, totals, "row", radix_digits(lax.axis_size("row")))
+
+
+def gather_col(x):
+    size = lax.axis_size("col")
+    return jnp.concatenate(exchange(x, "col", 1, size), axis=0)
 
 
 def per_device(queries, passages, mean_cost):
@@ -53,7 +91,7 @@
     col_count = lax.axis_size("col")
     all_queries = queries.shape[0] * row_count * col_count
     all_passages = passages.shape[0] * row_count * col_count
-    query_block = lax.all_gather(queries, "col", axis=0, tiled=True)
+    query_block = gather_col(queries)
     cost_tile = inner_costs(query_block, lax.all_gather(passages, "row", axis=0, tiled=True))
     col_potential = jnp.zeros((cost_tile.shape[1],), jnp.float32)
     row_potential = jnp.zeros((cost_tile.shape[0],), jnp.float32)

time: 328 us -> 301 us (0.918)
  waiting for transfers between devices: 126 us -> 81 us
  other arithmetic: 103 us -> 117 us
    all_gather x1 -> x0, waiting for transfers between devices: 28.2 us -> none  [per_device(): query_block = lax.all_gather(queries, 'col', axis=0, tiled=True)]
    all_gather x1, waiting for transfers between devices: 52.2 us -> 27.3 us  [per_device(): lax.all_gather(passages, 'row', axis=0, tiled=True)]
    reduce_max x2, other arithmetic: 7.99 us -> 19.7 us  [logsum_col(): peak = jnp.max(scores, axis=1)]
    ppermute x21 -> x37, waiting for transfers between devices: 44.8 us -> 53 us  [exchange(): lax.ppermute(x, axis, digit_partners(axis, size, stride, width, k))]
    reduce_sum x3, other arithmetic: 30.9 us -> 39.2 us  [logsum_col(): totals = jnp.sum(jnp.exp(scores - peak[:, None]), axis=1)]
    ppermute x21 -> x37, starting transfers between devices: 43.8 us -> 44.4 us  [exchange(): lax.ppermute(x, axis, digit_partners(axis, size, stride, width, k))]
  transfers between devices with their start and end apart: 23 -> 38, of which waited for: 23 -> 35; matrix products, arithmetic and copies ran while one was open for 1% -> 1% of each run, Pallas kernels for 0% -> 0%
where the time goes in v2:
time: 301 us; the launch traced here: 300 us
  other arithmetic  117 us (39%)
  waiting for transfers between devices  81 us (27%)
  starting transfers between devices  44.4 us (15%)
  matrix products  38.8 us (13%)
  between operations  15.5 us (5%)
  local copies, waits for them, and re-layouts  3.27 us (1%)
    ppermute x37, waiting for transfers between devices, exchange(): lax.ppermute(x, axis, digit_partners(axis, size, stride, width, k))  53 us
    ppermute x37, starting transfers between devices, exchange(): lax.ppermute(x, axis, digit_partners(axis, size, stride, width, k))  44.4 us
    reduce_sum x3, other arithmetic, logsum_col(): totals = jnp.sum(jnp.exp(scores - peak[:, None]), axis=1)  39.2 us
    dot_general x1, matrix products, inner_costs(): lax.dot_general(left, right, (((1,), (1,)), ((), ())), precision=lax.Prec...  38.8 us
    reduce_sum x3, other arithmetic, logsum_row(): totals = jnp.sum(jnp.exp(scores - peak[None, :]), axis=0)  29.7 us
    all_gather x1, waiting for transfers between devices, per_device(): lax.all_gather(passages, 'row', axis=0, tiled=True)  27.3 us
    reduce_max x3, other arithmetic, logsum_row(): peak = jnp.max(scores, axis=0)  23.2 us
    reduce_max x2, other arithmetic, logsum_col(): peak = jnp.max(scores, axis=1)  19.7 us
  transfers between devices with their start and end apart: 38, of which 35 were waited for; matrix products, arithmetic and copies ran while one was open for 1% of the time, Pallas kernels for 0%

profile of v2, /device:TPU:0, one launch (start us, length us, event | category | flops | bytes accessed | tf_op | source)
XLA Modules:
  0.0 300.2 jit_solution(9306308177571397797)
XLA Ops:
  7.9 1.7 collective-permute-start.1
  9.6 2.0 collective-permute-start.2
  11.6 2.0 collective-permute-start.3
  13.7 1.6 collective-permute-start.4
  17.3 1.7 collective-permute-start.5
  19.0 5.3 %collective-permute-start.6 = (f32[256,256]{1,0:T(8,128)}, f32[256,256]{1,0:T(8,128)S(1)}, u32[]{:S(2)}, u32[]{:S(2)}) collective-permute-start(f32[256,256]{1,0:T(8,128)} %param.3), channel_id=1, source_target_pairs={{0,7},{1,0},{2,1},{3,2},{4,3},{5,4},{6,5},{7,6},{8,15},{9,8},{10,9... | collective-permute-start | bytes 786440 | tf_op jit(solution)/shard_map/ppermute | solution.py:35
  24.3 5.3 %collective-permute-done.2 = f32[256,256]{1,0:T(8,128)S(1)} collective-permute-done((f32[256,256]{1,0:T(8,128)}, f32[256,256]{1,0:T(8,128)S(1)}, u32[]{:S(2)}, u32[]{:S(2)}) %collective-permute-start.2) | collective-permute-done | bytes 262176 | tf_op jit(solution)/shard_map/ppermute | solution.py:35
  29.6 1.3 collective-permute-done.3
  30.9 1.9 collective-permute-done.4
  33.0 1.8 collective-permute-done.6
  35.1 1.3 copy-done
  36.8 27.3 %all-gather.2.cloned.1.call-done = f32[4096,256]{1,0:T(8,128)} async-done(((f32[256,256]{1,0:T(8,128)}), f32[4096,256]{1,0:T(8,128)}) %all-gather.2.cloned.1.call-update) | async-done | bytes 4194320 | tf_op jit(solution)/shard_map/all_gather | solution.py:95
  64.1 2.8 multiply_reduce_fusion
  66.9 38.8 %fusion = (f32[2048]{0:T(1024)S(1)}, f32[2048,4096]{1,0:T(8,128)}) fusion(f32[]{:T(128)} %bitcast, f32[2048,256]{1,0:T(8,128)} %copy-done, f32[4096,256]{1,0:T(8,128)} %all-gather.2.cloned.1.call-done, f32[4096]{0:T(1024)S(1)} %multiply_reduce_fusion, f32[2048]{0:T(1024)S(1)} %multiply_reduce_fusion.1), kind=kOutput, calls=%fused_computation.13 | convolution fusion | flops 25820133376 | bytes 39878660 | tf_op jit(solution)/shard_map/dot_general | solution.py:14
  105.7 14.5 %exponential_reduce_fusion.5 = f32[2048]{0:T(1024)S(1)} fusion(f32[2048]{0:T(1024)S(1)} %get-tuple-element.92, f32[]{:T(128)} %bitcast, f32[2048,4096]{1,0:T(8,128)} %get-tuple-element.93), kind=kLoop, calls=%fused_computation.10 | loop fusion | flops 33552384 | bytes 33570820 | tf_op jit(solution)/shard_map/reduce_sum | solution.py:73
  120.4 1.1 collective-permute-done.7
  121.6 2.8 collective-permute-start.10
  126.1 3.5 %collective-permute-done.9 = f32[2,2048]{1,0:T(2,128)S(1)} collective-permute-done((f32[2,2048]{1,0:T(2,128)S(1)}, f32[2,2048]{1,0:T(2,128)S(1)}, u32[]{:S(2)}, u32[]{:S(2)}) %collective-permute-start.9) | collective-permute-done | bytes 16416 | tf_op jit(solution)/shard_map/ppermute | solution.py:35
  130.3 13.1 %fusion.3 = f32[4096]{0:T(1024)S(1)} fusion(f32[]{:T(128)} %bitcast, f32[2048,4096]{1,0:T(8,128)} %get-tuple-element.93, f32[2048]{0:T(1024)S(1)} %multiply_subtract_fusion.6), kind=kLoop, calls=%fused_computation.17 | loop fusion | flops 25161728 | bytes 33579012 | tf_op jit(solution)/shard_map/reduce_max | solution.py:78
  143.5 14.4 %exponential_reduce_fusion.4 = f32[4096]{0:T(1024)S(1)} fusion(f32[4096]{0:T(1024)S(1)} %fusion.3, f32[]{:T(128)} %bitcast, f32[2048,4096]{1,0:T(8,128)} %get-tuple-element.93, f32[2048]{0:T(1024)S(1)} %multiply_subtract_fusion.6), kind=kLoop, calls=%fused_computation.8 | loop fusion | flops 33550336 | bytes 33595396 | tf_op jit(solution)/shard_map/reduce_sum | solution.py:79
  157.9 2.8 collective-permute-start.13
  162.4 3.7 %collective-permute-done.12 = f32[2,4096]{1,0:T(2,128)S(1)} collective-permute-done((f32[2,4096]{1,0:T(2,128)S(1)}, f32[2,4096]{1,0:T(2,128)S(1)}, u32[]{:S(2)}, u32[]{:S(2)}) %collective-permute-start.12) | collective-permute-done | bytes 32800 | tf_op jit(solution)/shard_map/ppermute | solution.py:35
  166.9 1.5 collective-permute-start.16
  170.9 3.0 collective-permute-done.15
  174.6 15.7 %fusion.1 = f32[2048]{0:T(1024)S(1)} fusion(f32[]{:T(128)} %bitcast, f32[2048,4096]{1,0:T(8,128)} %get-tuple-element.93, f32[4096]{0:T(1024)S(1)} %multiply_subtract_fusion.3), kind=kLoop, calls=%fused_computation.14 | loop fusion | flops 25163776 | bytes 33579012 | tf_op jit(solution)/shard_map/reduce_max | solution.py:72
  190.4 16.6 %exponential_reduce_fusion.3 = f32[2048]{0:T(1024)S(1)} fusion(f32[2048]{0:T(1024)S(1)} %fusion.1, f32[]{:T(128)} %bitcast, f32[2048,4096]{1,0:T(8,128)} %get-tuple-element.93, f32[4096]{0:T(1024)S(1)} %multiply_subtract_fusion.3), kind=kLoop, calls=%fused_computation.6 | loop fusion | flops 33552384 | bytes 33587204 | tf_op jit(solution)/shard_map/reduce_sum | solution.py:73
  207.1 1.2 collective-permute-done.17
  208.8 1.4 collective-permute-start.19
  210.2 1.2 collective-permute-start.18
  212.2 1.9 collective-permute-done.19
  215.4 5.0 %fusion.4 = f32[4096]{0:T(1024)S(1)} fusion(f32[]{:T(128)} %bitcast, f32[2048,4096]{1,0:T(8,128)S(1)} %bitcast.408, f32[2048]{0:T(1024)S(1)} %multiply_subtract_fusion.5), kind=kLoop, calls=%fused_computation.18 | loop fusion | flops 25161728 | bytes 33579012 | tf_op jit(solution)/shard_map/reduce_max | solution.py:78
  220.4 7.6 %exponential_reduce_fusion.2 = f32[4096]{0:T(1024)S(1)} fusion(f32[4096]{0:T(1024)S(1)} %fusion.4, f32[]{:T(128)} %bitcast, f32[2048,4096]{1,0:T(8,128)S(1)} %bitcast.408, f32[2048]{0:T(1024)S(1)} %multiply_subtract_fusion.5), kind=kLoop, calls=%fused_computation.4 | loop fusion | flops 33550336 | bytes 33595396 | tf_op jit(solution)/shard_map/reduce_sum | solution.py:79
  228.1 1.2 collective-permute-start.23
  232.1 2.6 collective-permute-done.22
  237.5 1.2 collective-permute-start.24
  239.6 2.5 collective-permute-done.25
  242.9 4.0 %fusion.2 = f32[2048]{0:T(1024)S(1)} fusion(f32[]{:T(128)} %bitcast, f32[2048,4096]{1,0:T(8,128)S(1)} %bitcast.408, f32[4096]{0:T(1024)S(1)} %multiply_subtract_fusion.2), kind=kLoop, calls=%fused_computation.15 | loop fusion | flops 25163776 | bytes 33579012 | tf_op jit(solution)/shard_map/reduce_max | solution.py:72
  246.9 8.0 %exponential_reduce_fusion.1 = f32[2048]{0:T(1024)S(1)} fusion(f32[2048]{0:T(1024)S(1)} %fusion.2, f32[]{:T(128)} %bitcast, f32[2048,4096]{1,0:T(8,128)S(1)} %bitcast.408, f32[4096]{0:T(1024)S(1)} %multiply_subtract_fusion.2), kind=kLoop, calls=%fused_computation.2 | loop fusion | flops 33552384 | bytes 33587204 | tf_op jit(solution)/shard_map/reduce_sum | solution.py:73
  255.1 1.2 collective-permute-done.27
  256.4 1.8 collective-permute-start.30
  260.2 3.2 %collective-permute-done.29 = f32[2,2048]{1,0:T(2,128)S(1)} collective-permute-done((f32[2,2048]{1,0:T(2,128)S(1)}, f32[2,2048]{1,0:T(2,128)S(1)}, u32[]{:S(2)}, u32[]{:S(2)}) %collective-permute-start.29) | collective-permute-done | bytes 16416 | tf_op jit(solution)/shard_map/ppermute | solution.py:35
  264.2 5.0 %fusion.5 = f32[4096]{0:T(1024)S(1)} fusion(f32[]{:T(128)} %bitcast, f32[2048,4096]{1,0:T(8,128)S(1)} %bitcast.408, f32[2048]{0:T(1024)S(1)} %multiply_subtract_fusion.4), kind=kLoop, calls=%fused_computation.19 | loop fusion | flops 25161728 | bytes 33579012 | tf_op jit(solution)/shard_map/reduce_max | solution.py:78
  269.3 7.6 %exponential_reduce_fusion = f32[4096]{0:T(1024)S(1)} fusion(f32[4096]{0:T(1024)S(1)} %fusion.5, f32[]{:T(128)} %bitcast, f32[2048,4096]{1,0:T(8,128)S(1)} %bitcast.408, f32[2048]{0:T(1024)S(1)} %multiply_subtract_fusion.4), kind=kLoop, calls=%fused_computation | loop fusion | flops 33550336 | bytes 33595396 | tf_op jit(solution)/shard_map/reduce_sum | solution.py:79
  277.0 1.8 collective-permute-start.33
  279.8 1.2 collective-permute-done.33
  280.9 3.3 %collective-permute-done.32 = f32[2,4096]{1,0:T(2,128)S(1)} collective-permute-done((f32[2,4096]{1,0:T(2,128)S(1)}, f32[2,4096]{1,0:T(2,128)S(1)}, u32[]{:S(2)}, u32[]{:S(2)}) %collective-permute-start.32) | collective-permute-done | bytes 32800 | tf_op jit(solution)/shard_map/ppermute | solution.py:35
  285.1 1.4 collective-permute-start.36
  289.1 2.8 collective-permute-done.35
  (122 shorter events, 29.8 us)
Async XLA Ops:
  7.2 57.0 %all-gather.2.cloned.1.call-start = ((), (), s32[]{:S(2)}) async-start(), calls=%async_computation | async-start | bytes 4456448 | tf_op jit(solution)/shard_map/all_gather | solution.py:95
  7.9 9.4 %collective-permute-start = (f32[256,256]{1,0:T(8,128)}, f32[256,256]{1,0:T(8,128)S(1)}, u32[]{:S(2)}, u32[]{:S(2)}) collective-permute-start(f32[256,256]{1,0:T(8,128)} %param.3), channel_id=1, source_target_pairs={{0,1},{1,2},{2,3},{3,4},{4,5},{5,6},{6,7},{7,0},{8,9},{9,10},{10,1... | collective-permute-start | bytes 786440 | tf_op jit(solution)/shard_map/ppermute | solution.py:35
  7.9 11.0 %collective-permute-start.1 = (f32[256,256]{1,0:T(8,128)}, f32[256,256]{1,0:T(8,128)S(1)}, u32[]{:S(2)}, u32[]{:S(2)}) collective-permute-start(f32[256,256]{1,0:T(8,128)} %param.3), channel_id=1, source_target_pairs={{0,2},{1,3},{2,4},{3,5},{4,6},{5,7},{6,0},{7,1},{8,10},{9,11},{10,... | collective-permute-start | bytes 786440 | tf_op jit(solution)/shard_map/ppermute | solution.py:35
  9.6 20.0 %collective-permute-start.2 = (f32[256,256]{1,0:T(8,128)}, f32[256,256]{1,0:T(8,128)S(1)}, u32[]{:S(2)}, u32[]{:S(2)}) collective-permute-start(f32[256,256]{1,0:T(8,128)} %param.3), channel_id=1, source_target_pairs={{0,3},{1,4},{2,5},{3,6},{4,7},{5,0},{6,1},{7,2},{8,11},{9,12},{10,... | collective-permute-start | bytes 786440 | tf_op jit(solution)/shard_map/ppermute | solution.py:35
  11.6 19.3 %collective-permute-start.3 = (f32[256,256]{1,0:T(8,128)}, f32[256,256]{1,0:T(8,128)S(1)}, u32[]{:S(2)}, u32[]{:S(2)}) collective-permute-start(f32[256,256]{1,0:T(8,128)} %param.3), channel_id=1, source_target_pairs={{0,4},{1,5},{2,6},{3,7},{4,0},{5,1},{6,2},{7,3},{8,12},{9,13},{10,... | collective-permute-start | bytes 786440 | tf_op jit(solution)/shard_map/ppermute | solution.py:35
  13.7 19.2 %collective-permute-start.4 = (f32[256,256]{1,0:T(8,128)}, f32[256,256]{1,0:T(8,128)S(1)}, u32[]{:S(2)}, u32[]{:S(2)}) collective-permute-start(f32[256,256]{1,0:T(8,128)} %param.3), channel_id=1, source_target_pairs={{0,5},{1,6},{2,7},{3,0},{4,1},{5,2},{6,3},{7,4},{8,13},{9,14},{10,... | collective-permute-start | bytes 786440 | tf_op jit(solution)/shard_map/ppermute | solution.py:35
  17.3 15.7 %collective-permute-start.5 = (f32[256,256]{1,0:T(8,128)}, f32[256,256]{1,0:T(8,128)S(1)}, u32[]{:S(2)}, u32[]{:S(2)}) collective-permute-start(f32[256,256]{1,0:T(8,128)} %param.3), channel_id=1, source_target_pairs={{0,6},{1,7},{2,0},{3,1},{4,2},{5,3},{6,4},{7,5},{8,14},{9,15},{10,... | collective-permute-start | bytes 786440 | tf_op jit(solution)/shard_map/ppermute | solution.py:35
  19.0 15.9 %collective-permute-start.6 = (f32[256,256]{1,0:T(8,128)}, f32[256,256]{1,0:T(8,128)S(1)}, u32[]{:S(2)}, u32[]{:S(2)}) collective-permute-start(f32[256,256]{1,0:T(8,128)} %param.3), channel_id=1, source_target_pairs={{0,7},{1,0},{2,1},{3,2},{4,3},{5,4},{6,5},{7,6},{8,15},{9,8},{10,9... | collective-permute-start | bytes 786440 | tf_op jit(solution)/shard_map/ppermute | solution.py:35
  35.1 1.3 copy-start
  120.2 1.3 collective-permute-start.7
  121.6 4.5 %collective-permute-start.10 = (f32[2,2048]{1,0:T(2,128)S(1)}, f32[2,2048]{1,0:T(2,128)S(1)}, u32[]{:S(2)}, u32[]{:S(2)}) collective-permute-start(f32[2,2048]{1,0:T(2,128)S(1)} %get-tuple-element.89), channel_id=1, source_target_pairs={{0,6},{1,7},{2,0},{3,1},{4,2},{5,3},{6,4},{7,5},{8,14},{9,15},{10,... | collective-permute-start | bytes 49160 | tf_op jit(solution)/shard_map/ppermute | solution.py:35
  124.4 5.2 %collective-permute-start.9 = (f32[2,2048]{1,0:T(2,128)S(1)}, f32[2,2048]{1,0:T(2,128)S(1)}, u32[]{:S(2)}, u32[]{:S(2)}) collective-permute-start(f32[2,2048]{1,0:T(2,128)S(1)} %get-tuple-element.89), channel_id=1, source_target_pairs={{0,4},{1,5},{2,6},{3,7},{4,0},{5,1},{6,2},{7,3},{8,12},{9,13},{10,... | collective-permute-start | bytes 49160 | tf_op jit(solution)/shard_map/ppermute | solution.py:35
  125.2 4.9 %collective-permute-start.8 = (f32[2,2048]{1,0:T(2,128)S(1)}, f32[2,2048]{1,0:T(2,128)S(1)}, u32[]{:S(2)}, u32[]{:S(2)}) collective-permute-start(f32[2,2048]{1,0:T(2,128)S(1)} %get-tuple-element.89), channel_id=1, source_target_pairs={{0,2},{1,3},{2,4},{3,5},{4,6},{5,7},{6,0},{7,1},{8,10},{9,11},{10,... | collective-permute-start | bytes 49160 | tf_op jit(solution)/shard_map/ppermute | solution.py:35
  157.9 4.5 %collective-permute-start.13 = (f32[2,4096]{1,0:T(2,128)S(1)}, f32[2,4096]{1,0:T(2,128)S(1)}, u32[]{:S(2)}, u32[]{:S(2)}) collective-permute-start(f32[2,4096]{1,0:T(2,128)S(1)} %get-tuple-element.77), channel_id=1, source_target_pairs={{0,24},{8,0},{16,8},{24,16},{32,56},{40,32},{48,40},{56,48},{64,88... | collective-permute-start | bytes 98312 | tf_op jit(solution)/shard_map/ppermute | solution.py:35
  160.7 5.4 %collective-permute-start.12 = (f32[2,4096]{1,0:T(2,128)S(1)}, f32[2,4096]{1,0:T(2,128)S(1)}, u32[]{:S(2)}, u32[]{:S(2)}) collective-permute-start(f32[2,4096]{1,0:T(2,128)S(1)} %get-tuple-element.77), channel_id=1, source_target_pairs={{0,16},{8,24},{16,0},{24,8},{32,48},{40,56},{48,32},{56,40},{64,80... | collective-permute-start | bytes 98312 | tf_op jit(solution)/shard_map/ppermute | solution.py:35
  161.5 5.1 %collective-permute-start.11 = (f32[2,4096]{1,0:T(2,128)S(1)}, f32[2,4096]{1,0:T(2,128)S(1)}, u32[]{:S(2)}, u32[]{:S(2)}) collective-permute-start(f32[2,4096]{1,0:T(2,128)S(1)} %get-tuple-element.77), channel_id=1, source_target_pairs={{0,8},{8,16},{16,24},{24,0},{32,40},{40,48},{48,56},{56,32},{64,72... | collective-permute-start | bytes 98312 | tf_op jit(solution)/shard_map/ppermute | solution.py:35
  166.9 4.0 %collective-permute-start.16 = (f32[2,4096]{1,0:T(2,128)S(1)}, f32[2,4096]{1,0:T(2,128)S(1)}, u32[]{:S(2)}, u32[]{:S(2)}) collective-permute-start(f32[2,4096]{1,0:T(2,128)S(1)} %get-tuple-element.75), channel_id=1, source_target_pairs={{0,96},{8,104},{16,112},{24,120},{32,0},{40,8},{48,16},{56,24},{64... | collective-permute-start | bytes 98312 | tf_op jit(solution)/shard_map/ppermute | solution.py:35
  168.5 5.4 %collective-permute-start.15 = (f32[2,4096]{1,0:T(2,128)S(1)}, f32[2,4096]{1,0:T(2,128)S(1)}, u32[]{:S(2)}, u32[]{:S(2)}) collective-permute-start(f32[2,4096]{1,0:T(2,128)S(1)} %get-tuple-element.75), channel_id=1, source_target_pairs={{0,64},{8,72},{16,80},{24,88},{32,96},{40,104},{48,112},{56,120},{... | collective-permute-start | bytes 98312 | tf_op jit(solution)/shard_map/ppermute | solution.py:35
  169.2 5.1 %collective-permute-start.14 = (f32[2,4096]{1,0:T(2,128)S(1)}, f32[2,4096]{1,0:T(2,128)S(1)}, u32[]{:S(2)}, u32[]{:S(2)}) collective-permute-start(f32[2,4096]{1,0:T(2,128)S(1)} %get-tuple-element.75), channel_id=1, source_target_pairs={{0,32},{8,40},{16,48},{24,56},{32,64},{40,72},{48,80},{56,88},{64,... | collective-permute-start | bytes 98312 | tf_op jit(solution)/shard_map/ppermute | solution.py:35
  174.6 40.7 %slice-start = ((s8[33554432]{0:T(1024)(128)(4,1)}), s8[4194304]{0:T(1024)(128)(4,1)S(1)}, s32[]{:S(2)}) async-start(s8[33554432]{0:T(1024)(128)(4,1)} %bitcast.407), calls=%async_computation.1 | async-start | bytes 8388608
  174.6 40.7 %slice-start.1 = ((s8[33554432]{0:T(1024)(128)(4,1)}), s8[4194304]{0:T(1024)(128)(4,1)S(1)}, s32[]{:S(2)}) async-start(s8[33554432]{0:T(1024)(128)(4,1)} %bitcast.407), calls=%async_computation.2 | async-start | bytes 8388608
  174.6 40.7 %slice-start.2 = ((s8[33554432]{0:T(1024)(128)(4,1)}), s8[4194304]{0:T(1024)(128)(4,1)S(1)}, s32[]{:S(2)}) async-start(s8[33554432]{0:T(1024)(128)(4,1)} %bitcast.407), calls=%async_computation.3 | async-start | bytes 8388608
  174.6 40.7 %slice-start.3 = ((s8[33554432]{0:T(1024)(128)(4,1)}), s8[4194304]{0:T(1024)(128)(4,1)S(1)}, s32[]{:S(2)}) async-start(s8[33554432]{0:T(1024)(128)(4,1)} %bitcast.407), calls=%async_computation.4 | async-start | bytes 8388608
  190.4 25.0 %slice-start.4 = ((s8[33554432]{0:T(1024)(128)(4,1)}), s8[4194304]{0:T(1024)(128)(4,1)S(1)}, s32[]{:S(2)}) async-start(s8[33554432]{0:T(1024)(128)(4,1)} %bitcast.407), calls=%async_computation.5 | async-start | bytes 8388608
  190.4 25.0 %slice-start.5 = ((s8[33554432]{0:T(1024)(128)(4,1)}), s8[4194304]{0:T(1024)(128)(4,1)S(1)}, s32[]{:S(2)}) async-start(s8[33554432]{0:T(1024)(128)(4,1)} %bitcast.407), calls=%async_computation.6 | async-start | bytes 8388608
  190.4 25.0 %slice-start.6 = ((s8[33554432]{0:T(1024)(128)(4,1)}), s8[4194304]{0:T(1024)(128)(4,1)S(1)}, s32[]{:S(2)}) async-start(s8[33554432]{0:T(1024)(128)(4,1)} %bitcast.407), calls=%async_computation.7 | async-start | bytes 8388608
  190.4 25.0 %slice-start.7 = ((s8[33554432]{0:T(1024)(128)(4,1)}), s8[4194304]{0:T(1024)(128)(4,1)S(1)}, s32[]{:S(2)}) async-start(s8[33554432]{0:T(1024)(128)(4,1)} %bitcast.407), calls=%async_computation.8 | async-start | bytes 8388608
  207.0 1.3 collective-permute-start.17
  208.4 3.8 %collective-permute-start.20 = (f32[2,2048]{1,0:T(2,128)S(1)}, f32[2,2048]{1,0:T(2,128)S(1)}, u32[]{:S(2)}, u32[]{:S(2)}) collective-permute-start(f32[2,2048]{1,0:T(2,128)S(1)} %get-tuple-element.85), channel_id=1, source_target_pairs={{0,6},{1,7},{2,0},{3,1},{4,2},{5,3},{6,4},{7,5},{8,14},{9,15},{10,... | collective-permute-start | bytes 49160 | tf_op jit(solution)/shard_map/ppermute | solution.py:35
  208.8 5.3 %collective-permute-start.19 = (f32[2,2048]{1,0:T(2,128)S(1)}, f32[2,2048]{1,0:T(2,128)S(1)}, u32[]{:S(2)}, u32[]{:S(2)}) collective-permute-start(f32[2,2048]{1,0:T(2,128)S(1)} %get-tuple-element.85), channel_id=1, source_target_pairs={{0,4},{1,5},{2,6},{3,7},{4,0},{5,1},{6,2},{7,3},{8,12},{9,13},{10,... | collective-permute-start | bytes 49160 | tf_op jit(solution)/shard_map/ppermute | solution.py:35
  210.2 4.9 %collective-permute-start.18 = (f32[2,2048]{1,0:T(2,128)S(1)}, f32[2,2048]{1,0:T(2,128)S(1)}, u32[]{:S(2)}, u32[]{:S(2)}) collective-permute-start(f32[2,2048]{1,0:T(2,128)S(1)} %get-tuple-element.85), channel_id=1, source_target_pairs={{0,2},{1,3},{2,4},{3,5},{4,6},{5,7},{6,0},{7,1},{8,10},{9,11},{10,... | collective-permute-start | bytes 49160 | tf_op jit(solution)/shard_map/ppermute | solution.py:35
  228.1 4.0 %collective-permute-start.23 = (f32[2,4096]{1,0:T(2,128)S(1)}, f32[2,4096]{1,0:T(2,128)S(1)}, u32[]{:S(2)}, u32[]{:S(2)}) collective-permute-start(f32[2,4096]{1,0:T(2,128)S(1)} %get-tuple-element.71), channel_id=1, source_target_pairs={{0,24},{8,0},{16,8},{24,16},{32,56},{40,32},{48,40},{56,48},{64,88... | collective-permute-start | bytes 98312 | tf_op jit(solution)/shard_map/ppermute | solution.py:35
  229.3 5.4 %collective-permute-start.22 = (f32[2,4096]{1,0:T(2,128)S(1)}, f32[2,4096]{1,0:T(2,128)S(1)}, u32[]{:S(2)}, u32[]{:S(2)}) collective-permute-start(f32[2,4096]{1,0:T(2,128)S(1)} %get-tuple-element.71), channel_id=1, source_target_pairs={{0,16},{8,24},{16,0},{24,8},{32,48},{40,56},{48,32},{56,40},{64,80... | collective-permute-start | bytes 98312 | tf_op jit(solution)/shard_map/ppermute | solution.py:35
  230.2 5.1 %collective-permute-start.21 = (f32[2,4096]{1,0:T(2,128)S(1)}, f32[2,4096]{1,0:T(2,128)S(1)}, u32[]{:S(2)}, u32[]{:S(2)}) collective-permute-start(f32[2,4096]{1,0:T(2,128)S(1)} %get-tuple-element.71), channel_id=1, source_target_pairs={{0,8},{8,16},{16,24},{24,0},{32,40},{40,48},{48,56},{56,32},{64,72... | collective-permute-start | bytes 98312 | tf_op jit(solution)/shard_map/ppermute | solution.py:35
  235.6 4.0 %collective-permute-start.26 = (f32[2,4096]{1,0:T(2,128)S(1)}, f32[2,4096]{1,0:T(2,128)S(1)}, u32[]{:S(2)}, u32[]{:S(2)}) collective-permute-start(f32[2,4096]{1,0:T(2,128)S(1)} %get-tuple-element.69), channel_id=1, source_target_pairs={{0,96},{8,104},{16,112},{24,120},{32,0},{40,8},{48,16},{56,24},{64... | collective-permute-start | bytes 98312 | tf_op jit(solution)/shard_map/ppermute | solution.py:35
  236.6 5.4 %collective-permute-start.25 = (f32[2,4096]{1,0:T(2,128)S(1)}, f32[2,4096]{1,0:T(2,128)S(1)}, u32[]{:S(2)}, u32[]{:S(2)}) collective-permute-start(f32[2,4096]{1,0:T(2,128)S(1)} %get-tuple-element.69), channel_id=1, source_target_pairs={{0,64},{8,72},{16,80},{24,88},{32,96},{40,104},{48,112},{56,120},{... | collective-permute-start | bytes 98312 | tf_op jit(solution)/shard_map/ppermute | solution.py:35
  237.5 5.1 %collective-permute-start.24 = (f32[2,4096]{1,0:T(2,128)S(1)}, f32[2,4096]{1,0:T(2,128)S(1)}, u32[]{:S(2)}, u32[]{:S(2)}) collective-permute-start(f32[2,4096]{1,0:T(2,128)S(1)} %get-tuple-element.69), channel_id=1, source_target_pairs={{0,32},{8,40},{16,48},{24,56},{32,64},{40,72},{48,80},{56,88},{64,... | collective-permute-start | bytes 98312 | tf_op jit(solution)/shard_map/ppermute | solution.py:35
  255.0 1.3 collective-permute-start.27
  256.4 3.9 %collective-permute-start.30 = (f32[2,2048]{1,0:T(2,128)S(1)}, f32[2,2048]{1,0:T(2,128)S(1)}, u32[]{:S(2)}, u32[]{:S(2)}) collective-permute-start(f32[2,2048]{1,0:T(2,128)S(1)} %get-tuple-element.81), channel_id=1, source_target_pairs={{0,6},{1,7},{2,0},{3,1},{4,2},{5,3},{6,4},{7,5},{8,14},{9,15},{10,... | collective-permute-start | bytes 49160 | tf_op jit(solution)/shard_map/ppermute | solution.py:35
  258.2 5.2 %collective-permute-start.29 = (f32[2,2048]{1,0:T(2,128)S(1)}, f32[2,2048]{1,0:T(2,128)S(1)}, u32[]{:S(2)}, u32[]{:S(2)}) collective-permute-start(f32[2,2048]{1,0:T(2,128)S(1)} %get-tuple-element.81), channel_id=1, source_target_pairs={{0,4},{1,5},{2,6},{3,7},{4,0},{5,1},{6,2},{7,3},{8,12},{9,13},{10,... | collective-permute-start | bytes 49160 | tf_op jit(solution)/shard_map/ppermute | solution.py:35
  259.1 4.9 %collective-permute-start.28 = (f32[2,2048]{1,0:T(2,128)S(1)}, f32[2,2048]{1,0:T(2,128)S(1)}, u32[]{:S(2)}, u32[]{:S(2)}) collective-permute-start(f32[2,2048]{1,0:T(2,128)S(1)} %get-tuple-element.81), channel_id=1, source_target_pairs={{0,2},{1,3},{2,4},{3,5},{4,6},{5,7},{6,0},{7,1},{8,10},{9,11},{10,... | collective-permute-start | bytes 49160 | tf_op jit(solution)/shard_map/ppermute | solution.py:35
  264.2 12.7 %copy-start.1 = (f32[2048]{0:T(1024)}, f32[2048]{0:T(1024)S(1)}, u32[]{:S(2)}) copy-start(f32[2048]{0:T(1024)S(1)} %multiply_subtract_fusion.4) | copy-start | bytes 24580
  277.0 4.0 %collective-permute-start.33 = (f32[2,4096]{1,0:T(2,128)S(1)}, f32[2,4096]{1,0:T(2,128)S(1)}, u32[]{:S(2)}, u32[]{:S(2)}) collective-permute-start(f32[2,4096]{1,0:T(2,128)S(1)} %get-tuple-element.65), channel_id=1, source_target_pairs={{0,24},{8,0},{16,8},{24,16},{32,56},{40,32},{48,40},{56,48},{64,88... | collective-permute-start | bytes 98312 | tf_op jit(solution)/shard_map/ppermute | solution.py:35
  278.8 5.4 %collective-permute-start.32 = (f32[2,4096]{1,0:T(2,128)S(1)}, f32[2,4096]{1,0:T(2,128)S(1)}, u32[]{:S(2)}, u32[]{:S(2)}) collective-permute-start(f32[2,4096]{1,0:T(2,128)S(1)} %get-tuple-element.65), channel_id=1, source_target_pairs={{0,16},{8,24},{16,0},{24,8},{32,48},{40,56},{48,32},{56,40},{64,80... | collective-permute-start | bytes 98312 | tf_op jit(solution)/shard_map/ppermute | solution.py:35
  279.7 5.1 %collective-permute-start.31 = (f32[2,4096]{1,0:T(2,128)S(1)}, f32[2,4096]{1,0:T(2,128)S(1)}, u32[]{:S(2)}, u32[]{:S(2)}) collective-permute-start(f32[2,4096]{1,0:T(2,128)S(1)} %get-tuple-element.65), channel_id=1, source_target_pairs={{0,8},{8,16},{16,24},{24,0},{32,40},{40,48},{48,56},{56,32},{64,72... | collective-permute-start | bytes 98312 | tf_op jit(solution)/shard_map/ppermute | solution.py:35
  285.1 4.0 %collective-permute-start.36 = (f32[2,4096]{1,0:T(2,128)S(1)}, f32[2,4096]{1,0:T(2,128)S(1)}, u32[]{:S(2)}, u32[]{:S(2)}) collective-permute-start(f32[2,4096]{1,0:T(2,128)S(1)} %get-tuple-element.63), channel_id=1, source_target_pairs={{0,96},{8,104},{16,112},{24,120},{32,0},{40,8},{48,16},{56,24},{64... | collective-permute-start | bytes 98312 | tf_op jit(solution)/shard_map/ppermute | solution.py:35
  286.5 5.4 %collective-permute-start.35 = (f32[2,4096]{1,0:T(2,128)S(1)}, f32[2,4096]{1,0:T(2,128)S(1)}, u32[]{:S(2)}, u32[]{:S(2)}) collective-permute-start(f32[2,4096]{1,0:T(2,128)S(1)} %get-tuple-element.63), channel_id=1, source_target_pairs={{0,64},{8,72},{16,80},{24,88},{32,96},{40,104},{48,112},{56,120},{... | collective-permute-start | bytes 98312 | tf_op jit(solution)/shard_map/ppermute | solution.py:35
  287.4 5.1 %collective-permute-start.34 = (f32[2,4096]{1,0:T(2,128)S(1)}, f32[2,4096]{1,0:T(2,128)S(1)}, u32[]{:S(2)}, u32[]{:S(2)}) collective-permute-start(f32[2,4096]{1,0:T(2,128)S(1)} %get-tuple-element.63), channel_id=1, source_target_pairs={{0,32},{8,40},{16,48},{24,56},{32,64},{40,72},{48,80},{56,88},{64,... | collective-permute-start | bytes 98312 | tf_op jit(solution)/shard_map/ppermute | solution.py:35
Sparse Core Ops, SparseCore 0:
  10.1 53.9 all-gather.1

commit v3 on v2

--- a/solution.py
+++ b/solution.py
@@ -95,12 +95,16 @@
     cost_tile = inner_costs(query_block, lax.all_gather(passages, "row", axis=0, tiled=True))
     col_potential = jnp.zeros((cost_tile.shape[1],), jnp.float32)
     row_potential = jnp.zeros((cost_tile.shape[0],), jnp.float32)
-    for repeat in range(ITERS):
+
+    def one_iteration(repeat, potentials):
+        row_potential, col_potential = potentials
         scores = (col_potential[None, :] - cost_tile) / entropy_scale
         row_potential = -entropy_scale * math.log(all_queries) - entropy_scale * logsum_col(scores)
         scores = (row_potential[:, None] - cost_tile) / entropy_scale
         col_potential = -entropy_scale * math.log(all_passages) - entropy_scale * logsum_row(scores)
-    return (row_potential, col_potential)
+        return (row_potential, col_potential)
+
+    return lax.fori_loop(0, ITERS, one_iteration, (row_potential, col_potential))
 
 
 def solution(mesh):

time: 301 us -> 352 us (1.17)
  other arithmetic: 117 us -> 151 us
  local copies, waits for them, and re-layouts: 3.27 us -> 26 us
  matrix products: 38.8 us -> 33.5 us
    while x0 -> x12, local copies, waits for them, and re-layouts: none -> 21.7 us
    reduce_max x2 -> x3, other arithmetic: 19.7 us -> 39.1 us  [logsum_col(): peak = jnp.max(scores, axis=1)]
    reduce_max x3, other arithmetic: 23.2 us -> 39.4 us  [logsum_row(): peak = jnp.max(scores, axis=0)]
    reduce_sum x3, other arithmetic: 39.2 us -> 24.1 us  [logsum_col(): totals = jnp.sum(jnp.exp(scores - peak[:, None]), axis=1)]
    reduce_sum x3, other arithmetic: 29.7 us -> 43.2 us  [logsum_row(): totals = jnp.sum(jnp.exp(scores - peak[None, :]), axis=0)]
    dot_general x1, matrix products: 38.8 us -> 33.5 us  [inner_costs(): lax.dot_general(left, right, (((1,), (1,)), ((), ())), precision=lax.Prec...]
  transfers between devices with their start and end apart: 38 -> 38, of which waited for: 35 -> 34; matrix products, arithmetic and copies ran while one was open for 1% -> 0% of each run, Pallas kernels for 0% -> 0%
where the time goes in v3:
time: 352 us; the launch traced here: 351 us
  other arithmetic  151 us (43%)
  waiting for transfers between devices  80.8 us (23%)
  starting transfers between devices  44.5 us (13%)
  matrix products  33.5 us (10%)
  local copies, waits for them, and re-layouts  26 us (7%)
  between operations  15.1 us (4%)
    ppermute x37, waiting for transfers between devices, exchange(): lax.ppermute(x, axis, digit_partners(axis, size, stride, width, k))  52.6 us
    ppermute x37, starting transfers between devices, exchange(): lax.ppermute(x, axis, digit_partners(axis, size, stride, width, k))  44.5 us
    reduce_sum x3, other arithmetic, logsum_row(): totals = jnp.sum(jnp.exp(scores - peak[None, :]), axis=0)  43.2 us
    reduce_max x3, other arithmetic, logsum_row(): peak = jnp.max(scores, axis=0)  39.4 us
    reduce_max x3, other arithmetic, logsum_col(): peak = jnp.max(scores, axis=1)  39.1 us
    dot_general x1, matrix products, inner_costs(): lax.dot_general(left, right, (((1,), (1,)), ((), ())), precision=lax.Prec...  33.5 us
    all_gather x1, waiting for transfers between devices, per_device(): lax.all_gather(passages, 'row', axis=0, tiled=True)  27.5 us
    reduce_sum x3, other arithmetic, logsum_col(): totals = jnp.sum(jnp.exp(scores - peak[:, None]), axis=1)  24.1 us
  transfers between devices with their start and end apart: 38, of which 34 were waited for; matrix products, arithmetic and copies ran while one was open for 0% of the time, Pallas kernels for 0%

profile of v3, /device:TPU:0, one launch (start us, length us, event | category | flops | bytes accessed | tf_op | source)
XLA Modules:
  0.0 351.2 jit_solution(4683915687375267168)
XLA Ops:
  7.9 1.7 collective-permute-start.11
  9.6 2.0 collective-permute-start.12
  11.7 2.0 collective-permute-start.13
  15.5 1.7 collective-permute-start.14
  17.3 1.7 collective-permute-start.15
  19.1 5.3 %collective-permute-start.16 = (f32[256,256]{1,0:T(8,128)S(1)}, f32[256,256]{1,0:T(8,128)S(1)}, u32[]{:S(2)}, u32[]{:S(2)}) collective-permute-start(f32[256,256]{1,0:T(8,128)S(1)} %copy-done.5), channel_id=1, source_target_pairs={{0,7},{1,0},{2,1},{3,2},{4,3},{5,4},{6,5},{7,6},{8,15},{9,8},{10,9... | collective-permute-start | bytes 786440 | tf_op jit(solution)/shard_map/ppermute | solution.py:35
  24.3 5.3 %collective-permute-done.12 = f32[256,256]{1,0:T(8,128)S(1)} collective-permute-done((f32[256,256]{1,0:T(8,128)}, f32[256,256]{1,0:T(8,128)S(1)}, u32[]{:S(2)}, u32[]{:S(2)}) %collective-permute-start.12) | collective-permute-done | bytes 262176 | tf_op jit(solution)/shard_map/ppermute | solution.py:35
  29.6 1.3 collective-permute-done.13
  31.0 1.9 collective-permute-done.14
  33.0 1.7 collective-permute-done.16
  35.0 1.3 copy-done.2
  36.7 27.5 %all-gather.2.cloned.1.call-done = f32[4096,256]{1,0:T(8,128)} async-done(((f32[256,256]{1,0:T(8,128)}), f32[4096,256]{1,0:T(8,128)}) %all-gather.2.cloned.1.call-update) | async-done | bytes 4194320 | tf_op jit(solution)/shard_map/all_gather | solution.py:95
  64.1 3.0 multiply_reduce_fusion
  67.6 33.5 %multiply_subtract_fusion.2 = f32[2048,4096]{1,0:T(8,128)} fusion(f32[4096]{0:T(1024)S(1)} %multiply_reduce_fusion, f32[2048]{0:T(1024)S(1)} %multiply_reduce_fusion.1, f32[2048,256]{1,0:T(8,128)} %copy-done.2, f32[4096,256]{1,0:T(8,128)S(1)} %copy-done.1), kind=kOutput, calls=%fused_computation.66 | convolution fusion | flops 25794969600 | bytes 39870464 | tf_op jit(solution)/shard_map/dot_general | solution.py:14
  101.0 242.7 %while.16 = (s32[]{:T(128)}, f32[2048]{0:T(1024)}, f32[4096]{0:T(1024)S(1)}, f32[]{:T(128)}, f32[]{:T(128)}, /*index=5*/f32[2048,4096]{1,0:T(8,128)}, s32[]{:T(1...) while((s32[]{:T(128)}, f32[2048]{0:T(1024)}, ...), condition=%wide.region_7.8_spmd.clone, body=%wide.region_2.7_spmd.clone.sunk | while | flops 117884960 | bytes 271517696 | solution.py:107
  101.0 13.0 %fusion.30 = f32[2048]{0:T(1024)S(1)} fusion(f32[]{:T(128)} %get-tuple-element.334, f32[2048,4096]{1,0:T(8,128)} %get-tuple-element.335, f32[4096]{0:T(1024)S(1)} %broadcast_select_fusion.2), kind=kLoop, calls=%fused_computation.4.clone.1 | loop fusion | flops 25163776 | bytes 33579012 | tf_op jit(solution)/shard_map/while/body/eval_jaxpr/reduce_max | solution.py:72
  114.1 7.2 %copy-done = f32[2048,4096]{1,0:T(8,128)S(1)} copy-done((f32[2048,4096]{1,0:T(8,128)S(1)}, f32[2048,4096]{1,0:T(8,128)}, u32[]{:S(2)}) %copy-start) | copy-done | bytes 33554456 | tf_op jit(solution)/shard_map/while
  121.3 8.0 %exponential_reduce_fusion.4 = f32[2048]{0:T(1024)S(1)} fusion(f32[2048]{0:T(1024)S(1)} %fusion.30, f32[]{:T(128)} %get-tuple-element.334, f32[2048,4096]{1,0:T(8,128)S(1)} %copy-done, f32[4096]{0:T(1024)S(1)} %broadcast_select_fusion.2), kind=kLoop, calls=%fused_computation.2.clone.1 | loop fusion | flops 33552384 | bytes 33587204 | tf_op jit(solution)/shard_map/while/body/eval_jaxpr/reduce_sum | solution.py:73
  130.8 2.8 collective-permute-start.1
  135.2 3.5 %collective-permute-done.2 = f32[2,2048]{1,0:T(2,128)S(1)} collective-permute-done((f32[2,2048]{1,0:T(2,128)S(1)}, f32[2,2048]{1,0:T(2,128)S(1)}, u32[]{:S(2)}, u32[]{:S(2)}) %collective-permute-start.2) | collective-permute-done | bytes 16416 | tf_op jit(solution)/shard_map/while/body/eval_jaxpr/ppermute | solution.py:35
  139.5 13.1 %fusion.34 = f32[4096]{0:T(1024)S(1)} fusion(f32[]{:T(128)} %get-tuple-element.334, f32[2048,4096]{1,0:T(8,128)} %get-tuple-element.335, f32[2048]{0:T(1024)S(1)} %multiply_subtract_fusion.5), kind=kLoop, calls=%fused_computation.5.clone.1 | loop fusion | flops 25161728 | bytes 33579012 | tf_op jit(solution)/shard_map/while/body/eval_jaxpr/reduce_max | solution.py:78
  152.6 14.4 %exponential_reduce_fusion.5 = f32[4096]{0:T(1024)S(1)} fusion(f32[4096]{0:T(1024)S(1)} %fusion.34, f32[]{:T(128)} %get-tuple-element.334, f32[2048,4096]{1,0:T(8,128)} %get-tuple-element.335, f32[2048]{0:T(1024)S(1)} %multiply_subtract_fusion.5), kind=kLoop, calls=%fused_computation.clone.1 | loop fusion | flops 33550336 | bytes 33595396 | tf_op jit(solution)/shard_map/while/body/eval_jaxpr/reduce_sum | solution.py:79
  167.1 2.8 collective-permute-start.4
  171.6 3.7 %collective-permute-done.5 = f32[2,4096]{1,0:T(2,128)S(1)} collective-permute-done((f32[2,4096]{1,0:T(2,128)S(1)}, f32[2,4096]{1,0:T(2,128)S(1)}, u32[]{:S(2)}, u32[]{:S(2)}) %collective-permute-start.5) | collective-permute-done | bytes 32800 | tf_op jit(solution)/shard_map/while/body/eval_jaxpr/ppermute | solution.py:35
  176.1 1.5 collective-permute-start.7
  180.1 3.0 collective-permute-done.8
  183.8 13.0 %fusion.30 = f32[2048]{0:T(1024)S(1)} fusion(f32[]{:T(128)} %get-tuple-element.334, f32[2048,4096]{1,0:T(8,128)} %get-tuple-element.335, f32[4096]{0:T(1024)S(1)} %broadcast_select_fusion.2), kind=kLoop, calls=%fused_computation.4.clone.1 | loop fusion | flops 25163776 | bytes 33579012 | tf_op jit(solution)/shard_map/while/body/eval_jaxpr/reduce_max | solution.py:72
  196.8 7.2 %copy-done = f32[2048,4096]{1,0:T(8,128)S(1)} copy-done((f32[2048,4096]{1,0:T(8,128)S(1)}, f32[2048,4096]{1,0:T(8,128)}, u32[]{:S(2)}) %copy-start) | copy-done | bytes 33554456 | tf_op jit(solution)/shard_map/while
  204.1 8.0 %exponential_reduce_fusion.4 = f32[2048]{0:T(1024)S(1)} fusion(f32[2048]{0:T(1024)S(1)} %fusion.30, f32[]{:T(128)} %get-tuple-element.334, f32[2048,4096]{1,0:T(8,128)S(1)} %copy-done, f32[4096]{0:T(1024)S(1)} %broadcast_select_fusion.2), kind=kLoop, calls=%fused_computation.2.clone.1 | loop fusion | flops 33552384 | bytes 33587204 | tf_op jit(solution)/shard_map/while/body/eval_jaxpr/reduce_sum | solution.py:73
  213.9 1.4 collective-permute-start.2
  217.3 1.9 collective-permute-done.2
  220.4 13.1 %fusion.34 = f32[4096]{0:T(1024)S(1)} fusion(f32[]{:T(128)} %get-tuple-element.334, f32[2048,4096]{1,0:T(8,128)} %get-tuple-element.335, f32[2048]{0:T(1024)S(1)} %multiply_subtract_fusion.5), kind=kLoop, calls=%fused_computation.5.clone.1 | loop fusion | flops 25161728 | bytes 33579012 | tf_op jit(solution)/shard_map/while/body/eval_jaxpr/reduce_max | solution.py:78
  233.5 14.4 %exponential_reduce_fusion.5 = f32[4096]{0:T(1024)S(1)} fusion(f32[4096]{0:T(1024)S(1)} %fusion.34, f32[]{:T(128)} %get-tuple-element.334, f32[2048,4096]{1,0:T(8,128)} %get-tuple-element.335, f32[2048]{0:T(1024)S(1)} %multiply_subtract_fusion.5), kind=kLoop, calls=%fused_computation.clone.1 | loop fusion | flops 33550336 | bytes 33595396 | tf_op jit(solution)/shard_map/while/body/eval_jaxpr/reduce_sum | solution.py:79
  248.0 1.2 collective-permute-start.4
  252.0 2.6 collective-permute-done.5
  257.4 1.2 collective-permute-start.9
  259.5 2.5 collective-permute-done.8
  262.8 13.0 %fusion.30 = f32[2048]{0:T(1024)S(1)} fusion(f32[]{:T(128)} %get-tuple-element.334, f32[2048,4096]{1,0:T(8,128)} %get-tuple-element.335, f32[4096]{0:T(1024)S(1)} %broadcast_select_fusion.2), kind=kLoop, calls=%fused_computation.4.clone.1 | loop fusion | flops 25163776 | bytes 33579012 | tf_op jit(solution)/shard_map/while/body/eval_jaxpr/reduce_max | solution.py:72
  275.9 7.2 %copy-done = f32[2048,4096]{1,0:T(8,128)S(1)} copy-done((f32[2048,4096]{1,0:T(8,128)S(1)}, f32[2048,4096]{1,0:T(8,128)}, u32[]{:S(2)}) %copy-start) | copy-done | bytes 33554456 | tf_op jit(solution)/shard_map/while
  283.1 8.0 %exponential_reduce_fusion.4 = f32[2048]{0:T(1024)S(1)} fusion(f32[2048]{0:T(1024)S(1)} %fusion.30, f32[]{:T(128)} %get-tuple-element.334, f32[2048,4096]{1,0:T(8,128)S(1)} %copy-done, f32[4096]{0:T(1024)S(1)} %broadcast_select_fusion.2), kind=kLoop, calls=%fused_computation.2.clone.1 | loop fusion | flops 33552384 | bytes 33587204 | tf_op jit(solution)/shard_map/while/body/eval_jaxpr/reduce_sum | solution.py:73
  292.5 1.8 collective-permute-start.1
  296.4 3.2 collective-permute-done.2
  300.4 13.1 %fusion.34 = f32[4096]{0:T(1024)S(1)} fusion(f32[]{:T(128)} %get-tuple-element.334, f32[2048,4096]{1,0:T(8,128)} %get-tuple-element.335, f32[2048]{0:T(1024)S(1)} %multiply_subtract_fusion.5), kind=kLoop, calls=%fused_computation.5.clone.1 | loop fusion | flops 25161728 | bytes 33579012 | tf_op jit(solution)/shard_map/while/body/eval_jaxpr/reduce_max | solution.py:78
  313.5 14.4 %exponential_reduce_fusion.5 = f32[4096]{0:T(1024)S(1)} fusion(f32[4096]{0:T(1024)S(1)} %fusion.34, f32[]{:T(128)} %get-tuple-element.334, f32[2048,4096]{1,0:T(8,128)} %get-tuple-element.335, f32[2048]{0:T(1024)S(1)} %multiply_subtract_fusion.5), kind=kLoop, calls=%fused_computation.clone.1 | loop fusion | flops 33550336 | bytes 33595396 | tf_op jit(solution)/shard_map/while/body/eval_jaxpr/reduce_sum | solution.py:79
  328.0 1.8 collective-permute-start.4
  332.0 3.3 collective-permute-done.5
  336.1 1.4 collective-permute-start.7
  340.1 2.8 collective-permute-done.8
  (128 shorter events, 35.8 us)
Async XLA Ops:
  7.2 11.9 %copy-start.5 = (f32[256,256]{1,0:T(8,128)S(1)}, f32[256,256]{1,0:T(8,128)}, u32[]{:S(2)}) copy-start(f32[256,256]{1,0:T(8,128)} %param.5) | copy-start | bytes 786436
  7.2 57.0 %all-gather.2.cloned.1.call-start = ((), (), s32[]{:S(2)}) async-start(), calls=%async_computation | async-start | bytes 4456448 | tf_op jit(solution)/shard_map/all_gather | solution.py:95
  7.9 9.4 %collective-permute-start.10 = (f32[256,256]{1,0:T(8,128)}, f32[256,256]{1,0:T(8,128)S(1)}, u32[]{:S(2)}, u32[]{:S(2)}) collective-permute-start(f32[256,256]{1,0:T(8,128)} %param.5), channel_id=1, source_target_pairs={{0,1},{1,2},{2,3},{3,4},{4,5},{5,6},{6,7},{7,0},{8,9},{9,10},{10,1... | collective-permute-start | bytes 786440 | tf_op jit(solution)/shard_map/ppermute | solution.py:35
  7.9 11.1 %collective-permute-start.11 = (f32[256,256]{1,0:T(8,128)}, f32[256,256]{1,0:T(8,128)S(1)}, u32[]{:S(2)}, u32[]{:S(2)}) collective-permute-start(f32[256,256]{1,0:T(8,128)} %param.5), channel_id=1, source_target_pairs={{0,2},{1,3},{2,4},{3,5},{4,6},{5,7},{6,0},{7,1},{8,10},{9,11},{10,... | collective-permute-start | bytes 786440 | tf_op jit(solution)/shard_map/ppermute | solution.py:35
  9.6 20.0 %collective-permute-start.12 = (f32[256,256]{1,0:T(8,128)}, f32[256,256]{1,0:T(8,128)S(1)}, u32[]{:S(2)}, u32[]{:S(2)}) collective-permute-start(f32[256,256]{1,0:T(8,128)} %param.5), channel_id=1, source_target_pairs={{0,3},{1,4},{2,5},{3,6},{4,7},{5,0},{6,1},{7,2},{8,11},{9,12},{10,... | collective-permute-start | bytes 786440 | tf_op jit(solution)/shard_map/ppermute | solution.py:35
  11.7 19.3 %collective-permute-start.13 = (f32[256,256]{1,0:T(8,128)}, f32[256,256]{1,0:T(8,128)S(1)}, u32[]{:S(2)}, u32[]{:S(2)}) collective-permute-start(f32[256,256]{1,0:T(8,128)} %param.5), channel_id=1, source_target_pairs={{0,4},{1,5},{2,6},{3,7},{4,0},{5,1},{6,2},{7,3},{8,12},{9,13},{10,... | collective-permute-start | bytes 786440 | tf_op jit(solution)/shard_map/ppermute | solution.py:35
  15.5 17.3 %collective-permute-start.14 = (f32[256,256]{1,0:T(8,128)}, f32[256,256]{1,0:T(8,128)S(1)}, u32[]{:S(2)}, u32[]{:S(2)}) collective-permute-start(f32[256,256]{1,0:T(8,128)} %param.5), channel_id=1, source_target_pairs={{0,5},{1,6},{2,7},{3,0},{4,1},{5,2},{6,3},{7,4},{8,13},{9,14},{10,... | collective-permute-start | bytes 786440 | tf_op jit(solution)/shard_map/ppermute | solution.py:35
  17.3 15.7 %collective-permute-start.15 = (f32[256,256]{1,0:T(8,128)}, f32[256,256]{1,0:T(8,128)S(1)}, u32[]{:S(2)}, u32[]{:S(2)}) collective-permute-start(f32[256,256]{1,0:T(8,128)} %param.5), channel_id=1, source_target_pairs={{0,6},{1,7},{2,0},{3,1},{4,2},{5,3},{6,4},{7,5},{8,14},{9,15},{10,... | collective-permute-start | bytes 786440 | tf_op jit(solution)/shard_map/ppermute | solution.py:35
  19.1 15.7 %collective-permute-start.16 = (f32[256,256]{1,0:T(8,128)S(1)}, f32[256,256]{1,0:T(8,128)S(1)}, u32[]{:S(2)}, u32[]{:S(2)}) collective-permute-start(f32[256,256]{1,0:T(8,128)S(1)} %copy-done.5), channel_id=1, source_target_pairs={{0,7},{1,0},{2,1},{3,2},{4,3},{5,4},{6,5},{7,6},{8,15},{9,8},{10,9... | collective-permute-start | bytes 786440 | tf_op jit(solution)/shard_map/ppermute | solution.py:35
  35.0 1.3 copy-start.2
  64.1 3.4 copy-start.1
  101.0 20.3 %copy-start = (f32[2048,4096]{1,0:T(8,128)S(1)}, f32[2048,4096]{1,0:T(8,128)}, u32[]{:S(2)}) copy-start(f32[2048,4096]{1,0:T(8,128)} %get-tuple-element.335) | copy-start | bytes 100663296 | tf_op jit(solution)/shard_map/while
  129.4 1.3 collective-permute-start
  130.8 4.5 %collective-permute-start.1 = (f32[2,2048]{1,0:T(2,128)S(1)}, f32[2,2048]{1,0:T(2,128)S(1)}, u32[]{:S(2)}, u32[]{:S(2)}) collective-permute-start(f32[2,2048]{1,0:T(2,128)S(1)} %get-tuple-element.270), channel_id=1, source_target_pairs={{0,6},{1,7},{2,0},{3,1},{4,2},{5,3},{6,4},{7,5},{8,14},{9,15},{10,... | collective-permute-start | bytes 49160 | tf_op jit(solution)/shard_map/while/body/eval_jaxpr/ppermute | solution.py:35
  133.5 5.2 %collective-permute-start.2 = (f32[2,2048]{1,0:T(2,128)S(1)}, f32[2,2048]{1,0:T(2,128)S(1)}, u32[]{:S(2)}, u32[]{:S(2)}) collective-permute-start(f32[2,2048]{1,0:T(2,128)S(1)} %get-tuple-element.270), channel_id=1, source_target_pairs={{0,4},{1,5},{2,6},{3,7},{4,0},{5,1},{6,2},{7,3},{8,12},{9,13},{10,... | collective-permute-start | bytes 49160 | tf_op jit(solution)/shard_map/while/body/eval_jaxpr/ppermute | solution.py:35
  134.4 4.9 %collective-permute-start.3 = (f32[2,2048]{1,0:T(2,128)S(1)}, f32[2,2048]{1,0:T(2,128)S(1)}, u32[]{:S(2)}, u32[]{:S(2)}) collective-permute-start(f32[2,2048]{1,0:T(2,128)S(1)} %get-tuple-element.270), channel_id=1, source_target_pairs={{0,2},{1,3},{2,4},{3,5},{4,6},{5,7},{6,0},{7,1},{8,10},{9,11},{10,... | collective-permute-start | bytes 49160 | tf_op jit(solution)/shard_map/while/body/eval_jaxpr/ppermute | solution.py:35
  139.5 13.2 %copy-start.3 = (f32[2048]{0:T(1024)}, f32[2048]{0:T(1024)S(1)}, u32[]{:S(2)}) copy-start(f32[2048]{0:T(1024)S(1)} %multiply_subtract_fusion.5) | copy-start | bytes 24580 | tf_op jit(solution)/shard_map/while
  167.1 4.5 %collective-permute-start.4 = (f32[2,4096]{1,0:T(2,128)S(1)}, f32[2,4096]{1,0:T(2,128)S(1)}, u32[]{:S(2)}, u32[]{:S(2)}) collective-permute-start(f32[2,4096]{1,0:T(2,128)S(1)} %get-tuple-element.280), channel_id=1, source_target_pairs={{0,24},{8,0},{16,8},{24,16},{32,56},{40,32},{48,40},{56,48},{64,88... | collective-permute-start | bytes 98312 | tf_op jit(solution)/shard_map/while/body/eval_jaxpr/ppermute | solution.py:35
  169.9 5.4 %collective-permute-start.5 = (f32[2,4096]{1,0:T(2,128)S(1)}, f32[2,4096]{1,0:T(2,128)S(1)}, u32[]{:S(2)}, u32[]{:S(2)}) collective-permute-start(f32[2,4096]{1,0:T(2,128)S(1)} %get-tuple-element.280), channel_id=1, source_target_pairs={{0,16},{8,24},{16,0},{24,8},{32,48},{40,56},{48,32},{56,40},{64,80... | collective-permute-start | bytes 98312 | tf_op jit(solution)/shard_map/while/body/eval_jaxpr/ppermute | solution.py:35
  170.7 5.1 %collective-permute-start.6 = (f32[2,4096]{1,0:T(2,128)S(1)}, f32[2,4096]{1,0:T(2,128)S(1)}, u32[]{:S(2)}, u32[]{:S(2)}) collective-permute-start(f32[2,4096]{1,0:T(2,128)S(1)} %get-tuple-element.280), channel_id=1, source_target_pairs={{0,8},{8,16},{16,24},{24,0},{32,40},{40,48},{48,56},{56,32},{64,72... | collective-permute-start | bytes 98312 | tf_op jit(solution)/shard_map/while/body/eval_jaxpr/ppermute | solution.py:35
  176.1 4.0 %collective-permute-start.7 = (f32[2,4096]{1,0:T(2,128)S(1)}, f32[2,4096]{1,0:T(2,128)S(1)}, u32[]{:S(2)}, u32[]{:S(2)}) collective-permute-start(f32[2,4096]{1,0:T(2,128)S(1)} %get-tuple-element.284), channel_id=1, source_target_pairs={{0,96},{8,104},{16,112},{24,120},{32,0},{40,8},{48,16},{56,24},{64... | collective-permute-start | bytes 98312 | tf_op jit(solution)/shard_map/while/body/eval_jaxpr/ppermute | solution.py:35
  177.6 5.4 %collective-permute-start.8 = (f32[2,4096]{1,0:T(2,128)S(1)}, f32[2,4096]{1,0:T(2,128)S(1)}, u32[]{:S(2)}, u32[]{:S(2)}) collective-permute-start(f32[2,4096]{1,0:T(2,128)S(1)} %get-tuple-element.284), channel_id=1, source_target_pairs={{0,64},{8,72},{16,80},{24,88},{32,96},{40,104},{48,112},{56,120},{... | collective-permute-start | bytes 98312 | tf_op jit(solution)/shard_map/while/body/eval_jaxpr/ppermute | solution.py:35
  178.4 5.1 %collective-permute-start.9 = (f32[2,4096]{1,0:T(2,128)S(1)}, f32[2,4096]{1,0:T(2,128)S(1)}, u32[]{:S(2)}, u32[]{:S(2)}) collective-permute-start(f32[2,4096]{1,0:T(2,128)S(1)} %get-tuple-element.284), channel_id=1, source_target_pairs={{0,32},{8,40},{16,48},{24,56},{32,64},{40,72},{48,80},{56,88},{64,... | collective-permute-start | bytes 98312 | tf_op jit(solution)/shard_map/while/body/eval_jaxpr/ppermute | solution.py:35
  183.8 20.3 %copy-start = (f32[2048,4096]{1,0:T(8,128)S(1)}, f32[2048,4096]{1,0:T(8,128)}, u32[]{:S(2)}) copy-start(f32[2048,4096]{1,0:T(8,128)} %get-tuple-element.335) | copy-start | bytes 100663296 | tf_op jit(solution)/shard_map/while
  212.1 1.3 collective-permute-start
  213.5 3.8 %collective-permute-start.1 = (f32[2,2048]{1,0:T(2,128)S(1)}, f32[2,2048]{1,0:T(2,128)S(1)}, u32[]{:S(2)}, u32[]{:S(2)}) collective-permute-start(f32[2,2048]{1,0:T(2,128)S(1)} %get-tuple-element.270), channel_id=1, source_target_pairs={{0,6},{1,7},{2,0},{3,1},{4,2},{5,3},{6,4},{7,5},{8,14},{9,15},{10,... | collective-permute-start | bytes 49160 | tf_op jit(solution)/shard_map/while/body/eval_jaxpr/ppermute | solution.py:35
  213.9 5.3 %collective-permute-start.2 = (f32[2,2048]{1,0:T(2,128)S(1)}, f32[2,2048]{1,0:T(2,128)S(1)}, u32[]{:S(2)}, u32[]{:S(2)}) collective-permute-start(f32[2,2048]{1,0:T(2,128)S(1)} %get-tuple-element.270), channel_id=1, source_target_pairs={{0,4},{1,5},{2,6},{3,7},{4,0},{5,1},{6,2},{7,3},{8,12},{9,13},{10,... | collective-permute-start | bytes 49160 | tf_op jit(solution)/shard_map/while/body/eval_jaxpr/ppermute | solution.py:35
  215.3 4.9 %collective-permute-start.3 = (f32[2,2048]{1,0:T(2,128)S(1)}, f32[2,2048]{1,0:T(2,128)S(1)}, u32[]{:S(2)}, u32[]{:S(2)}) collective-permute-start(f32[2,2048]{1,0:T(2,128)S(1)} %get-tuple-element.270), channel_id=1, source_target_pairs={{0,2},{1,3},{2,4},{3,5},{4,6},{5,7},{6,0},{7,1},{8,10},{9,11},{10,... | collective-permute-start | bytes 49160 | tf_op jit(solution)/shard_map/while/body/eval_jaxpr/ppermute | solution.py:35
  220.4 13.2 %copy-start.3 = (f32[2048]{0:T(1024)}, f32[2048]{0:T(1024)S(1)}, u32[]{:S(2)}) copy-start(f32[2048]{0:T(1024)S(1)} %multiply_subtract_fusion.5) | copy-start | bytes 24580 | tf_op jit(solution)/shard_map/while
  248.0 4.0 %collective-permute-start.4 = (f32[2,4096]{1,0:T(2,128)S(1)}, f32[2,4096]{1,0:T(2,128)S(1)}, u32[]{:S(2)}, u32[]{:S(2)}) collective-permute-start(f32[2,4096]{1,0:T(2,128)S(1)} %get-tuple-element.280), channel_id=1, source_target_pairs={{0,24},{8,0},{16,8},{24,16},{32,56},{40,32},{48,40},{56,48},{64,88... | collective-permute-start | bytes 98312 | tf_op jit(solution)/shard_map/while/body/eval_jaxpr/ppermute | solution.py:35
  249.2 5.4 %collective-permute-start.5 = (f32[2,4096]{1,0:T(2,128)S(1)}, f32[2,4096]{1,0:T(2,128)S(1)}, u32[]{:S(2)}, u32[]{:S(2)}) collective-permute-start(f32[2,4096]{1,0:T(2,128)S(1)} %get-tuple-element.280), channel_id=1, source_target_pairs={{0,16},{8,24},{16,0},{24,8},{32,48},{40,56},{48,32},{56,40},{64,80... | collective-permute-start | bytes 98312 | tf_op jit(solution)/shard_map/while/body/eval_jaxpr/ppermute | solution.py:35
  250.1 5.1 %collective-permute-start.6 = (f32[2,4096]{1,0:T(2,128)S(1)}, f32[2,4096]{1,0:T(2,128)S(1)}, u32[]{:S(2)}, u32[]{:S(2)}) collective-permute-start(f32[2,4096]{1,0:T(2,128)S(1)} %get-tuple-element.280), channel_id=1, source_target_pairs={{0,8},{8,16},{16,24},{24,0},{32,40},{40,48},{48,56},{56,32},{64,72... | collective-permute-start | bytes 98312 | tf_op jit(solution)/shard_map/while/body/eval_jaxpr/ppermute | solution.py:35
  255.5 4.0 %collective-permute-start.7 = (f32[2,4096]{1,0:T(2,128)S(1)}, f32[2,4096]{1,0:T(2,128)S(1)}, u32[]{:S(2)}, u32[]{:S(2)}) collective-permute-start(f32[2,4096]{1,0:T(2,128)S(1)} %get-tuple-element.284), channel_id=1, source_target_pairs={{0,96},{8,104},{16,112},{24,120},{32,0},{40,8},{48,16},{56,24},{64... | collective-permute-start | bytes 98312 | tf_op jit(solution)/shard_map/while/body/eval_jaxpr/ppermute | solution.py:35
  256.5 5.4 %collective-permute-start.8 = (f32[2,4096]{1,0:T(2,128)S(1)}, f32[2,4096]{1,0:T(2,128)S(1)}, u32[]{:S(2)}, u32[]{:S(2)}) collective-permute-start(f32[2,4096]{1,0:T(2,128)S(1)} %get-tuple-element.284), channel_id=1, source_target_pairs={{0,64},{8,72},{16,80},{24,88},{32,96},{40,104},{48,112},{56,120},{... | collective-permute-start | bytes 98312 | tf_op jit(solution)/shard_map/while/body/eval_jaxpr/ppermute | solution.py:35
  257.4 5.1 %collective-permute-start.9 = (f32[2,4096]{1,0:T(2,128)S(1)}, f32[2,4096]{1,0:T(2,128)S(1)}, u32[]{:S(2)}, u32[]{:S(2)}) collective-permute-start(f32[2,4096]{1,0:T(2,128)S(1)} %get-tuple-element.284), channel_id=1, source_target_pairs={{0,32},{8,40},{16,48},{24,56},{32,64},{40,72},{48,80},{56,88},{64,... | collective-permute-start | bytes 98312 | tf_op jit(solution)/shard_map/while/body/eval_jaxpr/ppermute | solution.py:35
  262.8 20.3 %copy-start = (f32[2048,4096]{1,0:T(8,128)S(1)}, f32[2048,4096]{1,0:T(8,128)}, u32[]{:S(2)}) copy-start(f32[2048,4096]{1,0:T(8,128)} %get-tuple-element.335) | copy-start | bytes 100663296 | tf_op jit(solution)/shard_map/while
  291.2 1.3 collective-permute-start
  292.5 3.9 %collective-permute-start.1 = (f32[2,2048]{1,0:T(2,128)S(1)}, f32[2,2048]{1,0:T(2,128)S(1)}, u32[]{:S(2)}, u32[]{:S(2)}) collective-permute-start(f32[2,2048]{1,0:T(2,128)S(1)} %get-tuple-element.270), channel_id=1, source_target_pairs={{0,6},{1,7},{2,0},{3,1},{4,2},{5,3},{6,4},{7,5},{8,14},{9,15},{10,... | collective-permute-start | bytes 49160 | tf_op jit(solution)/shard_map/while/body/eval_jaxpr/ppermute | solution.py:35
  294.4 5.2 %collective-permute-start.2 = (f32[2,2048]{1,0:T(2,128)S(1)}, f32[2,2048]{1,0:T(2,128)S(1)}, u32[]{:S(2)}, u32[]{:S(2)}) collective-permute-start(f32[2,2048]{1,0:T(2,128)S(1)} %get-tuple-element.270), channel_id=1, source_target_pairs={{0,4},{1,5},{2,6},{3,7},{4,0},{5,1},{6,2},{7,3},{8,12},{9,13},{10,... | collective-permute-start | bytes 49160 | tf_op jit(solution)/shard_map/while/body/eval_jaxpr/ppermute | solution.py:35
  295.3 4.9 %collective-permute-start.3 = (f32[2,2048]{1,0:T(2,128)S(1)}, f32[2,2048]{1,0:T(2,128)S(1)}, u32[]{:S(2)}, u32[]{:S(2)}) collective-permute-start(f32[2,2048]{1,0:T(2,128)S(1)} %get-tuple-element.270), channel_id=1, source_target_pairs={{0,2},{1,3},{2,4},{3,5},{4,6},{5,7},{6,0},{7,1},{8,10},{9,11},{10,... | collective-permute-start | bytes 49160 | tf_op jit(solution)/shard_map/while/body/eval_jaxpr/ppermute | solution.py:35
  300.4 13.2 %copy-start.3 = (f32[2048]{0:T(1024)}, f32[2048]{0:T(1024)S(1)}, u32[]{:S(2)}) copy-start(f32[2048]{0:T(1024)S(1)} %multiply_subtract_fusion.5) | copy-start | bytes 24580 | tf_op jit(solution)/shard_map/while
  328.0 4.0 %collective-permute-start.4 = (f32[2,4096]{1,0:T(2,128)S(1)}, f32[2,4096]{1,0:T(2,128)S(1)}, u32[]{:S(2)}, u32[]{:S(2)}) collective-permute-start(f32[2,4096]{1,0:T(2,128)S(1)} %get-tuple-element.280), channel_id=1, source_target_pairs={{0,24},{8,0},{16,8},{24,16},{32,56},{40,32},{48,40},{56,48},{64,88... | collective-permute-start | bytes 98312 | tf_op jit(solution)/shard_map/while/body/eval_jaxpr/ppermute | solution.py:35
  329.8 5.4 %collective-permute-start.5 = (f32[2,4096]{1,0:T(2,128)S(1)}, f32[2,4096]{1,0:T(2,128)S(1)}, u32[]{:S(2)}, u32[]{:S(2)}) collective-permute-start(f32[2,4096]{1,0:T(2,128)S(1)} %get-tuple-element.280), channel_id=1, source_target_pairs={{0,16},{8,24},{16,0},{24,8},{32,48},{40,56},{48,32},{56,40},{64,80... | collective-permute-start | bytes 98312 | tf_op jit(solution)/shard_map/while/body/eval_jaxpr/ppermute | solution.py:35
  330.7 5.1 %collective-permute-start.6 = (f32[2,4096]{1,0:T(2,128)S(1)}, f32[2,4096]{1,0:T(2,128)S(1)}, u32[]{:S(2)}, u32[]{:S(2)}) collective-permute-start(f32[2,4096]{1,0:T(2,128)S(1)} %get-tuple-element.280), channel_id=1, source_target_pairs={{0,8},{8,16},{16,24},{24,0},{32,40},{40,48},{48,56},{56,32},{64,72... | collective-permute-start | bytes 98312 | tf_op jit(solution)/shard_map/while/body/eval_jaxpr/ppermute | solution.py:35
  336.1 4.0 %collective-permute-start.7 = (f32[2,4096]{1,0:T(2,128)S(1)}, f32[2,4096]{1,0:T(2,128)S(1)}, u32[]{:S(2)}, u32[]{:S(2)}) collective-permute-start(f32[2,4096]{1,0:T(2,128)S(1)} %get-tuple-element.284), channel_id=1, source_target_pairs={{0,96},{8,104},{16,112},{24,120},{32,0},{40,8},{48,16},{56,24},{64... | collective-permute-start | bytes 98312 | tf_op jit(solution)/shard_map/while/body/eval_jaxpr/ppermute | solution.py:35
  337.5 5.4 %collective-permute-start.8 = (f32[2,4096]{1,0:T(2,128)S(1)}, f32[2,4096]{1,0:T(2,128)S(1)}, u32[]{:S(2)}, u32[]{:S(2)}) collective-permute-start(f32[2,4096]{1,0:T(2,128)S(1)} %get-tuple-element.284), channel_id=1, source_target_pairs={{0,64},{8,72},{16,80},{24,88},{32,96},{40,104},{48,112},{56,120},{... | collective-permute-start | bytes 98312 | tf_op jit(solution)/shard_map/while/body/eval_jaxpr/ppermute | solution.py:35
  338.4 5.1 %collective-permute-start.9 = (f32[2,4096]{1,0:T(2,128)S(1)}, f32[2,4096]{1,0:T(2,128)S(1)}, u32[]{:S(2)}, u32[]{:S(2)}) collective-permute-start(f32[2,4096]{1,0:T(2,128)S(1)} %get-tuple-element.284), channel_id=1, source_target_pairs={{0,32},{8,40},{16,48},{24,56},{32,64},{40,72},{48,80},{56,88},{64,... | collective-permute-start | bytes 98312 | tf_op jit(solution)/shard_map/while/body/eval_jaxpr/ppermute | solution.py:35
  343.8 0.6 copy-start.4
Sparse Core Ops, SparseCore 0:
  10.1 53.9 all-gather.1

commit v4 on v2

--- a/solution.py
+++ b/solution.py
@@ -38,16 +38,21 @@
 
 
 def combine_over(peak, total, axis, digits):
+    size = lax.axis_size(axis)
     packed = jnp.stack([peak, total])
     stride = 1
     for width in digits:
-        parts = exchange(packed, axis, stride, width)
+        parts = [packed] + [
+            lax.ppermute(packed, axis, digit_partners(axis, size, stride, width, k)) for k in range(1, width)
+        ]
         new_peak = parts[0][0]
         for part in parts[1:]:
             new_peak = jnp.maximum(new_peak, part[0])
-        new_total = parts[0][1] * jnp.exp(parts[0][0] - new_peak)
-        for part in parts[1:]:
-            new_total = new_total + part[1] * jnp.exp(part[0] - new_peak)
+        terms = [part[1] * jnp.exp(part[0] - new_peak) for part in parts]
+        if width == 4:
+            new_total = (terms[0] + terms[2]) + (terms[1] + terms[3])
+        else:
+            new_total = terms[0] + terms[1]
         packed = jnp.stack([new_peak, new_total])
         stride *= width
     return packed[0] + jnp.log(packed[1])

time: 301 us -> 282 us (0.937)
  other arithmetic: 117 us -> 102 us
  waiting for transfers between devices: 81 us -> 67.6 us
  starting transfers between devices: 44.4 us -> 55.9 us
    ppermute x37 -> x7, waiting for transfers between devices: 53 us -> 10.6 us  [exchange(): lax.ppermute(x, axis, digit_partners(axis, size, stride, width, k))]
    ppermute x0 -> x30, starting transfers between devices: none -> 41.5 us  [combine_over(): lax.ppermute(packed, axis, digit_partners(axis, size, stride, width, k))]
    ppermute x37 -> x7, starting transfers between devices: 44.4 us -> 14.4 us  [exchange(): lax.ppermute(x, axis, digit_partners(axis, size, stride, width, k))]
    ppermute x0 -> x30, waiting for transfers between devices: none -> 29 us  [combine_over(): lax.ppermute(packed, axis, digit_partners(axis, size, stride, width, k))]
    reduce_max x2, other arithmetic: 19.7 us -> 7.99 us  [logsum_col(): peak = jnp.max(scores, axis=1)]
    reduce_sum x3, other arithmetic: 39.2 us -> 30.9 us  [logsum_col(): totals = jnp.sum(jnp.exp(scores - peak[:, None]), axis=1)]
where the time goes in v4:
time: 282 us
  other arithmetic  102 us (36%)
  waiting for transfers between devices  67.6 us (24%)
  starting transfers between devices  55.9 us (20%)
  matrix products  38.7 us (14%)
  between operations  15.4 us (5%)
  local copies, waits for them, and re-layouts  2.88 us (1%)
    ppermute x30, starting transfers between devices, combine_over(): lax.ppermute(packed, axis, digit_partners(axis, size, stride, width, k))  41.5 us
    dot_general x1, matrix products, inner_costs(): lax.dot_general(left, right, (((1,), (1,)), ((), ())), precision=lax.Prec...  38.7 us
    reduce_sum x3, other arithmetic, logsum_row(): totals = jnp.sum(jnp.exp(scores - peak[None, :]), axis=0)  31.7 us
    reduce_sum x3, other arithmetic, logsum_col(): totals = jnp.sum(jnp.exp(scores - peak[:, None]), axis=1)  30.9 us
    ppermute x30, waiting for transfers between devices, combine_over(): lax.ppermute(packed, axis, digit_partners(axis, size, stride, width, k))  29 us
    all_gather x1, waiting for transfers between devices, per_device(): lax.all_gather(passages, 'row', axis=0, tiled=True)  27.4 us
    reduce_max x3, other arithmetic, logsum_row(): peak = jnp.max(scores, axis=0)  25.9 us
    ppermute x7, starting transfers between devices, exchange(): lax.ppermute(x, axis, digit_partners(axis, size, stride, width, k))  14.4 us
  transfers between devices with their start and end apart: 38, of which 35 were waited for; matrix products, arithmetic and copies ran while one was open for 1% of the time, Pallas kernels for 0%

profile of v4, /device:TPU:0, one launch (start us, length us, event | category | flops | bytes accessed | tf_op | source)
XLA Modules:
  0.0 282.1 jit_solution(8551512878929761182)
XLA Ops:
  7.9 1.7 collective-permute-start.1
  9.6 2.0 collective-permute-start.2
  11.6 2.0 collective-permute-start.3
  13.7 1.6 collective-permute-start.4
  17.3 1.7 collective-permute-start.5
  19.0 5.3 %collective-permute-start.6 = (f32[256,256]{1,0:T(8,128)}, f32[256,256]{1,0:T(8,128)S(1)}, u32[]{:S(2)}, u32[]{:S(2)}) collective-permute-start(f32[256,256]{1,0:T(8,128)} %param.3), channel_id=1, source_target_pairs={{0,7},{1,0},{2,1},{3,2},{4,3},{5,4},{6,5},{7,6},{8,15},{9,8},{10,9... | collective-permute-start | bytes 786440 | tf_op jit(solution)/shard_map/ppermute | solution.py:35
  24.3 5.3 %collective-permute-done.2 = f32[256,256]{1,0:T(8,128)S(1)} collective-permute-done((f32[256,256]{1,0:T(8,128)}, f32[256,256]{1,0:T(8,128)S(1)}, u32[]{:S(2)}, u32[]{:S(2)}) %collective-permute-start.2) | collective-permute-done | bytes 262176 | tf_op jit(solution)/shard_map/ppermute | solution.py:35
  29.6 1.3 collective-permute-done.3
  30.9 1.9 collective-permute-done.4
  33.0 1.8 collective-permute-done.6
  35.1 1.3 copy-done
  36.8 27.4 %all-gather.2.cloned.1.call-done = f32[4096,256]{1,0:T(8,128)} async-done(((f32[256,256]{1,0:T(8,128)}), f32[4096,256]{1,0:T(8,128)}) %all-gather.2.cloned.1.call-update) | async-done | bytes 4194320 | tf_op jit(solution)/shard_map/all_gather | solution.py:100
  64.1 2.8 multiply_reduce_fusion
  66.9 38.7 %fusion = (f32[2048]{0:T(1024)S(1)}, f32[2048,4096]{1,0:T(8,128)}) fusion(f32[]{:T(128)} %bitcast, f32[2048,256]{1,0:T(8,128)} %copy-done, f32[4096,256]{1,0:T(8,128)} %all-gather.2.cloned.1.call-done, f32[4096]{0:T(1024)S(1)} %multiply_reduce_fusion, f32[2048]{0:T(1024)S(1)} %multiply_reduce_fusion.1), kind=kOutput, calls=%fused_computation.13 | convolution fusion | flops 25820133376 | bytes 39878660 | tf_op jit(solution)/shard_map/dot_general | solution.py:14
  105.6 14.5 %exponential_reduce_fusion.5 = f32[2048]{0:T(1024)S(1)} fusion(f32[2048]{0:T(1024)S(1)} %get-tuple-element.50, f32[]{:T(128)} %bitcast, f32[2048,4096]{1,0:T(8,128)} %get-tuple-element.51), kind=kLoop, calls=%fused_computation.10 | loop fusion | flops 33552384 | bytes 33570820 | tf_op jit(solution)/shard_map/reduce_sum | solution.py:78
  121.5 1.5 collective-permute-start.8
  123.0 2.7 collective-permute-start.9
  125.7 1.5 collective-permute-start.10
  129.6 15.8 %fusion.3 = f32[4096]{0:T(1024)S(1)} fusion(f32[]{:T(128)} %bitcast, f32[2048,4096]{1,0:T(8,128)} %get-tuple-element.51, f32[2048]{0:T(1024)S(1)} %multiply_subtract_fusion.6), kind=kLoop, calls=%fused_computation.17 | loop fusion | flops 25161728 | bytes 33579012 | tf_op jit(solution)/shard_map/reduce_max | solution.py:83
  145.4 16.4 %exponential_reduce_fusion.4 = f32[4096]{0:T(1024)S(1)} fusion(f32[4096]{0:T(1024)S(1)} %fusion.3, f32[]{:T(128)} %bitcast, f32[2048,4096]{1,0:T(8,128)} %get-tuple-element.51, f32[2048]{0:T(1024)S(1)} %multiply_subtract_fusion.6), kind=kLoop, calls=%fused_computation.8 | loop fusion | flops 33550336 | bytes 33595396 | tf_op jit(solution)/shard_map/reduce_sum | solution.py:84
  161.9 1.6 collective-permute-start.11
  163.5 2.7 collective-permute-start.12
  166.2 1.4 collective-permute-start.13
  167.6 1.3 collective-permute-done.12
  170.5 2.3 collective-permute-start.15
  172.8 1.7 collective-permute-start.16
  176.9 4.0 %fusion.1 = f32[2048]{0:T(1024)S(1)} fusion(f32[]{:T(128)} %bitcast, f32[2048,4096]{1,0:T(8,128)S(1)} %bitcast.86, f32[4096]{0:T(1024)S(1)} %bitcast.99), kind=kLoop, calls=%fused_computation.14 | loop fusion | flops 25163776 | bytes 33579012 | tf_op jit(solution)/shard_map/reduce_max | solution.py:77
  180.9 8.2 %exponential_reduce_fusion.3 = f32[2048]{0:T(1024)S(1)} fusion(f32[2048]{0:T(1024)S(1)} %fusion.1, f32[]{:T(128)} %bitcast, f32[2048,4096]{1,0:T(8,128)S(1)} %bitcast.86, f32[4096]{0:T(1024)S(1)} %bitcast.100), kind=kLoop, calls=%fused_computation.6 | loop fusion | flops 33552384 | bytes 33587204 | tf_op jit(solution)/shard_map/reduce_sum | solution.py:78
  190.9 3.8 %collective-permute-start.19 = (f32[2,2048]{1,0:T(2,128)S(1)}, f32[2,2048]{1,0:T(2,128)S(1)}, u32[]{:S(2)}, u32[]{:S(2)}) collective-permute-start(f32[2,2048]{1,0:T(2,128)S(1)} %pad_maximum_fusion.9), channel_id=1, source_target_pairs={{0,4},{1,5},{2,6},{3,7},{4,0},{5,1},{6,2},{7,3},{8,12},{9,13},{10,... | collective-permute-start | bytes 49160 | tf_op jit(solution)/shard_map/ppermute | solution.py:46
  196.6 1.8 collective-permute-done.20
  198.5 5.0 %fusion.4 = f32[4096]{0:T(1024)S(1)} fusion(f32[]{:T(128)} %bitcast, f32[2048,4096]{1,0:T(8,128)S(1)} %bitcast.86, f32[2048]{0:T(1024)S(1)} %multiply_subtract_fusion.5), kind=kLoop, calls=%fused_computation.18 | loop fusion | flops 25161728 | bytes 33579012 | tf_op jit(solution)/shard_map/reduce_max | solution.py:83
  203.5 7.6 %exponential_reduce_fusion.2 = f32[4096]{0:T(1024)S(1)} fusion(f32[4096]{0:T(1024)S(1)} %fusion.4, f32[]{:T(128)} %bitcast, f32[2048,4096]{1,0:T(8,128)S(1)} %bitcast.86, f32[2048]{0:T(1024)S(1)} %multiply_subtract_fusion.5), kind=kLoop, calls=%fused_computation.4 | loop fusion | flops 33550336 | bytes 33595396 | tf_op jit(solution)/shard_map/reduce_sum | solution.py:84
  211.2 1.7 collective-permute-start.21
  213.0 2.7 collective-permute-start.22
  216.4 2.0 collective-permute-done.22
  219.7 1.5 collective-permute-start.24
  221.3 2.7 collective-permute-start.25
  224.9 1.7 collective-permute-done.25
  228.0 4.0 %fusion.2 = f32[2048]{0:T(1024)S(1)} fusion(f32[]{:T(128)} %bitcast, f32[2048,4096]{1,0:T(8,128)S(1)} %bitcast.86, f32[4096]{0:T(1024)S(1)} %bitcast.101), kind=kLoop, calls=%fused_computation.15 | loop fusion | flops 25163776 | bytes 33579012 | tf_op jit(solution)/shard_map/reduce_max | solution.py:77
  232.0 8.2 %exponential_reduce_fusion.1 = f32[2048]{0:T(1024)S(1)} fusion(f32[2048]{0:T(1024)S(1)} %fusion.2, f32[]{:T(128)} %bitcast, f32[2048,4096]{1,0:T(8,128)S(1)} %bitcast.86, f32[4096]{0:T(1024)S(1)} %bitcast.102), kind=kLoop, calls=%fused_computation.2 | loop fusion | flops 33552384 | bytes 33587204 | tf_op jit(solution)/shard_map/reduce_sum | solution.py:78
  241.7 2.7 collective-permute-start.29
  244.4 1.5 collective-permute-start.30
  248.2 5.0 %fusion.5 = f32[4096]{0:T(1024)S(1)} fusion(f32[]{:T(128)} %bitcast, f32[2048,4096]{1,0:T(8,128)S(1)} %bitcast.86, f32[2048]{0:T(1024)S(1)} %multiply_subtract_fusion.4), kind=kLoop, calls=%fused_computation.19 | loop fusion | flops 25161728 | bytes 33579012 | tf_op jit(solution)/shard_map/reduce_max | solution.py:83
  253.2 7.6 %exponential_reduce_fusion = f32[4096]{0:T(1024)S(1)} fusion(f32[4096]{0:T(1024)S(1)} %fusion.5, f32[]{:T(128)} %bitcast, f32[2048,4096]{1,0:T(8,128)S(1)} %bitcast.86, f32[2048]{0:T(1024)S(1)} %multiply_subtract_fusion.4), kind=kLoop, calls=%fused_computation | loop fusion | flops 33550336 | bytes 33595396 | tf_op jit(solution)/shard_map/reduce_sum | solution.py:84
  261.0 2.7 collective-permute-start.32
  263.7 1.4 collective-permute-start.33
  267.9 2.7 collective-permute-start.35
  270.6 1.4 collective-permute-start.36
  (116 shorter events, 28.4 us)
Async XLA Ops:
  7.2 57.0 %all-gather.2.cloned.1.call-start = ((), (), s32[]{:S(2)}) async-start(), calls=%async_computation | async-start | bytes 4456448 | tf_op jit(solution)/shard_map/all_gather | solution.py:100
  7.9 9.4 %collective-permute-start = (f32[256,256]{1,0:T(8,128)}, f32[256,256]{1,0:T(8,128)S(1)}, u32[]{:S(2)}, u32[]{:S(2)}) collective-permute-start(f32[256,256]{1,0:T(8,128)} %param.3), channel_id=1, source_target_pairs={{0,1},{1,2},{2,3},{3,4},{4,5},{5,6},{6,7},{7,0},{8,9},{9,10},{10,1... | collective-permute-start | bytes 786440 | tf_op jit(solution)/shard_map/ppermute | solution.py:35
  7.9 11.0 %collective-permute-start.1 = (f32[256,256]{1,0:T(8,128)}, f32[256,256]{1,0:T(8,128)S(1)}, u32[]{:S(2)}, u32[]{:S(2)}) collective-permute-start(f32[256,256]{1,0:T(8,128)} %param.3), channel_id=1, source_target_pairs={{0,2},{1,3},{2,4},{3,5},{4,6},{5,7},{6,0},{7,1},{8,10},{9,11},{10,... | collective-permute-start | bytes 786440 | tf_op jit(solution)/shard_map/ppermute | solution.py:35
  9.6 20.0 %collective-permute-start.2 = (f32[256,256]{1,0:T(8,128)}, f32[256,256]{1,0:T(8,128)S(1)}, u32[]{:S(2)}, u32[]{:S(2)}) collective-permute-start(f32[256,256]{1,0:T(8,128)} %param.3), channel_id=1, source_target_pairs={{0,3},{1,4},{2,5},{3,6},{4,7},{5,0},{6,1},{7,2},{8,11},{9,12},{10,... | collective-permute-start | bytes 786440 | tf_op jit(solution)/shard_map/ppermute | solution.py:35
  11.6 19.3 %collective-permute-start.3 = (f32[256,256]{1,0:T(8,128)}, f32[256,256]{1,0:T(8,128)S(1)}, u32[]{:S(2)}, u32[]{:S(2)}) collective-permute-start(f32[256,256]{1,0:T(8,128)} %param.3), channel_id=1, source_target_pairs={{0,4},{1,5},{2,6},{3,7},{4,0},{5,1},{6,2},{7,3},{8,12},{9,13},{10,... | collective-permute-start | bytes 786440 | tf_op jit(solution)/shard_map/ppermute | solution.py:35
  13.7 19.2 %collective-permute-start.4 = (f32[256,256]{1,0:T(8,128)}, f32[256,256]{1,0:T(8,128)S(1)}, u32[]{:S(2)}, u32[]{:S(2)}) collective-permute-start(f32[256,256]{1,0:T(8,128)} %param.3), channel_id=1, source_target_pairs={{0,5},{1,6},{2,7},{3,0},{4,1},{5,2},{6,3},{7,4},{8,13},{9,14},{10,... | collective-permute-start | bytes 786440 | tf_op jit(solution)/shard_map/ppermute | solution.py:35
  17.3 15.7 %collective-permute-start.5 = (f32[256,256]{1,0:T(8,128)}, f32[256,256]{1,0:T(8,128)S(1)}, u32[]{:S(2)}, u32[]{:S(2)}) collective-permute-start(f32[256,256]{1,0:T(8,128)} %param.3), channel_id=1, source_target_pairs={{0,6},{1,7},{2,0},{3,1},{4,2},{5,3},{6,4},{7,5},{8,14},{9,15},{10,... | collective-permute-start | bytes 786440 | tf_op jit(solution)/shard_map/ppermute | solution.py:35
  19.0 15.9 %collective-permute-start.6 = (f32[256,256]{1,0:T(8,128)}, f32[256,256]{1,0:T(8,128)S(1)}, u32[]{:S(2)}, u32[]{:S(2)}) collective-permute-start(f32[256,256]{1,0:T(8,128)} %param.3), channel_id=1, source_target_pairs={{0,7},{1,0},{2,1},{3,2},{4,3},{5,4},{6,5},{7,6},{8,15},{9,8},{10,9... | collective-permute-start | bytes 786440 | tf_op jit(solution)/shard_map/ppermute | solution.py:35
  35.1 1.3 copy-start
  120.2 1.3 collective-permute-start.7
  121.5 5.7 %collective-permute-start.8 = (f32[2,2048]{1,0:T(2,128)S(1)}, f32[2,2048]{1,0:T(2,128)S(1)}, u32[]{:S(2)}, u32[]{:S(2)}) collective-permute-start(f32[2,2048]{1,0:T(2,128)S(1)} %pad_maximum_fusion.7), channel_id=1, source_target_pairs={{0,2},{1,3},{2,4},{3,5},{4,6},{5,7},{6,0},{7,1},{8,10},{9,11},{10,... | collective-permute-start | bytes 49160 | tf_op jit(solution)/shard_map/ppermute | solution.py:46
  123.0 5.2 %collective-permute-start.9 = (f32[2,2048]{1,0:T(2,128)S(1)}, f32[2,2048]{1,0:T(2,128)S(1)}, u32[]{:S(2)}, u32[]{:S(2)}) collective-permute-start(f32[2,2048]{1,0:T(2,128)S(1)} %pad_maximum_fusion.7), channel_id=1, source_target_pairs={{0,4},{1,5},{2,6},{3,7},{4,0},{5,1},{6,2},{7,3},{8,12},{9,13},{10,... | collective-permute-start | bytes 49160 | tf_op jit(solution)/shard_map/ppermute | solution.py:46
  125.7 3.7 %collective-permute-start.10 = (f32[2,2048]{1,0:T(2,128)S(1)}, f32[2,2048]{1,0:T(2,128)S(1)}, u32[]{:S(2)}, u32[]{:S(2)}) collective-permute-start(f32[2,2048]{1,0:T(2,128)S(1)} %pad_maximum_fusion.7), channel_id=1, source_target_pairs={{0,6},{1,7},{2,0},{3,1},{4,2},{5,3},{6,4},{7,5},{8,14},{9,15},{10,... | collective-permute-start | bytes 49160 | tf_op jit(solution)/shard_map/ppermute | solution.py:46
  129.5 47.3 %slice-start = ((s8[33554432]{0:T(1024)(128)(4,1)}), s8[4194304]{0:T(1024)(128)(4,1)S(1)}, s32[]{:S(2)}) async-start(s8[33554432]{0:T(1024)(128)(4,1)} %bitcast.85), calls=%async_computation.1 | async-start | bytes 8388608
  129.5 47.3 %slice-start.1 = ((s8[33554432]{0:T(1024)(128)(4,1)}), s8[4194304]{0:T(1024)(128)(4,1)S(1)}, s32[]{:S(2)}) async-start(s8[33554432]{0:T(1024)(128)(4,1)} %bitcast.85), calls=%async_computation.2 | async-start | bytes 8388608
  129.5 47.3 %slice-start.2 = ((s8[33554432]{0:T(1024)(128)(4,1)}), s8[4194304]{0:T(1024)(128)(4,1)S(1)}, s32[]{:S(2)}) async-start(s8[33554432]{0:T(1024)(128)(4,1)} %bitcast.85), calls=%async_computation.3 | async-start | bytes 8388608
  129.6 47.3 %slice-start.3 = ((s8[33554432]{0:T(1024)(128)(4,1)}), s8[4194304]{0:T(1024)(128)(4,1)S(1)}, s32[]{:S(2)}) async-start(s8[33554432]{0:T(1024)(128)(4,1)} %bitcast.85), calls=%async_computation.4 | async-start | bytes 8388608
  145.4 31.5 %slice-start.4 = ((s8[33554432]{0:T(1024)(128)(4,1)}), s8[4194304]{0:T(1024)(128)(4,1)S(1)}, s32[]{:S(2)}) async-start(s8[33554432]{0:T(1024)(128)(4,1)} %bitcast.85), calls=%async_computation.5 | async-start | bytes 8388608
  145.4 31.5 %slice-start.5 = ((s8[33554432]{0:T(1024)(128)(4,1)}), s8[4194304]{0:T(1024)(128)(4,1)S(1)}, s32[]{:S(2)}) async-start(s8[33554432]{0:T(1024)(128)(4,1)} %bitcast.85), calls=%async_computation.6 | async-start | bytes 8388608
  145.4 31.5 %slice-start.6 = ((s8[33554432]{0:T(1024)(128)(4,1)}), s8[4194304]{0:T(1024)(128)(4,1)S(1)}, s32[]{:S(2)}) async-start(s8[33554432]{0:T(1024)(128)(4,1)} %bitcast.85), calls=%async_computation.7 | async-start | bytes 8388608
  145.4 31.5 %slice-start.7 = ((s8[33554432]{0:T(1024)(128)(4,1)}), s8[4194304]{0:T(1024)(128)(4,1)S(1)}, s32[]{:S(2)}) async-start(s8[33554432]{0:T(1024)(128)(4,1)} %bitcast.85), calls=%async_computation.8 | async-start | bytes 8388608
  161.9 5.7 %collective-permute-start.11 = (f32[2,4096]{1,0:T(2,128)S(1)}, f32[2,4096]{1,0:T(2,128)S(1)}, u32[]{:S(2)}, u32[]{:S(2)}) collective-permute-start(f32[2,4096]{1,0:T(2,128)S(1)} %pad_maximum_fusion), channel_id=1, source_target_pairs={{0,8},{8,16},{16,24},{24,0},{32,40},{40,48},{48,56},{56,32},{64,72... | collective-permute-start | bytes 98312 | tf_op jit(solution)/shard_map/ppermute | solution.py:46
  163.5 5.4 %collective-permute-start.12 = (f32[2,4096]{1,0:T(2,128)S(1)}, f32[2,4096]{1,0:T(2,128)S(1)}, u32[]{:S(2)}, u32[]{:S(2)}) collective-permute-start(f32[2,4096]{1,0:T(2,128)S(1)} %pad_maximum_fusion), channel_id=1, source_target_pairs={{0,16},{8,24},{16,0},{24,8},{32,48},{40,56},{48,32},{56,40},{64,80... | collective-permute-start | bytes 98312 | tf_op jit(solution)/shard_map/ppermute | solution.py:46
  166.2 3.9 %collective-permute-start.13 = (f32[2,4096]{1,0:T(2,128)S(1)}, f32[2,4096]{1,0:T(2,128)S(1)}, u32[]{:S(2)}, u32[]{:S(2)}) collective-permute-start(f32[2,4096]{1,0:T(2,128)S(1)} %pad_maximum_fusion), channel_id=1, source_target_pairs={{0,24},{8,0},{16,8},{24,16},{32,56},{40,32},{48,40},{56,48},{64,88... | collective-permute-start | bytes 98312 | tf_op jit(solution)/shard_map/ppermute | solution.py:46
  170.3 5.2 %collective-permute-start.14 = (f32[2,4096]{1,0:T(2,128)S(1)}, f32[2,4096]{1,0:T(2,128)S(1)}, u32[]{:S(2)}, u32[]{:S(2)}) collective-permute-start(f32[2,4096]{1,0:T(2,128)S(1)} %pad_maximum_fusion.1), channel_id=1, source_target_pairs={{0,32},{8,40},{16,48},{24,56},{32,64},{40,72},{48,80},{56,88},{64,... | collective-permute-start | bytes 98312 | tf_op jit(solution)/shard_map/ppermute | solution.py:46
  170.5 5.4 %collective-permute-start.15 = (f32[2,4096]{1,0:T(2,128)S(1)}, f32[2,4096]{1,0:T(2,128)S(1)}, u32[]{:S(2)}, u32[]{:S(2)}) collective-permute-start(f32[2,4096]{1,0:T(2,128)S(1)} %pad_maximum_fusion.1), channel_id=1, source_target_pairs={{0,64},{8,72},{16,80},{24,88},{32,96},{40,104},{48,112},{56,120},{... | collective-permute-start | bytes 98312 | tf_op jit(solution)/shard_map/ppermute | solution.py:46
  172.8 3.9 %collective-permute-start.16 = (f32[2,4096]{1,0:T(2,128)S(1)}, f32[2,4096]{1,0:T(2,128)S(1)}, u32[]{:S(2)}, u32[]{:S(2)}) collective-permute-start(f32[2,4096]{1,0:T(2,128)S(1)} %pad_maximum_fusion.1), channel_id=1, source_target_pairs={{0,96},{8,104},{16,112},{24,120},{32,0},{40,8},{48,16},{56,24},{64... | collective-permute-start | bytes 98312 | tf_op jit(solution)/shard_map/ppermute | solution.py:46
  189.2 1.3 collective-permute-start.17
  190.5 5.0 %collective-permute-start.18 = (f32[2,2048]{1,0:T(2,128)S(1)}, f32[2,2048]{1,0:T(2,128)S(1)}, u32[]{:S(2)}, u32[]{:S(2)}) collective-permute-start(f32[2,2048]{1,0:T(2,128)S(1)} %pad_maximum_fusion.9), channel_id=1, source_target_pairs={{0,2},{1,3},{2,4},{3,5},{4,6},{5,7},{6,0},{7,1},{8,10},{9,11},{10,... | collective-permute-start | bytes 49160 | tf_op jit(solution)/shard_map/ppermute | solution.py:46
  190.9 5.7 %collective-permute-start.19 = (f32[2,2048]{1,0:T(2,128)S(1)}, f32[2,2048]{1,0:T(2,128)S(1)}, u32[]{:S(2)}, u32[]{:S(2)}) collective-permute-start(f32[2,2048]{1,0:T(2,128)S(1)} %pad_maximum_fusion.9), channel_id=1, source_target_pairs={{0,4},{1,5},{2,6},{3,7},{4,0},{5,1},{6,2},{7,3},{8,12},{9,13},{10,... | collective-permute-start | bytes 49160 | tf_op jit(solution)/shard_map/ppermute | solution.py:46
  194.7 3.7 %collective-permute-start.20 = (f32[2,2048]{1,0:T(2,128)S(1)}, f32[2,2048]{1,0:T(2,128)S(1)}, u32[]{:S(2)}, u32[]{:S(2)}) collective-permute-start(f32[2,2048]{1,0:T(2,128)S(1)} %pad_maximum_fusion.9), channel_id=1, source_target_pairs={{0,6},{1,7},{2,0},{3,1},{4,2},{5,3},{6,4},{7,5},{8,14},{9,15},{10,... | collective-permute-start | bytes 49160 | tf_op jit(solution)/shard_map/ppermute | solution.py:46
  211.2 5.2 %collective-permute-start.21 = (f32[2,4096]{1,0:T(2,128)S(1)}, f32[2,4096]{1,0:T(2,128)S(1)}, u32[]{:S(2)}, u32[]{:S(2)}) collective-permute-start(f32[2,4096]{1,0:T(2,128)S(1)} %pad_maximum_fusion.2), channel_id=1, source_target_pairs={{0,8},{8,16},{16,24},{24,0},{32,40},{40,48},{48,56},{56,32},{64,72... | collective-permute-start | bytes 98312 | tf_op jit(solution)/shard_map/ppermute | solution.py:46
  213.0 5.4 %collective-permute-start.22 = (f32[2,4096]{1,0:T(2,128)S(1)}, f32[2,4096]{1,0:T(2,128)S(1)}, u32[]{:S(2)}, u32[]{:S(2)}) collective-permute-start(f32[2,4096]{1,0:T(2,128)S(1)} %pad_maximum_fusion.2), channel_id=1, source_target_pairs={{0,16},{8,24},{16,0},{24,8},{32,48},{40,56},{48,32},{56,40},{64,80... | collective-permute-start | bytes 98312 | tf_op jit(solution)/shard_map/ppermute | solution.py:46
  215.7 3.9 %collective-permute-start.23 = (f32[2,4096]{1,0:T(2,128)S(1)}, f32[2,4096]{1,0:T(2,128)S(1)}, u32[]{:S(2)}, u32[]{:S(2)}) collective-permute-start(f32[2,4096]{1,0:T(2,128)S(1)} %pad_maximum_fusion.2), channel_id=1, source_target_pairs={{0,24},{8,0},{16,8},{24,16},{32,56},{40,32},{48,40},{56,48},{64,88... | collective-permute-start | bytes 98312 | tf_op jit(solution)/shard_map/ppermute | solution.py:46
  219.7 5.2 %collective-permute-start.24 = (f32[2,4096]{1,0:T(2,128)S(1)}, f32[2,4096]{1,0:T(2,128)S(1)}, u32[]{:S(2)}, u32[]{:S(2)}) collective-permute-start(f32[2,4096]{1,0:T(2,128)S(1)} %pad_maximum_fusion.3), channel_id=1, source_target_pairs={{0,32},{8,40},{16,48},{24,56},{32,64},{40,72},{48,80},{56,88},{64,... | collective-permute-start | bytes 98312 | tf_op jit(solution)/shard_map/ppermute | solution.py:46
  221.3 5.4 %collective-permute-start.25 = (f32[2,4096]{1,0:T(2,128)S(1)}, f32[2,4096]{1,0:T(2,128)S(1)}, u32[]{:S(2)}, u32[]{:S(2)}) collective-permute-start(f32[2,4096]{1,0:T(2,128)S(1)} %pad_maximum_fusion.3), channel_id=1, source_target_pairs={{0,64},{8,72},{16,80},{24,88},{32,96},{40,104},{48,112},{56,120},{... | collective-permute-start | bytes 98312 | tf_op jit(solution)/shard_map/ppermute | solution.py:46
  223.9 3.9 %collective-permute-start.26 = (f32[2,4096]{1,0:T(2,128)S(1)}, f32[2,4096]{1,0:T(2,128)S(1)}, u32[]{:S(2)}, u32[]{:S(2)}) collective-permute-start(f32[2,4096]{1,0:T(2,128)S(1)} %pad_maximum_fusion.3), channel_id=1, source_target_pairs={{0,96},{8,104},{16,112},{24,120},{32,0},{40,8},{48,16},{56,24},{64... | collective-permute-start | bytes 98312 | tf_op jit(solution)/shard_map/ppermute | solution.py:46
  240.2 1.3 collective-permute-start.27
  241.6 5.0 %collective-permute-start.28 = (f32[2,2048]{1,0:T(2,128)S(1)}, f32[2,2048]{1,0:T(2,128)S(1)}, u32[]{:S(2)}, u32[]{:S(2)}) collective-permute-start(f32[2,2048]{1,0:T(2,128)S(1)} %pad_maximum_fusion.11), channel_id=1, source_target_pairs={{0,2},{1,3},{2,4},{3,5},{4,6},{5,7},{6,0},{7,1},{8,10},{9,11},{10,... | collective-permute-start | bytes 49160 | tf_op jit(solution)/shard_map/ppermute | solution.py:46
  241.7 5.3 %collective-permute-start.29 = (f32[2,2048]{1,0:T(2,128)S(1)}, f32[2,2048]{1,0:T(2,128)S(1)}, u32[]{:S(2)}, u32[]{:S(2)}) collective-permute-start(f32[2,2048]{1,0:T(2,128)S(1)} %pad_maximum_fusion.11), channel_id=1, source_target_pairs={{0,4},{1,5},{2,6},{3,7},{4,0},{5,1},{6,2},{7,3},{8,12},{9,13},{10,... | collective-permute-start | bytes 49160 | tf_op jit(solution)/shard_map/ppermute | solution.py:46
  244.4 3.7 %collective-permute-start.30 = (f32[2,2048]{1,0:T(2,128)S(1)}, f32[2,2048]{1,0:T(2,128)S(1)}, u32[]{:S(2)}, u32[]{:S(2)}) collective-permute-start(f32[2,2048]{1,0:T(2,128)S(1)} %pad_maximum_fusion.11), channel_id=1, source_target_pairs={{0,6},{1,7},{2,0},{3,1},{4,2},{5,3},{6,4},{7,5},{8,14},{9,15},{10,... | collective-permute-start | bytes 49160 | tf_op jit(solution)/shard_map/ppermute | solution.py:46
  248.2 12.7 %copy-start.1 = (f32[2048]{0:T(1024)}, f32[2048]{0:T(1024)S(1)}, u32[]{:S(2)}) copy-start(f32[2048]{0:T(1024)S(1)} %multiply_subtract_fusion.4) | copy-start | bytes 24580
  260.9 5.2 %collective-permute-start.31 = (f32[2,4096]{1,0:T(2,128)S(1)}, f32[2,4096]{1,0:T(2,128)S(1)}, u32[]{:S(2)}, u32[]{:S(2)}) collective-permute-start(f32[2,4096]{1,0:T(2,128)S(1)} %pad_maximum_fusion.4), channel_id=1, source_target_pairs={{0,8},{8,16},{16,24},{24,0},{32,40},{40,48},{48,56},{56,32},{64,72... | collective-permute-start | bytes 98312 | tf_op jit(solution)/shard_map/ppermute | solution.py:46
  261.0 5.5 %collective-permute-start.32 = (f32[2,4096]{1,0:T(2,128)S(1)}, f32[2,4096]{1,0:T(2,128)S(1)}, u32[]{:S(2)}, u32[]{:S(2)}) collective-permute-start(f32[2,4096]{1,0:T(2,128)S(1)} %pad_maximum_fusion.4), channel_id=1, source_target_pairs={{0,16},{8,24},{16,0},{24,8},{32,48},{40,56},{48,32},{56,40},{64,80... | collective-permute-start | bytes 98312 | tf_op jit(solution)/shard_map/ppermute | solution.py:46
  263.7 3.9 %collective-permute-start.33 = (f32[2,4096]{1,0:T(2,128)S(1)}, f32[2,4096]{1,0:T(2,128)S(1)}, u32[]{:S(2)}, u32[]{:S(2)}) collective-permute-start(f32[2,4096]{1,0:T(2,128)S(1)} %pad_maximum_fusion.4), channel_id=1, source_target_pairs={{0,24},{8,0},{16,8},{24,16},{32,56},{40,32},{48,40},{56,48},{64,88... | collective-permute-start | bytes 98312 | tf_op jit(solution)/shard_map/ppermute | solution.py:46
  267.8 5.2 %collective-permute-start.34 = (f32[2,4096]{1,0:T(2,128)S(1)}, f32[2,4096]{1,0:T(2,128)S(1)}, u32[]{:S(2)}, u32[]{:S(2)}) collective-permute-start(f32[2,4096]{1,0:T(2,128)S(1)} %pad_maximum_fusion.5), channel_id=1, source_target_pairs={{0,32},{8,40},{16,48},{24,56},{32,64},{40,72},{48,80},{56,88},{64,... | collective-permute-start | bytes 98312 | tf_op jit(solution)/shard_map/ppermute | solution.py:46
  267.9 5.5 %collective-permute-start.35 = (f32[2,4096]{1,0:T(2,128)S(1)}, f32[2,4096]{1,0:T(2,128)S(1)}, u32[]{:S(2)}, u32[]{:S(2)}) collective-permute-start(f32[2,4096]{1,0:T(2,128)S(1)} %pad_maximum_fusion.5), channel_id=1, source_target_pairs={{0,64},{8,72},{16,80},{24,88},{32,96},{40,104},{48,112},{56,120},{... | collective-permute-start | bytes 98312 | tf_op jit(solution)/shard_map/ppermute | solution.py:46
  270.6 3.9 %collective-permute-start.36 = (f32[2,4096]{1,0:T(2,128)S(1)}, f32[2,4096]{1,0:T(2,128)S(1)}, u32[]{:S(2)}, u32[]{:S(2)}) collective-permute-start(f32[2,4096]{1,0:T(2,128)S(1)} %pad_maximum_fusion.5), channel_id=1, source_target_pairs={{0,96},{8,104},{16,112},{24,120},{32,0},{40,8},{48,16},{56,24},{64... | collective-permute-start | bytes 98312 | tf_op jit(solution)/shard_map/ppermute | solution.py:46
Sparse Core Ops, SparseCore 0:
  10.1 53.9 all-gather.1

commit v5 on v4

--- a/solution.py
+++ b/solution.py
@@ -90,6 +90,14 @@
     return jnp.concatenate(exchange(x, "col", 1, size), axis=0)
 
 
+def gather_row(x):
+    stride = 1
+    for width in radix_digits(lax.axis_size("row")):
+        x = jnp.concatenate(exchange(x, "row", stride, width), axis=0)
+        stride *= width
+    return x
+
+
 def per_device(queries, passages, mean_cost):
     entropy_scale = 0.1 * mean_cost[0]
     row_count = lax.axis_size("row")
@@ -97,7 +105,7 @@
     all_queries = queries.shape[0] * row_count * col_count
     all_passages = passages.shape[0] * row_count * col_count
     query_block = gather_col(queries)
-    cost_tile = inner_costs(query_block, lax.all_gather(passages, "row", axis=0, tiled=True))
+    cost_tile = inner_costs(query_block, gather_row(passages))
     col_potential = jnp.zeros((cost_tile.shape[1],), jnp.float32)
     row_potential = jnp.zeros((cost_tile.shape[0],), jnp.float32)
     for repeat in range(ITERS):

time: 282 us -> 290 us (1.028); the launches traced: 282 us -> 286 us
  waiting for transfers between devices: 67.6 us -> 82 us
  between operations: 15.4 us -> 2.3 us
  other arithmetic: 102 us -> 90.5 us
  starting transfers between devices: 55.9 us -> 65.7 us
  local copies, waits for them, and re-layouts: 2.88 us -> 7.92 us
    ppermute x7 -> x13, waiting for transfers between devices: 10.6 us -> 53.1 us  [exchange(): lax.ppermute(x, axis, digit_partners(axis, size, stride, width, k))]
    all_gather x1 -> x0, waiting for transfers between devices: 27.4 us -> none  [per_device(): lax.all_gather(passages, 'row', axis=0, tiled=True)]
    reduce_sum x3, other arithmetic: 31.7 us -> 22.9 us  [logsum_row(): totals = jnp.sum(jnp.exp(scores - peak[None, :]), axis=0)]
    ppermute x7 -> x13, starting transfers between devices: 14.4 us -> 22.2 us  [exchange(): lax.ppermute(x, axis, digit_partners(axis, size, stride, width, k))]
    unnamed x34 -> x18, local copies, waits for them, and re-layouts: 2.63 us -> 7.27 us
  transfers between devices with their start and end apart: 38 -> 43, of which waited for: 35 -> 36; matrix products, arithmetic and copies ran while one was open for 1% -> 1% of each run, Pallas kernels for 0% -> 0%
where the time goes in v5:
time: 290 us; the launch traced here: 286 us
  other arithmetic  90.5 us (31%)
  waiting for transfers between devices  82 us (28%)
  starting transfers between devices  65.7 us (23%)
  matrix products  38.1 us (13%)
  local copies, waits for them, and re-layouts  7.92 us (3%)
    ppermute x13, waiting for transfers between devices, exchange(): lax.ppermute(x, axis, digit_partners(axis, size, stride, width, k))  53.1 us
    ppermute x30, starting transfers between devices, combine_over(): lax.ppermute(packed, axis, digit_partners(axis, size, stride, width, k))  43.5 us
    dot_general x1, matrix products, inner_costs(): lax.dot_general(left, right, (((1,), (1,)), ((), ())), precision=lax.Prec...  38.1 us
    reduce_sum x3, other arithmetic, logsum_col(): totals = jnp.sum(jnp.exp(scores - peak[:, None]), axis=1)  30.9 us
    ppermute x30, waiting for transfers between devices, combine_over(): lax.ppermute(packed, axis, digit_partners(axis, size, stride, width, k))  28.9 us
    reduce_max x3, other arithmetic, logsum_row(): peak = jnp.max(scores, axis=0)  24.2 us
    reduce_sum x3, other arithmetic, logsum_row(): totals = jnp.sum(jnp.exp(scores - peak[None, :]), axis=0)  22.9 us
    ppermute x13, starting transfers between devices, exchange(): lax.ppermute(x, axis, digit_partners(axis, size, stride, width, k))  22.2 us
  transfers between devices with their start and end apart: 43, of which 36 were waited for; matrix products, arithmetic and copies ran while one was open for 1% of the time, Pallas kernels for 0%

profile of v5, /device:TPU:0, one launch (start us, length us, event | category | flops | bytes accessed | tf_op | source)
XLA Modules:
  0.0 286.5 jit_solution(1280386697246608055)
XLA Ops:
  0.6 1.8 collective-permute-start.7
  2.4 2.9 %collective-permute-start.8 = (f32[256,256]{1,0:T(8,128)}, f32[256,256]{1,0:T(8,128)S(1)}, u32[]{:S(2)}, u32[]{:S(2)}) collective-permute-start(f32[256,256]{1,0:T(8,128)} %param.4), channel_id=1, source_target_pairs={{0,16},{8,24},{16,0},{24,8},{32,48},{40,56},{48,32},{56,40},{64,80... | collective-permute-start | bytes 786440 | tf_op jit(solution)/shard_map/ppermute | solution.py:35
  10.3 1.7 collective-permute-start.2
  12.0 5.1 %collective-permute-done.8 = f32[256,256]{1,0:T(8,128)S(1)} collective-permute-done((f32[256,256]{1,0:T(8,128)}, f32[256,256]{1,0:T(8,128)S(1)}, u32[]{:S(2)}, u32[]{:S(2)}) %collective-permute-start.8) | collective-permute-done | bytes 262176 | tf_op jit(solution)/shard_map/ppermute | solution.py:35
  17.1 3.0 %collective-permute-start.3 = (f32[256,256]{1,0:T(8,128)}, f32[256,256]{1,0:T(8,128)S(1)}, u32[]{:S(2)}, u32[]{:S(2)}) collective-permute-start(f32[256,256]{1,0:T(8,128)} %param.3), channel_id=1, source_target_pairs={{0,4},{1,5},{2,6},{3,7},{4,0},{5,1},{6,2},{7,3},{8,12},{9,13},{10,... | collective-permute-start | bytes 786440 | tf_op jit(solution)/shard_map/ppermute | solution.py:35
  21.2 1.6 collective-permute-start.5
  24.2 4.1 %collective-permute-done.2 = f32[256,256]{1,0:T(8,128)S(1)} collective-permute-done((f32[256,256]{1,0:T(8,128)}, f32[256,256]{1,0:T(8,128)S(1)}, u32[]{:S(2)}, u32[]{:S(2)}) %collective-permute-start.2) | collective-permute-done | bytes 262176 | tf_op jit(solution)/shard_map/ppermute | solution.py:35
  28.3 1.9 collective-permute-start.10
  30.3 3.7 %collective-permute-start.11 = (f32[1024,256]{1,0:T(8,128)S(1)}, f32[1024,256]{1,0:T(8,128)S(1)}, u32[]{:S(2)}, u32[]{:S(2)}) collective-permute-start(f32[1024,256]{1,0:T(8,128)S(1)} %get-tuple-element.11), channel_id=1, source_target_pairs={{0,64},{8,72},{16,80},{24,88},{32,96},{40,104},{48,112},{56,120},{... | collective-permute-start | bytes 3145736 | tf_op jit(solution)/shard_map/ppermute | solution.py:35
  33.9 1.7 collective-permute-start.12
  35.6 1.7 collective-permute-done.5
  37.4 1.9 collective-permute-done.6
  39.9 15.5 %collective-permute-done.10 = f32[1024,256]{1,0:T(8,128)S(1)} collective-permute-done((f32[1024,256]{1,0:T(8,128)S(1)}, f32[1024,256]{1,0:T(8,128)S(1)}, u32[]{:S(2)}, u32[]{:S(2)}) %collective-permute-start.10) | collective-permute-done | bytes 1048608 | tf_op jit(solution)/shard_map/ppermute | solution.py:35
  55.4 20.1 %collective-permute-done.11 = f32[1024,256]{1,0:T(8,128)S(1)} collective-permute-done((f32[1024,256]{1,0:T(8,128)S(1)}, f32[1024,256]{1,0:T(8,128)S(1)}, u32[]{:S(2)}, u32[]{:S(2)}) %collective-permute-start.11) | collective-permute-done | bytes 1048608 | tf_op jit(solution)/shard_map/ppermute | solution.py:35
  75.6 4.2 %collective-permute-done.12 = f32[1024,256]{1,0:T(8,128)S(1)} collective-permute-done((f32[1024,256]{1,0:T(8,128)S(1)}, f32[1024,256]{1,0:T(8,128)S(1)}, u32[]{:S(2)}, u32[]{:S(2)}) %collective-permute-start.12) | collective-permute-done | bytes 1048608 | tf_op jit(solution)/shard_map/ppermute | solution.py:35
  81.0 38.1 %fusion = (f32[2048]{0:T(1024)S(1)}, f32[2048,4096]{1,0:T(8,128)}) fusion(f32[]{:T(128)} %bitcast, f32[2048,256]{1,0:T(8,128)S(1)} %bitcast_dynamic-update-slice_fusion, f32[1024,256]{1,0:T(8,128)S(1)} %get-tuple-element.7, f32[1024,256]{1,0:T(8,128)S(1)} %get-tuple-element.8, f32[1024,256]{1,0:T(8,128)S(1)} %get-tuple-element.9, ...), kind=kOutput, calls=%fused_computation.13 | convolution fusion | flops 25823279104 | bytes 39878660 | tf_op jit(solution)/shard_map/dot_general | solution.py:14
  119.1 14.5 %exponential_reduce_fusion.5 = f32[2048]{0:T(1024)S(1)} fusion(f32[2048]{0:T(1024)S(1)} %get-tuple-element.60, f32[]{:T(128)} %bitcast, f32[2048,4096]{1,0:T(8,128)} %get-tuple-element.61), kind=kLoop, calls=%fused_computation.10 | loop fusion | flops 33552384 | bytes 33570820 | tf_op jit(solution)/shard_map/reduce_sum | solution.py:78
  135.9 1.7 collective-permute-start.15
  137.6 2.5 collective-permute-start.16
  142.0 14.1 %fusion.3 = f32[4096]{0:T(1024)S(1)} fusion(f32[]{:T(128)} %bitcast, f32[2048,4096]{1,0:T(8,128)} %get-tuple-element.61, f32[2048]{0:T(1024)S(1)} %multiply_subtract_fusion.6), kind=kLoop, calls=%fused_computation.19 | loop fusion | flops 25161728 | bytes 33579012 | tf_op jit(solution)/shard_map/reduce_max | solution.py:83
  156.1 6.0 %copy-done = f32[2048,4096]{1,0:T(8,128)S(1)} copy-done((f32[2048,4096]{1,0:T(8,128)S(1)}, f32[2048,4096]{1,0:T(8,128)}, u32[]{:S(2)}) %copy-start) | copy-done | bytes 33554456
  162.1 7.6 %exponential_reduce_fusion.4 = f32[4096]{0:T(1024)S(1)} fusion(f32[4096]{0:T(1024)S(1)} %fusion.3, f32[]{:T(128)} %bitcast, f32[2048,4096]{1,0:T(8,128)S(1)} %copy-done, f32[2048]{0:T(1024)S(1)} %multiply_subtract_fusion.6), kind=kLoop, calls=%fused_computation.8 | loop fusion | flops 33550336 | bytes 33595396 | tf_op jit(solution)/shard_map/reduce_sum | solution.py:84
  170.5 3.4 %collective-permute-start.18 = (f32[2,4096]{1,0:T(2,128)S(1)}, f32[2,4096]{1,0:T(2,128)S(1)}, u32[]{:S(2)}, u32[]{:S(2)}) collective-permute-start(f32[2,4096]{1,0:T(2,128)S(1)} %pad_maximum_fusion.5), channel_id=1, source_target_pairs={{0,16},{8,24},{16,0},{24,8},{32,48},{40,56},{48,32},{56,40},{64,80... | collective-permute-start | bytes 98312 | tf_op jit(solution)/shard_map/ppermute | solution.py:46
  173.9 2.5 collective-permute-start.19
  176.4 1.6 collective-permute-done.19
  178.8 3.6 %collective-permute-start.21 = (f32[2,4096]{1,0:T(2,128)S(1)}, f32[2,4096]{1,0:T(2,128)S(1)}, u32[]{:S(2)}, u32[]{:S(2)}) collective-permute-start(f32[2,4096]{1,0:T(2,128)S(1)} %pad_maximum_fusion.6), channel_id=1, source_target_pairs={{0,64},{8,72},{16,80},{24,88},{32,96},{40,104},{48,112},{56,120},{... | collective-permute-start | bytes 98312 | tf_op jit(solution)/shard_map/ppermute | solution.py:46
  184.6 1.7 collective-permute-done.22
  186.4 4.0 %fusion.1 = f32[2048]{0:T(1024)S(1)} fusion(f32[]{:T(128)} %bitcast, f32[2048,4096]{1,0:T(8,128)S(1)} %copy-done, f32[4096]{0:T(1024)S(1)} %bitcast.128), kind=kLoop, calls=%fused_computation.14 | loop fusion | flops 25163776 | bytes 33579012 | tf_op jit(solution)/shard_map/reduce_max | solution.py:77
  190.4 8.2 %exponential_reduce_fusion.3 = f32[2048]{0:T(1024)S(1)} fusion(f32[2048]{0:T(1024)S(1)} %fusion.1, f32[]{:T(128)} %bitcast, f32[2048,4096]{1,0:T(8,128)S(1)} %copy-done, f32[4096]{0:T(1024)S(1)} %bitcast.129), kind=kLoop, calls=%fused_computation.6 | loop fusion | flops 33552384 | bytes 33587204 | tf_op jit(solution)/shard_map/reduce_sum | solution.py:78
  200.0 1.9 collective-permute-start.24
  201.9 2.1 collective-permute-start.25
  205.1 2.1 collective-permute-done.25
  207.9 5.0 %fusion.4 = f32[4096]{0:T(1024)S(1)} fusion(f32[]{:T(128)} %bitcast, f32[2048,4096]{1,0:T(8,128)S(1)} %copy-done, f32[2048]{0:T(1024)S(1)} %multiply_subtract_fusion.5), kind=kLoop, calls=%fused_computation.20 | loop fusion | flops 25161728 | bytes 33579012 | tf_op jit(solution)/shard_map/reduce_max | solution.py:83
  212.9 7.6 %exponential_reduce_fusion.2 = f32[4096]{0:T(1024)S(1)} fusion(f32[4096]{0:T(1024)S(1)} %fusion.4, f32[]{:T(128)} %bitcast, f32[2048,4096]{1,0:T(8,128)S(1)} %copy-done, f32[2048]{0:T(1024)S(1)} %multiply_subtract_fusion.5), kind=kLoop, calls=%fused_computation.4 | loop fusion | flops 33550336 | bytes 33595396 | tf_op jit(solution)/shard_map/reduce_sum | solution.py:84
  222.0 3.6 %collective-permute-start.28 = (f32[2,4096]{1,0:T(2,128)S(1)}, f32[2,4096]{1,0:T(2,128)S(1)}, u32[]{:S(2)}, u32[]{:S(2)}) collective-permute-start(f32[2,4096]{1,0:T(2,128)S(1)} %pad_maximum_fusion.7), channel_id=1, source_target_pairs={{0,16},{8,24},{16,0},{24,8},{32,48},{40,56},{48,32},{56,40},{64,80... | collective-permute-start | bytes 98312 | tf_op jit(solution)/shard_map/ppermute | solution.py:46
  226.1 1.8 collective-permute-done.28
  227.9 1.7 collective-permute-done.29
  229.8 2.7 collective-permute-start.31
  232.5 1.8 collective-permute-start.32
  236.8 4.0 %fusion.2 = f32[2048]{0:T(1024)S(1)} fusion(f32[]{:T(128)} %bitcast, f32[2048,4096]{1,0:T(8,128)S(1)} %copy-done, f32[4096]{0:T(1024)S(1)} %bitcast.130), kind=kLoop, calls=%fused_computation.15 | loop fusion | flops 25163776 | bytes 33579012 | tf_op jit(solution)/shard_map/reduce_max | solution.py:77
  240.8 8.2 %exponential_reduce_fusion.1 = f32[2048]{0:T(1024)S(1)} fusion(f32[2048]{0:T(1024)S(1)} %fusion.2, f32[]{:T(128)} %bitcast, f32[2048,4096]{1,0:T(8,128)S(1)} %copy-done, f32[4096]{0:T(1024)S(1)} %bitcast.131), kind=kLoop, calls=%fused_computation.2 | loop fusion | flops 33552384 | bytes 33587204 | tf_op jit(solution)/shard_map/reduce_sum | solution.py:78
  250.6 3.2 %collective-permute-start.35 = (f32[2,2048]{1,0:T(2,128)S(1)}, f32[2,2048]{1,0:T(2,128)S(1)}, u32[]{:S(2)}, u32[]{:S(2)}) collective-permute-start(f32[2,2048]{1,0:T(2,128)S(1)} %pad_maximum_fusion.16), channel_id=1, source_target_pairs={{0,4},{1,5},{2,6},{3,7},{4,0},{5,1},{6,2},{7,3},{8,12},{9,13},{10,... | collective-permute-start | bytes 49160 | tf_op jit(solution)/shard_map/ppermute | solution.py:46
  255.8 1.7 collective-permute-done.36
  257.6 5.0 %fusion.5 = f32[4096]{0:T(1024)S(1)} fusion(f32[]{:T(128)} %bitcast, f32[2048,4096]{1,0:T(8,128)S(1)} %copy-done, f32[2048]{0:T(1024)S(1)} %multiply_subtract_fusion.4), kind=kLoop, calls=%fused_computation.21 | loop fusion | flops 25161728 | bytes 33579012 | tf_op jit(solution)/shard_map/reduce_max | solution.py:83
  262.6 7.6 %exponential_reduce_fusion = f32[4096]{0:T(1024)S(1)} fusion(f32[4096]{0:T(1024)S(1)} %fusion.5, f32[]{:T(128)} %bitcast, f32[2048,4096]{1,0:T(8,128)S(1)} %copy-done, f32[2048]{0:T(1024)S(1)} %multiply_subtract_fusion.4), kind=kLoop, calls=%fused_computation | loop fusion | flops 33550336 | bytes 33595396 | tf_op jit(solution)/shard_map/reduce_sum | solution.py:84
  270.4 2.7 collective-permute-start.38
  278.7 2.8 collective-permute-start.41
  282.4 1.7 collective-permute-done.41
  (113 shorter events, 36.5 us)
Async XLA Ops:
  0.6 9.7 %collective-permute-start.7 = (f32[256,256]{1,0:T(8,128)}, f32[256,256]{1,0:T(8,128)S(1)}, u32[]{:S(2)}, u32[]{:S(2)}) collective-permute-start(f32[256,256]{1,0:T(8,128)} %param.4), channel_id=1, source_target_pairs={{0,8},{8,16},{16,24},{24,0},{32,40},{40,48},{48,56},{56,32},{64,72... | collective-permute-start | bytes 786440 | tf_op jit(solution)/shard_map/ppermute | solution.py:35
  2.4 14.7 %collective-permute-start.8 = (f32[256,256]{1,0:T(8,128)}, f32[256,256]{1,0:T(8,128)S(1)}, u32[]{:S(2)}, u32[]{:S(2)}) collective-permute-start(f32[256,256]{1,0:T(8,128)} %param.4), channel_id=1, source_target_pairs={{0,16},{8,24},{16,0},{24,8},{32,48},{40,56},{48,32},{56,40},{64,80... | collective-permute-start | bytes 786440 | tf_op jit(solution)/shard_map/ppermute | solution.py:35
  5.3 14.9 %collective-permute-start.9 = (f32[256,256]{1,0:T(8,128)}, f32[256,256]{1,0:T(8,128)S(1)}, u32[]{:S(2)}, u32[]{:S(2)}) collective-permute-start(f32[256,256]{1,0:T(8,128)} %param.4), channel_id=1, source_target_pairs={{0,24},{8,0},{16,8},{24,16},{32,56},{40,32},{48,40},{56,48},{64,88... | collective-permute-start | bytes 786440 | tf_op jit(solution)/shard_map/ppermute | solution.py:35
  6.6 14.6 %collective-permute-start = (f32[256,256]{1,0:T(8,128)}, f32[256,256]{1,0:T(8,128)S(1)}, u32[]{:S(2)}, u32[]{:S(2)}) collective-permute-start(f32[256,256]{1,0:T(8,128)} %param.3), channel_id=1, source_target_pairs={{0,1},{1,2},{2,3},{3,4},{4,5},{5,6},{6,7},{7,0},{8,9},{9,10},{10,1... | collective-permute-start | bytes 786440 | tf_op jit(solution)/shard_map/ppermute | solution.py:35
  6.6 16.2 %collective-permute-start.1 = (f32[256,256]{1,0:T(8,128)}, f32[256,256]{1,0:T(8,128)S(1)}, u32[]{:S(2)}, u32[]{:S(2)}) collective-permute-start(f32[256,256]{1,0:T(8,128)} %param.3), channel_id=1, source_target_pairs={{0,2},{1,3},{2,4},{3,5},{4,6},{5,7},{6,0},{7,1},{8,10},{9,11},{10,... | collective-permute-start | bytes 786440 | tf_op jit(solution)/shard_map/ppermute | solution.py:35
  10.3 18.0 %collective-permute-start.2 = (f32[256,256]{1,0:T(8,128)}, f32[256,256]{1,0:T(8,128)S(1)}, u32[]{:S(2)}, u32[]{:S(2)}) collective-permute-start(f32[256,256]{1,0:T(8,128)} %param.3), channel_id=1, source_target_pairs={{0,3},{1,4},{2,5},{3,6},{4,7},{5,0},{6,1},{7,2},{8,11},{9,12},{10,... | collective-permute-start | bytes 786440 | tf_op jit(solution)/shard_map/ppermute | solution.py:35
  17.1 13.1 %collective-permute-start.3 = (f32[256,256]{1,0:T(8,128)}, f32[256,256]{1,0:T(8,128)S(1)}, u32[]{:S(2)}, u32[]{:S(2)}) collective-permute-start(f32[256,256]{1,0:T(8,128)} %param.3), channel_id=1, source_target_pairs={{0,4},{1,5},{2,6},{3,7},{4,0},{5,1},{6,2},{7,3},{8,12},{9,13},{10,... | collective-permute-start | bytes 786440 | tf_op jit(solution)/shard_map/ppermute | solution.py:35
  20.2 13.8 %collective-permute-start.4 = (f32[256,256]{1,0:T(8,128)}, f32[256,256]{1,0:T(8,128)S(1)}, u32[]{:S(2)}, u32[]{:S(2)}) collective-permute-start(f32[256,256]{1,0:T(8,128)} %param.3), channel_id=1, source_target_pairs={{0,5},{1,6},{2,7},{3,0},{4,1},{5,2},{6,3},{7,4},{8,13},{9,14},{10,... | collective-permute-start | bytes 786440 | tf_op jit(solution)/shard_map/ppermute | solution.py:35
  21.2 16.2 %collective-permute-start.5 = (f32[256,256]{1,0:T(8,128)}, f32[256,256]{1,0:T(8,128)S(1)}, u32[]{:S(2)}, u32[]{:S(2)}) collective-permute-start(f32[256,256]{1,0:T(8,128)} %param.3), channel_id=1, source_target_pairs={{0,6},{1,7},{2,0},{3,1},{4,2},{5,3},{6,4},{7,5},{8,14},{9,15},{10,... | collective-permute-start | bytes 786440 | tf_op jit(solution)/shard_map/ppermute | solution.py:35
  22.9 16.4 %collective-permute-start.6 = (f32[256,256]{1,0:T(8,128)}, f32[256,256]{1,0:T(8,128)S(1)}, u32[]{:S(2)}, u32[]{:S(2)}) collective-permute-start(f32[256,256]{1,0:T(8,128)} %param.3), channel_id=1, source_target_pairs={{0,7},{1,0},{2,1},{3,2},{4,3},{5,4},{6,5},{7,6},{8,15},{9,8},{10,9... | collective-permute-start | bytes 786440 | tf_op jit(solution)/shard_map/ppermute | solution.py:35
  28.3 27.1 %collective-permute-start.10 = (f32[1024,256]{1,0:T(8,128)S(1)}, f32[1024,256]{1,0:T(8,128)S(1)}, u32[]{:S(2)}, u32[]{:S(2)}) collective-permute-start(f32[1024,256]{1,0:T(8,128)S(1)} %get-tuple-element.11), channel_id=1, source_target_pairs={{0,32},{8,40},{16,48},{24,56},{32,64},{40,72},{48,80},{56,88},{64,... | collective-permute-start | bytes 3145736 | tf_op jit(solution)/shard_map/ppermute | solution.py:35
  30.3 45.3 %collective-permute-start.11 = (f32[1024,256]{1,0:T(8,128)S(1)}, f32[1024,256]{1,0:T(8,128)S(1)}, u32[]{:S(2)}, u32[]{:S(2)}) collective-permute-start(f32[1024,256]{1,0:T(8,128)S(1)} %get-tuple-element.11), channel_id=1, source_target_pairs={{0,64},{8,72},{16,80},{24,88},{32,96},{40,104},{48,112},{56,120},{... | collective-permute-start | bytes 3145736 | tf_op jit(solution)/shard_map/ppermute | solution.py:35
  33.9 45.8 %collective-permute-start.12 = (f32[1024,256]{1,0:T(8,128)S(1)}, f32[1024,256]{1,0:T(8,128)S(1)}, u32[]{:S(2)}, u32[]{:S(2)}) collective-permute-start(f32[1024,256]{1,0:T(8,128)S(1)} %get-tuple-element.11), channel_id=1, source_target_pairs={{0,96},{8,104},{16,112},{24,120},{32,0},{40,8},{48,16},{56,24},{64... | collective-permute-start | bytes 3145736 | tf_op jit(solution)/shard_map/ppermute | solution.py:35
  133.7 2.1 collective-permute-start.13
  135.8 5.0 %collective-permute-start.14 = (f32[2,2048]{1,0:T(2,128)S(1)}, f32[2,2048]{1,0:T(2,128)S(1)}, u32[]{:S(2)}, u32[]{:S(2)}) collective-permute-start(f32[2,2048]{1,0:T(2,128)S(1)} %pad_maximum_fusion.12), channel_id=1, source_target_pairs={{0,2},{1,3},{2,4},{3,5},{4,6},{5,7},{6,0},{7,1},{8,10},{9,11},{10,... | collective-permute-start | bytes 49160 | tf_op jit(solution)/shard_map/ppermute | solution.py:46
  135.9 5.3 %collective-permute-start.15 = (f32[2,2048]{1,0:T(2,128)S(1)}, f32[2,2048]{1,0:T(2,128)S(1)}, u32[]{:S(2)}, u32[]{:S(2)}) collective-permute-start(f32[2,2048]{1,0:T(2,128)S(1)} %pad_maximum_fusion.12), channel_id=1, source_target_pairs={{0,4},{1,5},{2,6},{3,7},{4,0},{5,1},{6,2},{7,3},{8,12},{9,13},{10,... | collective-permute-start | bytes 49160 | tf_op jit(solution)/shard_map/ppermute | solution.py:46
  137.6 4.3 %collective-permute-start.16 = (f32[2,2048]{1,0:T(2,128)S(1)}, f32[2,2048]{1,0:T(2,128)S(1)}, u32[]{:S(2)}, u32[]{:S(2)}) collective-permute-start(f32[2,2048]{1,0:T(2,128)S(1)} %pad_maximum_fusion.12), channel_id=1, source_target_pairs={{0,6},{1,7},{2,0},{3,1},{4,2},{5,3},{6,4},{7,5},{8,14},{9,15},{10,... | collective-permute-start | bytes 49160 | tf_op jit(solution)/shard_map/ppermute | solution.py:46
  142.0 20.2 %copy-start = (f32[2048,4096]{1,0:T(8,128)S(1)}, f32[2048,4096]{1,0:T(8,128)}, u32[]{:S(2)}) copy-start(f32[2048,4096]{1,0:T(8,128)} %get-tuple-element.61) | copy-start | bytes 100663296
  169.8 6.7 %collective-permute-start.17 = (f32[2,4096]{1,0:T(2,128)S(1)}, f32[2,4096]{1,0:T(2,128)S(1)}, u32[]{:S(2)}, u32[]{:S(2)}) collective-permute-start(f32[2,4096]{1,0:T(2,128)S(1)} %pad_maximum_fusion.5), channel_id=1, source_target_pairs={{0,8},{8,16},{16,24},{24,0},{32,40},{40,48},{48,56},{56,32},{64,72... | collective-permute-start | bytes 98312 | tf_op jit(solution)/shard_map/ppermute | solution.py:46
  170.5 5.9 %collective-permute-start.18 = (f32[2,4096]{1,0:T(2,128)S(1)}, f32[2,4096]{1,0:T(2,128)S(1)}, u32[]{:S(2)}, u32[]{:S(2)}) collective-permute-start(f32[2,4096]{1,0:T(2,128)S(1)} %pad_maximum_fusion.5), channel_id=1, source_target_pairs={{0,16},{8,24},{16,0},{24,8},{32,48},{40,56},{48,32},{56,40},{64,80... | collective-permute-start | bytes 98312 | tf_op jit(solution)/shard_map/ppermute | solution.py:46
  173.9 4.1 %collective-permute-start.19 = (f32[2,4096]{1,0:T(2,128)S(1)}, f32[2,4096]{1,0:T(2,128)S(1)}, u32[]{:S(2)}, u32[]{:S(2)}) collective-permute-start(f32[2,4096]{1,0:T(2,128)S(1)} %pad_maximum_fusion.5), channel_id=1, source_target_pairs={{0,24},{8,0},{16,8},{24,16},{32,56},{40,32},{48,40},{56,48},{64,88... | collective-permute-start | bytes 98312 | tf_op jit(solution)/shard_map/ppermute | solution.py:46
  178.2 5.2 %collective-permute-start.20 = (f32[2,4096]{1,0:T(2,128)S(1)}, f32[2,4096]{1,0:T(2,128)S(1)}, u32[]{:S(2)}, u32[]{:S(2)}) collective-permute-start(f32[2,4096]{1,0:T(2,128)S(1)} %pad_maximum_fusion.6), channel_id=1, source_target_pairs={{0,32},{8,40},{16,48},{24,56},{32,64},{40,72},{48,80},{56,88},{64,... | collective-permute-start | bytes 98312 | tf_op jit(solution)/shard_map/ppermute | solution.py:46
  178.8 5.8 %collective-permute-start.21 = (f32[2,4096]{1,0:T(2,128)S(1)}, f32[2,4096]{1,0:T(2,128)S(1)}, u32[]{:S(2)}, u32[]{:S(2)}) collective-permute-start(f32[2,4096]{1,0:T(2,128)S(1)} %pad_maximum_fusion.6), channel_id=1, source_target_pairs={{0,64},{8,72},{16,80},{24,88},{32,96},{40,104},{48,112},{56,120},{... | collective-permute-start | bytes 98312 | tf_op jit(solution)/shard_map/ppermute | solution.py:46
  182.4 3.9 %collective-permute-start.22 = (f32[2,4096]{1,0:T(2,128)S(1)}, f32[2,4096]{1,0:T(2,128)S(1)}, u32[]{:S(2)}, u32[]{:S(2)}) collective-permute-start(f32[2,4096]{1,0:T(2,128)S(1)} %pad_maximum_fusion.6), channel_id=1, source_target_pairs={{0,96},{8,104},{16,112},{24,120},{32,0},{40,8},{48,16},{56,24},{64... | collective-permute-start | bytes 98312 | tf_op jit(solution)/shard_map/ppermute | solution.py:46
  198.7 1.3 collective-permute-start.23
  200.0 5.0 %collective-permute-start.24 = (f32[2,2048]{1,0:T(2,128)S(1)}, f32[2,2048]{1,0:T(2,128)S(1)}, u32[]{:S(2)}, u32[]{:S(2)}) collective-permute-start(f32[2,2048]{1,0:T(2,128)S(1)} %pad_maximum_fusion.14), channel_id=1, source_target_pairs={{0,2},{1,3},{2,4},{3,5},{4,6},{5,7},{6,0},{7,1},{8,10},{9,11},{10,... | collective-permute-start | bytes 49160 | tf_op jit(solution)/shard_map/ppermute | solution.py:46
  201.9 5.2 %collective-permute-start.25 = (f32[2,2048]{1,0:T(2,128)S(1)}, f32[2,2048]{1,0:T(2,128)S(1)}, u32[]{:S(2)}, u32[]{:S(2)}) collective-permute-start(f32[2,2048]{1,0:T(2,128)S(1)} %pad_maximum_fusion.14), channel_id=1, source_target_pairs={{0,4},{1,5},{2,6},{3,7},{4,0},{5,1},{6,2},{7,3},{8,12},{9,13},{10,... | collective-permute-start | bytes 49160 | tf_op jit(solution)/shard_map/ppermute | solution.py:46
  204.1 3.7 %collective-permute-start.26 = (f32[2,2048]{1,0:T(2,128)S(1)}, f32[2,2048]{1,0:T(2,128)S(1)}, u32[]{:S(2)}, u32[]{:S(2)}) collective-permute-start(f32[2,2048]{1,0:T(2,128)S(1)} %pad_maximum_fusion.14), channel_id=1, source_target_pairs={{0,6},{1,7},{2,0},{3,1},{4,2},{5,3},{6,4},{7,5},{8,14},{9,15},{10,... | collective-permute-start | bytes 49160 | tf_op jit(solution)/shard_map/ppermute | solution.py:46
  220.6 5.5 %collective-permute-start.27 = (f32[2,4096]{1,0:T(2,128)S(1)}, f32[2,4096]{1,0:T(2,128)S(1)}, u32[]{:S(2)}, u32[]{:S(2)}) collective-permute-start(f32[2,4096]{1,0:T(2,128)S(1)} %pad_maximum_fusion.7), channel_id=1, source_target_pairs={{0,8},{8,16},{16,24},{24,0},{32,40},{40,48},{48,56},{56,32},{64,72... | collective-permute-start | bytes 98312 | tf_op jit(solution)/shard_map/ppermute | solution.py:46
  222.0 5.9 %collective-permute-start.28 = (f32[2,4096]{1,0:T(2,128)S(1)}, f32[2,4096]{1,0:T(2,128)S(1)}, u32[]{:S(2)}, u32[]{:S(2)}) collective-permute-start(f32[2,4096]{1,0:T(2,128)S(1)} %pad_maximum_fusion.7), channel_id=1, source_target_pairs={{0,16},{8,24},{16,0},{24,8},{32,48},{40,56},{48,32},{56,40},{64,80... | collective-permute-start | bytes 98312 | tf_op jit(solution)/shard_map/ppermute | solution.py:46
  225.7 3.9 %collective-permute-start.29 = (f32[2,4096]{1,0:T(2,128)S(1)}, f32[2,4096]{1,0:T(2,128)S(1)}, u32[]{:S(2)}, u32[]{:S(2)}) collective-permute-start(f32[2,4096]{1,0:T(2,128)S(1)} %pad_maximum_fusion.7), channel_id=1, source_target_pairs={{0,24},{8,0},{16,8},{24,16},{32,56},{40,32},{48,40},{56,48},{64,88... | collective-permute-start | bytes 98312 | tf_op jit(solution)/shard_map/ppermute | solution.py:46
  229.8 5.2 %collective-permute-start.30 = (f32[2,4096]{1,0:T(2,128)S(1)}, f32[2,4096]{1,0:T(2,128)S(1)}, u32[]{:S(2)}, u32[]{:S(2)}) collective-permute-start(f32[2,4096]{1,0:T(2,128)S(1)} %pad_maximum_fusion.8), channel_id=1, source_target_pairs={{0,32},{8,40},{16,48},{24,56},{32,64},{40,72},{48,80},{56,88},{64,... | collective-permute-start | bytes 98312 | tf_op jit(solution)/shard_map/ppermute | solution.py:46
  229.8 5.5 %collective-permute-start.31 = (f32[2,4096]{1,0:T(2,128)S(1)}, f32[2,4096]{1,0:T(2,128)S(1)}, u32[]{:S(2)}, u32[]{:S(2)}) collective-permute-start(f32[2,4096]{1,0:T(2,128)S(1)} %pad_maximum_fusion.8), channel_id=1, source_target_pairs={{0,64},{8,72},{16,80},{24,88},{32,96},{40,104},{48,112},{56,120},{... | collective-permute-start | bytes 98312 | tf_op jit(solution)/shard_map/ppermute | solution.py:46
  232.5 4.2 %collective-permute-start.32 = (f32[2,4096]{1,0:T(2,128)S(1)}, f32[2,4096]{1,0:T(2,128)S(1)}, u32[]{:S(2)}, u32[]{:S(2)}) collective-permute-start(f32[2,4096]{1,0:T(2,128)S(1)} %pad_maximum_fusion.8), channel_id=1, source_target_pairs={{0,96},{8,104},{16,112},{24,120},{32,0},{40,8},{48,16},{56,24},{64... | collective-permute-start | bytes 98312 | tf_op jit(solution)/shard_map/ppermute | solution.py:46
  249.1 1.3 collective-permute-start.33
  250.4 5.0 %collective-permute-start.34 = (f32[2,2048]{1,0:T(2,128)S(1)}, f32[2,2048]{1,0:T(2,128)S(1)}, u32[]{:S(2)}, u32[]{:S(2)}) collective-permute-start(f32[2,2048]{1,0:T(2,128)S(1)} %pad_maximum_fusion.16), channel_id=1, source_target_pairs={{0,2},{1,3},{2,4},{3,5},{4,6},{5,7},{6,0},{7,1},{8,10},{9,11},{10,... | collective-permute-start | bytes 49160 | tf_op jit(solution)/shard_map/ppermute | solution.py:46
  250.6 5.2 %collective-permute-start.35 = (f32[2,2048]{1,0:T(2,128)S(1)}, f32[2,2048]{1,0:T(2,128)S(1)}, u32[]{:S(2)}, u32[]{:S(2)}) collective-permute-start(f32[2,2048]{1,0:T(2,128)S(1)} %pad_maximum_fusion.16), channel_id=1, source_target_pairs={{0,4},{1,5},{2,6},{3,7},{4,0},{5,1},{6,2},{7,3},{8,12},{9,13},{10,... | collective-permute-start | bytes 49160 | tf_op jit(solution)/shard_map/ppermute | solution.py:46
  253.8 3.7 %collective-permute-start.36 = (f32[2,2048]{1,0:T(2,128)S(1)}, f32[2,2048]{1,0:T(2,128)S(1)}, u32[]{:S(2)}, u32[]{:S(2)}) collective-permute-start(f32[2,2048]{1,0:T(2,128)S(1)} %pad_maximum_fusion.16), channel_id=1, source_target_pairs={{0,6},{1,7},{2,0},{3,1},{4,2},{5,3},{6,4},{7,5},{8,14},{9,15},{10,... | collective-permute-start | bytes 49160 | tf_op jit(solution)/shard_map/ppermute | solution.py:46
  257.6 5.1 %copy-start.1 = (f32[2048]{0:T(1024)}, f32[2048]{0:T(1024)S(1)}, u32[]{:S(2)}) copy-start(f32[2048]{0:T(1024)S(1)} %multiply_subtract_fusion.4) | copy-start | bytes 24580
  270.3 5.2 %collective-permute-start.37 = (f32[2,4096]{1,0:T(2,128)S(1)}, f32[2,4096]{1,0:T(2,128)S(1)}, u32[]{:S(2)}, u32[]{:S(2)}) collective-permute-start(f32[2,4096]{1,0:T(2,128)S(1)} %pad_maximum_fusion.9), channel_id=1, source_target_pairs={{0,8},{8,16},{16,24},{24,0},{32,40},{40,48},{48,56},{56,32},{64,72... | collective-permute-start | bytes 98312 | tf_op jit(solution)/shard_map/ppermute | solution.py:46
  270.4 5.5 %collective-permute-start.38 = (f32[2,4096]{1,0:T(2,128)S(1)}, f32[2,4096]{1,0:T(2,128)S(1)}, u32[]{:S(2)}, u32[]{:S(2)}) collective-permute-start(f32[2,4096]{1,0:T(2,128)S(1)} %pad_maximum_fusion.9), channel_id=1, source_target_pairs={{0,16},{8,24},{16,0},{24,8},{32,48},{40,56},{48,32},{56,40},{64,80... | collective-permute-start | bytes 98312 | tf_op jit(solution)/shard_map/ppermute | solution.py:46
  273.1 3.9 %collective-permute-start.39 = (f32[2,4096]{1,0:T(2,128)S(1)}, f32[2,4096]{1,0:T(2,128)S(1)}, u32[]{:S(2)}, u32[]{:S(2)}) collective-permute-start(f32[2,4096]{1,0:T(2,128)S(1)} %pad_maximum_fusion.9), channel_id=1, source_target_pairs={{0,24},{8,0},{16,8},{24,16},{32,56},{40,32},{48,40},{56,48},{64,88... | collective-permute-start | bytes 98312 | tf_op jit(solution)/shard_map/ppermute | solution.py:46
  277.2 5.2 %collective-permute-start.40 = (f32[2,4096]{1,0:T(2,128)S(1)}, f32[2,4096]{1,0:T(2,128)S(1)}, u32[]{:S(2)}, u32[]{:S(2)}) collective-permute-start(f32[2,4096]{1,0:T(2,128)S(1)} %pad_maximum_fusion.10), channel_id=1, source_target_pairs={{0,32},{8,40},{16,48},{24,56},{32,64},{40,72},{48,80},{56,88},{64,... | collective-permute-start | bytes 98312 | tf_op jit(solution)/shard_map/ppermute | solution.py:46
  278.7 5.4 %collective-permute-start.41 = (f32[2,4096]{1,0:T(2,128)S(1)}, f32[2,4096]{1,0:T(2,128)S(1)}, u32[]{:S(2)}, u32[]{:S(2)}) collective-permute-start(f32[2,4096]{1,0:T(2,128)S(1)} %pad_maximum_fusion.10), channel_id=1, source_target_pairs={{0,64},{8,72},{16,80},{24,88},{32,96},{40,104},{48,112},{56,120},{... | collective-permute-start | bytes 98312 | tf_op jit(solution)/shard_map/ppermute | solution.py:46
  281.4 3.9 %collective-permute-start.42 = (f32[2,4096]{1,0:T(2,128)S(1)}, f32[2,4096]{1,0:T(2,128)S(1)}, u32[]{:S(2)}, u32[]{:S(2)}) collective-permute-start(f32[2,4096]{1,0:T(2,128)S(1)} %pad_maximum_fusion.10), channel_id=1, source_target_pairs={{0,96},{8,104},{16,112},{24,120},{32,0},{40,8},{48,16},{56,24},{64... | collective-permute-start | bytes 98312 | tf_op jit(solution)/shard_map/ppermute | solution.py:46

commit v6 on v4

--- a/solution.py
+++ b/solution.py
@@ -73,15 +73,15 @@
     return radix_digits(size)
 
 
-def logsum_col(scores):
-    peak = jnp.max(scores, axis=1)
-    totals = jnp.sum(jnp.exp(scores - peak[:, None]), axis=1)
+def logsum_col(gaps, scale):
+    peak = jnp.max(gaps, axis=1) / scale
+    totals = jnp.sum(jnp.exp(gaps / scale - peak[:, None]), axis=1)
     return combine_over(peak, totals, "col", col_digits(lax.axis_size("col")))
 
 
-def logsum_row(scores):
-    peak = jnp.max(scores, axis=0)
-    totals = jnp.sum(jnp.exp(scores - peak[None, :]), axis=0)
+def logsum_row(gaps, scale):
+    peak = jnp.max(gaps, axis=0) / scale
+    totals = jnp.sum(jnp.exp(gaps / scale - peak[None, :]), axis=0)
     return combine_over(peak, totals, "row", radix_digits(lax.axis_size("row")))
 
 
@@ -101,10 +101,10 @@
     col_potential = jnp.zeros((cost_tile.shape[1],), jnp.float32)
     row_potential = jnp.zeros((cost_tile.shape[0],), jnp.float32)
     for repeat in range(ITERS):
-        scores = (col_potential[None, :] - cost_tile) / entropy_scale
-        row_potential = -entropy_scale * math.log(all_queries) - entropy_scale * logsum_col(scores)
-        scores = (row_potential[:, None] - cost_tile) / entropy_scale
-        col_potential = -entropy_scale * math.log(all_passages) - entropy_scale * logsum_row(scores)
+        gaps = col_potential[None, :] - cost_tile
+        row_potential = -entropy_scale * math.log(all_queries) - entropy_scale * logsum_col(gaps, entropy_scale)
+        gaps = row_potential[:, None] - cost_tile
+        col_potential = -entropy_scale * math.log(all_passages) - entropy_scale * logsum_row(gaps, entropy_scale)
     return (row_potential, col_potential)
 
 

time: 282 us -> 278 us (0.986)
  other arithmetic: 102 us -> 98.8 us
where the time goes in v6:
time: 278 us
  other arithmetic  98.8 us (36%)
  waiting for transfers between devices  67.6 us (24%)
  starting transfers between devices  55.9 us (20%)
  matrix products  37.4 us (13%)
  between operations  15.5 us (6%)
  local copies, waits for them, and re-layouts  2.88 us (1%)
    ppermute x30, starting transfers between devices, combine_over(): lax.ppermute(packed, axis, digit_partners(axis, size, stride, width, k))  41.5 us
    dot_general x1, matrix products, inner_costs(): lax.dot_general(left, right, (((1,), (1,)), ((), ())), precision=lax.Prec...  37.4 us
    reduce_sum x3, other arithmetic, logsum_row(): totals = jnp.sum(jnp.exp(gaps / scale - peak[None, :]), axis=0)  31.7 us
    reduce_sum x3, other arithmetic, logsum_col(): totals = jnp.sum(jnp.exp(gaps / scale - peak[:, None]), axis=1)  30.6 us
    ppermute x30, waiting for transfers between devices, combine_over(): lax.ppermute(packed, axis, digit_partners(axis, size, stride, width, k))  29 us
    all_gather x1, waiting for transfers between devices, per_device(): lax.all_gather(passages, 'row', axis=0, tiled=True)  27.4 us
    reduce_max x3, other arithmetic, logsum_row(): peak = jnp.max(gaps, axis=0) / scale  25.4 us
    ppermute x7, starting transfers between devices, exchange(): lax.ppermute(x, axis, digit_partners(axis, size, stride, width, k))  14.4 us
  transfers between devices with their start and end apart: 38, of which 35 were waited for; matrix products, arithmetic and copies ran while one was open for 1% of the time, Pallas kernels for 0%

profile of v6, /device:TPU:0, one launch (start us, length us, event | category | flops | bytes accessed | tf_op | source)
XLA Modules:
  0.0 278.0 jit_solution(5777233211555126254)
XLA Ops:
  7.9 1.7 collective-permute-start.1
  9.6 2.0 collective-permute-start.2
  11.6 2.0 collective-permute-start.3
  13.7 1.6 collective-permute-start.4
  17.3 1.7 collective-permute-start.5
  19.0 5.3 %collective-permute-start.6 = (f32[256,256]{1,0:T(8,128)}, f32[256,256]{1,0:T(8,128)S(1)}, u32[]{:S(2)}, u32[]{:S(2)}) collective-permute-start(f32[256,256]{1,0:T(8,128)} %param.3), channel_id=1, source_target_pairs={{0,7},{1,0},{2,1},{3,2},{4,3},{5,4},{6,5},{7,6},{8,15},{9,8},{10,9... | collective-permute-start | bytes 786440 | tf_op jit(solution)/shard_map/ppermute | solution.py:35
  24.3 5.3 %collective-permute-done.2 = f32[256,256]{1,0:T(8,128)S(1)} collective-permute-done((f32[256,256]{1,0:T(8,128)}, f32[256,256]{1,0:T(8,128)S(1)}, u32[]{:S(2)}, u32[]{:S(2)}) %collective-permute-start.2) | collective-permute-done | bytes 262176 | tf_op jit(solution)/shard_map/ppermute | solution.py:35
  29.6 1.3 collective-permute-done.3
  30.9 1.9 collective-permute-done.4
  33.0 1.8 collective-permute-done.6
  35.1 1.3 copy-done
  36.8 27.4 %all-gather.2.cloned.1.call-done = f32[4096,256]{1,0:T(8,128)} async-done(((f32[256,256]{1,0:T(8,128)}), f32[4096,256]{1,0:T(8,128)}) %all-gather.2.cloned.1.call-update) | async-done | bytes 4194320 | tf_op jit(solution)/shard_map/all_gather | solution.py:100
  64.1 2.8 %multiply_reduce_fusion = f32[4096]{0:T(1024)S(1)} fusion(f32[4096,256]{1,0:T(8,128)} %all-gather.2.cloned.1.call-done), kind=kLoop, calls=%fused_computation.13 | loop fusion | flops 2093056 | bytes 4210688 | tf_op jit(solution)/shard_map/reduce_sum | solution.py:13
  66.9 37.4 %subtract_reduce_fusion.5 = (f32[2048]{0:T(1024)S(1)}, f32[2048,4096]{1,0:T(8,128)}) fusion(f32[2048,256]{1,0:T(8,128)} %copy-done, f32[4096,256]{1,0:T(8,128)} %all-gather.2.cloned.1.call-done, f32[4096]{0:T(1024)S(1)} %multiply_reduce_fusion, f32[2048]{0:T(1024)S(1)} %multiply_reduce_fusion.1), kind=kOutput, calls=%fused_computation.12 | convolution fusion | flops 25811744768 | bytes 39878656 | tf_op jit(solution)/shard_map/dot_general | solution.py:14
  104.3 14.5 %exponential_reduce_fusion.5 = f32[2048]{0:T(1024)S(1)} fusion(f32[2048,4096]{1,0:T(8,128)} %get-tuple-element.51, f32[2048]{0:T(1024)S(1)} %broadcast_divide_fusion.5, f32[]{:T(128)} %bitcast), kind=kLoop, calls=%fused_computation.5 | loop fusion | flops 33552384 | bytes 33570820 | tf_op jit(solution)/shard_map/reduce_sum | solution.py:78
  120.2 1.5 collective-permute-start.8
  121.7 2.7 collective-permute-start.9
  124.4 1.5 collective-permute-start.10
  128.3 15.9 %subtract_reduce_fusion.4 = f32[4096]{0:T(1024)S(1)} fusion(f32[2048,4096]{1,0:T(8,128)} %get-tuple-element.51, f32[2048]{0:T(1024)S(1)} %multiply_subtract_fusion.6), kind=kLoop, calls=%fused_computation.11 | loop fusion | flops 16773120 | bytes 33579008 | tf_op jit(solution)/shard_map/reduce_max | solution.py:83
  144.2 16.4 %exponential_reduce_fusion.4 = f32[4096]{0:T(1024)S(1)} fusion(f32[2048,4096]{1,0:T(8,128)} %get-tuple-element.51, f32[4096]{0:T(1024)S(1)} %broadcast_divide_fusion.2, f32[2048]{0:T(1024)S(1)} %multiply_subtract_fusion.6, f32[]{:T(128)} %bitcast), kind=kLoop, calls=%fused_computation.4 | loop fusion | flops 33550336 | bytes 33595396 | tf_op jit(solution)/shard_map/reduce_sum | solution.py:84
  160.7 1.6 collective-permute-start.11
  162.3 2.7 collective-permute-start.12
  165.0 1.4 collective-permute-start.13
  166.4 1.3 collective-permute-done.12
  169.3 2.3 collective-permute-start.15
  171.6 1.7 collective-permute-start.16
  175.7 3.0 %subtract_reduce_fusion.3 = f32[2048]{0:T(1024)S(1)} fusion(f32[2048,4096]{1,0:T(8,128)S(1)} %bitcast.86, f32[4096]{0:T(1024)S(1)} %bitcast.95), kind=kLoop, calls=%fused_computation.10 | loop fusion | flops 16775168 | bytes 33579008 | tf_op jit(solution)/shard_map/reduce_max | solution.py:77
  178.8 8.0 %exponential_reduce_fusion.3 = f32[2048]{0:T(1024)S(1)} fusion(f32[2048,4096]{1,0:T(8,128)S(1)} %bitcast.86, f32[2048]{0:T(1024)S(1)} %broadcast_divide_fusion.4, f32[4096]{0:T(1024)S(1)} %bitcast.96, f32[]{:T(128)} %bitcast), kind=kLoop, calls=%fused_computation.3 | loop fusion | flops 33552384 | bytes 33587204 | tf_op jit(solution)/shard_map/reduce_sum | solution.py:78
  188.5 3.8 %collective-permute-start.19 = (f32[2,2048]{1,0:T(2,128)S(1)}, f32[2,2048]{1,0:T(2,128)S(1)}, u32[]{:S(2)}, u32[]{:S(2)}) collective-permute-start(f32[2,2048]{1,0:T(2,128)S(1)} %pad_maximum_fusion.9), channel_id=1, source_target_pairs={{0,4},{1,5},{2,6},{3,7},{4,0},{5,1},{6,2},{7,3},{8,12},{9,13},{10,... | collective-permute-start | bytes 49160 | tf_op jit(solution)/shard_map/ppermute | solution.py:46
  194.3 1.8 collective-permute-done.20
  196.2 4.7 %subtract_reduce_fusion.2 = f32[4096]{0:T(1024)S(1)} fusion(f32[2048,4096]{1,0:T(8,128)S(1)} %bitcast.86, f32[2048]{0:T(1024)S(1)} %multiply_subtract_fusion.5), kind=kLoop, calls=%fused_computation.9 | loop fusion | flops 16773120 | bytes 33579008 | tf_op jit(solution)/shard_map/reduce_max | solution.py:83
  200.9 7.6 %exponential_reduce_fusion.2 = f32[4096]{0:T(1024)S(1)} fusion(f32[2048,4096]{1,0:T(8,128)S(1)} %bitcast.86, f32[4096]{0:T(1024)S(1)} %broadcast_divide_fusion.1, f32[2048]{0:T(1024)S(1)} %multiply_subtract_fusion.5, f32[]{:T(128)} %bitcast), kind=kLoop, calls=%fused_computation.2 | loop fusion | flops 33550336 | bytes 33595396 | tf_op jit(solution)/shard_map/reduce_sum | solution.py:84
  208.6 1.7 collective-permute-start.21
  210.3 2.7 collective-permute-start.22
  213.8 2.0 collective-permute-done.22
  217.1 1.5 collective-permute-start.24
  218.6 2.7 collective-permute-start.25
  222.3 1.7 collective-permute-done.25
  225.3 3.0 %subtract_reduce_fusion.1 = f32[2048]{0:T(1024)S(1)} fusion(f32[2048,4096]{1,0:T(8,128)S(1)} %bitcast.86, f32[4096]{0:T(1024)S(1)} %bitcast.97), kind=kLoop, calls=%fused_computation.8 | loop fusion | flops 16775168 | bytes 33579008 | tf_op jit(solution)/shard_map/reduce_max | solution.py:77
  228.4 8.0 %exponential_reduce_fusion.1 = f32[2048]{0:T(1024)S(1)} fusion(f32[2048,4096]{1,0:T(8,128)S(1)} %bitcast.86, f32[2048]{0:T(1024)S(1)} %broadcast_divide_fusion.3, f32[4096]{0:T(1024)S(1)} %bitcast.98, f32[]{:T(128)} %bitcast), kind=kLoop, calls=%fused_computation.1 | loop fusion | flops 33552384 | bytes 33587204 | tf_op jit(solution)/shard_map/reduce_sum | solution.py:78
  237.8 2.7 collective-permute-start.29
  240.5 1.5 collective-permute-start.30
  244.3 4.7 %subtract_reduce_fusion = f32[4096]{0:T(1024)S(1)} fusion(f32[2048,4096]{1,0:T(8,128)S(1)} %bitcast.86, f32[2048]{0:T(1024)S(1)} %multiply_subtract_fusion.4), kind=kLoop, calls=%fused_computation.7 | loop fusion | flops 16773120 | bytes 33579008 | tf_op jit(solution)/shard_map/reduce_max | solution.py:83
  249.1 7.6 %exponential_reduce_fusion = f32[4096]{0:T(1024)S(1)} fusion(f32[2048,4096]{1,0:T(8,128)S(1)} %bitcast.86, f32[4096]{0:T(1024)S(1)} %broadcast_divide_fusion, f32[2048]{0:T(1024)S(1)} %multiply_subtract_fusion.4, f32[]{:T(128)} %bitcast), kind=kLoop, calls=%fused_computation | loop fusion | flops 33550336 | bytes 33595396 | tf_op jit(solution)/shard_map/reduce_sum | solution.py:84
  256.9 2.7 collective-permute-start.32
  259.6 1.4 collective-permute-start.33
  263.8 2.7 collective-permute-start.35
  266.5 1.4 collective-permute-start.36
  (122 shorter events, 28.5 us)
Async XLA Ops:
  7.2 57.0 %all-gather.2.cloned.1.call-start = ((), (), s32[]{:S(2)}) async-start(), calls=%async_computation | async-start | bytes 4456448 | tf_op jit(solution)/shard_map/all_gather | solution.py:100
  7.9 9.4 %collective-permute-start = (f32[256,256]{1,0:T(8,128)}, f32[256,256]{1,0:T(8,128)S(1)}, u32[]{:S(2)}, u32[]{:S(2)}) collective-permute-start(f32[256,256]{1,0:T(8,128)} %param.3), channel_id=1, source_target_pairs={{0,1},{1,2},{2,3},{3,4},{4,5},{5,6},{6,7},{7,0},{8,9},{9,10},{10,1... | collective-permute-start | bytes 786440 | tf_op jit(solution)/shard_map/ppermute | solution.py:35
  7.9 11.0 %collective-permute-start.1 = (f32[256,256]{1,0:T(8,128)}, f32[256,256]{1,0:T(8,128)S(1)}, u32[]{:S(2)}, u32[]{:S(2)}) collective-permute-start(f32[256,256]{1,0:T(8,128)} %param.3), channel_id=1, source_target_pairs={{0,2},{1,3},{2,4},{3,5},{4,6},{5,7},{6,0},{7,1},{8,10},{9,11},{10,... | collective-permute-start | bytes 786440 | tf_op jit(solution)/shard_map/ppermute | solution.py:35
  9.6 20.0 %collective-permute-start.2 = (f32[256,256]{1,0:T(8,128)}, f32[256,256]{1,0:T(8,128)S(1)}, u32[]{:S(2)}, u32[]{:S(2)}) collective-permute-start(f32[256,256]{1,0:T(8,128)} %param.3), channel_id=1, source_target_pairs={{0,3},{1,4},{2,5},{3,6},{4,7},{5,0},{6,1},{7,2},{8,11},{9,12},{10,... | collective-permute-start | bytes 786440 | tf_op jit(solution)/shard_map/ppermute | solution.py:35
  11.6 19.3 %collective-permute-start.3 = (f32[256,256]{1,0:T(8,128)}, f32[256,256]{1,0:T(8,128)S(1)}, u32[]{:S(2)}, u32[]{:S(2)}) collective-permute-start(f32[256,256]{1,0:T(8,128)} %param.3), channel_id=1, source_target_pairs={{0,4},{1,5},{2,6},{3,7},{4,0},{5,1},{6,2},{7,3},{8,12},{9,13},{10,... | collective-permute-start | bytes 786440 | tf_op jit(solution)/shard_map/ppermute | solution.py:35
  13.7 19.2 %collective-permute-start.4 = (f32[256,256]{1,0:T(8,128)}, f32[256,256]{1,0:T(8,128)S(1)}, u32[]{:S(2)}, u32[]{:S(2)}) collective-permute-start(f32[256,256]{1,0:T(8,128)} %param.3), channel_id=1, source_target_pairs={{0,5},{1,6},{2,7},{3,0},{4,1},{5,2},{6,3},{7,4},{8,13},{9,14},{10,... | collective-permute-start | bytes 786440 | tf_op jit(solution)/shard_map/ppermute | solution.py:35
  17.3 15.7 %collective-permute-start.5 = (f32[256,256]{1,0:T(8,128)}, f32[256,256]{1,0:T(8,128)S(1)}, u32[]{:S(2)}, u32[]{:S(2)}) collective-permute-start(f32[256,256]{1,0:T(8,128)} %param.3), channel_id=1, source_target_pairs={{0,6},{1,7},{2,0},{3,1},{4,2},{5,3},{6,4},{7,5},{8,14},{9,15},{10,... | collective-permute-start | bytes 786440 | tf_op jit(solution)/shard_map/ppermute | solution.py:35
  19.0 15.9 %collective-permute-start.6 = (f32[256,256]{1,0:T(8,128)}, f32[256,256]{1,0:T(8,128)S(1)}, u32[]{:S(2)}, u32[]{:S(2)}) collective-permute-start(f32[256,256]{1,0:T(8,128)} %param.3), channel_id=1, source_target_pairs={{0,7},{1,0},{2,1},{3,2},{4,3},{5,4},{6,5},{7,6},{8,15},{9,8},{10,9... | collective-permute-start | bytes 786440 | tf_op jit(solution)/shard_map/ppermute | solution.py:35
  35.1 1.3 copy-start
  118.9 1.3 collective-permute-start.7
  120.2 5.7 %collective-permute-start.8 = (f32[2,2048]{1,0:T(2,128)S(1)}, f32[2,2048]{1,0:T(2,128)S(1)}, u32[]{:S(2)}, u32[]{:S(2)}) collective-permute-start(f32[2,2048]{1,0:T(2,128)S(1)} %pad_maximum_fusion.7), channel_id=1, source_target_pairs={{0,2},{1,3},{2,4},{3,5},{4,6},{5,7},{6,0},{7,1},{8,10},{9,11},{10,... | collective-permute-start | bytes 49160 | tf_op jit(solution)/shard_map/ppermute | solution.py:46
  121.7 5.2 %collective-permute-start.9 = (f32[2,2048]{1,0:T(2,128)S(1)}, f32[2,2048]{1,0:T(2,128)S(1)}, u32[]{:S(2)}, u32[]{:S(2)}) collective-permute-start(f32[2,2048]{1,0:T(2,128)S(1)} %pad_maximum_fusion.7), channel_id=1, source_target_pairs={{0,4},{1,5},{2,6},{3,7},{4,0},{5,1},{6,2},{7,3},{8,12},{9,13},{10,... | collective-permute-start | bytes 49160 | tf_op jit(solution)/shard_map/ppermute | solution.py:46
  124.4 3.7 %collective-permute-start.10 = (f32[2,2048]{1,0:T(2,128)S(1)}, f32[2,2048]{1,0:T(2,128)S(1)}, u32[]{:S(2)}, u32[]{:S(2)}) collective-permute-start(f32[2,2048]{1,0:T(2,128)S(1)} %pad_maximum_fusion.7), channel_id=1, source_target_pairs={{0,6},{1,7},{2,0},{3,1},{4,2},{5,3},{6,4},{7,5},{8,14},{9,15},{10,... | collective-permute-start | bytes 49160 | tf_op jit(solution)/shard_map/ppermute | solution.py:46
  128.2 47.4 %slice-start = ((s8[33554432]{0:T(1024)(128)(4,1)}), s8[4194304]{0:T(1024)(128)(4,1)S(1)}, s32[]{:S(2)}) async-start(s8[33554432]{0:T(1024)(128)(4,1)} %bitcast.85), calls=%async_computation.1 | async-start | bytes 8388608
  128.2 47.4 %slice-start.1 = ((s8[33554432]{0:T(1024)(128)(4,1)}), s8[4194304]{0:T(1024)(128)(4,1)S(1)}, s32[]{:S(2)}) async-start(s8[33554432]{0:T(1024)(128)(4,1)} %bitcast.85), calls=%async_computation.2 | async-start | bytes 8388608
  128.2 47.4 %slice-start.2 = ((s8[33554432]{0:T(1024)(128)(4,1)}), s8[4194304]{0:T(1024)(128)(4,1)S(1)}, s32[]{:S(2)}) async-start(s8[33554432]{0:T(1024)(128)(4,1)} %bitcast.85), calls=%async_computation.3 | async-start | bytes 8388608
  128.2 47.4 %slice-start.3 = ((s8[33554432]{0:T(1024)(128)(4,1)}), s8[4194304]{0:T(1024)(128)(4,1)S(1)}, s32[]{:S(2)}) async-start(s8[33554432]{0:T(1024)(128)(4,1)} %bitcast.85), calls=%async_computation.4 | async-start | bytes 8388608
  144.2 31.5 %slice-start.4 = ((s8[33554432]{0:T(1024)(128)(4,1)}), s8[4194304]{0:T(1024)(128)(4,1)S(1)}, s32[]{:S(2)}) async-start(s8[33554432]{0:T(1024)(128)(4,1)} %bitcast.85), calls=%async_computation.5 | async-start | bytes 8388608
  144.2 31.5 %slice-start.5 = ((s8[33554432]{0:T(1024)(128)(4,1)}), s8[4194304]{0:T(1024)(128)(4,1)S(1)}, s32[]{:S(2)}) async-start(s8[33554432]{0:T(1024)(128)(4,1)} %bitcast.85), calls=%async_computation.6 | async-start | bytes 8388608
  144.2 31.5 %slice-start.6 = ((s8[33554432]{0:T(1024)(128)(4,1)}), s8[4194304]{0:T(1024)(128)(4,1)S(1)}, s32[]{:S(2)}) async-start(s8[33554432]{0:T(1024)(128)(4,1)} %bitcast.85), calls=%async_computation.7 | async-start | bytes 8388608
  144.2 31.5 %slice-start.7 = ((s8[33554432]{0:T(1024)(128)(4,1)}), s8[4194304]{0:T(1024)(128)(4,1)S(1)}, s32[]{:S(2)}) async-start(s8[33554432]{0:T(1024)(128)(4,1)} %bitcast.85), calls=%async_computation.8 | async-start | bytes 8388608
  160.7 5.7 %collective-permute-start.11 = (f32[2,4096]{1,0:T(2,128)S(1)}, f32[2,4096]{1,0:T(2,128)S(1)}, u32[]{:S(2)}, u32[]{:S(2)}) collective-permute-start(f32[2,4096]{1,0:T(2,128)S(1)} %pad_maximum_fusion), channel_id=1, source_target_pairs={{0,8},{8,16},{16,24},{24,0},{32,40},{40,48},{48,56},{56,32},{64,72... | collective-permute-start | bytes 98312 | tf_op jit(solution)/shard_map/ppermute | solution.py:46
  162.3 5.4 %collective-permute-start.12 = (f32[2,4096]{1,0:T(2,128)S(1)}, f32[2,4096]{1,0:T(2,128)S(1)}, u32[]{:S(2)}, u32[]{:S(2)}) collective-permute-start(f32[2,4096]{1,0:T(2,128)S(1)} %pad_maximum_fusion), channel_id=1, source_target_pairs={{0,16},{8,24},{16,0},{24,8},{32,48},{40,56},{48,32},{56,40},{64,80... | collective-permute-start | bytes 98312 | tf_op jit(solution)/shard_map/ppermute | solution.py:46
  165.0 3.9 %collective-permute-start.13 = (f32[2,4096]{1,0:T(2,128)S(1)}, f32[2,4096]{1,0:T(2,128)S(1)}, u32[]{:S(2)}, u32[]{:S(2)}) collective-permute-start(f32[2,4096]{1,0:T(2,128)S(1)} %pad_maximum_fusion), channel_id=1, source_target_pairs={{0,24},{8,0},{16,8},{24,16},{32,56},{40,32},{48,40},{56,48},{64,88... | collective-permute-start | bytes 98312 | tf_op jit(solution)/shard_map/ppermute | solution.py:46
  169.1 5.2 %collective-permute-start.14 = (f32[2,4096]{1,0:T(2,128)S(1)}, f32[2,4096]{1,0:T(2,128)S(1)}, u32[]{:S(2)}, u32[]{:S(2)}) collective-permute-start(f32[2,4096]{1,0:T(2,128)S(1)} %pad_maximum_fusion.1), channel_id=1, source_target_pairs={{0,32},{8,40},{16,48},{24,56},{32,64},{40,72},{48,80},{56,88},{64,... | collective-permute-start | bytes 98312 | tf_op jit(solution)/shard_map/ppermute | solution.py:46
  169.3 5.4 %collective-permute-start.15 = (f32[2,4096]{1,0:T(2,128)S(1)}, f32[2,4096]{1,0:T(2,128)S(1)}, u32[]{:S(2)}, u32[]{:S(2)}) collective-permute-start(f32[2,4096]{1,0:T(2,128)S(1)} %pad_maximum_fusion.1), channel_id=1, source_target_pairs={{0,64},{8,72},{16,80},{24,88},{32,96},{40,104},{48,112},{56,120},{... | collective-permute-start | bytes 98312 | tf_op jit(solution)/shard_map/ppermute | solution.py:46
  171.6 3.9 %collective-permute-start.16 = (f32[2,4096]{1,0:T(2,128)S(1)}, f32[2,4096]{1,0:T(2,128)S(1)}, u32[]{:S(2)}, u32[]{:S(2)}) collective-permute-start(f32[2,4096]{1,0:T(2,128)S(1)} %pad_maximum_fusion.1), channel_id=1, source_target_pairs={{0,96},{8,104},{16,112},{24,120},{32,0},{40,8},{48,16},{56,24},{64... | collective-permute-start | bytes 98312 | tf_op jit(solution)/shard_map/ppermute | solution.py:46
  186.8 1.3 collective-permute-start.17
  188.2 5.0 %collective-permute-start.18 = (f32[2,2048]{1,0:T(2,128)S(1)}, f32[2,2048]{1,0:T(2,128)S(1)}, u32[]{:S(2)}, u32[]{:S(2)}) collective-permute-start(f32[2,2048]{1,0:T(2,128)S(1)} %pad_maximum_fusion.9), channel_id=1, source_target_pairs={{0,2},{1,3},{2,4},{3,5},{4,6},{5,7},{6,0},{7,1},{8,10},{9,11},{10,... | collective-permute-start | bytes 49160 | tf_op jit(solution)/shard_map/ppermute | solution.py:46
  188.5 5.7 %collective-permute-start.19 = (f32[2,2048]{1,0:T(2,128)S(1)}, f32[2,2048]{1,0:T(2,128)S(1)}, u32[]{:S(2)}, u32[]{:S(2)}) collective-permute-start(f32[2,2048]{1,0:T(2,128)S(1)} %pad_maximum_fusion.9), channel_id=1, source_target_pairs={{0,4},{1,5},{2,6},{3,7},{4,0},{5,1},{6,2},{7,3},{8,12},{9,13},{10,... | collective-permute-start | bytes 49160 | tf_op jit(solution)/shard_map/ppermute | solution.py:46
  192.4 3.7 %collective-permute-start.20 = (f32[2,2048]{1,0:T(2,128)S(1)}, f32[2,2048]{1,0:T(2,128)S(1)}, u32[]{:S(2)}, u32[]{:S(2)}) collective-permute-start(f32[2,2048]{1,0:T(2,128)S(1)} %pad_maximum_fusion.9), channel_id=1, source_target_pairs={{0,6},{1,7},{2,0},{3,1},{4,2},{5,3},{6,4},{7,5},{8,14},{9,15},{10,... | collective-permute-start | bytes 49160 | tf_op jit(solution)/shard_map/ppermute | solution.py:46
  208.6 5.2 %collective-permute-start.21 = (f32[2,4096]{1,0:T(2,128)S(1)}, f32[2,4096]{1,0:T(2,128)S(1)}, u32[]{:S(2)}, u32[]{:S(2)}) collective-permute-start(f32[2,4096]{1,0:T(2,128)S(1)} %pad_maximum_fusion.2), channel_id=1, source_target_pairs={{0,8},{8,16},{16,24},{24,0},{32,40},{40,48},{48,56},{56,32},{64,72... | collective-permute-start | bytes 98312 | tf_op jit(solution)/shard_map/ppermute | solution.py:46
  210.3 5.4 %collective-permute-start.22 = (f32[2,4096]{1,0:T(2,128)S(1)}, f32[2,4096]{1,0:T(2,128)S(1)}, u32[]{:S(2)}, u32[]{:S(2)}) collective-permute-start(f32[2,4096]{1,0:T(2,128)S(1)} %pad_maximum_fusion.2), channel_id=1, source_target_pairs={{0,16},{8,24},{16,0},{24,8},{32,48},{40,56},{48,32},{56,40},{64,80... | collective-permute-start | bytes 98312 | tf_op jit(solution)/shard_map/ppermute | solution.py:46
  213.0 3.9 %collective-permute-start.23 = (f32[2,4096]{1,0:T(2,128)S(1)}, f32[2,4096]{1,0:T(2,128)S(1)}, u32[]{:S(2)}, u32[]{:S(2)}) collective-permute-start(f32[2,4096]{1,0:T(2,128)S(1)} %pad_maximum_fusion.2), channel_id=1, source_target_pairs={{0,24},{8,0},{16,8},{24,16},{32,56},{40,32},{48,40},{56,48},{64,88... | collective-permute-start | bytes 98312 | tf_op jit(solution)/shard_map/ppermute | solution.py:46
  217.1 5.2 %collective-permute-start.24 = (f32[2,4096]{1,0:T(2,128)S(1)}, f32[2,4096]{1,0:T(2,128)S(1)}, u32[]{:S(2)}, u32[]{:S(2)}) collective-permute-start(f32[2,4096]{1,0:T(2,128)S(1)} %pad_maximum_fusion.3), channel_id=1, source_target_pairs={{0,32},{8,40},{16,48},{24,56},{32,64},{40,72},{48,80},{56,88},{64,... | collective-permute-start | bytes 98312 | tf_op jit(solution)/shard_map/ppermute | solution.py:46
  218.6 5.4 %collective-permute-start.25 = (f32[2,4096]{1,0:T(2,128)S(1)}, f32[2,4096]{1,0:T(2,128)S(1)}, u32[]{:S(2)}, u32[]{:S(2)}) collective-permute-start(f32[2,4096]{1,0:T(2,128)S(1)} %pad_maximum_fusion.3), channel_id=1, source_target_pairs={{0,64},{8,72},{16,80},{24,88},{32,96},{40,104},{48,112},{56,120},{... | collective-permute-start | bytes 98312 | tf_op jit(solution)/shard_map/ppermute | solution.py:46
  221.3 3.9 %collective-permute-start.26 = (f32[2,4096]{1,0:T(2,128)S(1)}, f32[2,4096]{1,0:T(2,128)S(1)}, u32[]{:S(2)}, u32[]{:S(2)}) collective-permute-start(f32[2,4096]{1,0:T(2,128)S(1)} %pad_maximum_fusion.3), channel_id=1, source_target_pairs={{0,96},{8,104},{16,112},{24,120},{32,0},{40,8},{48,16},{56,24},{64... | collective-permute-start | bytes 98312 | tf_op jit(solution)/shard_map/ppermute | solution.py:46
  236.4 1.3 collective-permute-start.27
  237.8 5.0 %collective-permute-start.28 = (f32[2,2048]{1,0:T(2,128)S(1)}, f32[2,2048]{1,0:T(2,128)S(1)}, u32[]{:S(2)}, u32[]{:S(2)}) collective-permute-start(f32[2,2048]{1,0:T(2,128)S(1)} %pad_maximum_fusion.11), channel_id=1, source_target_pairs={{0,2},{1,3},{2,4},{3,5},{4,6},{5,7},{6,0},{7,1},{8,10},{9,11},{10,... | collective-permute-start | bytes 49160 | tf_op jit(solution)/shard_map/ppermute | solution.py:46
  237.8 5.3 %collective-permute-start.29 = (f32[2,2048]{1,0:T(2,128)S(1)}, f32[2,2048]{1,0:T(2,128)S(1)}, u32[]{:S(2)}, u32[]{:S(2)}) collective-permute-start(f32[2,2048]{1,0:T(2,128)S(1)} %pad_maximum_fusion.11), channel_id=1, source_target_pairs={{0,4},{1,5},{2,6},{3,7},{4,0},{5,1},{6,2},{7,3},{8,12},{9,13},{10,... | collective-permute-start | bytes 49160 | tf_op jit(solution)/shard_map/ppermute | solution.py:46
  240.5 3.7 %collective-permute-start.30 = (f32[2,2048]{1,0:T(2,128)S(1)}, f32[2,2048]{1,0:T(2,128)S(1)}, u32[]{:S(2)}, u32[]{:S(2)}) collective-permute-start(f32[2,2048]{1,0:T(2,128)S(1)} %pad_maximum_fusion.11), channel_id=1, source_target_pairs={{0,6},{1,7},{2,0},{3,1},{4,2},{5,3},{6,4},{7,5},{8,14},{9,15},{10,... | collective-permute-start | bytes 49160 | tf_op jit(solution)/shard_map/ppermute | solution.py:46
  244.3 12.4 %copy-start.1 = (f32[2048]{0:T(1024)}, f32[2048]{0:T(1024)S(1)}, u32[]{:S(2)}) copy-start(f32[2048]{0:T(1024)S(1)} %multiply_subtract_fusion.4) | copy-start | bytes 24580
  256.8 5.2 %collective-permute-start.31 = (f32[2,4096]{1,0:T(2,128)S(1)}, f32[2,4096]{1,0:T(2,128)S(1)}, u32[]{:S(2)}, u32[]{:S(2)}) collective-permute-start(f32[2,4096]{1,0:T(2,128)S(1)} %pad_maximum_fusion.4), channel_id=1, source_target_pairs={{0,8},{8,16},{16,24},{24,0},{32,40},{40,48},{48,56},{56,32},{64,72... | collective-permute-start | bytes 98312 | tf_op jit(solution)/shard_map/ppermute | solution.py:46
  256.9 5.5 %collective-permute-start.32 = (f32[2,4096]{1,0:T(2,128)S(1)}, f32[2,4096]{1,0:T(2,128)S(1)}, u32[]{:S(2)}, u32[]{:S(2)}) collective-permute-start(f32[2,4096]{1,0:T(2,128)S(1)} %pad_maximum_fusion.4), channel_id=1, source_target_pairs={{0,16},{8,24},{16,0},{24,8},{32,48},{40,56},{48,32},{56,40},{64,80... | collective-permute-start | bytes 98312 | tf_op jit(solution)/shard_map/ppermute | solution.py:46
  259.6 3.9 %collective-permute-start.33 = (f32[2,4096]{1,0:T(2,128)S(1)}, f32[2,4096]{1,0:T(2,128)S(1)}, u32[]{:S(2)}, u32[]{:S(2)}) collective-permute-start(f32[2,4096]{1,0:T(2,128)S(1)} %pad_maximum_fusion.4), channel_id=1, source_target_pairs={{0,24},{8,0},{16,8},{24,16},{32,56},{40,32},{48,40},{56,48},{64,88... | collective-permute-start | bytes 98312 | tf_op jit(solution)/shard_map/ppermute | solution.py:46
  263.7 5.2 %collective-permute-start.34 = (f32[2,4096]{1,0:T(2,128)S(1)}, f32[2,4096]{1,0:T(2,128)S(1)}, u32[]{:S(2)}, u32[]{:S(2)}) collective-permute-start(f32[2,4096]{1,0:T(2,128)S(1)} %pad_maximum_fusion.5), channel_id=1, source_target_pairs={{0,32},{8,40},{16,48},{24,56},{32,64},{40,72},{48,80},{56,88},{64,... | collective-permute-start | bytes 98312 | tf_op jit(solution)/shard_map/ppermute | solution.py:46
  263.8 5.5 %collective-permute-start.35 = (f32[2,4096]{1,0:T(2,128)S(1)}, f32[2,4096]{1,0:T(2,128)S(1)}, u32[]{:S(2)}, u32[]{:S(2)}) collective-permute-start(f32[2,4096]{1,0:T(2,128)S(1)} %pad_maximum_fusion.5), channel_id=1, source_target_pairs={{0,64},{8,72},{16,80},{24,88},{32,96},{40,104},{48,112},{56,120},{... | collective-permute-start | bytes 98312 | tf_op jit(solution)/shard_map/ppermute | solution.py:46
  266.5 3.9 %collective-permute-start.36 = (f32[2,4096]{1,0:T(2,128)S(1)}, f32[2,4096]{1,0:T(2,128)S(1)}, u32[]{:S(2)}, u32[]{:S(2)}) collective-permute-start(f32[2,4096]{1,0:T(2,128)S(1)} %pad_maximum_fusion.5), channel_id=1, source_target_pairs={{0,96},{8,104},{16,112},{24,120},{32,0},{40,8},{48,16},{56,24},{64... | collective-permute-start | bytes 98312 | tf_op jit(solution)/shard_map/ppermute | solution.py:46
Sparse Core Ops, SparseCore 0:
  10.1 53.9 all-gather.1

commit v7 on v6

--- a/solution.py
+++ b/solution.py
@@ -90,6 +90,14 @@
     return jnp.concatenate(exchange(x, "col", 1, size), axis=0)
 
 
+def gather_row(x):
+    stride = 1
+    for width in radix_digits(lax.axis_size("row")):
+        x = jnp.concatenate(exchange(x, "row", stride, width), axis=0)
+        stride *= width
+    return x
+
+
 def per_device(queries, passages, mean_cost):
     entropy_scale = 0.1 * mean_cost[0]
     row_count = lax.axis_size("row")
@@ -97,7 +105,11 @@
     all_queries = queries.shape[0] * row_count * col_count
     all_passages = passages.shape[0] * row_count * col_count
     query_block = gather_col(queries)
-    cost_tile = inner_costs(query_block, lax.all_gather(passages, "row", axis=0, tiled=True))
+    half = passages.shape[1] // 2
+    passage_block = jnp.concatenate(
+        [lax.all_gather(passages[:, :half], "row", axis=0, tiled=True), gather_row(passages[:, half:])], axis=1
+    )
+    cost_tile = inner_costs(query_block, passage_block)
     col_potential = jnp.zeros((cost_tile.shape[1],), jnp.float32)
     row_potential = jnp.zeros((cost_tile.shape[0],), jnp.float32)
     for repeat in range(ITERS):

time: 278 us -> 283 us (1.018)
  other arithmetic: 98.8 us -> 88 us
  starting transfers between devices: 55.9 us -> 66.5 us
  local copies, waits for them, and re-layouts: 2.88 us -> 10.8 us
    all_gather x1, waiting for transfers between devices: 27.4 us -> 0.01 us  [per_device(): lax.all_gather(passages[:, :half], 'row', axis=0, tiled=True)]
    ppermute x7 -> x13, waiting for transfers between devices: 10.6 us -> 34.9 us  [exchange(): lax.ppermute(x, axis, digit_partners(axis, size, stride, width, k))]
    ppermute x7 -> x13, starting transfers between devices: 14.4 us -> 27.2 us  [exchange(): lax.ppermute(x, axis, digit_partners(axis, size, stride, width, k))]
    reduce_sum x3, other arithmetic: 31.7 us -> 22.9 us  [logsum_row(): totals = jnp.sum(jnp.exp(gaps / scale - peak[None, :]), axis=0)]
    unnamed x34 -> x26, local copies, waits for them, and re-layouts: 2.63 us -> 7.68 us
  transfers between devices with their start and end apart: 38 -> 44, of which waited for: 35 -> 35; matrix products, arithmetic and copies ran while one was open for 1% -> 1% of each run, Pallas kernels for 0% -> 0%
where the time goes in v7:
time: 283 us; the launch traced here: 282 us
  other arithmetic  88 us (31%)
  starting transfers between devices  66.5 us (23%)
  waiting for transfers between devices  65.5 us (23%)
  matrix products  36.4 us (13%)
  between operations  15.3 us (5%)
  local copies, waits for them, and re-layouts  10.8 us (4%)
    ppermute x30, starting transfers between devices, combine_over(): lax.ppermute(packed, axis, digit_partners(axis, size, stride, width, k))  39.2 us
    dot_general x1, matrix products, inner_costs(): lax.dot_general(left, right, (((1,), (1,)), ((), ())), precision=lax.Prec...  36.4 us
    ppermute x13, waiting for transfers between devices, exchange(): lax.ppermute(x, axis, digit_partners(axis, size, stride, width, k))  34.9 us
    reduce_sum x3, other arithmetic, logsum_col(): totals = jnp.sum(jnp.exp(gaps / scale - peak[:, None]), axis=1)  30.6 us
    ppermute x30, waiting for transfers between devices, combine_over(): lax.ppermute(packed, axis, digit_partners(axis, size, stride, width, k))  30.6 us
    ppermute x13, starting transfers between devices, exchange(): lax.ppermute(x, axis, digit_partners(axis, size, stride, width, k))  27.2 us
    reduce_max x3, other arithmetic, logsum_row(): peak = jnp.max(gaps, axis=0) / scale  23.2 us
    reduce_sum x3, other arithmetic, logsum_row(): totals = jnp.sum(jnp.exp(gaps / scale - peak[None, :]), axis=0)  22.9 us
  transfers between devices with their start and end apart: 44, of which 35 were waited for; matrix products, arithmetic and copies ran while one was open for 1% of the time, Pallas kernels for 0%

profile of v7, /device:TPU:0, one launch (start us, length us, event | category | flops | bytes accessed | tf_op | source)
XLA Modules:
  0.0 282.5 jit_solution(16313833999598683521)
XLA Ops:
  7.2 1.7 fusion.17
  8.9 1.8 collective-permute-start.7
  10.7 2.9 %collective-permute-start.8 = (f32[256,128]{1,0:T(8,128)S(1)}, f32[256,128]{1,0:T(8,128)S(1)}, u32[]{:S(2)}, u32[]{:S(2)}) collective-permute-start(f32[256,128]{1,0:T(8,128)S(1)} %get-tuple-element.18), channel_id=1, source_target_pairs={{0,16},{8,24},{16,0},{24,8},{32,48},{40,56},{48,32},{56,40},{64,80... | collective-permute-start | bytes 393224 | tf_op jit(solution)/shard_map/ppermute | solution.py:35
  14.9 1.5 collective-permute-start.1
  18.1 2.2 collective-permute-start.2
  20.3 2.3 collective-permute-start.3
  24.4 1.5 collective-permute-start.5
  25.9 5.3 %collective-permute-start.6 = (f32[256,256]{1,0:T(8,128)S(1)}, f32[256,256]{1,0:T(8,128)S(1)}, u32[]{:S(2)}, u32[]{:S(2)}) collective-permute-start(f32[256,256]{1,0:T(8,128)S(1)} %copy-done.4), channel_id=1, source_target_pairs={{0,7},{1,0},{2,1},{3,2},{4,3},{5,4},{6,5},{7,6},{8,15},{9,8},{10,9... | collective-permute-start | bytes 786440 | tf_op jit(solution)/shard_map/ppermute | solution.py:35
  31.3 5.3 %collective-permute-done.2 = f32[256,256]{1,0:T(8,128)S(1)} collective-permute-done((f32[256,256]{1,0:T(8,128)}, f32[256,256]{1,0:T(8,128)S(1)}, u32[]{:S(2)}, u32[]{:S(2)}) %collective-permute-start.2) | collective-permute-done | bytes 262176 | tf_op jit(solution)/shard_map/ppermute | solution.py:35
  36.6 1.9 collective-permute-start.10
  38.5 3.7 %collective-permute-start.11 = (f32[1024,128]{1,0:T(8,128)S(1)}, f32[1024,128]{1,0:T(8,128)S(1)}, u32[]{:S(2)}, u32[]{:S(2)}) collective-permute-start(f32[1024,128]{1,0:T(8,128)S(1)} %get-tuple-element.11), channel_id=1, source_target_pairs={{0,64},{8,72},{16,80},{24,88},{32,96},{40,104},{48,112},{56,120},{... | collective-permute-start | bytes 1572872 | tf_op jit(solution)/shard_map/ppermute | solution.py:35
  42.2 1.5 collective-permute-start.12
  44.5 14.8 %collective-permute-done.10 = f32[1024,128]{1,0:T(8,128)S(1)} collective-permute-done((f32[1024,128]{1,0:T(8,128)S(1)}, f32[1024,128]{1,0:T(8,128)S(1)}, u32[]{:S(2)}, u32[]{:S(2)}) %collective-permute-start.10) | collective-permute-done | bytes 524320 | tf_op jit(solution)/shard_map/ppermute | solution.py:35
  59.3 11.4 %collective-permute-done.11 = f32[1024,128]{1,0:T(8,128)S(1)} collective-permute-done((f32[1024,128]{1,0:T(8,128)S(1)}, f32[1024,128]{1,0:T(8,128)S(1)}, u32[]{:S(2)}, u32[]{:S(2)}) %collective-permute-start.11) | collective-permute-done | bytes 524320 | tf_op jit(solution)/shard_map/ppermute | solution.py:35
  70.7 3.0 %collective-permute-done.12 = f32[1024,128]{1,0:T(8,128)S(1)} collective-permute-done((f32[1024,128]{1,0:T(8,128)S(1)}, f32[1024,128]{1,0:T(8,128)S(1)}, u32[]{:S(2)}, u32[]{:S(2)}) %collective-permute-start.12) | collective-permute-done | bytes 524320 | tf_op jit(solution)/shard_map/ppermute | solution.py:35
  75.0 2.7 multiply_reduce_fusion
  77.8 36.4 %subtract_reduce_fusion.5 = (f32[2048]{0:T(1024)S(1)}, f32[2048,4096]{1,0:T(8,128)}) fusion(f32[2048,256]{1,0:T(8,128)S(1)} %bitcast_dynamic-update-slice_fusion, f32[1024,128]{1,0:T(8,128)S(1)} %get-tuple-element.7, f32[1024,128]{1,0:T(8,128)S(1)} %copy-done.2, f32[1024,128]{1,0:T(8,128)S(1)} %copy-done.3, f32[1024,128]{1,0:T(8,128)S(1)} %get-tuple-element.6, ...), kind=kOutput, calls=%fused_computation.12 | convolution fusion | flops 25815939072 | bytes 39878656 | tf_op jit(solution)/shard_map/dot_general | solution.py:14
  114.2 14.5 %exponential_reduce_fusion.5 = f32[2048]{0:T(1024)S(1)} fusion(f32[2048,4096]{1,0:T(8,128)} %get-tuple-element.64, f32[2048]{0:T(1024)S(1)} %broadcast_divide_fusion.5, f32[]{:T(128)} %bitcast), kind=kLoop, calls=%fused_computation.5 | loop fusion | flops 33552384 | bytes 33570820 | tf_op jit(solution)/shard_map/reduce_sum | solution.py:78
  132.1 2.3 collective-permute-start.16
  134.5 1.6 collective-permute-done.14
  137.0 13.8 %subtract_reduce_fusion.4 = f32[4096]{0:T(1024)S(1)} fusion(f32[2048,4096]{1,0:T(8,128)} %get-tuple-element.64, f32[2048]{0:T(1024)S(1)} %multiply_subtract_fusion.6), kind=kLoop, calls=%fused_computation.11 | loop fusion | flops 16773120 | bytes 33579008 | tf_op jit(solution)/shard_map/reduce_max | solution.py:83
  150.9 6.3 %copy-done = f32[2048,4096]{1,0:T(8,128)S(1)} copy-done((f32[2048,4096]{1,0:T(8,128)S(1)}, f32[2048,4096]{1,0:T(8,128)}, u32[]{:S(2)}) %copy-start) | copy-done | bytes 33554456
  157.2 7.6 %exponential_reduce_fusion.4 = f32[4096]{0:T(1024)S(1)} fusion(f32[2048,4096]{1,0:T(8,128)S(1)} %copy-done, f32[4096]{0:T(1024)S(1)} %broadcast_divide_fusion.2, f32[2048]{0:T(1024)S(1)} %multiply_subtract_fusion.6, f32[]{:T(128)} %bitcast), kind=kLoop, calls=%fused_computation.4 | loop fusion | flops 33550336 | bytes 33595396 | tf_op jit(solution)/shard_map/reduce_sum | solution.py:84
  166.4 2.0 collective-permute-start.19
  168.4 1.7 collective-permute-done.17
  171.5 1.5 collective-permute-start.20
  173.0 2.6 collective-permute-start.21
  176.6 1.7 collective-permute-done.21
  179.6 3.0 %subtract_reduce_fusion.3 = f32[2048]{0:T(1024)S(1)} fusion(f32[2048,4096]{1,0:T(8,128)S(1)} %copy-done, f32[4096]{0:T(1024)S(1)} %bitcast.121), kind=kLoop, calls=%fused_computation.10 | loop fusion | flops 16775168 | bytes 33579008 | tf_op jit(solution)/shard_map/reduce_max | solution.py:77
  182.6 8.0 %exponential_reduce_fusion.3 = f32[2048]{0:T(1024)S(1)} fusion(f32[2048,4096]{1,0:T(8,128)S(1)} %copy-done, f32[2048]{0:T(1024)S(1)} %broadcast_divide_fusion.4, f32[4096]{0:T(1024)S(1)} %bitcast.122, f32[]{:T(128)} %bitcast), kind=kLoop, calls=%fused_computation.3 | loop fusion | flops 33552384 | bytes 33587204 | tf_op jit(solution)/shard_map/reduce_sum | solution.py:78
  192.0 1.9 collective-permute-start.24
  193.9 2.7 collective-permute-start.25
  197.1 2.1 collective-permute-done.25
  200.4 4.7 %subtract_reduce_fusion.2 = f32[4096]{0:T(1024)S(1)} fusion(f32[2048,4096]{1,0:T(8,128)S(1)} %copy-done, f32[2048]{0:T(1024)S(1)} %multiply_subtract_fusion.5), kind=kLoop, calls=%fused_computation.9 | loop fusion | flops 16773120 | bytes 33579008 | tf_op jit(solution)/shard_map/reduce_max | solution.py:83
  205.2 7.6 %exponential_reduce_fusion.2 = f32[4096]{0:T(1024)S(1)} fusion(f32[2048,4096]{1,0:T(8,128)S(1)} %copy-done, f32[4096]{0:T(1024)S(1)} %broadcast_divide_fusion.1, f32[2048]{0:T(1024)S(1)} %multiply_subtract_fusion.5, f32[]{:T(128)} %bitcast), kind=kLoop, calls=%fused_computation.2 | loop fusion | flops 33550336 | bytes 33595396 | tf_op jit(solution)/shard_map/reduce_sum | solution.py:84
  212.9 1.7 collective-permute-start.27
  214.6 2.4 collective-permute-start.28
  218.1 2.0 collective-permute-done.28
  221.2 2.9 %collective-permute-start.31 = (f32[2,4096]{1,0:T(2,128)S(1)}, f32[2,4096]{1,0:T(2,128)S(1)}, u32[]{:S(2)}, u32[]{:S(2)}) collective-permute-start(f32[2,4096]{1,0:T(2,128)S(1)} %pad_maximum_fusion.6), channel_id=1, source_target_pairs={{0,64},{8,72},{16,80},{24,88},{32,96},{40,104},{48,112},{56,120},{... | collective-permute-start | bytes 98312 | tf_op jit(solution)/shard_map/ppermute | solution.py:46
  228.1 3.0 %subtract_reduce_fusion.1 = f32[2048]{0:T(1024)S(1)} fusion(f32[2048,4096]{1,0:T(8,128)S(1)} %copy-done, f32[4096]{0:T(1024)S(1)} %bitcast.123), kind=kLoop, calls=%fused_computation.8 | loop fusion | flops 16775168 | bytes 33579008 | tf_op jit(solution)/shard_map/reduce_max | solution.py:77
  231.1 8.0 %exponential_reduce_fusion.1 = f32[2048]{0:T(1024)S(1)} fusion(f32[2048,4096]{1,0:T(8,128)S(1)} %copy-done, f32[2048]{0:T(1024)S(1)} %broadcast_divide_fusion.3, f32[4096]{0:T(1024)S(1)} %bitcast.124, f32[]{:T(128)} %bitcast), kind=kLoop, calls=%fused_computation.1 | loop fusion | flops 33552384 | bytes 33587204 | tf_op jit(solution)/shard_map/reduce_sum | solution.py:78
  240.6 3.2 %collective-permute-start.35 = (f32[2,2048]{1,0:T(2,128)S(1)}, f32[2,2048]{1,0:T(2,128)S(1)}, u32[]{:S(2)}, u32[]{:S(2)}) collective-permute-start(f32[2,2048]{1,0:T(2,128)S(1)} %pad_maximum_fusion.14), channel_id=1, source_target_pairs={{0,4},{1,5},{2,6},{3,7},{4,0},{5,1},{6,2},{7,3},{8,12},{9,13},{10,... | collective-permute-start | bytes 49160 | tf_op jit(solution)/shard_map/ppermute | solution.py:46
  245.9 1.6 collective-permute-done.36
  247.6 4.7 %subtract_reduce_fusion = f32[4096]{0:T(1024)S(1)} fusion(f32[2048,4096]{1,0:T(8,128)S(1)} %copy-done, f32[2048]{0:T(1024)S(1)} %multiply_subtract_fusion.4), kind=kLoop, calls=%fused_computation.7 | loop fusion | flops 16773120 | bytes 33579008 | tf_op jit(solution)/shard_map/reduce_max | solution.py:83
  252.3 7.6 %exponential_reduce_fusion = f32[4096]{0:T(1024)S(1)} fusion(f32[2048,4096]{1,0:T(8,128)S(1)} %copy-done, f32[4096]{0:T(1024)S(1)} %broadcast_divide_fusion, f32[2048]{0:T(1024)S(1)} %multiply_subtract_fusion.4, f32[]{:T(128)} %bitcast), kind=kLoop, calls=%fused_computation | loop fusion | flops 33550336 | bytes 33595396 | tf_op jit(solution)/shard_map/reduce_sum | solution.py:84
  260.1 3.0 %collective-permute-start.38 = (f32[2,4096]{1,0:T(2,128)S(1)}, f32[2,4096]{1,0:T(2,128)S(1)}, u32[]{:S(2)}, u32[]{:S(2)}) collective-permute-start(f32[2,4096]{1,0:T(2,128)S(1)} %pad_maximum_fusion.7), channel_id=1, source_target_pairs={{0,16},{8,24},{16,0},{24,8},{32,48},{40,56},{48,32},{56,40},{64,80... | collective-permute-start | bytes 98312 | tf_op jit(solution)/shard_map/ppermute | solution.py:46
  265.6 1.5 collective-permute-done.39
  268.3 2.7 collective-permute-start.41
  (131 shorter events, 37.1 us)
Async XLA Ops:
  7.2 17.2 %copy-start.4 = (f32[256,256]{1,0:T(8,128)S(1)}, f32[256,256]{1,0:T(8,128)}, u32[]{:S(2)}) copy-start(f32[256,256]{1,0:T(8,128)} %param.3) | copy-start | bytes 786436
  7.2 67.8 %all-gather.2.cloned.1.call-start = ((), (), s32[]{:S(2)}) async-start(), calls=%async_computation | async-start | bytes 2228224 | tf_op jit(solution)/shard_map/all_gather | solution.py:110
  8.9 9.2 %collective-permute-start.7 = (f32[256,128]{1,0:T(8,128)S(1)}, f32[256,128]{1,0:T(8,128)S(1)}, u32[]{:S(2)}, u32[]{:S(2)}) collective-permute-start(f32[256,128]{1,0:T(8,128)S(1)} %get-tuple-element.18), channel_id=1, source_target_pairs={{0,8},{8,16},{16,24},{24,0},{32,40},{40,48},{48,56},{56,32},{64,72... | collective-permute-start | bytes 393224 | tf_op jit(solution)/shard_map/ppermute | solution.py:35
  10.7 9.6 %collective-permute-start.8 = (f32[256,128]{1,0:T(8,128)S(1)}, f32[256,128]{1,0:T(8,128)S(1)}, u32[]{:S(2)}, u32[]{:S(2)}) collective-permute-start(f32[256,128]{1,0:T(8,128)S(1)} %get-tuple-element.18), channel_id=1, source_target_pairs={{0,16},{8,24},{16,0},{24,8},{32,48},{40,56},{48,32},{56,40},{64,80... | collective-permute-start | bytes 393224 | tf_op jit(solution)/shard_map/ppermute | solution.py:35
  13.6 9.0 %collective-permute-start.9 = (f32[256,128]{1,0:T(8,128)S(1)}, f32[256,128]{1,0:T(8,128)S(1)}, u32[]{:S(2)}, u32[]{:S(2)}) collective-permute-start(f32[256,128]{1,0:T(8,128)S(1)} %get-tuple-element.18), channel_id=1, source_target_pairs={{0,24},{8,0},{16,8},{24,16},{32,56},{40,32},{48,40},{56,48},{64,88... | collective-permute-start | bytes 393224 | tf_op jit(solution)/shard_map/ppermute | solution.py:35
  14.9 9.4 %collective-permute-start = (f32[256,256]{1,0:T(8,128)}, f32[256,256]{1,0:T(8,128)S(1)}, u32[]{:S(2)}, u32[]{:S(2)}) collective-permute-start(f32[256,256]{1,0:T(8,128)} %param.3), channel_id=1, source_target_pairs={{0,1},{1,2},{2,3},{3,4},{4,5},{5,6},{6,7},{7,0},{8,9},{9,10},{10,1... | collective-permute-start | bytes 786440 | tf_op jit(solution)/shard_map/ppermute | solution.py:35
  14.9 11.0 %collective-permute-start.1 = (f32[256,256]{1,0:T(8,128)}, f32[256,256]{1,0:T(8,128)S(1)}, u32[]{:S(2)}, u32[]{:S(2)}) collective-permute-start(f32[256,256]{1,0:T(8,128)} %param.3), channel_id=1, source_target_pairs={{0,2},{1,3},{2,4},{3,5},{4,6},{5,7},{6,0},{7,1},{8,10},{9,11},{10,... | collective-permute-start | bytes 786440 | tf_op jit(solution)/shard_map/ppermute | solution.py:35
  18.1 18.5 %collective-permute-start.2 = (f32[256,256]{1,0:T(8,128)}, f32[256,256]{1,0:T(8,128)S(1)}, u32[]{:S(2)}, u32[]{:S(2)}) collective-permute-start(f32[256,256]{1,0:T(8,128)} %param.3), channel_id=1, source_target_pairs={{0,3},{1,4},{2,5},{3,6},{4,7},{5,0},{6,1},{7,2},{8,11},{9,12},{10,... | collective-permute-start | bytes 786440 | tf_op jit(solution)/shard_map/ppermute | solution.py:35
  20.3 18.2 %collective-permute-start.3 = (f32[256,256]{1,0:T(8,128)}, f32[256,256]{1,0:T(8,128)S(1)}, u32[]{:S(2)}, u32[]{:S(2)}) collective-permute-start(f32[256,256]{1,0:T(8,128)} %param.3), channel_id=1, source_target_pairs={{0,4},{1,5},{2,6},{3,7},{4,0},{5,1},{6,2},{7,3},{8,12},{9,13},{10,... | collective-permute-start | bytes 786440 | tf_op jit(solution)/shard_map/ppermute | solution.py:35
  22.6 19.6 %collective-permute-start.4 = (f32[256,256]{1,0:T(8,128)}, f32[256,256]{1,0:T(8,128)S(1)}, u32[]{:S(2)}, u32[]{:S(2)}) collective-permute-start(f32[256,256]{1,0:T(8,128)} %param.3), channel_id=1, source_target_pairs={{0,5},{1,6},{2,7},{3,0},{4,1},{5,2},{6,3},{7,4},{8,13},{9,14},{10,... | collective-permute-start | bytes 786440 | tf_op jit(solution)/shard_map/ppermute | solution.py:35
  24.4 19.4 %collective-permute-start.5 = (f32[256,256]{1,0:T(8,128)S(1)}, f32[256,256]{1,0:T(8,128)S(1)}, u32[]{:S(2)}, u32[]{:S(2)}) collective-permute-start(f32[256,256]{1,0:T(8,128)S(1)} %copy-done.4), channel_id=1, source_target_pairs={{0,6},{1,7},{2,0},{3,1},{4,2},{5,3},{6,4},{7,5},{8,14},{9,15},{10,... | collective-permute-start | bytes 786440 | tf_op jit(solution)/shard_map/ppermute | solution.py:35
  25.9 17.9 %collective-permute-start.6 = (f32[256,256]{1,0:T(8,128)S(1)}, f32[256,256]{1,0:T(8,128)S(1)}, u32[]{:S(2)}, u32[]{:S(2)}) collective-permute-start(f32[256,256]{1,0:T(8,128)S(1)} %copy-done.4), channel_id=1, source_target_pairs={{0,7},{1,0},{2,1},{3,2},{4,3},{5,4},{6,5},{7,6},{8,15},{9,8},{10,9... | collective-permute-start | bytes 786440 | tf_op jit(solution)/shard_map/ppermute | solution.py:35
  36.6 22.7 %collective-permute-start.10 = (f32[1024,128]{1,0:T(8,128)S(1)}, f32[1024,128]{1,0:T(8,128)S(1)}, u32[]{:S(2)}, u32[]{:S(2)}) collective-permute-start(f32[1024,128]{1,0:T(8,128)S(1)} %get-tuple-element.11), channel_id=1, source_target_pairs={{0,32},{8,40},{16,48},{24,56},{32,64},{40,72},{48,80},{56,88},{64,... | collective-permute-start | bytes 1572872 | tf_op jit(solution)/shard_map/ppermute | solution.py:35
  38.5 32.2 %collective-permute-start.11 = (f32[1024,128]{1,0:T(8,128)S(1)}, f32[1024,128]{1,0:T(8,128)S(1)}, u32[]{:S(2)}, u32[]{:S(2)}) collective-permute-start(f32[1024,128]{1,0:T(8,128)S(1)} %get-tuple-element.11), channel_id=1, source_target_pairs={{0,64},{8,72},{16,80},{24,88},{32,96},{40,104},{48,112},{56,120},{... | collective-permute-start | bytes 1572872 | tf_op jit(solution)/shard_map/ppermute | solution.py:35
  42.2 31.5 %collective-permute-start.12 = (f32[1024,128]{1,0:T(8,128)S(1)}, f32[1024,128]{1,0:T(8,128)S(1)}, u32[]{:S(2)}, u32[]{:S(2)}) collective-permute-start(f32[1024,128]{1,0:T(8,128)S(1)} %get-tuple-element.11), channel_id=1, source_target_pairs={{0,96},{8,104},{16,112},{24,120},{32,0},{40,8},{48,16},{56,24},{64... | collective-permute-start | bytes 1572872 | tf_op jit(solution)/shard_map/ppermute | solution.py:35
  75.0 2.8 copy-start.3
  128.8 2.1 collective-permute-start.13
  130.9 5.2 %collective-permute-start.14 = (f32[2,2048]{1,0:T(2,128)S(1)}, f32[2,2048]{1,0:T(2,128)S(1)}, u32[]{:S(2)}, u32[]{:S(2)}) collective-permute-start(f32[2,2048]{1,0:T(2,128)S(1)} %pad_maximum_fusion.10), channel_id=1, source_target_pairs={{0,2},{1,3},{2,4},{3,5},{4,6},{5,7},{6,0},{7,1},{8,10},{9,11},{10,... | collective-permute-start | bytes 49160 | tf_op jit(solution)/shard_map/ppermute | solution.py:46
  131.0 5.5 %collective-permute-start.15 = (f32[2,2048]{1,0:T(2,128)S(1)}, f32[2,2048]{1,0:T(2,128)S(1)}, u32[]{:S(2)}, u32[]{:S(2)}) collective-permute-start(f32[2,2048]{1,0:T(2,128)S(1)} %pad_maximum_fusion.10), channel_id=1, source_target_pairs={{0,4},{1,5},{2,6},{3,7},{4,0},{5,1},{6,2},{7,3},{8,12},{9,13},{10,... | collective-permute-start | bytes 49160 | tf_op jit(solution)/shard_map/ppermute | solution.py:46
  132.1 4.8 %collective-permute-start.16 = (f32[2,2048]{1,0:T(2,128)S(1)}, f32[2,2048]{1,0:T(2,128)S(1)}, u32[]{:S(2)}, u32[]{:S(2)}) collective-permute-start(f32[2,2048]{1,0:T(2,128)S(1)} %pad_maximum_fusion.10), channel_id=1, source_target_pairs={{0,6},{1,7},{2,0},{3,1},{4,2},{5,3},{6,4},{7,5},{8,14},{9,15},{10,... | collective-permute-start | bytes 49160 | tf_op jit(solution)/shard_map/ppermute | solution.py:46
  137.0 20.2 %copy-start = (f32[2048,4096]{1,0:T(8,128)S(1)}, f32[2048,4096]{1,0:T(8,128)}, u32[]{:S(2)}) copy-start(f32[2048,4096]{1,0:T(8,128)} %get-tuple-element.64) | copy-start | bytes 100663296
  164.9 5.2 %collective-permute-start.17 = (f32[2,4096]{1,0:T(2,128)S(1)}, f32[2,4096]{1,0:T(2,128)S(1)}, u32[]{:S(2)}, u32[]{:S(2)}) collective-permute-start(f32[2,4096]{1,0:T(2,128)S(1)} %pad_maximum_fusion.3), channel_id=1, source_target_pairs={{0,8},{8,16},{16,24},{24,0},{32,40},{40,48},{48,56},{56,32},{64,72... | collective-permute-start | bytes 98312 | tf_op jit(solution)/shard_map/ppermute | solution.py:46
  165.6 5.4 %collective-permute-start.18 = (f32[2,4096]{1,0:T(2,128)S(1)}, f32[2,4096]{1,0:T(2,128)S(1)}, u32[]{:S(2)}, u32[]{:S(2)}) collective-permute-start(f32[2,4096]{1,0:T(2,128)S(1)} %pad_maximum_fusion.3), channel_id=1, source_target_pairs={{0,16},{8,24},{16,0},{24,8},{32,48},{40,56},{48,32},{56,40},{64,80... | collective-permute-start | bytes 98312 | tf_op jit(solution)/shard_map/ppermute | solution.py:46
  166.4 4.9 %collective-permute-start.19 = (f32[2,4096]{1,0:T(2,128)S(1)}, f32[2,4096]{1,0:T(2,128)S(1)}, u32[]{:S(2)}, u32[]{:S(2)}) collective-permute-start(f32[2,4096]{1,0:T(2,128)S(1)} %pad_maximum_fusion.3), channel_id=1, source_target_pairs={{0,24},{8,0},{16,8},{24,16},{32,56},{40,32},{48,40},{56,48},{64,88... | collective-permute-start | bytes 98312 | tf_op jit(solution)/shard_map/ppermute | solution.py:46
  171.5 5.2 %collective-permute-start.20 = (f32[2,4096]{1,0:T(2,128)S(1)}, f32[2,4096]{1,0:T(2,128)S(1)}, u32[]{:S(2)}, u32[]{:S(2)}) collective-permute-start(f32[2,4096]{1,0:T(2,128)S(1)} %pad_maximum_fusion.4), channel_id=1, source_target_pairs={{0,32},{8,40},{16,48},{24,56},{32,64},{40,72},{48,80},{56,88},{64,... | collective-permute-start | bytes 98312 | tf_op jit(solution)/shard_map/ppermute | solution.py:46
  173.0 5.4 %collective-permute-start.21 = (f32[2,4096]{1,0:T(2,128)S(1)}, f32[2,4096]{1,0:T(2,128)S(1)}, u32[]{:S(2)}, u32[]{:S(2)}) collective-permute-start(f32[2,4096]{1,0:T(2,128)S(1)} %pad_maximum_fusion.4), channel_id=1, source_target_pairs={{0,64},{8,72},{16,80},{24,88},{32,96},{40,104},{48,112},{56,120},{... | collective-permute-start | bytes 98312 | tf_op jit(solution)/shard_map/ppermute | solution.py:46
  175.5 3.9 %collective-permute-start.22 = (f32[2,4096]{1,0:T(2,128)S(1)}, f32[2,4096]{1,0:T(2,128)S(1)}, u32[]{:S(2)}, u32[]{:S(2)}) collective-permute-start(f32[2,4096]{1,0:T(2,128)S(1)} %pad_maximum_fusion.4), channel_id=1, source_target_pairs={{0,96},{8,104},{16,112},{24,120},{32,0},{40,8},{48,16},{56,24},{64... | collective-permute-start | bytes 98312 | tf_op jit(solution)/shard_map/ppermute | solution.py:46
  190.7 1.3 collective-permute-start.23
  192.0 5.0 %collective-permute-start.24 = (f32[2,2048]{1,0:T(2,128)S(1)}, f32[2,2048]{1,0:T(2,128)S(1)}, u32[]{:S(2)}, u32[]{:S(2)}) collective-permute-start(f32[2,2048]{1,0:T(2,128)S(1)} %pad_maximum_fusion.12), channel_id=1, source_target_pairs={{0,2},{1,3},{2,4},{3,5},{4,6},{5,7},{6,0},{7,1},{8,10},{9,11},{10,... | collective-permute-start | bytes 49160 | tf_op jit(solution)/shard_map/ppermute | solution.py:46
  193.9 5.2 %collective-permute-start.25 = (f32[2,2048]{1,0:T(2,128)S(1)}, f32[2,2048]{1,0:T(2,128)S(1)}, u32[]{:S(2)}, u32[]{:S(2)}) collective-permute-start(f32[2,2048]{1,0:T(2,128)S(1)} %pad_maximum_fusion.12), channel_id=1, source_target_pairs={{0,4},{1,5},{2,6},{3,7},{4,0},{5,1},{6,2},{7,3},{8,12},{9,13},{10,... | collective-permute-start | bytes 49160 | tf_op jit(solution)/shard_map/ppermute | solution.py:46
  196.6 3.7 %collective-permute-start.26 = (f32[2,2048]{1,0:T(2,128)S(1)}, f32[2,2048]{1,0:T(2,128)S(1)}, u32[]{:S(2)}, u32[]{:S(2)}) collective-permute-start(f32[2,2048]{1,0:T(2,128)S(1)} %pad_maximum_fusion.12), channel_id=1, source_target_pairs={{0,6},{1,7},{2,0},{3,1},{4,2},{5,3},{6,4},{7,5},{8,14},{9,15},{10,... | collective-permute-start | bytes 49160 | tf_op jit(solution)/shard_map/ppermute | solution.py:46
  212.9 5.2 %collective-permute-start.27 = (f32[2,4096]{1,0:T(2,128)S(1)}, f32[2,4096]{1,0:T(2,128)S(1)}, u32[]{:S(2)}, u32[]{:S(2)}) collective-permute-start(f32[2,4096]{1,0:T(2,128)S(1)} %pad_maximum_fusion.5), channel_id=1, source_target_pairs={{0,8},{8,16},{16,24},{24,0},{32,40},{40,48},{48,56},{56,32},{64,72... | collective-permute-start | bytes 98312 | tf_op jit(solution)/shard_map/ppermute | solution.py:46
  214.6 5.4 %collective-permute-start.28 = (f32[2,4096]{1,0:T(2,128)S(1)}, f32[2,4096]{1,0:T(2,128)S(1)}, u32[]{:S(2)}, u32[]{:S(2)}) collective-permute-start(f32[2,4096]{1,0:T(2,128)S(1)} %pad_maximum_fusion.5), channel_id=1, source_target_pairs={{0,16},{8,24},{16,0},{24,8},{32,48},{40,56},{48,32},{56,40},{64,80... | collective-permute-start | bytes 98312 | tf_op jit(solution)/shard_map/ppermute | solution.py:46
  217.0 3.9 %collective-permute-start.29 = (f32[2,4096]{1,0:T(2,128)S(1)}, f32[2,4096]{1,0:T(2,128)S(1)}, u32[]{:S(2)}, u32[]{:S(2)}) collective-permute-start(f32[2,4096]{1,0:T(2,128)S(1)} %pad_maximum_fusion.5), channel_id=1, source_target_pairs={{0,24},{8,0},{16,8},{24,16},{32,56},{40,32},{48,40},{56,48},{64,88... | collective-permute-start | bytes 98312 | tf_op jit(solution)/shard_map/ppermute | solution.py:46
  221.1 5.2 %collective-permute-start.30 = (f32[2,4096]{1,0:T(2,128)S(1)}, f32[2,4096]{1,0:T(2,128)S(1)}, u32[]{:S(2)}, u32[]{:S(2)}) collective-permute-start(f32[2,4096]{1,0:T(2,128)S(1)} %pad_maximum_fusion.6), channel_id=1, source_target_pairs={{0,32},{8,40},{16,48},{24,56},{32,64},{40,72},{48,80},{56,88},{64,... | collective-permute-start | bytes 98312 | tf_op jit(solution)/shard_map/ppermute | solution.py:46
  221.2 5.5 %collective-permute-start.31 = (f32[2,4096]{1,0:T(2,128)S(1)}, f32[2,4096]{1,0:T(2,128)S(1)}, u32[]{:S(2)}, u32[]{:S(2)}) collective-permute-start(f32[2,4096]{1,0:T(2,128)S(1)} %pad_maximum_fusion.6), channel_id=1, source_target_pairs={{0,64},{8,72},{16,80},{24,88},{32,96},{40,104},{48,112},{56,120},{... | collective-permute-start | bytes 98312 | tf_op jit(solution)/shard_map/ppermute | solution.py:46
  224.0 3.9 %collective-permute-start.32 = (f32[2,4096]{1,0:T(2,128)S(1)}, f32[2,4096]{1,0:T(2,128)S(1)}, u32[]{:S(2)}, u32[]{:S(2)}) collective-permute-start(f32[2,4096]{1,0:T(2,128)S(1)} %pad_maximum_fusion.6), channel_id=1, source_target_pairs={{0,96},{8,104},{16,112},{24,120},{32,0},{40,8},{48,16},{56,24},{64... | collective-permute-start | bytes 98312 | tf_op jit(solution)/shard_map/ppermute | solution.py:46
  239.2 1.3 collective-permute-start.33
  240.5 5.0 %collective-permute-start.34 = (f32[2,2048]{1,0:T(2,128)S(1)}, f32[2,2048]{1,0:T(2,128)S(1)}, u32[]{:S(2)}, u32[]{:S(2)}) collective-permute-start(f32[2,2048]{1,0:T(2,128)S(1)} %pad_maximum_fusion.14), channel_id=1, source_target_pairs={{0,2},{1,3},{2,4},{3,5},{4,6},{5,7},{6,0},{7,1},{8,10},{9,11},{10,... | collective-permute-start | bytes 49160 | tf_op jit(solution)/shard_map/ppermute | solution.py:46
  240.6 5.3 %collective-permute-start.35 = (f32[2,2048]{1,0:T(2,128)S(1)}, f32[2,2048]{1,0:T(2,128)S(1)}, u32[]{:S(2)}, u32[]{:S(2)}) collective-permute-start(f32[2,2048]{1,0:T(2,128)S(1)} %pad_maximum_fusion.14), channel_id=1, source_target_pairs={{0,4},{1,5},{2,6},{3,7},{4,0},{5,1},{6,2},{7,3},{8,12},{9,13},{10,... | collective-permute-start | bytes 49160 | tf_op jit(solution)/shard_map/ppermute | solution.py:46
  243.8 3.7 %collective-permute-start.36 = (f32[2,2048]{1,0:T(2,128)S(1)}, f32[2,2048]{1,0:T(2,128)S(1)}, u32[]{:S(2)}, u32[]{:S(2)}) collective-permute-start(f32[2,2048]{1,0:T(2,128)S(1)} %pad_maximum_fusion.14), channel_id=1, source_target_pairs={{0,6},{1,7},{2,0},{3,1},{4,2},{5,3},{6,4},{7,5},{8,14},{9,15},{10,... | collective-permute-start | bytes 49160 | tf_op jit(solution)/shard_map/ppermute | solution.py:46
  247.6 4.8 %copy-start.5 = (f32[2048]{0:T(1024)}, f32[2048]{0:T(1024)S(1)}, u32[]{:S(2)}) copy-start(f32[2048]{0:T(1024)S(1)} %multiply_subtract_fusion.4) | copy-start | bytes 24580
  260.0 5.2 %collective-permute-start.37 = (f32[2,4096]{1,0:T(2,128)S(1)}, f32[2,4096]{1,0:T(2,128)S(1)}, u32[]{:S(2)}, u32[]{:S(2)}) collective-permute-start(f32[2,4096]{1,0:T(2,128)S(1)} %pad_maximum_fusion.7), channel_id=1, source_target_pairs={{0,8},{8,16},{16,24},{24,0},{32,40},{40,48},{48,56},{56,32},{64,72... | collective-permute-start | bytes 98312 | tf_op jit(solution)/shard_map/ppermute | solution.py:46
  260.1 5.5 %collective-permute-start.38 = (f32[2,4096]{1,0:T(2,128)S(1)}, f32[2,4096]{1,0:T(2,128)S(1)}, u32[]{:S(2)}, u32[]{:S(2)}) collective-permute-start(f32[2,4096]{1,0:T(2,128)S(1)} %pad_maximum_fusion.7), channel_id=1, source_target_pairs={{0,16},{8,24},{16,0},{24,8},{32,48},{40,56},{48,32},{56,40},{64,80... | collective-permute-start | bytes 98312 | tf_op jit(solution)/shard_map/ppermute | solution.py:46
  263.2 3.9 %collective-permute-start.39 = (f32[2,4096]{1,0:T(2,128)S(1)}, f32[2,4096]{1,0:T(2,128)S(1)}, u32[]{:S(2)}, u32[]{:S(2)}) collective-permute-start(f32[2,4096]{1,0:T(2,128)S(1)} %pad_maximum_fusion.7), channel_id=1, source_target_pairs={{0,24},{8,0},{16,8},{24,16},{32,56},{40,32},{48,40},{56,48},{64,88... | collective-permute-start | bytes 98312 | tf_op jit(solution)/shard_map/ppermute | solution.py:46
  267.3 5.2 %collective-permute-start.40 = (f32[2,4096]{1,0:T(2,128)S(1)}, f32[2,4096]{1,0:T(2,128)S(1)}, u32[]{:S(2)}, u32[]{:S(2)}) collective-permute-start(f32[2,4096]{1,0:T(2,128)S(1)} %pad_maximum_fusion.8), channel_id=1, source_target_pairs={{0,32},{8,40},{16,48},{24,56},{32,64},{40,72},{48,80},{56,88},{64,... | collective-permute-start | bytes 98312 | tf_op jit(solution)/shard_map/ppermute | solution.py:46
  268.3 5.4 %collective-permute-start.41 = (f32[2,4096]{1,0:T(2,128)S(1)}, f32[2,4096]{1,0:T(2,128)S(1)}, u32[]{:S(2)}, u32[]{:S(2)}) collective-permute-start(f32[2,4096]{1,0:T(2,128)S(1)} %pad_maximum_fusion.8), channel_id=1, source_target_pairs={{0,64},{8,72},{16,80},{24,88},{32,96},{40,104},{48,112},{56,120},{... | collective-permute-start | bytes 98312 | tf_op jit(solution)/shard_map/ppermute | solution.py:46
  271.0 3.9 %collective-permute-start.42 = (f32[2,4096]{1,0:T(2,128)S(1)}, f32[2,4096]{1,0:T(2,128)S(1)}, u32[]{:S(2)}, u32[]{:S(2)}) collective-permute-start(f32[2,4096]{1,0:T(2,128)S(1)} %pad_maximum_fusion.8), channel_id=1, source_target_pairs={{0,96},{8,104},{16,112},{24,120},{32,0},{40,8},{48,16},{56,24},{64... | collective-permute-start | bytes 98312 | tf_op jit(solution)/shard_map/ppermute | solution.py:46
  (2 other events, 5.4 us)
Sparse Core Ops, SparseCore 0:
  10.1 62.0 all-gather.1

commit v8 on v7

--- a/solution.py
+++ b/solution.py
@@ -105,9 +105,10 @@
     all_queries = queries.shape[0] * row_count * col_count
     all_passages = passages.shape[0] * row_count * col_count
     query_block = gather_col(queries)
-    half = passages.shape[1] // 2
+    rows = passages.shape[0]
+    split = rows - rows // 4
     passage_block = jnp.concatenate(
-        [lax.all_gather(passages[:, :half], "row", axis=0, tiled=True), gather_row(passages[:, half:])], axis=1
+        [lax.all_gather(passages[:split], "row", axis=0, tiled=True), gather_row(passages[split:])], axis=0
     )
     cost_tile = inner_costs(query_block, passage_block)
     col_potential = jnp.zeros((cost_tile.shape[1],), jnp.float32)
@@ -117,7 +118,9 @@
         row_potential = -entropy_scale * math.log(all_queries) - entropy_scale * logsum_col(gaps, entropy_scale)
         gaps = row_potential[:, None] - cost_tile
         col_potential = -entropy_scale * math.log(all_passages) - entropy_scale * logsum_row(gaps, entropy_scale)
-    return (row_potential, col_potential)
+    head = col_potential[: split * row_count].reshape(row_count, split)
+    tail = col_potential[split * row_count :].reshape(row_count, rows - split)
+    return (row_potential, jnp.concatenate([head, tail], axis=1).reshape(-1))
 
 
 def solution(mesh):

time: 283 us -> 276 us (0.975)
  waiting for transfers between devices: 65.5 us -> 59.1 us
  local copies, waits for them, and re-layouts: 10.8 us -> 15.6 us
    ppermute x13, waiting for transfers between devices: 34.9 us -> 23.5 us  [exchange(): lax.ppermute(x, axis, digit_partners(axis, size, stride, width, k))]
    all_gather x1, waiting for transfers between devices: 0.01 us -> 5.66 us  [per_device(): lax.all_gather(passages[:split], 'row', axis=0, tiled=True)]
    unnamed x26 -> x29, local copies, waits for them, and re-layouts: 7.68 us -> 11.3 us
where the time goes in v8:
time: 276 us
  other arithmetic  85.4 us (31%)
  starting transfers between devices  65.3 us (24%)
  waiting for transfers between devices  59.1 us (21%)
  matrix products  34.8 us (13%)
  between operations  15.7 us (6%)
  local copies, waits for them, and re-layouts  15.6 us (6%)
    ppermute x30, starting transfers between devices, combine_over(): lax.ppermute(packed, axis, digit_partners(axis, size, stride, width, k))  37.9 us
    dot_general x1, matrix products, inner_costs(): lax.dot_general(left, right, (((1,), (1,)), ((), ())), precision=lax.Prec...  34.8 us
    reduce_sum x3, other arithmetic, logsum_col(): totals = jnp.sum(jnp.exp(gaps / scale - peak[:, None]), axis=1)  30.6 us
    ppermute x30, waiting for transfers between devices, combine_over(): lax.ppermute(packed, axis, digit_partners(axis, size, stride, width, k))  29.9 us
    ppermute x13, starting transfers between devices, exchange(): lax.ppermute(x, axis, digit_partners(axis, size, stride, width, k))  27.3 us
    ppermute x13, waiting for transfers between devices, exchange(): lax.ppermute(x, axis, digit_partners(axis, size, stride, width, k))  23.5 us
    reduce_max x3, other arithmetic, logsum_row(): peak = jnp.max(gaps, axis=0) / scale  23.2 us
    reduce_sum x3, other arithmetic, logsum_row(): totals = jnp.sum(jnp.exp(gaps / scale - peak[None, :]), axis=0)  22.9 us
  transfers between devices with their start and end apart: 44, of which 35 were waited for; matrix products, arithmetic and copies ran while one was open for 1% of the time, Pallas kernels for 0%

profile of v8, /device:TPU:0, one launch (start us, length us, event | category | flops | bytes accessed | tf_op | source)
XLA Modules:
  0.0 275.8 jit_solution(9641693681091126703)
XLA Ops:
  7.2 1.6 slice.223
  9.7 1.8 collective-permute-start.7
  11.5 2.9 %collective-permute-start.8 = (f32[64,256]{1,0:T(8,128)S(1)}, f32[64,256]{1,0:T(8,128)S(1)}, u32[]{:S(2)}, u32[]{:S(2)}) collective-permute-start(f32[64,256]{1,0:T(8,128)S(1)} %get-tuple-element.29), channel_id=1, source_target_pairs={{0,16},{8,24},{16,0},{24,8},{32,48},{40,56},{48,32},{56,40},{64,80... | collective-permute-start | bytes 196616 | tf_op jit(solution)/shard_map/ppermute | solution.py:35
  15.8 1.5 collective-permute-start.1
  19.3 2.2 collective-permute-start.2
  21.5 2.0 collective-permute-start.3
  23.5 1.6 collective-permute-start.4
  25.2 1.5 collective-permute-start.5
  26.8 5.4 %collective-permute-start.6 = (f32[256,256]{1,0:T(8,128)S(1)}, f32[256,256]{1,0:T(8,128)S(1)}, u32[]{:S(2)}, u32[]{:S(2)}) collective-permute-start(f32[256,256]{1,0:T(8,128)S(1)} %copy-done.3), channel_id=1, source_target_pairs={{0,7},{1,0},{2,1},{3,2},{4,3},{5,4},{6,5},{7,6},{8,15},{9,8},{10,9... | collective-permute-start | bytes 786440 | tf_op jit(solution)/shard_map/ppermute | solution.py:35
  32.2 5.2 %collective-permute-done.2 = f32[256,256]{1,0:T(8,128)S(1)} collective-permute-done((f32[256,256]{1,0:T(8,128)}, f32[256,256]{1,0:T(8,128)S(1)}, u32[]{:S(2)}, u32[]{:S(2)}) %collective-permute-start.2) | collective-permute-done | bytes 262176 | tf_op jit(solution)/shard_map/ppermute | solution.py:35
  37.4 1.9 collective-permute-start.10
  39.4 3.7 %collective-permute-start.11 = (f32[256,256]{1,0:T(8,128)S(1)}, f32[256,256]{1,0:T(8,128)S(1)}, u32[]{:S(2)}, u32[]{:S(2)}) collective-permute-start(f32[256,256]{1,0:T(8,128)S(1)} %get-tuple-element.23), channel_id=1, source_target_pairs={{0,64},{8,72},{16,80},{24,88},{32,96},{40,104},{48,112},{56,120},{... | collective-permute-start | bytes 786440 | tf_op jit(solution)/shard_map/ppermute | solution.py:35
  43.1 1.5 collective-permute-start.12
  45.8 14.0 %collective-permute-done.11 = f32[256,256]{1,0:T(8,128)S(1)} collective-permute-done((f32[256,256]{1,0:T(8,128)S(1)}, f32[256,256]{1,0:T(8,128)S(1)}, u32[]{:S(2)}, u32[]{:S(2)}) %collective-permute-start.11) | collective-permute-done | bytes 262176 | tf_op jit(solution)/shard_map/ppermute | solution.py:35
  59.8 3.8 %collective-permute-done.12 = f32[256,256]{1,0:T(8,128)S(1)} collective-permute-done((f32[256,256]{1,0:T(8,128)S(1)}, f32[256,256]{1,0:T(8,128)S(1)}, u32[]{:S(2)}, u32[]{:S(2)}) %collective-permute-start.12) | collective-permute-done | bytes 262176 | tf_op jit(solution)/shard_map/ppermute | solution.py:35
  63.7 5.7 %all-gather.2.cloned.1.call-done = f32[3072,256]{1,0:T(8,128)} async-done(((f32[192,256]{1,0:T(8,128)}), f32[3072,256]{1,0:T(8,128)}) %all-gather.2.cloned.1.call-update) | async-done | bytes 3145744 | tf_op jit(solution)/shard_map/all_gather | solution.py:111
  69.3 2.1 constant_dynamic-update-slice_fusion
  73.0 34.8 %subtract_reduce_fusion.5 = (f32[2048]{0:T(1024)S(1)}, f32[2048,4096]{1,0:T(8,128)}) fusion(f32[2048,256]{1,0:T(8,128)S(1)} %copy-done.2, f32[4096,256]{1,0:T(8,128)S(1)} %bitcast_dynamic-update-slice_fusion, f32[4096]{0:T(1024)S(1)} %multiply_reduce_fusion, f32[2048]{0:T(1024)S(1)} %multiply_reduce_fusion.1), kind=kOutput, calls=%fused_computation.12 | convolution fusion | flops 25811744768 | bytes 39878656 | tf_op jit(solution)/shard_map/dot_general | solution.py:14
  107.8 14.5 %exponential_reduce_fusion.5 = f32[2048]{0:T(1024)S(1)} fusion(f32[2048,4096]{1,0:T(8,128)} %get-tuple-element.83, f32[2048]{0:T(1024)S(1)} %broadcast_divide_fusion.5, f32[]{:T(128)} %bitcast), kind=kLoop, calls=%fused_computation.5 | loop fusion | flops 33552384 | bytes 33570820 | tf_op jit(solution)/shard_map/reduce_sum | solution.py:78
  124.7 2.5 collective-permute-start.16
  129.8 13.7 %subtract_reduce_fusion.4 = f32[4096]{0:T(1024)S(1)} fusion(f32[2048,4096]{1,0:T(8,128)} %get-tuple-element.83, f32[2048]{0:T(1024)S(1)} %multiply_subtract_fusion.5), kind=kLoop, calls=%fused_computation.11 | loop fusion | flops 16773120 | bytes 33579008 | tf_op jit(solution)/shard_map/reduce_max | solution.py:83
  143.6 6.4 %copy-done = f32[2048,4096]{1,0:T(8,128)S(1)} copy-done((f32[2048,4096]{1,0:T(8,128)S(1)}, f32[2048,4096]{1,0:T(8,128)}, u32[]{:S(2)}) %copy-start) | copy-done | bytes 33554456
  149.9 7.6 %exponential_reduce_fusion.4 = f32[4096]{0:T(1024)S(1)} fusion(f32[2048,4096]{1,0:T(8,128)S(1)} %copy-done, f32[4096]{0:T(1024)S(1)} %broadcast_divide_fusion.2, f32[2048]{0:T(1024)S(1)} %multiply_subtract_fusion.5, f32[]{:T(128)} %bitcast), kind=kLoop, calls=%fused_computation.4 | loop fusion | flops 33550336 | bytes 33595396 | tf_op jit(solution)/shard_map/reduce_sum | solution.py:84
  159.4 1.8 collective-permute-start.19
  161.2 1.6 collective-permute-done.17
  164.2 2.0 collective-permute-start.20
  166.2 1.9 collective-permute-start.21
  169.4 2.2 collective-permute-done.21
  172.2 3.0 %subtract_reduce_fusion.3 = f32[2048]{0:T(1024)S(1)} fusion(f32[2048,4096]{1,0:T(8,128)S(1)} %copy-done, f32[4096]{0:T(1024)S(1)} %bitcast.125), kind=kLoop, calls=%fused_computation.10 | loop fusion | flops 16775168 | bytes 33579008 | tf_op jit(solution)/shard_map/reduce_max | solution.py:77
  175.2 8.0 %exponential_reduce_fusion.3 = f32[2048]{0:T(1024)S(1)} fusion(f32[2048,4096]{1,0:T(8,128)S(1)} %copy-done, f32[2048]{0:T(1024)S(1)} %broadcast_divide_fusion.4, f32[4096]{0:T(1024)S(1)} %bitcast.126, f32[]{:T(128)} %bitcast), kind=kLoop, calls=%fused_computation.3 | loop fusion | flops 33552384 | bytes 33587204 | tf_op jit(solution)/shard_map/reduce_sum | solution.py:78
  184.6 1.9 collective-permute-start.24
  186.5 2.8 %collective-permute-start.25 = (f32[2,2048]{1,0:T(2,128)S(1)}, f32[2,2048]{1,0:T(2,128)S(1)}, u32[]{:S(2)}, u32[]{:S(2)}) collective-permute-start(f32[2,2048]{1,0:T(2,128)S(1)} %pad_maximum_fusion.12), channel_id=1, source_target_pairs={{0,4},{1,5},{2,6},{3,7},{4,0},{5,1},{6,2},{7,3},{8,12},{9,13},{10,... | collective-permute-start | bytes 49160 | tf_op jit(solution)/shard_map/ppermute | solution.py:46
  189.6 2.1 collective-permute-done.25
  193.1 4.7 %subtract_reduce_fusion.2 = f32[4096]{0:T(1024)S(1)} fusion(f32[2048,4096]{1,0:T(8,128)S(1)} %copy-done, f32[2048]{0:T(1024)S(1)} %multiply_subtract_fusion.4), kind=kLoop, calls=%fused_computation.9 | loop fusion | flops 16773120 | bytes 33579008 | tf_op jit(solution)/shard_map/reduce_max | solution.py:83
  197.8 7.6 %exponential_reduce_fusion.2 = f32[4096]{0:T(1024)S(1)} fusion(f32[2048,4096]{1,0:T(8,128)S(1)} %copy-done, f32[4096]{0:T(1024)S(1)} %broadcast_divide_fusion.1, f32[2048]{0:T(1024)S(1)} %multiply_subtract_fusion.4, f32[]{:T(128)} %bitcast), kind=kLoop, calls=%fused_computation.2 | loop fusion | flops 33550336 | bytes 33595396 | tf_op jit(solution)/shard_map/reduce_sum | solution.py:84
  206.9 2.5 collective-permute-start.28
  210.7 1.5 collective-permute-done.28
  213.6 3.4 %collective-permute-start.31 = (f32[2,4096]{1,0:T(2,128)S(1)}, f32[2,4096]{1,0:T(2,128)S(1)}, u32[]{:S(2)}, u32[]{:S(2)}) collective-permute-start(f32[2,4096]{1,0:T(2,128)S(1)} %pad_maximum_fusion.6), channel_id=1, source_target_pairs={{0,64},{8,72},{16,80},{24,88},{32,96},{40,104},{48,112},{56,120},{... | collective-permute-start | bytes 98312 | tf_op jit(solution)/shard_map/ppermute | solution.py:46
  219.2 1.7 collective-permute-done.32
  221.0 3.0 %subtract_reduce_fusion.1 = f32[2048]{0:T(1024)S(1)} fusion(f32[2048,4096]{1,0:T(8,128)S(1)} %copy-done, f32[4096]{0:T(1024)S(1)} %bitcast.127), kind=kLoop, calls=%fused_computation.8 | loop fusion | flops 16775168 | bytes 33579008 | tf_op jit(solution)/shard_map/reduce_max | solution.py:77
  224.0 8.0 %exponential_reduce_fusion.1 = f32[2048]{0:T(1024)S(1)} fusion(f32[2048,4096]{1,0:T(8,128)S(1)} %copy-done, f32[2048]{0:T(1024)S(1)} %broadcast_divide_fusion.3, f32[4096]{0:T(1024)S(1)} %bitcast.128, f32[]{:T(128)} %bitcast), kind=kLoop, calls=%fused_computation.1 | loop fusion | flops 33552384 | bytes 33587204 | tf_op jit(solution)/shard_map/reduce_sum | solution.py:78
  233.5 3.1 %collective-permute-start.35 = (f32[2,2048]{1,0:T(2,128)S(1)}, f32[2,2048]{1,0:T(2,128)S(1)}, u32[]{:S(2)}, u32[]{:S(2)}) collective-permute-start(f32[2,2048]{1,0:T(2,128)S(1)} %pad_maximum_fusion.14), channel_id=1, source_target_pairs={{0,4},{1,5},{2,6},{3,7},{4,0},{5,1},{6,2},{7,3},{8,12},{9,13},{10,... | collective-permute-start | bytes 49160 | tf_op jit(solution)/shard_map/ppermute | solution.py:46
  238.8 1.5 collective-permute-done.36
  240.4 4.7 %subtract_reduce_fusion = f32[4096]{0:T(1024)S(1)} fusion(f32[2048,4096]{1,0:T(8,128)S(1)} %copy-done, f32[2048]{0:T(1024)S(1)} %multiply_subtract_fusion.3), kind=kLoop, calls=%fused_computation.7 | loop fusion | flops 16773120 | bytes 33579008 | tf_op jit(solution)/shard_map/reduce_max | solution.py:83
  245.2 7.6 %exponential_reduce_fusion = f32[4096]{0:T(1024)S(1)} fusion(f32[2048,4096]{1,0:T(8,128)S(1)} %copy-done, f32[4096]{0:T(1024)S(1)} %broadcast_divide_fusion, f32[2048]{0:T(1024)S(1)} %multiply_subtract_fusion.3, f32[]{:T(128)} %bitcast), kind=kLoop, calls=%fused_computation | loop fusion | flops 33550336 | bytes 33595396 | tf_op jit(solution)/shard_map/reduce_sum | solution.py:84
  253.0 3.2 %collective-permute-start.38 = (f32[2,4096]{1,0:T(2,128)S(1)}, f32[2,4096]{1,0:T(2,128)S(1)}, u32[]{:S(2)}, u32[]{:S(2)}) collective-permute-start(f32[2,4096]{1,0:T(2,128)S(1)} %pad_maximum_fusion.7), channel_id=1, source_target_pairs={{0,16},{8,24},{16,0},{24,8},{32,48},{40,56},{48,32},{56,40},{64,80... | collective-permute-start | bytes 98312 | tf_op jit(solution)/shard_map/ppermute | solution.py:46
  258.5 1.6 collective-permute-done.39
  260.8 2.7 collective-permute-start.41
  (158 shorter events, 37.7 us)
Async XLA Ops:
  7.2 19.6 %copy-start.3 = (f32[256,256]{1,0:T(8,128)S(1)}, f32[256,256]{1,0:T(8,128)}, u32[]{:S(2)}) copy-start(f32[256,256]{1,0:T(8,128)} %param.3) | copy-start | bytes 786436
  7.2 62.1 %all-gather.2.cloned.1.call-start = ((), (), s32[]{:S(2)}) async-start(), calls=%async_computation | async-start | bytes 3342336 | tf_op jit(solution)/shard_map/all_gather | solution.py:111
  9.7 9.5 %collective-permute-start.7 = (f32[64,256]{1,0:T(8,128)S(1)}, f32[64,256]{1,0:T(8,128)S(1)}, u32[]{:S(2)}, u32[]{:S(2)}) collective-permute-start(f32[64,256]{1,0:T(8,128)S(1)} %get-tuple-element.29), channel_id=1, source_target_pairs={{0,8},{8,16},{16,24},{24,0},{32,40},{40,48},{48,56},{56,32},{64,72... | collective-permute-start | bytes 196616 | tf_op jit(solution)/shard_map/ppermute | solution.py:35
  11.5 10.0 %collective-permute-start.8 = (f32[64,256]{1,0:T(8,128)S(1)}, f32[64,256]{1,0:T(8,128)S(1)}, u32[]{:S(2)}, u32[]{:S(2)}) collective-permute-start(f32[64,256]{1,0:T(8,128)S(1)} %get-tuple-element.29), channel_id=1, source_target_pairs={{0,16},{8,24},{16,0},{24,8},{32,48},{40,56},{48,32},{56,40},{64,80... | collective-permute-start | bytes 196616 | tf_op jit(solution)/shard_map/ppermute | solution.py:35
  14.4 9.1 %collective-permute-start.9 = (f32[64,256]{1,0:T(8,128)S(1)}, f32[64,256]{1,0:T(8,128)S(1)}, u32[]{:S(2)}, u32[]{:S(2)}) collective-permute-start(f32[64,256]{1,0:T(8,128)S(1)} %get-tuple-element.29), channel_id=1, source_target_pairs={{0,24},{8,0},{16,8},{24,16},{32,56},{40,32},{48,40},{56,48},{64,88... | collective-permute-start | bytes 196616 | tf_op jit(solution)/shard_map/ppermute | solution.py:35
  15.8 9.4 %collective-permute-start = (f32[256,256]{1,0:T(8,128)}, f32[256,256]{1,0:T(8,128)S(1)}, u32[]{:S(2)}, u32[]{:S(2)}) collective-permute-start(f32[256,256]{1,0:T(8,128)} %param.3), channel_id=1, source_target_pairs={{0,1},{1,2},{2,3},{3,4},{4,5},{5,6},{6,7},{7,0},{8,9},{9,10},{10,1... | collective-permute-start | bytes 786440 | tf_op jit(solution)/shard_map/ppermute | solution.py:35
  15.8 11.0 %collective-permute-start.1 = (f32[256,256]{1,0:T(8,128)}, f32[256,256]{1,0:T(8,128)S(1)}, u32[]{:S(2)}, u32[]{:S(2)}) collective-permute-start(f32[256,256]{1,0:T(8,128)} %param.3), channel_id=1, source_target_pairs={{0,2},{1,3},{2,4},{3,5},{4,6},{5,7},{6,0},{7,1},{8,10},{9,11},{10,... | collective-permute-start | bytes 786440 | tf_op jit(solution)/shard_map/ppermute | solution.py:35
  19.3 18.1 %collective-permute-start.2 = (f32[256,256]{1,0:T(8,128)}, f32[256,256]{1,0:T(8,128)S(1)}, u32[]{:S(2)}, u32[]{:S(2)}) collective-permute-start(f32[256,256]{1,0:T(8,128)} %param.3), channel_id=1, source_target_pairs={{0,3},{1,4},{2,5},{3,6},{4,7},{5,0},{6,1},{7,2},{8,11},{9,12},{10,... | collective-permute-start | bytes 786440 | tf_op jit(solution)/shard_map/ppermute | solution.py:35
  21.5 17.9 %collective-permute-start.3 = (f32[256,256]{1,0:T(8,128)}, f32[256,256]{1,0:T(8,128)S(1)}, u32[]{:S(2)}, u32[]{:S(2)}) collective-permute-start(f32[256,256]{1,0:T(8,128)} %param.3), channel_id=1, source_target_pairs={{0,4},{1,5},{2,6},{3,7},{4,0},{5,1},{6,2},{7,3},{8,12},{9,13},{10,... | collective-permute-start | bytes 786440 | tf_op jit(solution)/shard_map/ppermute | solution.py:35
  23.5 19.6 %collective-permute-start.4 = (f32[256,256]{1,0:T(8,128)}, f32[256,256]{1,0:T(8,128)S(1)}, u32[]{:S(2)}, u32[]{:S(2)}) collective-permute-start(f32[256,256]{1,0:T(8,128)} %param.3), channel_id=1, source_target_pairs={{0,5},{1,6},{2,7},{3,0},{4,1},{5,2},{6,3},{7,4},{8,13},{9,14},{10,... | collective-permute-start | bytes 786440 | tf_op jit(solution)/shard_map/ppermute | solution.py:35
  25.2 19.4 %collective-permute-start.5 = (f32[256,256]{1,0:T(8,128)}, f32[256,256]{1,0:T(8,128)S(1)}, u32[]{:S(2)}, u32[]{:S(2)}) collective-permute-start(f32[256,256]{1,0:T(8,128)} %param.3), channel_id=1, source_target_pairs={{0,6},{1,7},{2,0},{3,1},{4,2},{5,3},{6,4},{7,5},{8,14},{9,15},{10,... | collective-permute-start | bytes 786440 | tf_op jit(solution)/shard_map/ppermute | solution.py:35
  26.8 17.8 %collective-permute-start.6 = (f32[256,256]{1,0:T(8,128)S(1)}, f32[256,256]{1,0:T(8,128)S(1)}, u32[]{:S(2)}, u32[]{:S(2)}) collective-permute-start(f32[256,256]{1,0:T(8,128)S(1)} %copy-done.3), channel_id=1, source_target_pairs={{0,7},{1,0},{2,1},{3,2},{4,3},{5,4},{6,5},{7,6},{8,15},{9,8},{10,9... | collective-permute-start | bytes 786440 | tf_op jit(solution)/shard_map/ppermute | solution.py:35
  37.4 8.4 %collective-permute-start.10 = (f32[256,256]{1,0:T(8,128)S(1)}, f32[256,256]{1,0:T(8,128)S(1)}, u32[]{:S(2)}, u32[]{:S(2)}) collective-permute-start(f32[256,256]{1,0:T(8,128)S(1)} %get-tuple-element.23), channel_id=1, source_target_pairs={{0,32},{8,40},{16,48},{24,56},{32,64},{40,72},{48,80},{56,88},{64,... | collective-permute-start | bytes 786440 | tf_op jit(solution)/shard_map/ppermute | solution.py:35
  39.4 20.4 %collective-permute-start.11 = (f32[256,256]{1,0:T(8,128)S(1)}, f32[256,256]{1,0:T(8,128)S(1)}, u32[]{:S(2)}, u32[]{:S(2)}) collective-permute-start(f32[256,256]{1,0:T(8,128)S(1)} %get-tuple-element.23), channel_id=1, source_target_pairs={{0,64},{8,72},{16,80},{24,88},{32,96},{40,104},{48,112},{56,120},{... | collective-permute-start | bytes 786440 | tf_op jit(solution)/shard_map/ppermute | solution.py:35
  43.1 20.5 %collective-permute-start.12 = (f32[256,256]{1,0:T(8,128)S(1)}, f32[256,256]{1,0:T(8,128)S(1)}, u32[]{:S(2)}, u32[]{:S(2)}) collective-permute-start(f32[256,256]{1,0:T(8,128)S(1)} %get-tuple-element.23), channel_id=1, source_target_pairs={{0,96},{8,104},{16,112},{24,120},{32,0},{40,8},{48,16},{56,24},{64... | collective-permute-start | bytes 786440 | tf_op jit(solution)/shard_map/ppermute | solution.py:35
  44.9 18.6 %copy-start.1 = (f32[2048,256]{1,0:T(8,128)}, f32[2048,256]{1,0:T(8,128)S(1)}, u32[]{:S(2)}) copy-start(f32[2048,256]{1,0:T(8,128)S(1)} %bitcast_dynamic-update-slice_fusion.4) | copy-start | bytes 6291460
  122.3 1.3 collective-permute-start.13
  123.7 5.0 %collective-permute-start.14 = (f32[2,2048]{1,0:T(2,128)S(1)}, f32[2,2048]{1,0:T(2,128)S(1)}, u32[]{:S(2)}, u32[]{:S(2)}) collective-permute-start(f32[2,2048]{1,0:T(2,128)S(1)} %pad_maximum_fusion.10), channel_id=1, source_target_pairs={{0,2},{1,3},{2,4},{3,5},{4,6},{5,7},{6,0},{7,1},{8,10},{9,11},{10,... | collective-permute-start | bytes 49160 | tf_op jit(solution)/shard_map/ppermute | solution.py:46
  123.8 5.3 %collective-permute-start.15 = (f32[2,2048]{1,0:T(2,128)S(1)}, f32[2,2048]{1,0:T(2,128)S(1)}, u32[]{:S(2)}, u32[]{:S(2)}) collective-permute-start(f32[2,2048]{1,0:T(2,128)S(1)} %pad_maximum_fusion.10), channel_id=1, source_target_pairs={{0,4},{1,5},{2,6},{3,7},{4,0},{5,1},{6,2},{7,3},{8,12},{9,13},{10,... | collective-permute-start | bytes 49160 | tf_op jit(solution)/shard_map/ppermute | solution.py:46
  124.7 5.0 %collective-permute-start.16 = (f32[2,2048]{1,0:T(2,128)S(1)}, f32[2,2048]{1,0:T(2,128)S(1)}, u32[]{:S(2)}, u32[]{:S(2)}) collective-permute-start(f32[2,2048]{1,0:T(2,128)S(1)} %pad_maximum_fusion.10), channel_id=1, source_target_pairs={{0,6},{1,7},{2,0},{3,1},{4,2},{5,3},{6,4},{7,5},{8,14},{9,15},{10,... | collective-permute-start | bytes 49160 | tf_op jit(solution)/shard_map/ppermute | solution.py:46
  129.8 20.2 %copy-start = (f32[2048,4096]{1,0:T(8,128)S(1)}, f32[2048,4096]{1,0:T(8,128)}, u32[]{:S(2)}) copy-start(f32[2048,4096]{1,0:T(8,128)} %get-tuple-element.83) | copy-start | bytes 100663296
  157.6 5.2 %collective-permute-start.17 = (f32[2,4096]{1,0:T(2,128)S(1)}, f32[2,4096]{1,0:T(2,128)S(1)}, u32[]{:S(2)}, u32[]{:S(2)}) collective-permute-start(f32[2,4096]{1,0:T(2,128)S(1)} %pad_maximum_fusion.3), channel_id=1, source_target_pairs={{0,8},{8,16},{16,24},{24,0},{32,40},{40,48},{48,56},{56,32},{64,72... | collective-permute-start | bytes 98312 | tf_op jit(solution)/shard_map/ppermute | solution.py:46
  158.4 5.4 %collective-permute-start.18 = (f32[2,4096]{1,0:T(2,128)S(1)}, f32[2,4096]{1,0:T(2,128)S(1)}, u32[]{:S(2)}, u32[]{:S(2)}) collective-permute-start(f32[2,4096]{1,0:T(2,128)S(1)} %pad_maximum_fusion.3), channel_id=1, source_target_pairs={{0,16},{8,24},{16,0},{24,8},{32,48},{40,56},{48,32},{56,40},{64,80... | collective-permute-start | bytes 98312 | tf_op jit(solution)/shard_map/ppermute | solution.py:46
  159.4 4.7 %collective-permute-start.19 = (f32[2,4096]{1,0:T(2,128)S(1)}, f32[2,4096]{1,0:T(2,128)S(1)}, u32[]{:S(2)}, u32[]{:S(2)}) collective-permute-start(f32[2,4096]{1,0:T(2,128)S(1)} %pad_maximum_fusion.3), channel_id=1, source_target_pairs={{0,24},{8,0},{16,8},{24,16},{32,56},{40,32},{48,40},{56,48},{64,88... | collective-permute-start | bytes 98312 | tf_op jit(solution)/shard_map/ppermute | solution.py:46
  164.2 5.2 %collective-permute-start.20 = (f32[2,4096]{1,0:T(2,128)S(1)}, f32[2,4096]{1,0:T(2,128)S(1)}, u32[]{:S(2)}, u32[]{:S(2)}) collective-permute-start(f32[2,4096]{1,0:T(2,128)S(1)} %pad_maximum_fusion.4), channel_id=1, source_target_pairs={{0,32},{8,40},{16,48},{24,56},{32,64},{40,72},{48,80},{56,88},{64,... | collective-permute-start | bytes 98312 | tf_op jit(solution)/shard_map/ppermute | solution.py:46
  166.2 5.4 %collective-permute-start.21 = (f32[2,4096]{1,0:T(2,128)S(1)}, f32[2,4096]{1,0:T(2,128)S(1)}, u32[]{:S(2)}, u32[]{:S(2)}) collective-permute-start(f32[2,4096]{1,0:T(2,128)S(1)} %pad_maximum_fusion.4), channel_id=1, source_target_pairs={{0,64},{8,72},{16,80},{24,88},{32,96},{40,104},{48,112},{56,120},{... | collective-permute-start | bytes 98312 | tf_op jit(solution)/shard_map/ppermute | solution.py:46
  168.1 3.9 %collective-permute-start.22 = (f32[2,4096]{1,0:T(2,128)S(1)}, f32[2,4096]{1,0:T(2,128)S(1)}, u32[]{:S(2)}, u32[]{:S(2)}) collective-permute-start(f32[2,4096]{1,0:T(2,128)S(1)} %pad_maximum_fusion.4), channel_id=1, source_target_pairs={{0,96},{8,104},{16,112},{24,120},{32,0},{40,8},{48,16},{56,24},{64... | collective-permute-start | bytes 98312 | tf_op jit(solution)/shard_map/ppermute | solution.py:46
  183.2 1.3 collective-permute-start.23
  184.6 5.0 %collective-permute-start.24 = (f32[2,2048]{1,0:T(2,128)S(1)}, f32[2,2048]{1,0:T(2,128)S(1)}, u32[]{:S(2)}, u32[]{:S(2)}) collective-permute-start(f32[2,2048]{1,0:T(2,128)S(1)} %pad_maximum_fusion.12), channel_id=1, source_target_pairs={{0,2},{1,3},{2,4},{3,5},{4,6},{5,7},{6,0},{7,1},{8,10},{9,11},{10,... | collective-permute-start | bytes 49160 | tf_op jit(solution)/shard_map/ppermute | solution.py:46
  186.5 5.2 %collective-permute-start.25 = (f32[2,2048]{1,0:T(2,128)S(1)}, f32[2,2048]{1,0:T(2,128)S(1)}, u32[]{:S(2)}, u32[]{:S(2)}) collective-permute-start(f32[2,2048]{1,0:T(2,128)S(1)} %pad_maximum_fusion.12), channel_id=1, source_target_pairs={{0,4},{1,5},{2,6},{3,7},{4,0},{5,1},{6,2},{7,3},{8,12},{9,13},{10,... | collective-permute-start | bytes 49160 | tf_op jit(solution)/shard_map/ppermute | solution.py:46
  189.3 3.7 %collective-permute-start.26 = (f32[2,2048]{1,0:T(2,128)S(1)}, f32[2,2048]{1,0:T(2,128)S(1)}, u32[]{:S(2)}, u32[]{:S(2)}) collective-permute-start(f32[2,2048]{1,0:T(2,128)S(1)} %pad_maximum_fusion.12), channel_id=1, source_target_pairs={{0,6},{1,7},{2,0},{3,1},{4,2},{5,3},{6,4},{7,5},{8,14},{9,15},{10,... | collective-permute-start | bytes 49160 | tf_op jit(solution)/shard_map/ppermute | solution.py:46
  205.5 5.2 %collective-permute-start.27 = (f32[2,4096]{1,0:T(2,128)S(1)}, f32[2,4096]{1,0:T(2,128)S(1)}, u32[]{:S(2)}, u32[]{:S(2)}) collective-permute-start(f32[2,4096]{1,0:T(2,128)S(1)} %pad_maximum_fusion.5), channel_id=1, source_target_pairs={{0,8},{8,16},{16,24},{24,0},{32,40},{40,48},{48,56},{56,32},{64,72... | collective-permute-start | bytes 98312 | tf_op jit(solution)/shard_map/ppermute | solution.py:46
  206.9 5.4 %collective-permute-start.28 = (f32[2,4096]{1,0:T(2,128)S(1)}, f32[2,4096]{1,0:T(2,128)S(1)}, u32[]{:S(2)}, u32[]{:S(2)}) collective-permute-start(f32[2,4096]{1,0:T(2,128)S(1)} %pad_maximum_fusion.5), channel_id=1, source_target_pairs={{0,16},{8,24},{16,0},{24,8},{32,48},{40,56},{48,32},{56,40},{64,80... | collective-permute-start | bytes 98312 | tf_op jit(solution)/shard_map/ppermute | solution.py:46
  209.3 3.9 %collective-permute-start.29 = (f32[2,4096]{1,0:T(2,128)S(1)}, f32[2,4096]{1,0:T(2,128)S(1)}, u32[]{:S(2)}, u32[]{:S(2)}) collective-permute-start(f32[2,4096]{1,0:T(2,128)S(1)} %pad_maximum_fusion.5), channel_id=1, source_target_pairs={{0,24},{8,0},{16,8},{24,16},{32,56},{40,32},{48,40},{56,48},{64,88... | collective-permute-start | bytes 98312 | tf_op jit(solution)/shard_map/ppermute | solution.py:46
  213.4 5.2 %collective-permute-start.30 = (f32[2,4096]{1,0:T(2,128)S(1)}, f32[2,4096]{1,0:T(2,128)S(1)}, u32[]{:S(2)}, u32[]{:S(2)}) collective-permute-start(f32[2,4096]{1,0:T(2,128)S(1)} %pad_maximum_fusion.6), channel_id=1, source_target_pairs={{0,32},{8,40},{16,48},{24,56},{32,64},{40,72},{48,80},{56,88},{64,... | collective-permute-start | bytes 98312 | tf_op jit(solution)/shard_map/ppermute | solution.py:46
  213.6 5.6 %collective-permute-start.31 = (f32[2,4096]{1,0:T(2,128)S(1)}, f32[2,4096]{1,0:T(2,128)S(1)}, u32[]{:S(2)}, u32[]{:S(2)}) collective-permute-start(f32[2,4096]{1,0:T(2,128)S(1)} %pad_maximum_fusion.6), channel_id=1, source_target_pairs={{0,64},{8,72},{16,80},{24,88},{32,96},{40,104},{48,112},{56,120},{... | collective-permute-start | bytes 98312 | tf_op jit(solution)/shard_map/ppermute | solution.py:46
  216.9 3.9 %collective-permute-start.32 = (f32[2,4096]{1,0:T(2,128)S(1)}, f32[2,4096]{1,0:T(2,128)S(1)}, u32[]{:S(2)}, u32[]{:S(2)}) collective-permute-start(f32[2,4096]{1,0:T(2,128)S(1)} %pad_maximum_fusion.6), channel_id=1, source_target_pairs={{0,96},{8,104},{16,112},{24,120},{32,0},{40,8},{48,16},{56,24},{64... | collective-permute-start | bytes 98312 | tf_op jit(solution)/shard_map/ppermute | solution.py:46
  232.1 1.3 collective-permute-start.33
  233.4 5.0 %collective-permute-start.34 = (f32[2,2048]{1,0:T(2,128)S(1)}, f32[2,2048]{1,0:T(2,128)S(1)}, u32[]{:S(2)}, u32[]{:S(2)}) collective-permute-start(f32[2,2048]{1,0:T(2,128)S(1)} %pad_maximum_fusion.14), channel_id=1, source_target_pairs={{0,2},{1,3},{2,4},{3,5},{4,6},{5,7},{6,0},{7,1},{8,10},{9,11},{10,... | collective-permute-start | bytes 49160 | tf_op jit(solution)/shard_map/ppermute | solution.py:46
  233.5 5.3 %collective-permute-start.35 = (f32[2,2048]{1,0:T(2,128)S(1)}, f32[2,2048]{1,0:T(2,128)S(1)}, u32[]{:S(2)}, u32[]{:S(2)}) collective-permute-start(f32[2,2048]{1,0:T(2,128)S(1)} %pad_maximum_fusion.14), channel_id=1, source_target_pairs={{0,4},{1,5},{2,6},{3,7},{4,0},{5,1},{6,2},{7,3},{8,12},{9,13},{10,... | collective-permute-start | bytes 49160 | tf_op jit(solution)/shard_map/ppermute | solution.py:46
  236.6 3.7 %collective-permute-start.36 = (f32[2,2048]{1,0:T(2,128)S(1)}, f32[2,2048]{1,0:T(2,128)S(1)}, u32[]{:S(2)}, u32[]{:S(2)}) collective-permute-start(f32[2,2048]{1,0:T(2,128)S(1)} %pad_maximum_fusion.14), channel_id=1, source_target_pairs={{0,6},{1,7},{2,0},{3,1},{4,2},{5,3},{6,4},{7,5},{8,14},{9,15},{10,... | collective-permute-start | bytes 49160 | tf_op jit(solution)/shard_map/ppermute | solution.py:46
  240.4 4.8 %copy-start.4 = (f32[2048]{0:T(1024)}, f32[2048]{0:T(1024)S(1)}, u32[]{:S(2)}) copy-start(f32[2048]{0:T(1024)S(1)} %multiply_subtract_fusion.3) | copy-start | bytes 24580
  252.9 5.2 %collective-permute-start.37 = (f32[2,4096]{1,0:T(2,128)S(1)}, f32[2,4096]{1,0:T(2,128)S(1)}, u32[]{:S(2)}, u32[]{:S(2)}) collective-permute-start(f32[2,4096]{1,0:T(2,128)S(1)} %pad_maximum_fusion.7), channel_id=1, source_target_pairs={{0,8},{8,16},{16,24},{24,0},{32,40},{40,48},{48,56},{56,32},{64,72... | collective-permute-start | bytes 98312 | tf_op jit(solution)/shard_map/ppermute | solution.py:46
  253.0 5.5 %collective-permute-start.38 = (f32[2,4096]{1,0:T(2,128)S(1)}, f32[2,4096]{1,0:T(2,128)S(1)}, u32[]{:S(2)}, u32[]{:S(2)}) collective-permute-start(f32[2,4096]{1,0:T(2,128)S(1)} %pad_maximum_fusion.7), channel_id=1, source_target_pairs={{0,16},{8,24},{16,0},{24,8},{32,48},{40,56},{48,32},{56,40},{64,80... | collective-permute-start | bytes 98312 | tf_op jit(solution)/shard_map/ppermute | solution.py:46
  256.2 3.9 %collective-permute-start.39 = (f32[2,4096]{1,0:T(2,128)S(1)}, f32[2,4096]{1,0:T(2,128)S(1)}, u32[]{:S(2)}, u32[]{:S(2)}) collective-permute-start(f32[2,4096]{1,0:T(2,128)S(1)} %pad_maximum_fusion.7), channel_id=1, source_target_pairs={{0,24},{8,0},{16,8},{24,16},{32,56},{40,32},{48,40},{56,48},{64,88... | collective-permute-start | bytes 98312 | tf_op jit(solution)/shard_map/ppermute | solution.py:46
  260.3 5.2 %collective-permute-start.40 = (f32[2,4096]{1,0:T(2,128)S(1)}, f32[2,4096]{1,0:T(2,128)S(1)}, u32[]{:S(2)}, u32[]{:S(2)}) collective-permute-start(f32[2,4096]{1,0:T(2,128)S(1)} %pad_maximum_fusion.8), channel_id=1, source_target_pairs={{0,32},{8,40},{16,48},{24,56},{32,64},{40,72},{48,80},{56,88},{64,... | collective-permute-start | bytes 98312 | tf_op jit(solution)/shard_map/ppermute | solution.py:46
  260.8 5.4 %collective-permute-start.41 = (f32[2,4096]{1,0:T(2,128)S(1)}, f32[2,4096]{1,0:T(2,128)S(1)}, u32[]{:S(2)}, u32[]{:S(2)}) collective-permute-start(f32[2,4096]{1,0:T(2,128)S(1)} %pad_maximum_fusion.8), channel_id=1, source_target_pairs={{0,64},{8,72},{16,80},{24,88},{32,96},{40,104},{48,112},{56,120},{... | collective-permute-start | bytes 98312 | tf_op jit(solution)/shard_map/ppermute | solution.py:46
  263.6 3.9 %collective-permute-start.42 = (f32[2,4096]{1,0:T(2,128)S(1)}, f32[2,4096]{1,0:T(2,128)S(1)}, u32[]{:S(2)}, u32[]{:S(2)}) collective-permute-start(f32[2,4096]{1,0:T(2,128)S(1)} %pad_maximum_fusion.8), channel_id=1, source_target_pairs={{0,96},{8,104},{16,112},{24,120},{32,0},{40,8},{48,16},{56,24},{64... | collective-permute-start | bytes 98312 | tf_op jit(solution)/shard_map/ppermute | solution.py:46
  (1 other events, 1.6 us)
Sparse Core Ops, SparseCore 0:
  10.1 59.1 all-gather.1

commit v9 on v8

--- a/solution.py
+++ b/solution.py
@@ -106,7 +106,7 @@
     all_passages = passages.shape[0] * row_count * col_count
     query_block = gather_col(queries)
     rows = passages.shape[0]
-    split = rows - rows // 4
+    split = rows - rows // 8
     passage_block = jnp.concatenate(
         [lax.all_gather(passages[:split], "row", axis=0, tiled=True), gather_row(passages[split:])], axis=0
     )

time: 276 us -> 271 us (0.982)
  starting transfers between devices: 65.3 us -> 61 us
    ppermute x13, starting transfers between devices: 27.3 us -> 20.2 us  [exchange(): lax.ppermute(x, axis, digit_partners(axis, size, stride, width, k))]
    all_gather x1, waiting for transfers between devices: 5.66 us -> 9.3 us  [per_device(): lax.all_gather(passages[:split], 'row', axis=0, tiled=True)]
    ppermute x30, starting transfers between devices: 37.9 us -> 40.7 us  [combine_over(): lax.ppermute(packed, axis, digit_partners(axis, size, stride, width, k))]
    unnamed x29 -> x25, local copies, waits for them, and re-layouts: 11.3 us -> 10.7 us
  transfers between devices with their start and end apart: 44 -> 44, of which waited for: 35 -> 37; matrix products, arithmetic and copies ran while one was open for 1% -> 1% of each run, Pallas kernels for 0% -> 0%
where the time goes in v9:
time: 271 us
  other arithmetic  85.3 us (31%)
  starting transfers between devices  61 us (23%)
  waiting for transfers between devices  59.3 us (22%)
  matrix products  34.8 us (13%)
  between operations  15.4 us (6%)
  local copies, waits for them, and re-layouts  14.9 us (5%)
    ppermute x30, starting transfers between devices, combine_over(): lax.ppermute(packed, axis, digit_partners(axis, size, stride, width, k))  40.7 us
    dot_general x1, matrix products, inner_costs(): lax.dot_general(left, right, (((1,), (1,)), ((), ())), precision=lax.Prec...  34.8 us
    reduce_sum x3, other arithmetic, logsum_col(): totals = jnp.sum(jnp.exp(gaps / scale - peak[:, None]), axis=1)  30.6 us
    ppermute x30, waiting for transfers between devices, combine_over(): lax.ppermute(packed, axis, digit_partners(axis, size, stride, width, k))  28.2 us
    reduce_max x3, other arithmetic, logsum_row(): peak = jnp.max(gaps, axis=0) / scale  23.1 us
    reduce_sum x3, other arithmetic, logsum_row(): totals = jnp.sum(jnp.exp(gaps / scale - peak[None, :]), axis=0)  22.9 us
    ppermute x13, waiting for transfers between devices, exchange(): lax.ppermute(x, axis, digit_partners(axis, size, stride, width, k))  21.8 us
    ppermute x13, starting transfers between devices, exchange(): lax.ppermute(x, axis, digit_partners(axis, size, stride, width, k))  20.2 us
  transfers between devices with their start and end apart: 44, of which 37 were waited for; matrix products, arithmetic and copies ran while one was open for 1% of the time, Pallas kernels for 0%

profile of v9, /device:TPU:0, one launch (start us, length us, event | category | flops | bytes accessed | tf_op | source)
XLA Modules:
  0.0 270.6 jit_solution(13294196213294468508)
XLA Ops:
  7.2 1.7 slice.223
  9.7 1.7 collective-permute-start.7
  11.4 2.9 %collective-permute-start.8 = (f32[32,256]{1,0:T(8,128)S(1)}, f32[32,256]{1,0:T(8,128)S(1)}, u32[]{:S(2)}, u32[]{:S(2)}) collective-permute-start(f32[32,256]{1,0:T(8,128)S(1)} %get-tuple-element.23), channel_id=1, source_target_pairs={{0,16},{8,24},{16,0},{24,8},{32,48},{40,56},{48,32},{56,40},{64,80... | collective-permute-start | bytes 98312 | tf_op jit(solution)/shard_map/ppermute | solution.py:35
  15.6 1.5 collective-permute-start.1
  18.3 2.0 collective-permute-start.10
  20.2 3.6 %collective-permute-start.11 = (f32[128,256]{1,0:T(8,128)S(1)}, f32[128,256]{1,0:T(8,128)S(1)}, u32[]{:S(2)}, u32[]{:S(2)}) collective-permute-start(f32[128,256]{1,0:T(8,128)S(1)} %get-tuple-element.25), channel_id=1, source_target_pairs={{0,64},{8,72},{16,80},{24,88},{32,96},{40,104},{48,112},{56,120},{... | collective-permute-start | bytes 393224 | tf_op jit(solution)/shard_map/ppermute | solution.py:35
  26.4 1.5 collective-permute-start.2
  27.9 5.0 %collective-permute-done.11 = f32[128,256]{1,0:T(8,128)S(1)} collective-permute-done((f32[128,256]{1,0:T(8,128)S(1)}, f32[128,256]{1,0:T(8,128)S(1)}, u32[]{:S(2)}, u32[]{:S(2)}) %collective-permute-start.11) | collective-permute-done | bytes 131104 | tf_op jit(solution)/shard_map/ppermute | solution.py:35
  34.2 1.8 collective-permute-start.4
  37.7 5.2 %collective-permute-done.3 = f32[256,256]{1,0:T(8,128)S(1)} collective-permute-done((f32[256,256]{1,0:T(8,128)}, f32[256,256]{1,0:T(8,128)S(1)}, u32[]{:S(2)}, u32[]{:S(2)}) %collective-permute-start.3) | collective-permute-done | bytes 262176 | tf_op jit(solution)/shard_map/ppermute | solution.py:35
  44.0 7.8 %collective-permute-done.5 = f32[256,256]{1,0:T(8,128)S(1)} collective-permute-done((f32[256,256]{1,0:T(8,128)}, f32[256,256]{1,0:T(8,128)S(1)}, u32[]{:S(2)}, u32[]{:S(2)}) %collective-permute-start.5) | collective-permute-done | bytes 262176 | tf_op jit(solution)/shard_map/ppermute | solution.py:35
  51.7 1.9 collective-permute-done.6
  54.3 9.3 %all-gather.2.cloned.1.call-done = f32[3584,256]{1,0:T(8,128)} async-done(((f32[224,256]{1,0:T(8,128)}), f32[3584,256]{1,0:T(8,128)}) %all-gather.2.cloned.1.call-update) | async-done | bytes 3670032 | tf_op jit(solution)/shard_map/all_gather | solution.py:111
  63.6 2.3 constant_dynamic-update-slice_fusion
  66.6 34.8 %subtract_reduce_fusion.5 = (f32[2048]{0:T(1024)S(1)}, f32[2048,4096]{1,0:T(8,128)}) fusion(f32[2048,256]{1,0:T(8,128)S(1)} %bitcast_dynamic-update-slice_fusion, f32[4096,256]{1,0:T(8,128)S(1)} %bitcast_dynamic-update-slice_fusion.16, f32[4096]{0:T(1024)S(1)} %multiply_reduce_fusion, f32[2048]{0:T(1024)S(1)} %multiply_reduce_fusion.1), kind=kOutput, calls=%fused_computation.12 | convolution fusion | flops 25811744768 | bytes 39878656 | tf_op jit(solution)/shard_map/dot_general | solution.py:14
  101.4 14.5 %exponential_reduce_fusion.5 = f32[2048]{0:T(1024)S(1)} fusion(f32[2048,4096]{1,0:T(8,128)} %get-tuple-element.83, f32[2048]{0:T(1024)S(1)} %broadcast_divide_fusion.5, f32[]{:T(128)} %bitcast), kind=kLoop, calls=%fused_computation.5 | loop fusion | flops 33552384 | bytes 33570820 | tf_op jit(solution)/shard_map/reduce_sum | solution.py:78
  117.3 1.5 collective-permute-start.14
  118.8 2.7 collective-permute-start.15
  121.5 1.5 collective-permute-start.16
  125.3 13.7 %subtract_reduce_fusion.4 = f32[4096]{0:T(1024)S(1)} fusion(f32[2048,4096]{1,0:T(8,128)} %get-tuple-element.83, f32[2048]{0:T(1024)S(1)} %multiply_subtract_fusion.5), kind=kLoop, calls=%fused_computation.11 | loop fusion | flops 16773120 | bytes 33579008 | tf_op jit(solution)/shard_map/reduce_max | solution.py:83
  139.0 6.4 %copy-done = f32[2048,4096]{1,0:T(8,128)S(1)} copy-done((f32[2048,4096]{1,0:T(8,128)S(1)}, f32[2048,4096]{1,0:T(8,128)}, u32[]{:S(2)}) %copy-start) | copy-done | bytes 33554456
  145.5 7.6 %exponential_reduce_fusion.4 = f32[4096]{0:T(1024)S(1)} fusion(f32[2048,4096]{1,0:T(8,128)S(1)} %copy-done, f32[4096]{0:T(1024)S(1)} %broadcast_divide_fusion.2, f32[2048]{0:T(1024)S(1)} %multiply_subtract_fusion.5, f32[]{:T(128)} %bitcast), kind=kLoop, calls=%fused_computation.4 | loop fusion | flops 33550336 | bytes 33595396 | tf_op jit(solution)/shard_map/reduce_sum | solution.py:84
  154.1 2.7 %collective-permute-start.18 = (f32[2,4096]{1,0:T(2,128)S(1)}, f32[2,4096]{1,0:T(2,128)S(1)}, u32[]{:S(2)}, u32[]{:S(2)}) collective-permute-start(f32[2,4096]{1,0:T(2,128)S(1)} %pad_maximum_fusion.3), channel_id=1, source_target_pairs={{0,16},{8,24},{16,0},{24,8},{32,48},{40,56},{48,32},{56,40},{64,80... | collective-permute-start | bytes 98312 | tf_op jit(solution)/shard_map/ppermute | solution.py:46
  156.8 1.4 collective-permute-start.19
  161.1 2.4 collective-permute-start.21
  163.5 1.5 collective-permute-start.22
  167.6 3.0 %subtract_reduce_fusion.3 = f32[2048]{0:T(1024)S(1)} fusion(f32[2048,4096]{1,0:T(8,128)S(1)} %copy-done, f32[4096]{0:T(1024)S(1)} %bitcast.122), kind=kLoop, calls=%fused_computation.10 | loop fusion | flops 16775168 | bytes 33579008 | tf_op jit(solution)/shard_map/reduce_max | solution.py:77
  170.6 8.0 %exponential_reduce_fusion.3 = f32[2048]{0:T(1024)S(1)} fusion(f32[2048,4096]{1,0:T(8,128)S(1)} %copy-done, f32[2048]{0:T(1024)S(1)} %broadcast_divide_fusion.4, f32[4096]{0:T(1024)S(1)} %bitcast.123, f32[]{:T(128)} %bitcast), kind=kLoop, calls=%fused_computation.3 | loop fusion | flops 33552384 | bytes 33587204 | tf_op jit(solution)/shard_map/reduce_sum | solution.py:78
  180.4 3.8 %collective-permute-start.25 = (f32[2,2048]{1,0:T(2,128)S(1)}, f32[2,2048]{1,0:T(2,128)S(1)}, u32[]{:S(2)}, u32[]{:S(2)}) collective-permute-start(f32[2,2048]{1,0:T(2,128)S(1)} %pad_maximum_fusion.12), channel_id=1, source_target_pairs={{0,4},{1,5},{2,6},{3,7},{4,0},{5,1},{6,2},{7,3},{8,12},{9,13},{10,... | collective-permute-start | bytes 49160 | tf_op jit(solution)/shard_map/ppermute | solution.py:46
  186.1 1.8 collective-permute-done.26
  188.0 4.7 %subtract_reduce_fusion.2 = f32[4096]{0:T(1024)S(1)} fusion(f32[2048,4096]{1,0:T(8,128)S(1)} %copy-done, f32[2048]{0:T(1024)S(1)} %multiply_subtract_fusion.4), kind=kLoop, calls=%fused_computation.9 | loop fusion | flops 16773120 | bytes 33579008 | tf_op jit(solution)/shard_map/reduce_max | solution.py:83
  192.8 7.6 %exponential_reduce_fusion.2 = f32[4096]{0:T(1024)S(1)} fusion(f32[2048,4096]{1,0:T(8,128)S(1)} %copy-done, f32[4096]{0:T(1024)S(1)} %broadcast_divide_fusion.1, f32[2048]{0:T(1024)S(1)} %multiply_subtract_fusion.4, f32[]{:T(128)} %bitcast), kind=kLoop, calls=%fused_computation.2 | loop fusion | flops 33550336 | bytes 33595396 | tf_op jit(solution)/shard_map/reduce_sum | solution.py:84
  200.5 1.6 collective-permute-start.27
  202.1 2.7 collective-permute-start.28
  205.6 1.8 collective-permute-done.28
  208.8 1.5 collective-permute-start.30
  210.3 2.7 collective-permute-start.31
  214.0 1.7 collective-permute-done.31
  217.1 3.0 %subtract_reduce_fusion.1 = f32[2048]{0:T(1024)S(1)} fusion(f32[2048,4096]{1,0:T(8,128)S(1)} %copy-done, f32[4096]{0:T(1024)S(1)} %bitcast.124), kind=kLoop, calls=%fused_computation.8 | loop fusion | flops 16775168 | bytes 33579008 | tf_op jit(solution)/shard_map/reduce_max | solution.py:77
  220.1 8.0 %exponential_reduce_fusion.1 = f32[2048]{0:T(1024)S(1)} fusion(f32[2048,4096]{1,0:T(8,128)S(1)} %copy-done, f32[2048]{0:T(1024)S(1)} %broadcast_divide_fusion.3, f32[4096]{0:T(1024)S(1)} %bitcast.125, f32[]{:T(128)} %bitcast), kind=kLoop, calls=%fused_computation.1 | loop fusion | flops 33552384 | bytes 33587204 | tf_op jit(solution)/shard_map/reduce_sum | solution.py:78
  229.6 2.7 collective-permute-start.35
  232.3 1.5 collective-permute-start.36
  236.1 4.7 %subtract_reduce_fusion = f32[4096]{0:T(1024)S(1)} fusion(f32[2048,4096]{1,0:T(8,128)S(1)} %copy-done, f32[2048]{0:T(1024)S(1)} %multiply_subtract_fusion.3), kind=kLoop, calls=%fused_computation.7 | loop fusion | flops 16773120 | bytes 33579008 | tf_op jit(solution)/shard_map/reduce_max | solution.py:83
  240.8 7.6 %exponential_reduce_fusion = f32[4096]{0:T(1024)S(1)} fusion(f32[2048,4096]{1,0:T(8,128)S(1)} %copy-done, f32[4096]{0:T(1024)S(1)} %broadcast_divide_fusion, f32[2048]{0:T(1024)S(1)} %multiply_subtract_fusion.3, f32[]{:T(128)} %bitcast), kind=kLoop, calls=%fused_computation | loop fusion | flops 33550336 | bytes 33595396 | tf_op jit(solution)/shard_map/reduce_sum | solution.py:84
  248.6 2.7 collective-permute-start.38
  251.3 1.4 collective-permute-start.39
  255.6 2.7 %collective-permute-start.41 = (f32[2,4096]{1,0:T(2,128)S(1)}, f32[2,4096]{1,0:T(2,128)S(1)}, u32[]{:S(2)}, u32[]{:S(2)}) collective-permute-start(f32[2,4096]{1,0:T(2,128)S(1)} %pad_maximum_fusion.8), channel_id=1, source_target_pairs={{0,64},{8,72},{16,80},{24,88},{32,96},{40,104},{48,112},{56,120},{... | collective-permute-start | bytes 98312 | tf_op jit(solution)/shard_map/ppermute | solution.py:46
  258.3 1.4 collective-permute-start.42
  (154 shorter events, 39.5 us)
Async XLA Ops:
  7.2 30.0 %copy-start.1 = (f32[256,256]{1,0:T(8,128)S(1)}, f32[256,256]{1,0:T(8,128)}, u32[]{:S(2)}) copy-start(f32[256,256]{1,0:T(8,128)} %param.3) | copy-start | bytes 786436
  7.2 56.4 %all-gather.2.cloned.1.call-start = ((), (), s32[]{:S(2)}) async-start(), calls=%async_computation | async-start | bytes 3899392 | tf_op jit(solution)/shard_map/all_gather | solution.py:111
  9.7 8.1 %collective-permute-start.7 = (f32[32,256]{1,0:T(8,128)S(1)}, f32[32,256]{1,0:T(8,128)S(1)}, u32[]{:S(2)}, u32[]{:S(2)}) collective-permute-start(f32[32,256]{1,0:T(8,128)S(1)} %get-tuple-element.23), channel_id=1, source_target_pairs={{0,8},{8,16},{16,24},{24,0},{32,40},{40,48},{48,56},{56,32},{64,72... | collective-permute-start | bytes 98312 | tf_op jit(solution)/shard_map/ppermute | solution.py:35
  11.4 6.5 %collective-permute-start.8 = (f32[32,256]{1,0:T(8,128)S(1)}, f32[32,256]{1,0:T(8,128)S(1)}, u32[]{:S(2)}, u32[]{:S(2)}) collective-permute-start(f32[32,256]{1,0:T(8,128)S(1)} %get-tuple-element.23), channel_id=1, source_target_pairs={{0,16},{8,24},{16,0},{24,8},{32,48},{40,56},{48,32},{56,40},{64,80... | collective-permute-start | bytes 98312 | tf_op jit(solution)/shard_map/ppermute | solution.py:35
  14.3 3.9 %collective-permute-start.9 = (f32[32,256]{1,0:T(8,128)S(1)}, f32[32,256]{1,0:T(8,128)S(1)}, u32[]{:S(2)}, u32[]{:S(2)}) collective-permute-start(f32[32,256]{1,0:T(8,128)S(1)} %get-tuple-element.23), channel_id=1, source_target_pairs={{0,24},{8,0},{16,8},{24,16},{32,56},{40,32},{48,40},{56,48},{64,88... | collective-permute-start | bytes 98312 | tf_op jit(solution)/shard_map/ppermute | solution.py:35
  15.6 20.3 %collective-permute-start = (f32[256,256]{1,0:T(8,128)}, f32[256,256]{1,0:T(8,128)S(1)}, u32[]{:S(2)}, u32[]{:S(2)}) collective-permute-start(f32[256,256]{1,0:T(8,128)} %param.3), channel_id=1, source_target_pairs={{0,1},{1,2},{2,3},{3,4},{4,5},{5,6},{6,7},{7,0},{8,9},{9,10},{10,1... | collective-permute-start | bytes 786440 | tf_op jit(solution)/shard_map/ppermute | solution.py:35
  15.6 21.6 %collective-permute-start.1 = (f32[256,256]{1,0:T(8,128)}, f32[256,256]{1,0:T(8,128)S(1)}, u32[]{:S(2)}, u32[]{:S(2)}) collective-permute-start(f32[256,256]{1,0:T(8,128)} %param.3), channel_id=1, source_target_pairs={{0,2},{1,3},{2,4},{3,5},{4,6},{5,7},{6,0},{7,1},{8,10},{9,11},{10,... | collective-permute-start | bytes 786440 | tf_op jit(solution)/shard_map/ppermute | solution.py:35
  18.3 8.1 %collective-permute-start.10 = (f32[128,256]{1,0:T(8,128)S(1)}, f32[128,256]{1,0:T(8,128)S(1)}, u32[]{:S(2)}, u32[]{:S(2)}) collective-permute-start(f32[128,256]{1,0:T(8,128)S(1)} %get-tuple-element.25), channel_id=1, source_target_pairs={{0,32},{8,40},{16,48},{24,56},{32,64},{40,72},{48,80},{56,88},{64,... | collective-permute-start | bytes 393224 | tf_op jit(solution)/shard_map/ppermute | solution.py:35
  20.2 12.6 %collective-permute-start.11 = (f32[128,256]{1,0:T(8,128)S(1)}, f32[128,256]{1,0:T(8,128)S(1)}, u32[]{:S(2)}, u32[]{:S(2)}) collective-permute-start(f32[128,256]{1,0:T(8,128)S(1)} %get-tuple-element.25), channel_id=1, source_target_pairs={{0,64},{8,72},{16,80},{24,88},{32,96},{40,104},{48,112},{56,120},{... | collective-permute-start | bytes 393224 | tf_op jit(solution)/shard_map/ppermute | solution.py:35
  23.8 10.3 %collective-permute-start.12 = (f32[128,256]{1,0:T(8,128)S(1)}, f32[128,256]{1,0:T(8,128)S(1)}, u32[]{:S(2)}, u32[]{:S(2)}) collective-permute-start(f32[128,256]{1,0:T(8,128)S(1)} %get-tuple-element.25), channel_id=1, source_target_pairs={{0,96},{8,104},{16,112},{24,120},{32,0},{40,8},{48,16},{56,24},{64... | collective-permute-start | bytes 393224 | tf_op jit(solution)/shard_map/ppermute | solution.py:35
  26.4 11.3 %collective-permute-start.2 = (f32[256,256]{1,0:T(8,128)}, f32[256,256]{1,0:T(8,128)S(1)}, u32[]{:S(2)}, u32[]{:S(2)}) collective-permute-start(f32[256,256]{1,0:T(8,128)} %param.3), channel_id=1, source_target_pairs={{0,3},{1,4},{2,5},{3,6},{4,7},{5,0},{6,1},{7,2},{8,11},{9,12},{10,... | collective-permute-start | bytes 786440 | tf_op jit(solution)/shard_map/ppermute | solution.py:35
  32.9 10.1 %collective-permute-start.3 = (f32[256,256]{1,0:T(8,128)}, f32[256,256]{1,0:T(8,128)S(1)}, u32[]{:S(2)}, u32[]{:S(2)}) collective-permute-start(f32[256,256]{1,0:T(8,128)} %param.3), channel_id=1, source_target_pairs={{0,4},{1,5},{2,6},{3,7},{4,0},{5,1},{6,2},{7,3},{8,12},{9,13},{10,... | collective-permute-start | bytes 786440 | tf_op jit(solution)/shard_map/ppermute | solution.py:35
  34.2 9.8 %collective-permute-start.4 = (f32[256,256]{1,0:T(8,128)}, f32[256,256]{1,0:T(8,128)S(1)}, u32[]{:S(2)}, u32[]{:S(2)}) collective-permute-start(f32[256,256]{1,0:T(8,128)} %param.3), channel_id=1, source_target_pairs={{0,5},{1,6},{2,7},{3,0},{4,1},{5,2},{6,3},{7,4},{8,13},{9,14},{10,... | collective-permute-start | bytes 786440 | tf_op jit(solution)/shard_map/ppermute | solution.py:35
  36.0 15.7 %collective-permute-start.5 = (f32[256,256]{1,0:T(8,128)}, f32[256,256]{1,0:T(8,128)S(1)}, u32[]{:S(2)}, u32[]{:S(2)}) collective-permute-start(f32[256,256]{1,0:T(8,128)} %param.3), channel_id=1, source_target_pairs={{0,6},{1,7},{2,0},{3,1},{4,2},{5,3},{6,4},{7,5},{8,14},{9,15},{10,... | collective-permute-start | bytes 786440 | tf_op jit(solution)/shard_map/ppermute | solution.py:35
  37.2 16.4 %collective-permute-start.6 = (f32[256,256]{1,0:T(8,128)S(1)}, f32[256,256]{1,0:T(8,128)S(1)}, u32[]{:S(2)}, u32[]{:S(2)}) collective-permute-start(f32[256,256]{1,0:T(8,128)S(1)} %copy-done.1), channel_id=1, source_target_pairs={{0,7},{1,0},{2,1},{3,2},{4,3},{5,4},{6,5},{7,6},{8,15},{9,8},{10,9... | collective-permute-start | bytes 786440 | tf_op jit(solution)/shard_map/ppermute | solution.py:35
  116.0 1.3 collective-permute-start.13
  117.3 5.7 %collective-permute-start.14 = (f32[2,2048]{1,0:T(2,128)S(1)}, f32[2,2048]{1,0:T(2,128)S(1)}, u32[]{:S(2)}, u32[]{:S(2)}) collective-permute-start(f32[2,2048]{1,0:T(2,128)S(1)} %pad_maximum_fusion.10), channel_id=1, source_target_pairs={{0,2},{1,3},{2,4},{3,5},{4,6},{5,7},{6,0},{7,1},{8,10},{9,11},{10,... | collective-permute-start | bytes 49160 | tf_op jit(solution)/shard_map/ppermute | solution.py:46
  118.8 5.2 %collective-permute-start.15 = (f32[2,2048]{1,0:T(2,128)S(1)}, f32[2,2048]{1,0:T(2,128)S(1)}, u32[]{:S(2)}, u32[]{:S(2)}) collective-permute-start(f32[2,2048]{1,0:T(2,128)S(1)} %pad_maximum_fusion.10), channel_id=1, source_target_pairs={{0,4},{1,5},{2,6},{3,7},{4,0},{5,1},{6,2},{7,3},{8,12},{9,13},{10,... | collective-permute-start | bytes 49160 | tf_op jit(solution)/shard_map/ppermute | solution.py:46
  121.5 3.7 %collective-permute-start.16 = (f32[2,2048]{1,0:T(2,128)S(1)}, f32[2,2048]{1,0:T(2,128)S(1)}, u32[]{:S(2)}, u32[]{:S(2)}) collective-permute-start(f32[2,2048]{1,0:T(2,128)S(1)} %pad_maximum_fusion.10), channel_id=1, source_target_pairs={{0,6},{1,7},{2,0},{3,1},{4,2},{5,3},{6,4},{7,5},{8,14},{9,15},{10,... | collective-permute-start | bytes 49160 | tf_op jit(solution)/shard_map/ppermute | solution.py:46
  125.3 20.2 %copy-start = (f32[2048,4096]{1,0:T(8,128)S(1)}, f32[2048,4096]{1,0:T(8,128)}, u32[]{:S(2)}) copy-start(f32[2048,4096]{1,0:T(8,128)} %get-tuple-element.83) | copy-start | bytes 100663296
  153.2 5.2 %collective-permute-start.17 = (f32[2,4096]{1,0:T(2,128)S(1)}, f32[2,4096]{1,0:T(2,128)S(1)}, u32[]{:S(2)}, u32[]{:S(2)}) collective-permute-start(f32[2,4096]{1,0:T(2,128)S(1)} %pad_maximum_fusion.3), channel_id=1, source_target_pairs={{0,8},{8,16},{16,24},{24,0},{32,40},{40,48},{48,56},{56,32},{64,72... | collective-permute-start | bytes 98312 | tf_op jit(solution)/shard_map/ppermute | solution.py:46
  154.1 5.4 %collective-permute-start.18 = (f32[2,4096]{1,0:T(2,128)S(1)}, f32[2,4096]{1,0:T(2,128)S(1)}, u32[]{:S(2)}, u32[]{:S(2)}) collective-permute-start(f32[2,4096]{1,0:T(2,128)S(1)} %pad_maximum_fusion.3), channel_id=1, source_target_pairs={{0,16},{8,24},{16,0},{24,8},{32,48},{40,56},{48,32},{56,40},{64,80... | collective-permute-start | bytes 98312 | tf_op jit(solution)/shard_map/ppermute | solution.py:46
  156.8 3.9 %collective-permute-start.19 = (f32[2,4096]{1,0:T(2,128)S(1)}, f32[2,4096]{1,0:T(2,128)S(1)}, u32[]{:S(2)}, u32[]{:S(2)}) collective-permute-start(f32[2,4096]{1,0:T(2,128)S(1)} %pad_maximum_fusion.3), channel_id=1, source_target_pairs={{0,24},{8,0},{16,8},{24,16},{32,56},{40,32},{48,40},{56,48},{64,88... | collective-permute-start | bytes 98312 | tf_op jit(solution)/shard_map/ppermute | solution.py:46
  160.9 5.2 %collective-permute-start.20 = (f32[2,4096]{1,0:T(2,128)S(1)}, f32[2,4096]{1,0:T(2,128)S(1)}, u32[]{:S(2)}, u32[]{:S(2)}) collective-permute-start(f32[2,4096]{1,0:T(2,128)S(1)} %pad_maximum_fusion.4), channel_id=1, source_target_pairs={{0,32},{8,40},{16,48},{24,56},{32,64},{40,72},{48,80},{56,88},{64,... | collective-permute-start | bytes 98312 | tf_op jit(solution)/shard_map/ppermute | solution.py:46
  161.1 5.4 %collective-permute-start.21 = (f32[2,4096]{1,0:T(2,128)S(1)}, f32[2,4096]{1,0:T(2,128)S(1)}, u32[]{:S(2)}, u32[]{:S(2)}) collective-permute-start(f32[2,4096]{1,0:T(2,128)S(1)} %pad_maximum_fusion.4), channel_id=1, source_target_pairs={{0,64},{8,72},{16,80},{24,88},{32,96},{40,104},{48,112},{56,120},{... | collective-permute-start | bytes 98312 | tf_op jit(solution)/shard_map/ppermute | solution.py:46
  163.5 3.9 %collective-permute-start.22 = (f32[2,4096]{1,0:T(2,128)S(1)}, f32[2,4096]{1,0:T(2,128)S(1)}, u32[]{:S(2)}, u32[]{:S(2)}) collective-permute-start(f32[2,4096]{1,0:T(2,128)S(1)} %pad_maximum_fusion.4), channel_id=1, source_target_pairs={{0,96},{8,104},{16,112},{24,120},{32,0},{40,8},{48,16},{56,24},{64... | collective-permute-start | bytes 98312 | tf_op jit(solution)/shard_map/ppermute | solution.py:46
  178.7 1.3 collective-permute-start.23
  180.0 5.0 %collective-permute-start.24 = (f32[2,2048]{1,0:T(2,128)S(1)}, f32[2,2048]{1,0:T(2,128)S(1)}, u32[]{:S(2)}, u32[]{:S(2)}) collective-permute-start(f32[2,2048]{1,0:T(2,128)S(1)} %pad_maximum_fusion.12), channel_id=1, source_target_pairs={{0,2},{1,3},{2,4},{3,5},{4,6},{5,7},{6,0},{7,1},{8,10},{9,11},{10,... | collective-permute-start | bytes 49160 | tf_op jit(solution)/shard_map/ppermute | solution.py:46
  180.4 5.7 %collective-permute-start.25 = (f32[2,2048]{1,0:T(2,128)S(1)}, f32[2,2048]{1,0:T(2,128)S(1)}, u32[]{:S(2)}, u32[]{:S(2)}) collective-permute-start(f32[2,2048]{1,0:T(2,128)S(1)} %pad_maximum_fusion.12), channel_id=1, source_target_pairs={{0,4},{1,5},{2,6},{3,7},{4,0},{5,1},{6,2},{7,3},{8,12},{9,13},{10,... | collective-permute-start | bytes 49160 | tf_op jit(solution)/shard_map/ppermute | solution.py:46
  184.2 3.7 %collective-permute-start.26 = (f32[2,2048]{1,0:T(2,128)S(1)}, f32[2,2048]{1,0:T(2,128)S(1)}, u32[]{:S(2)}, u32[]{:S(2)}) collective-permute-start(f32[2,2048]{1,0:T(2,128)S(1)} %pad_maximum_fusion.12), channel_id=1, source_target_pairs={{0,6},{1,7},{2,0},{3,1},{4,2},{5,3},{6,4},{7,5},{8,14},{9,15},{10,... | collective-permute-start | bytes 49160 | tf_op jit(solution)/shard_map/ppermute | solution.py:46
  200.5 5.2 %collective-permute-start.27 = (f32[2,4096]{1,0:T(2,128)S(1)}, f32[2,4096]{1,0:T(2,128)S(1)}, u32[]{:S(2)}, u32[]{:S(2)}) collective-permute-start(f32[2,4096]{1,0:T(2,128)S(1)} %pad_maximum_fusion.5), channel_id=1, source_target_pairs={{0,8},{8,16},{16,24},{24,0},{32,40},{40,48},{48,56},{56,32},{64,72... | collective-permute-start | bytes 98312 | tf_op jit(solution)/shard_map/ppermute | solution.py:46
  202.1 5.4 %collective-permute-start.28 = (f32[2,4096]{1,0:T(2,128)S(1)}, f32[2,4096]{1,0:T(2,128)S(1)}, u32[]{:S(2)}, u32[]{:S(2)}) collective-permute-start(f32[2,4096]{1,0:T(2,128)S(1)} %pad_maximum_fusion.5), channel_id=1, source_target_pairs={{0,16},{8,24},{16,0},{24,8},{32,48},{40,56},{48,32},{56,40},{64,80... | collective-permute-start | bytes 98312 | tf_op jit(solution)/shard_map/ppermute | solution.py:46
  204.7 3.9 %collective-permute-start.29 = (f32[2,4096]{1,0:T(2,128)S(1)}, f32[2,4096]{1,0:T(2,128)S(1)}, u32[]{:S(2)}, u32[]{:S(2)}) collective-permute-start(f32[2,4096]{1,0:T(2,128)S(1)} %pad_maximum_fusion.5), channel_id=1, source_target_pairs={{0,24},{8,0},{16,8},{24,16},{32,56},{40,32},{48,40},{56,48},{64,88... | collective-permute-start | bytes 98312 | tf_op jit(solution)/shard_map/ppermute | solution.py:46
  208.8 5.2 %collective-permute-start.30 = (f32[2,4096]{1,0:T(2,128)S(1)}, f32[2,4096]{1,0:T(2,128)S(1)}, u32[]{:S(2)}, u32[]{:S(2)}) collective-permute-start(f32[2,4096]{1,0:T(2,128)S(1)} %pad_maximum_fusion.6), channel_id=1, source_target_pairs={{0,32},{8,40},{16,48},{24,56},{32,64},{40,72},{48,80},{56,88},{64,... | collective-permute-start | bytes 98312 | tf_op jit(solution)/shard_map/ppermute | solution.py:46
  210.3 5.4 %collective-permute-start.31 = (f32[2,4096]{1,0:T(2,128)S(1)}, f32[2,4096]{1,0:T(2,128)S(1)}, u32[]{:S(2)}, u32[]{:S(2)}) collective-permute-start(f32[2,4096]{1,0:T(2,128)S(1)} %pad_maximum_fusion.6), channel_id=1, source_target_pairs={{0,64},{8,72},{16,80},{24,88},{32,96},{40,104},{48,112},{56,120},{... | collective-permute-start | bytes 98312 | tf_op jit(solution)/shard_map/ppermute | solution.py:46
  213.0 3.9 %collective-permute-start.32 = (f32[2,4096]{1,0:T(2,128)S(1)}, f32[2,4096]{1,0:T(2,128)S(1)}, u32[]{:S(2)}, u32[]{:S(2)}) collective-permute-start(f32[2,4096]{1,0:T(2,128)S(1)} %pad_maximum_fusion.6), channel_id=1, source_target_pairs={{0,96},{8,104},{16,112},{24,120},{32,0},{40,8},{48,16},{56,24},{64... | collective-permute-start | bytes 98312 | tf_op jit(solution)/shard_map/ppermute | solution.py:46
  228.1 1.3 collective-permute-start.33
  229.5 5.0 %collective-permute-start.34 = (f32[2,2048]{1,0:T(2,128)S(1)}, f32[2,2048]{1,0:T(2,128)S(1)}, u32[]{:S(2)}, u32[]{:S(2)}) collective-permute-start(f32[2,2048]{1,0:T(2,128)S(1)} %pad_maximum_fusion.14), channel_id=1, source_target_pairs={{0,2},{1,3},{2,4},{3,5},{4,6},{5,7},{6,0},{7,1},{8,10},{9,11},{10,... | collective-permute-start | bytes 49160 | tf_op jit(solution)/shard_map/ppermute | solution.py:46
  229.6 5.3 %collective-permute-start.35 = (f32[2,2048]{1,0:T(2,128)S(1)}, f32[2,2048]{1,0:T(2,128)S(1)}, u32[]{:S(2)}, u32[]{:S(2)}) collective-permute-start(f32[2,2048]{1,0:T(2,128)S(1)} %pad_maximum_fusion.14), channel_id=1, source_target_pairs={{0,4},{1,5},{2,6},{3,7},{4,0},{5,1},{6,2},{7,3},{8,12},{9,13},{10,... | collective-permute-start | bytes 49160 | tf_op jit(solution)/shard_map/ppermute | solution.py:46
  232.3 3.7 %collective-permute-start.36 = (f32[2,2048]{1,0:T(2,128)S(1)}, f32[2,2048]{1,0:T(2,128)S(1)}, u32[]{:S(2)}, u32[]{:S(2)}) collective-permute-start(f32[2,2048]{1,0:T(2,128)S(1)} %pad_maximum_fusion.14), channel_id=1, source_target_pairs={{0,6},{1,7},{2,0},{3,1},{4,2},{5,3},{6,4},{7,5},{8,14},{9,15},{10,... | collective-permute-start | bytes 49160 | tf_op jit(solution)/shard_map/ppermute | solution.py:46
  236.1 4.8 %copy-start.2 = (f32[2048]{0:T(1024)}, f32[2048]{0:T(1024)S(1)}, u32[]{:S(2)}) copy-start(f32[2048]{0:T(1024)S(1)} %multiply_subtract_fusion.3) | copy-start | bytes 24580
  248.5 5.2 %collective-permute-start.37 = (f32[2,4096]{1,0:T(2,128)S(1)}, f32[2,4096]{1,0:T(2,128)S(1)}, u32[]{:S(2)}, u32[]{:S(2)}) collective-permute-start(f32[2,4096]{1,0:T(2,128)S(1)} %pad_maximum_fusion.7), channel_id=1, source_target_pairs={{0,8},{8,16},{16,24},{24,0},{32,40},{40,48},{48,56},{56,32},{64,72... | collective-permute-start | bytes 98312 | tf_op jit(solution)/shard_map/ppermute | solution.py:46
  248.6 5.5 %collective-permute-start.38 = (f32[2,4096]{1,0:T(2,128)S(1)}, f32[2,4096]{1,0:T(2,128)S(1)}, u32[]{:S(2)}, u32[]{:S(2)}) collective-permute-start(f32[2,4096]{1,0:T(2,128)S(1)} %pad_maximum_fusion.7), channel_id=1, source_target_pairs={{0,16},{8,24},{16,0},{24,8},{32,48},{40,56},{48,32},{56,40},{64,80... | collective-permute-start | bytes 98312 | tf_op jit(solution)/shard_map/ppermute | solution.py:46
  251.3 3.9 %collective-permute-start.39 = (f32[2,4096]{1,0:T(2,128)S(1)}, f32[2,4096]{1,0:T(2,128)S(1)}, u32[]{:S(2)}, u32[]{:S(2)}) collective-permute-start(f32[2,4096]{1,0:T(2,128)S(1)} %pad_maximum_fusion.7), channel_id=1, source_target_pairs={{0,24},{8,0},{16,8},{24,16},{32,56},{40,32},{48,40},{56,48},{64,88... | collective-permute-start | bytes 98312 | tf_op jit(solution)/shard_map/ppermute | solution.py:46
  255.5 5.2 %collective-permute-start.40 = (f32[2,4096]{1,0:T(2,128)S(1)}, f32[2,4096]{1,0:T(2,128)S(1)}, u32[]{:S(2)}, u32[]{:S(2)}) collective-permute-start(f32[2,4096]{1,0:T(2,128)S(1)} %pad_maximum_fusion.8), channel_id=1, source_target_pairs={{0,32},{8,40},{16,48},{24,56},{32,64},{40,72},{48,80},{56,88},{64,... | collective-permute-start | bytes 98312 | tf_op jit(solution)/shard_map/ppermute | solution.py:46
  255.6 5.5 %collective-permute-start.41 = (f32[2,4096]{1,0:T(2,128)S(1)}, f32[2,4096]{1,0:T(2,128)S(1)}, u32[]{:S(2)}, u32[]{:S(2)}) collective-permute-start(f32[2,4096]{1,0:T(2,128)S(1)} %pad_maximum_fusion.8), channel_id=1, source_target_pairs={{0,64},{8,72},{16,80},{24,88},{32,96},{40,104},{48,112},{56,120},{... | collective-permute-start | bytes 98312 | tf_op jit(solution)/shard_map/ppermute | solution.py:46
  258.3 3.9 %collective-permute-start.42 = (f32[2,4096]{1,0:T(2,128)S(1)}, f32[2,4096]{1,0:T(2,128)S(1)}, u32[]{:S(2)}, u32[]{:S(2)}) collective-permute-start(f32[2,4096]{1,0:T(2,128)S(1)} %pad_maximum_fusion.8), channel_id=1, source_target_pairs={{0,96},{8,104},{16,112},{24,120},{32,0},{40,8},{48,16},{56,24},{64... | collective-permute-start | bytes 98312 | tf_op jit(solution)/shard_map/ppermute | solution.py:46
Sparse Core Ops, SparseCore 0:
  10.1 53.4 all-gather.1

commit v10 on v9

--- a/solution.py
+++ b/solution.py
@@ -106,7 +106,7 @@
     all_passages = passages.shape[0] * row_count * col_count
     query_block = gather_col(queries)
     rows = passages.shape[0]
-    split = rows - rows // 8
+    split = rows - rows // 16
     passage_block = jnp.concatenate(
         [lax.all_gather(passages[:split], "row", axis=0, tiled=True), gather_row(passages[split:])], axis=0
     )

time: 271 us -> 277 us (1.022); the launches traced: 271 us -> 273 us
  local copies, waits for them, and re-layouts: 14.9 us -> 18.4 us
    unnamed x25 -> x27, local copies, waits for them, and re-layouts: 10.7 us -> 12.9 us
  transfers between devices with their start and end apart: 44 -> 44, of which waited for: 37 -> 35; matrix products, arithmetic and copies ran while one was open for 1% -> 2% of each run, Pallas kernels for 0% -> 0%
where the time goes in v10:
time: 277 us; the launch traced here: 273 us
  other arithmetic  85.3 us (31%)
  starting transfers between devices  61.7 us (22%)
  waiting for transfers between devices  56.8 us (21%)
  matrix products  34.8 us (13%)
  local copies, waits for them, and re-layouts  18.4 us (7%)
  between operations  16.1 us (6%)
    ppermute x30, starting transfers between devices, combine_over(): lax.ppermute(packed, axis, digit_partners(axis, size, stride, width, k))  41.3 us
    dot_general x1, matrix products, inner_costs(): lax.dot_general(left, right, (((1,), (1,)), ((), ())), precision=lax.Prec...  34.8 us
    reduce_sum x3, other arithmetic, logsum_col(): totals = jnp.sum(jnp.exp(gaps / scale - peak[:, None]), axis=1)  30.6 us
    ppermute x30, waiting for transfers between devices, combine_over(): lax.ppermute(packed, axis, digit_partners(axis, size, stride, width, k))  27.6 us
    reduce_max x3, other arithmetic, logsum_row(): peak = jnp.max(gaps, axis=0) / scale  23.2 us
    reduce_sum x3, other arithmetic, logsum_row(): totals = jnp.sum(jnp.exp(gaps / scale - peak[None, :]), axis=0)  22.9 us
    ppermute x13, waiting for transfers between devices, exchange(): lax.ppermute(x, axis, digit_partners(axis, size, stride, width, k))  20.8 us
    ppermute x13, starting transfers between devices, exchange(): lax.ppermute(x, axis, digit_partners(axis, size, stride, width, k))  20.4 us
  transfers between devices with their start and end apart: 44, of which 35 were waited for; matrix products, arithmetic and copies ran while one was open for 2% of the time, Pallas kernels for 0%

profile of v10, /device:TPU:0, one launch (start us, length us, event | category | flops | bytes accessed | tf_op | source)
XLA Modules:
  0.0 273.3 jit_solution(520900921763381879)
XLA Ops:
  7.2 1.7 slice.223
  9.6 1.7 collective-permute-start.7
  11.3 2.9 %collective-permute-start.8 = (f32[16,256]{1,0:T(8,128)S(1)}, f32[16,256]{1,0:T(8,128)S(1)}, u32[]{:S(2)}, u32[]{:S(2)}) collective-permute-start(f32[16,256]{1,0:T(8,128)S(1)} %get-tuple-element.23), channel_id=1, source_target_pairs={{0,16},{8,24},{16,0},{24,8},{32,48},{40,56},{48,32},{56,40},{64,80... | collective-permute-start | bytes 49160 | tf_op jit(solution)/shard_map/ppermute | solution.py:35
  15.6 1.5 collective-permute-start.1
  18.0 2.0 collective-permute-start.10
  20.0 3.6 %collective-permute-start.11 = (f32[64,256]{1,0:T(8,128)S(1)}, f32[64,256]{1,0:T(8,128)S(1)}, u32[]{:S(2)}, u32[]{:S(2)}) collective-permute-start(f32[64,256]{1,0:T(8,128)S(1)} %get-tuple-element.27), channel_id=1, source_target_pairs={{0,64},{8,72},{16,80},{24,88},{32,96},{40,104},{48,112},{56,120},{... | collective-permute-start | bytes 196616 | tf_op jit(solution)/shard_map/ppermute | solution.py:35
  28.1 1.6 collective-permute-start.3
  29.7 2.9 %collective-permute-start.4 = (f32[256,256]{1,0:T(8,128)}, f32[256,256]{1,0:T(8,128)S(1)}, u32[]{:S(2)}, u32[]{:S(2)}) collective-permute-start(f32[256,256]{1,0:T(8,128)} %param.3), channel_id=1, source_target_pairs={{0,5},{1,6},{2,7},{3,0},{4,1},{5,2},{6,3},{7,4},{8,13},{9,14},{10,... | collective-permute-start | bytes 786440 | tf_op jit(solution)/shard_map/ppermute | solution.py:35
  34.0 2.7 %collective-permute-done.2 = f32[256,256]{1,0:T(8,128)S(1)} collective-permute-done((f32[256,256]{1,0:T(8,128)}, f32[256,256]{1,0:T(8,128)S(1)}, u32[]{:S(2)}, u32[]{:S(2)}) %collective-permute-start.2) | collective-permute-done | bytes 262176 | tf_op jit(solution)/shard_map/ppermute | solution.py:35
  36.8 5.7 %collective-permute-done.3 = f32[256,256]{1,0:T(8,128)S(1)} collective-permute-done((f32[256,256]{1,0:T(8,128)}, f32[256,256]{1,0:T(8,128)S(1)}, u32[]{:S(2)}, u32[]{:S(2)}) %collective-permute-start.3) | collective-permute-done | bytes 262176 | tf_op jit(solution)/shard_map/ppermute | solution.py:35
  42.5 5.0 %collective-permute-done.4 = f32[256,256]{1,0:T(8,128)S(1)} collective-permute-done((f32[256,256]{1,0:T(8,128)}, f32[256,256]{1,0:T(8,128)S(1)}, u32[]{:S(2)}, u32[]{:S(2)}) %collective-permute-start.4) | collective-permute-done | bytes 262176 | tf_op jit(solution)/shard_map/ppermute | solution.py:35
  48.9 4.0 %collective-permute-done.6 = f32[256,256]{1,0:T(8,128)S(1)} collective-permute-done((f32[256,256]{1,0:T(8,128)}, f32[256,256]{1,0:T(8,128)S(1)}, u32[]{:S(2)}, u32[]{:S(2)}) %collective-permute-start.6) | collective-permute-done | bytes 262176 | tf_op jit(solution)/shard_map/ppermute | solution.py:35
  54.9 8.5 %all-gather.2.cloned.1.call-done = f32[3840,256]{1,0:T(8,128)} async-done(((f32[240,256]{1,0:T(8,128)}), f32[3840,256]{1,0:T(8,128)}) %all-gather.2.cloned.1.call-update) | async-done | bytes 3932176 | tf_op jit(solution)/shard_map/all_gather | solution.py:111
  63.4 2.4 constant_dynamic-update-slice_fusion
  67.3 34.8 %subtract_reduce_fusion.5 = (f32[2048]{0:T(1024)S(1)}, f32[2048,4096]{1,0:T(8,128)}) fusion(f32[2048,256]{1,0:T(8,128)S(1)} %copy-done.2, f32[4096,256]{1,0:T(8,128)S(1)} %bitcast_dynamic-update-slice_fusion.16, f32[4096]{0:T(1024)S(1)} %multiply_reduce_fusion, f32[2048]{0:T(1024)S(1)} %multiply_reduce_fusion.1), kind=kOutput, calls=%fused_computation.12 | convolution fusion | flops 25811744768 | bytes 39878656 | tf_op jit(solution)/shard_map/dot_general | solution.py:14
  102.2 14.5 %exponential_reduce_fusion.5 = f32[2048]{0:T(1024)S(1)} fusion(f32[2048,4096]{1,0:T(8,128)} %get-tuple-element.83, f32[2048]{0:T(1024)S(1)} %broadcast_divide_fusion.5, f32[]{:T(128)} %bitcast), kind=kLoop, calls=%fused_computation.5 | loop fusion | flops 33552384 | bytes 33570820 | tf_op jit(solution)/shard_map/reduce_sum | solution.py:78
  118.1 1.5 collective-permute-start.14
  119.6 2.7 collective-permute-start.15
  122.3 1.7 collective-permute-start.16
  126.3 13.7 %subtract_reduce_fusion.4 = f32[4096]{0:T(1024)S(1)} fusion(f32[2048,4096]{1,0:T(8,128)} %get-tuple-element.83, f32[2048]{0:T(1024)S(1)} %multiply_subtract_fusion.5), kind=kLoop, calls=%fused_computation.11 | loop fusion | flops 16773120 | bytes 33579008 | tf_op jit(solution)/shard_map/reduce_max | solution.py:83
  140.1 6.4 %copy-done = f32[2048,4096]{1,0:T(8,128)S(1)} copy-done((f32[2048,4096]{1,0:T(8,128)S(1)}, f32[2048,4096]{1,0:T(8,128)}, u32[]{:S(2)}) %copy-start) | copy-done | bytes 33554456
  146.4 7.6 %exponential_reduce_fusion.4 = f32[4096]{0:T(1024)S(1)} fusion(f32[2048,4096]{1,0:T(8,128)S(1)} %copy-done, f32[4096]{0:T(1024)S(1)} %broadcast_divide_fusion.2, f32[2048]{0:T(1024)S(1)} %multiply_subtract_fusion.5, f32[]{:T(128)} %bitcast), kind=kLoop, calls=%fused_computation.4 | loop fusion | flops 33550336 | bytes 33595396 | tf_op jit(solution)/shard_map/reduce_sum | solution.py:84
  155.4 2.7 collective-permute-start.18
  158.1 1.4 collective-permute-start.19
  162.4 2.3 collective-permute-start.21
  164.7 1.7 collective-permute-start.22
  168.8 3.0 %subtract_reduce_fusion.3 = f32[2048]{0:T(1024)S(1)} fusion(f32[2048,4096]{1,0:T(8,128)S(1)} %copy-done, f32[4096]{0:T(1024)S(1)} %bitcast.122), kind=kLoop, calls=%fused_computation.10 | loop fusion | flops 16775168 | bytes 33579008 | tf_op jit(solution)/shard_map/reduce_max | solution.py:77
  171.8 8.0 %exponential_reduce_fusion.3 = f32[2048]{0:T(1024)S(1)} fusion(f32[2048,4096]{1,0:T(8,128)S(1)} %copy-done, f32[2048]{0:T(1024)S(1)} %broadcast_divide_fusion.4, f32[4096]{0:T(1024)S(1)} %bitcast.123, f32[]{:T(128)} %bitcast), kind=kLoop, calls=%fused_computation.3 | loop fusion | flops 33552384 | bytes 33587204 | tf_op jit(solution)/shard_map/reduce_sum | solution.py:78
  181.4 4.0 %collective-permute-start.25 = (f32[2,2048]{1,0:T(2,128)S(1)}, f32[2,2048]{1,0:T(2,128)S(1)}, u32[]{:S(2)}, u32[]{:S(2)}) collective-permute-start(f32[2,2048]{1,0:T(2,128)S(1)} %pad_maximum_fusion.12), channel_id=1, source_target_pairs={{0,4},{1,5},{2,6},{3,7},{4,0},{5,1},{6,2},{7,3},{8,12},{9,13},{10,... | collective-permute-start | bytes 49160 | tf_op jit(solution)/shard_map/ppermute | solution.py:46
  187.3 1.8 collective-permute-done.26
  189.2 4.7 %subtract_reduce_fusion.2 = f32[4096]{0:T(1024)S(1)} fusion(f32[2048,4096]{1,0:T(8,128)S(1)} %copy-done, f32[2048]{0:T(1024)S(1)} %multiply_subtract_fusion.4), kind=kLoop, calls=%fused_computation.9 | loop fusion | flops 16773120 | bytes 33579008 | tf_op jit(solution)/shard_map/reduce_max | solution.py:83
  193.9 7.6 %exponential_reduce_fusion.2 = f32[4096]{0:T(1024)S(1)} fusion(f32[2048,4096]{1,0:T(8,128)S(1)} %copy-done, f32[4096]{0:T(1024)S(1)} %broadcast_divide_fusion.1, f32[2048]{0:T(1024)S(1)} %multiply_subtract_fusion.4, f32[]{:T(128)} %bitcast), kind=kLoop, calls=%fused_computation.2 | loop fusion | flops 33550336 | bytes 33595396 | tf_op jit(solution)/shard_map/reduce_sum | solution.py:84
  201.6 1.7 collective-permute-start.27
  203.4 2.7 collective-permute-start.28
  206.8 2.0 collective-permute-done.28
  210.1 1.5 collective-permute-start.30
  211.6 2.7 collective-permute-start.31
  215.3 1.7 collective-permute-done.31
  217.0 1.4 collective-permute-done.32
  218.6 3.0 %subtract_reduce_fusion.1 = f32[2048]{0:T(1024)S(1)} fusion(f32[2048,4096]{1,0:T(8,128)S(1)} %copy-done, f32[4096]{0:T(1024)S(1)} %bitcast.124), kind=kLoop, calls=%fused_computation.8 | loop fusion | flops 16775168 | bytes 33579008 | tf_op jit(solution)/shard_map/reduce_max | solution.py:77
  221.6 8.0 %exponential_reduce_fusion.1 = f32[2048]{0:T(1024)S(1)} fusion(f32[2048,4096]{1,0:T(8,128)S(1)} %copy-done, f32[2048]{0:T(1024)S(1)} %broadcast_divide_fusion.3, f32[4096]{0:T(1024)S(1)} %bitcast.125, f32[]{:T(128)} %bitcast), kind=kLoop, calls=%fused_computation.1 | loop fusion | flops 33552384 | bytes 33587204 | tf_op jit(solution)/shard_map/reduce_sum | solution.py:78
  231.1 2.7 collective-permute-start.35
  233.8 1.5 collective-permute-start.36
  237.6 4.7 %subtract_reduce_fusion = f32[4096]{0:T(1024)S(1)} fusion(f32[2048,4096]{1,0:T(8,128)S(1)} %copy-done, f32[2048]{0:T(1024)S(1)} %multiply_subtract_fusion.3), kind=kLoop, calls=%fused_computation.7 | loop fusion | flops 16773120 | bytes 33579008 | tf_op jit(solution)/shard_map/reduce_max | solution.py:83
  242.3 7.6 %exponential_reduce_fusion = f32[4096]{0:T(1024)S(1)} fusion(f32[2048,4096]{1,0:T(8,128)S(1)} %copy-done, f32[4096]{0:T(1024)S(1)} %broadcast_divide_fusion, f32[2048]{0:T(1024)S(1)} %multiply_subtract_fusion.3, f32[]{:T(128)} %bitcast), kind=kLoop, calls=%fused_computation | loop fusion | flops 33550336 | bytes 33595396 | tf_op jit(solution)/shard_map/reduce_sum | solution.py:84
  250.1 2.7 collective-permute-start.38
  252.8 1.4 collective-permute-start.39
  257.1 2.7 collective-permute-start.41
  (171 shorter events, 42.6 us)
Async XLA Ops:
  7.2 56.2 %all-gather.2.cloned.1.call-start = ((), (), s32[]{:S(2)}) async-start(), calls=%async_computation | async-start | bytes 4177920 | tf_op jit(solution)/shard_map/all_gather | solution.py:111
  9.6 7.4 %collective-permute-start.7 = (f32[16,256]{1,0:T(8,128)S(1)}, f32[16,256]{1,0:T(8,128)S(1)}, u32[]{:S(2)}, u32[]{:S(2)}) collective-permute-start(f32[16,256]{1,0:T(8,128)S(1)} %get-tuple-element.23), channel_id=1, source_target_pairs={{0,8},{8,16},{16,24},{24,0},{32,40},{40,48},{48,56},{56,32},{64,72... | collective-permute-start | bytes 49160 | tf_op jit(solution)/shard_map/ppermute | solution.py:35
  11.3 5.8 %collective-permute-start.8 = (f32[16,256]{1,0:T(8,128)S(1)}, f32[16,256]{1,0:T(8,128)S(1)}, u32[]{:S(2)}, u32[]{:S(2)}) collective-permute-start(f32[16,256]{1,0:T(8,128)S(1)} %get-tuple-element.23), channel_id=1, source_target_pairs={{0,16},{8,24},{16,0},{24,8},{32,48},{40,56},{48,32},{56,40},{64,80... | collective-permute-start | bytes 49160 | tf_op jit(solution)/shard_map/ppermute | solution.py:35
  14.2 3.7 %collective-permute-start.9 = (f32[16,256]{1,0:T(8,128)S(1)}, f32[16,256]{1,0:T(8,128)S(1)}, u32[]{:S(2)}, u32[]{:S(2)}) collective-permute-start(f32[16,256]{1,0:T(8,128)S(1)} %get-tuple-element.23), channel_id=1, source_target_pairs={{0,24},{8,0},{16,8},{24,16},{32,56},{40,32},{48,40},{56,48},{64,88... | collective-permute-start | bytes 49160 | tf_op jit(solution)/shard_map/ppermute | solution.py:35
  15.6 17.0 %collective-permute-start = (f32[256,256]{1,0:T(8,128)}, f32[256,256]{1,0:T(8,128)S(1)}, u32[]{:S(2)}, u32[]{:S(2)}) collective-permute-start(f32[256,256]{1,0:T(8,128)} %param.3), channel_id=1, source_target_pairs={{0,1},{1,2},{2,3},{3,4},{4,5},{5,6},{6,7},{7,0},{8,9},{9,10},{10,1... | collective-permute-start | bytes 786440 | tf_op jit(solution)/shard_map/ppermute | solution.py:35
  15.6 18.4 %collective-permute-start.1 = (f32[256,256]{1,0:T(8,128)}, f32[256,256]{1,0:T(8,128)S(1)}, u32[]{:S(2)}, u32[]{:S(2)}) collective-permute-start(f32[256,256]{1,0:T(8,128)} %param.3), channel_id=1, source_target_pairs={{0,2},{1,3},{2,4},{3,5},{4,6},{5,7},{6,0},{7,1},{8,10},{9,11},{10,... | collective-permute-start | bytes 786440 | tf_op jit(solution)/shard_map/ppermute | solution.py:35
  18.0 8.5 %collective-permute-start.10 = (f32[64,256]{1,0:T(8,128)S(1)}, f32[64,256]{1,0:T(8,128)S(1)}, u32[]{:S(2)}, u32[]{:S(2)}) collective-permute-start(f32[64,256]{1,0:T(8,128)S(1)} %get-tuple-element.27), channel_id=1, source_target_pairs={{0,32},{8,40},{16,48},{24,56},{32,64},{40,72},{48,80},{56,88},{64,... | collective-permute-start | bytes 196616 | tf_op jit(solution)/shard_map/ppermute | solution.py:35
  20.0 8.1 %collective-permute-start.11 = (f32[64,256]{1,0:T(8,128)S(1)}, f32[64,256]{1,0:T(8,128)S(1)}, u32[]{:S(2)}, u32[]{:S(2)}) collective-permute-start(f32[64,256]{1,0:T(8,128)S(1)} %get-tuple-element.27), channel_id=1, source_target_pairs={{0,64},{8,72},{16,80},{24,88},{32,96},{40,104},{48,112},{56,120},{... | collective-permute-start | bytes 196616 | tf_op jit(solution)/shard_map/ppermute | solution.py:35
  23.6 6.1 %collective-permute-start.12 = (f32[64,256]{1,0:T(8,128)S(1)}, f32[64,256]{1,0:T(8,128)S(1)}, u32[]{:S(2)}, u32[]{:S(2)}) collective-permute-start(f32[64,256]{1,0:T(8,128)S(1)} %get-tuple-element.27), channel_id=1, source_target_pairs={{0,96},{8,104},{16,112},{24,120},{32,0},{40,8},{48,16},{56,24},{64... | collective-permute-start | bytes 196616 | tf_op jit(solution)/shard_map/ppermute | solution.py:35
  26.5 10.3 %collective-permute-start.2 = (f32[256,256]{1,0:T(8,128)}, f32[256,256]{1,0:T(8,128)S(1)}, u32[]{:S(2)}, u32[]{:S(2)}) collective-permute-start(f32[256,256]{1,0:T(8,128)} %param.3), channel_id=1, source_target_pairs={{0,3},{1,4},{2,5},{3,6},{4,7},{5,0},{6,1},{7,2},{8,11},{9,12},{10,... | collective-permute-start | bytes 786440 | tf_op jit(solution)/shard_map/ppermute | solution.py:35
  28.1 14.4 %collective-permute-start.3 = (f32[256,256]{1,0:T(8,128)}, f32[256,256]{1,0:T(8,128)S(1)}, u32[]{:S(2)}, u32[]{:S(2)}) collective-permute-start(f32[256,256]{1,0:T(8,128)} %param.3), channel_id=1, source_target_pairs={{0,4},{1,5},{2,6},{3,7},{4,0},{5,1},{6,2},{7,3},{8,12},{9,13},{10,... | collective-permute-start | bytes 786440 | tf_op jit(solution)/shard_map/ppermute | solution.py:35
  29.7 17.9 %collective-permute-start.4 = (f32[256,256]{1,0:T(8,128)}, f32[256,256]{1,0:T(8,128)S(1)}, u32[]{:S(2)}, u32[]{:S(2)}) collective-permute-start(f32[256,256]{1,0:T(8,128)} %param.3), channel_id=1, source_target_pairs={{0,5},{1,6},{2,7},{3,0},{4,1},{5,2},{6,3},{7,4},{8,13},{9,14},{10,... | collective-permute-start | bytes 786440 | tf_op jit(solution)/shard_map/ppermute | solution.py:35
  32.6 16.3 %collective-permute-start.5 = (f32[256,256]{1,0:T(8,128)}, f32[256,256]{1,0:T(8,128)S(1)}, u32[]{:S(2)}, u32[]{:S(2)}) collective-permute-start(f32[256,256]{1,0:T(8,128)} %param.3), channel_id=1, source_target_pairs={{0,6},{1,7},{2,0},{3,1},{4,2},{5,3},{6,4},{7,5},{8,14},{9,15},{10,... | collective-permute-start | bytes 786440 | tf_op jit(solution)/shard_map/ppermute | solution.py:35
  34.0 18.9 %collective-permute-start.6 = (f32[256,256]{1,0:T(8,128)}, f32[256,256]{1,0:T(8,128)S(1)}, u32[]{:S(2)}, u32[]{:S(2)}) collective-permute-start(f32[256,256]{1,0:T(8,128)} %param.3), channel_id=1, source_target_pairs={{0,7},{1,0},{2,1},{3,2},{4,3},{5,4},{6,5},{7,6},{8,15},{9,8},{10,9... | collective-permute-start | bytes 786440 | tf_op jit(solution)/shard_map/ppermute | solution.py:35
  53.2 1.3 copy-start.1
  65.7 1.6 copy-start.2
  116.7 1.3 collective-permute-start.13
  118.1 5.9 %collective-permute-start.14 = (f32[2,2048]{1,0:T(2,128)S(1)}, f32[2,2048]{1,0:T(2,128)S(1)}, u32[]{:S(2)}, u32[]{:S(2)}) collective-permute-start(f32[2,2048]{1,0:T(2,128)S(1)} %pad_maximum_fusion.10), channel_id=1, source_target_pairs={{0,2},{1,3},{2,4},{3,5},{4,6},{5,7},{6,0},{7,1},{8,10},{9,11},{10,... | collective-permute-start | bytes 49160 | tf_op jit(solution)/shard_map/ppermute | solution.py:46
  119.6 5.2 %collective-permute-start.15 = (f32[2,2048]{1,0:T(2,128)S(1)}, f32[2,2048]{1,0:T(2,128)S(1)}, u32[]{:S(2)}, u32[]{:S(2)}) collective-permute-start(f32[2,2048]{1,0:T(2,128)S(1)} %pad_maximum_fusion.10), channel_id=1, source_target_pairs={{0,4},{1,5},{2,6},{3,7},{4,0},{5,1},{6,2},{7,3},{8,12},{9,13},{10,... | collective-permute-start | bytes 49160 | tf_op jit(solution)/shard_map/ppermute | solution.py:46
  122.3 3.9 %collective-permute-start.16 = (f32[2,2048]{1,0:T(2,128)S(1)}, f32[2,2048]{1,0:T(2,128)S(1)}, u32[]{:S(2)}, u32[]{:S(2)}) collective-permute-start(f32[2,2048]{1,0:T(2,128)S(1)} %pad_maximum_fusion.10), channel_id=1, source_target_pairs={{0,6},{1,7},{2,0},{3,1},{4,2},{5,3},{6,4},{7,5},{8,14},{9,15},{10,... | collective-permute-start | bytes 49160 | tf_op jit(solution)/shard_map/ppermute | solution.py:46
  126.3 20.2 %copy-start = (f32[2048,4096]{1,0:T(8,128)S(1)}, f32[2048,4096]{1,0:T(8,128)}, u32[]{:S(2)}) copy-start(f32[2048,4096]{1,0:T(8,128)} %get-tuple-element.83) | copy-start | bytes 100663296
  154.1 5.4 %collective-permute-start.17 = (f32[2,4096]{1,0:T(2,128)S(1)}, f32[2,4096]{1,0:T(2,128)S(1)}, u32[]{:S(2)}, u32[]{:S(2)}) collective-permute-start(f32[2,4096]{1,0:T(2,128)S(1)} %pad_maximum_fusion.3), channel_id=1, source_target_pairs={{0,8},{8,16},{16,24},{24,0},{32,40},{40,48},{48,56},{56,32},{64,72... | collective-permute-start | bytes 98312 | tf_op jit(solution)/shard_map/ppermute | solution.py:46
  155.4 5.4 %collective-permute-start.18 = (f32[2,4096]{1,0:T(2,128)S(1)}, f32[2,4096]{1,0:T(2,128)S(1)}, u32[]{:S(2)}, u32[]{:S(2)}) collective-permute-start(f32[2,4096]{1,0:T(2,128)S(1)} %pad_maximum_fusion.3), channel_id=1, source_target_pairs={{0,16},{8,24},{16,0},{24,8},{32,48},{40,56},{48,32},{56,40},{64,80... | collective-permute-start | bytes 98312 | tf_op jit(solution)/shard_map/ppermute | solution.py:46
  158.1 3.9 %collective-permute-start.19 = (f32[2,4096]{1,0:T(2,128)S(1)}, f32[2,4096]{1,0:T(2,128)S(1)}, u32[]{:S(2)}, u32[]{:S(2)}) collective-permute-start(f32[2,4096]{1,0:T(2,128)S(1)} %pad_maximum_fusion.3), channel_id=1, source_target_pairs={{0,24},{8,0},{16,8},{24,16},{32,56},{40,32},{48,40},{56,48},{64,88... | collective-permute-start | bytes 98312 | tf_op jit(solution)/shard_map/ppermute | solution.py:46
  162.2 5.2 %collective-permute-start.20 = (f32[2,4096]{1,0:T(2,128)S(1)}, f32[2,4096]{1,0:T(2,128)S(1)}, u32[]{:S(2)}, u32[]{:S(2)}) collective-permute-start(f32[2,4096]{1,0:T(2,128)S(1)} %pad_maximum_fusion.4), channel_id=1, source_target_pairs={{0,32},{8,40},{16,48},{24,56},{32,64},{40,72},{48,80},{56,88},{64,... | collective-permute-start | bytes 98312 | tf_op jit(solution)/shard_map/ppermute | solution.py:46
  162.4 5.4 %collective-permute-start.21 = (f32[2,4096]{1,0:T(2,128)S(1)}, f32[2,4096]{1,0:T(2,128)S(1)}, u32[]{:S(2)}, u32[]{:S(2)}) collective-permute-start(f32[2,4096]{1,0:T(2,128)S(1)} %pad_maximum_fusion.4), channel_id=1, source_target_pairs={{0,64},{8,72},{16,80},{24,88},{32,96},{40,104},{48,112},{56,120},{... | collective-permute-start | bytes 98312 | tf_op jit(solution)/shard_map/ppermute | solution.py:46
  164.7 3.9 %collective-permute-start.22 = (f32[2,4096]{1,0:T(2,128)S(1)}, f32[2,4096]{1,0:T(2,128)S(1)}, u32[]{:S(2)}, u32[]{:S(2)}) collective-permute-start(f32[2,4096]{1,0:T(2,128)S(1)} %pad_maximum_fusion.4), channel_id=1, source_target_pairs={{0,96},{8,104},{16,112},{24,120},{32,0},{40,8},{48,16},{56,24},{64... | collective-permute-start | bytes 98312 | tf_op jit(solution)/shard_map/ppermute | solution.py:46
  179.9 1.3 collective-permute-start.23
  181.2 5.0 %collective-permute-start.24 = (f32[2,2048]{1,0:T(2,128)S(1)}, f32[2,2048]{1,0:T(2,128)S(1)}, u32[]{:S(2)}, u32[]{:S(2)}) collective-permute-start(f32[2,2048]{1,0:T(2,128)S(1)} %pad_maximum_fusion.12), channel_id=1, source_target_pairs={{0,2},{1,3},{2,4},{3,5},{4,6},{5,7},{6,0},{7,1},{8,10},{9,11},{10,... | collective-permute-start | bytes 49160 | tf_op jit(solution)/shard_map/ppermute | solution.py:46
  181.4 5.9 %collective-permute-start.25 = (f32[2,2048]{1,0:T(2,128)S(1)}, f32[2,2048]{1,0:T(2,128)S(1)}, u32[]{:S(2)}, u32[]{:S(2)}) collective-permute-start(f32[2,2048]{1,0:T(2,128)S(1)} %pad_maximum_fusion.12), channel_id=1, source_target_pairs={{0,4},{1,5},{2,6},{3,7},{4,0},{5,1},{6,2},{7,3},{8,12},{9,13},{10,... | collective-permute-start | bytes 49160 | tf_op jit(solution)/shard_map/ppermute | solution.py:46
  185.4 3.7 %collective-permute-start.26 = (f32[2,2048]{1,0:T(2,128)S(1)}, f32[2,2048]{1,0:T(2,128)S(1)}, u32[]{:S(2)}, u32[]{:S(2)}) collective-permute-start(f32[2,2048]{1,0:T(2,128)S(1)} %pad_maximum_fusion.12), channel_id=1, source_target_pairs={{0,6},{1,7},{2,0},{3,1},{4,2},{5,3},{6,4},{7,5},{8,14},{9,15},{10,... | collective-permute-start | bytes 49160 | tf_op jit(solution)/shard_map/ppermute | solution.py:46
  201.6 5.2 %collective-permute-start.27 = (f32[2,4096]{1,0:T(2,128)S(1)}, f32[2,4096]{1,0:T(2,128)S(1)}, u32[]{:S(2)}, u32[]{:S(2)}) collective-permute-start(f32[2,4096]{1,0:T(2,128)S(1)} %pad_maximum_fusion.5), channel_id=1, source_target_pairs={{0,8},{8,16},{16,24},{24,0},{32,40},{40,48},{48,56},{56,32},{64,72... | collective-permute-start | bytes 98312 | tf_op jit(solution)/shard_map/ppermute | solution.py:46
  203.4 5.4 %collective-permute-start.28 = (f32[2,4096]{1,0:T(2,128)S(1)}, f32[2,4096]{1,0:T(2,128)S(1)}, u32[]{:S(2)}, u32[]{:S(2)}) collective-permute-start(f32[2,4096]{1,0:T(2,128)S(1)} %pad_maximum_fusion.5), channel_id=1, source_target_pairs={{0,16},{8,24},{16,0},{24,8},{32,48},{40,56},{48,32},{56,40},{64,80... | collective-permute-start | bytes 98312 | tf_op jit(solution)/shard_map/ppermute | solution.py:46
  206.0 3.9 %collective-permute-start.29 = (f32[2,4096]{1,0:T(2,128)S(1)}, f32[2,4096]{1,0:T(2,128)S(1)}, u32[]{:S(2)}, u32[]{:S(2)}) collective-permute-start(f32[2,4096]{1,0:T(2,128)S(1)} %pad_maximum_fusion.5), channel_id=1, source_target_pairs={{0,24},{8,0},{16,8},{24,16},{32,56},{40,32},{48,40},{56,48},{64,88... | collective-permute-start | bytes 98312 | tf_op jit(solution)/shard_map/ppermute | solution.py:46
  210.1 5.2 %collective-permute-start.30 = (f32[2,4096]{1,0:T(2,128)S(1)}, f32[2,4096]{1,0:T(2,128)S(1)}, u32[]{:S(2)}, u32[]{:S(2)}) collective-permute-start(f32[2,4096]{1,0:T(2,128)S(1)} %pad_maximum_fusion.6), channel_id=1, source_target_pairs={{0,32},{8,40},{16,48},{24,56},{32,64},{40,72},{48,80},{56,88},{64,... | collective-permute-start | bytes 98312 | tf_op jit(solution)/shard_map/ppermute | solution.py:46
  211.6 5.4 %collective-permute-start.31 = (f32[2,4096]{1,0:T(2,128)S(1)}, f32[2,4096]{1,0:T(2,128)S(1)}, u32[]{:S(2)}, u32[]{:S(2)}) collective-permute-start(f32[2,4096]{1,0:T(2,128)S(1)} %pad_maximum_fusion.6), channel_id=1, source_target_pairs={{0,64},{8,72},{16,80},{24,88},{32,96},{40,104},{48,112},{56,120},{... | collective-permute-start | bytes 98312 | tf_op jit(solution)/shard_map/ppermute | solution.py:46
  214.3 4.1 %collective-permute-start.32 = (f32[2,4096]{1,0:T(2,128)S(1)}, f32[2,4096]{1,0:T(2,128)S(1)}, u32[]{:S(2)}, u32[]{:S(2)}) collective-permute-start(f32[2,4096]{1,0:T(2,128)S(1)} %pad_maximum_fusion.6), channel_id=1, source_target_pairs={{0,96},{8,104},{16,112},{24,120},{32,0},{40,8},{48,16},{56,24},{64... | collective-permute-start | bytes 98312 | tf_op jit(solution)/shard_map/ppermute | solution.py:46
  229.7 1.3 collective-permute-start.33
  231.0 5.0 %collective-permute-start.34 = (f32[2,2048]{1,0:T(2,128)S(1)}, f32[2,2048]{1,0:T(2,128)S(1)}, u32[]{:S(2)}, u32[]{:S(2)}) collective-permute-start(f32[2,2048]{1,0:T(2,128)S(1)} %pad_maximum_fusion.14), channel_id=1, source_target_pairs={{0,2},{1,3},{2,4},{3,5},{4,6},{5,7},{6,0},{7,1},{8,10},{9,11},{10,... | collective-permute-start | bytes 49160 | tf_op jit(solution)/shard_map/ppermute | solution.py:46
  231.1 5.3 %collective-permute-start.35 = (f32[2,2048]{1,0:T(2,128)S(1)}, f32[2,2048]{1,0:T(2,128)S(1)}, u32[]{:S(2)}, u32[]{:S(2)}) collective-permute-start(f32[2,2048]{1,0:T(2,128)S(1)} %pad_maximum_fusion.14), channel_id=1, source_target_pairs={{0,4},{1,5},{2,6},{3,7},{4,0},{5,1},{6,2},{7,3},{8,12},{9,13},{10,... | collective-permute-start | bytes 49160 | tf_op jit(solution)/shard_map/ppermute | solution.py:46
  233.8 3.7 %collective-permute-start.36 = (f32[2,2048]{1,0:T(2,128)S(1)}, f32[2,2048]{1,0:T(2,128)S(1)}, u32[]{:S(2)}, u32[]{:S(2)}) collective-permute-start(f32[2,2048]{1,0:T(2,128)S(1)} %pad_maximum_fusion.14), channel_id=1, source_target_pairs={{0,6},{1,7},{2,0},{3,1},{4,2},{5,3},{6,4},{7,5},{8,14},{9,15},{10,... | collective-permute-start | bytes 49160 | tf_op jit(solution)/shard_map/ppermute | solution.py:46
  237.6 4.8 %copy-start.3 = (f32[2048]{0:T(1024)}, f32[2048]{0:T(1024)S(1)}, u32[]{:S(2)}) copy-start(f32[2048]{0:T(1024)S(1)} %multiply_subtract_fusion.3) | copy-start | bytes 24580
  250.0 5.2 %collective-permute-start.37 = (f32[2,4096]{1,0:T(2,128)S(1)}, f32[2,4096]{1,0:T(2,128)S(1)}, u32[]{:S(2)}, u32[]{:S(2)}) collective-permute-start(f32[2,4096]{1,0:T(2,128)S(1)} %pad_maximum_fusion.7), channel_id=1, source_target_pairs={{0,8},{8,16},{16,24},{24,0},{32,40},{40,48},{48,56},{56,32},{64,72... | collective-permute-start | bytes 98312 | tf_op jit(solution)/shard_map/ppermute | solution.py:46
  250.1 5.5 %collective-permute-start.38 = (f32[2,4096]{1,0:T(2,128)S(1)}, f32[2,4096]{1,0:T(2,128)S(1)}, u32[]{:S(2)}, u32[]{:S(2)}) collective-permute-start(f32[2,4096]{1,0:T(2,128)S(1)} %pad_maximum_fusion.7), channel_id=1, source_target_pairs={{0,16},{8,24},{16,0},{24,8},{32,48},{40,56},{48,32},{56,40},{64,80... | collective-permute-start | bytes 98312 | tf_op jit(solution)/shard_map/ppermute | solution.py:46
  252.8 3.9 %collective-permute-start.39 = (f32[2,4096]{1,0:T(2,128)S(1)}, f32[2,4096]{1,0:T(2,128)S(1)}, u32[]{:S(2)}, u32[]{:S(2)}) collective-permute-start(f32[2,4096]{1,0:T(2,128)S(1)} %pad_maximum_fusion.7), channel_id=1, source_target_pairs={{0,24},{8,0},{16,8},{24,16},{32,56},{40,32},{48,40},{56,48},{64,88... | collective-permute-start | bytes 98312 | tf_op jit(solution)/shard_map/ppermute | solution.py:46
  257.0 5.2 %collective-permute-start.40 = (f32[2,4096]{1,0:T(2,128)S(1)}, f32[2,4096]{1,0:T(2,128)S(1)}, u32[]{:S(2)}, u32[]{:S(2)}) collective-permute-start(f32[2,4096]{1,0:T(2,128)S(1)} %pad_maximum_fusion.8), channel_id=1, source_target_pairs={{0,32},{8,40},{16,48},{24,56},{32,64},{40,72},{48,80},{56,88},{64,... | collective-permute-start | bytes 98312 | tf_op jit(solution)/shard_map/ppermute | solution.py:46
  257.1 5.5 %collective-permute-start.41 = (f32[2,4096]{1,0:T(2,128)S(1)}, f32[2,4096]{1,0:T(2,128)S(1)}, u32[]{:S(2)}, u32[]{:S(2)}) collective-permute-start(f32[2,4096]{1,0:T(2,128)S(1)} %pad_maximum_fusion.8), channel_id=1, source_target_pairs={{0,64},{8,72},{16,80},{24,88},{32,96},{40,104},{48,112},{56,120},{... | collective-permute-start | bytes 98312 | tf_op jit(solution)/shard_map/ppermute | solution.py:46
  259.8 3.9 %collective-permute-start.42 = (f32[2,4096]{1,0:T(2,128)S(1)}, f32[2,4096]{1,0:T(2,128)S(1)}, u32[]{:S(2)}, u32[]{:S(2)}) collective-permute-start(f32[2,4096]{1,0:T(2,128)S(1)} %pad_maximum_fusion.8), channel_id=1, source_target_pairs={{0,96},{8,104},{16,112},{24,120},{32,0},{40,8},{48,16},{56,24},{64... | collective-permute-start | bytes 98312 | tf_op jit(solution)/shard_map/ppermute | solution.py:46
Sparse Core Ops, SparseCore 0:
  10.1 53.2 all-gather.1

commit v11 on v10

--- a/solution.py
+++ b/solution.py
@@ -106,7 +106,7 @@
     all_passages = passages.shape[0] * row_count * col_count
     query_block = gather_col(queries)
     rows = passages.shape[0]
-    split = rows - rows // 16
+    split = rows - (rows * 3) // 32
     passage_block = jnp.concatenate(
         [lax.all_gather(passages[:split], "row", axis=0, tiled=True), gather_row(passages[split:])], axis=0
     )

time: 277 us -> 271 us (0.978); the launches traced: 273 us -> 271 us
  local copies, waits for them, and re-layouts: 18.4 us -> 15.6 us
  transfers between devices with their start and end apart: 44 -> 44, of which waited for: 35 -> 36; matrix products, arithmetic and copies ran while one was open for 2% -> 1% of each run, Pallas kernels for 0% -> 0%
where the time goes in v11:
time: 271 us
  other arithmetic  85.2 us (31%)
  starting transfers between devices  60.4 us (22%)
  waiting for transfers between devices  59 us (22%)
  matrix products  34.8 us (13%)
  local copies, waits for them, and re-layouts  15.6 us (6%)
  between operations  15.5 us (6%)
    ppermute x30, starting transfers between devices, combine_over(): lax.ppermute(packed, axis, digit_partners(axis, size, stride, width, k))  41 us
    dot_general x1, matrix products, inner_costs(): lax.dot_general(left, right, (((1,), (1,)), ((), ())), precision=lax.Prec...  34.8 us
    reduce_sum x3, other arithmetic, logsum_col(): totals = jnp.sum(jnp.exp(gaps / scale - peak[:, None]), axis=1)  30.6 us
    ppermute x30, waiting for transfers between devices, combine_over(): lax.ppermute(packed, axis, digit_partners(axis, size, stride, width, k))  29 us
    reduce_max x3, other arithmetic, logsum_row(): peak = jnp.max(gaps, axis=0) / scale  23.2 us
    reduce_sum x3, other arithmetic, logsum_row(): totals = jnp.sum(jnp.exp(gaps / scale - peak[None, :]), axis=0)  22.9 us
    ppermute x13, waiting for transfers between devices, exchange(): lax.ppermute(x, axis, digit_partners(axis, size, stride, width, k))  21.9 us
    ppermute x13, starting transfers between devices, exchange(): lax.ppermute(x, axis, digit_partners(axis, size, stride, width, k))  19.3 us
  transfers between devices with their start and end apart: 44, of which 36 were waited for; matrix products, arithmetic and copies ran while one was open for 1% of the time, Pallas kernels for 0%

profile of v11, /device:TPU:0, one launch (start us, length us, event | category | flops | bytes accessed | tf_op | source)
XLA Modules:
  0.0 270.5 jit_solution(14408212427115175500)
XLA Ops:
  7.2 1.6 slice.222
  9.6 1.7 collective-permute-start.7
  11.3 2.9 %collective-permute-start.8 = (f32[24,256]{1,0:T(8,128)S(1)}, f32[24,256]{1,0:T(8,128)S(1)}, u32[]{:S(2)}, u32[]{:S(2)}) collective-permute-start(f32[24,256]{1,0:T(8,128)S(1)} %get-tuple-element.7), channel_id=1, source_target_pairs={{0,16},{8,24},{16,0},{24,8},{32,48},{40,56},{48,32},{56,40},{64,80... | collective-permute-start | bytes 73736 | tf_op jit(solution)/shard_map/ppermute | solution.py:35
  15.6 1.5 collective-permute-start.1
  18.1 2.0 collective-permute-start.10
  20.1 3.6 %collective-permute-start.11 = (f32[96,256]{1,0:T(8,128)S(1)}, f32[96,256]{1,0:T(8,128)S(1)}, u32[]{:S(2)}, u32[]{:S(2)}) collective-permute-start(f32[96,256]{1,0:T(8,128)S(1)} %get-tuple-element.11), channel_id=1, source_target_pairs={{0,64},{8,72},{16,80},{24,88},{32,96},{40,104},{48,112},{56,120},{... | collective-permute-start | bytes 294920 | tf_op jit(solution)/shard_map/ppermute | solution.py:35
  27.0 3.1 %collective-permute-done.11 = f32[96,256]{1,0:T(8,128)S(1)} collective-permute-done((f32[96,256]{1,0:T(8,128)S(1)}, f32[96,256]{1,0:T(8,128)S(1)}, u32[]{:S(2)}, u32[]{:S(2)}) %collective-permute-start.11) | collective-permute-done | bytes 98336 | tf_op jit(solution)/shard_map/ppermute | solution.py:35
  32.7 1.6 collective-permute-start.5
  35.1 1.8 collective-permute-done.2
  36.9 5.7 %collective-permute-done.3 = f32[256,256]{1,0:T(8,128)S(1)} collective-permute-done((f32[256,256]{1,0:T(8,128)}, f32[256,256]{1,0:T(8,128)S(1)}, u32[]{:S(2)}, u32[]{:S(2)}) %collective-permute-start.3) | collective-permute-done | bytes 262176 | tf_op jit(solution)/shard_map/ppermute | solution.py:35
  42.6 2.7 %collective-permute-done.4 = f32[256,256]{1,0:T(8,128)S(1)} collective-permute-done((f32[256,256]{1,0:T(8,128)}, f32[256,256]{1,0:T(8,128)S(1)}, u32[]{:S(2)}, u32[]{:S(2)}) %collective-permute-start.4) | collective-permute-done | bytes 262176 | tf_op jit(solution)/shard_map/ppermute | solution.py:35
  45.4 5.8 %collective-permute-done.5 = f32[256,256]{1,0:T(8,128)S(1)} collective-permute-done((f32[256,256]{1,0:T(8,128)}, f32[256,256]{1,0:T(8,128)S(1)}, u32[]{:S(2)}, u32[]{:S(2)}) %collective-permute-start.5) | collective-permute-done | bytes 262176 | tf_op jit(solution)/shard_map/ppermute | solution.py:35
  51.2 1.8 collective-permute-done.6
  55.0 8.1 %all-gather.2.cloned.1.call-done = f32[3712,256]{1,0:T(8,128)} async-done(((f32[232,256]{1,0:T(8,128)}), f32[3712,256]{1,0:T(8,128)}) %all-gather.2.cloned.1.call-update) | async-done | bytes 3801104 | tf_op jit(solution)/shard_map/all_gather | solution.py:111
  63.0 2.3 constant_dynamic-update-slice_fusion
  67.0 34.8 %subtract_reduce_fusion.5 = (f32[2048]{0:T(1024)S(1)}, f32[2048,4096]{1,0:T(8,128)}) fusion(f32[2048,256]{1,0:T(8,128)S(1)} %copy-done.2, f32[4096,256]{1,0:T(8,128)S(1)} %bitcast_dynamic-update-slice_fusion.16, f32[4096]{0:T(1024)S(1)} %multiply_reduce_fusion, f32[2048]{0:T(1024)S(1)} %multiply_reduce_fusion.1), kind=kOutput, calls=%fused_computation.12 | convolution fusion | flops 25811744768 | bytes 39878656 | tf_op jit(solution)/shard_map/dot_general | solution.py:14
  101.8 14.5 %exponential_reduce_fusion.5 = f32[2048]{0:T(1024)S(1)} fusion(f32[2048,4096]{1,0:T(8,128)} %get-tuple-element.59, f32[2048]{0:T(1024)S(1)} %broadcast_divide_fusion.5, f32[]{:T(128)} %bitcast), kind=kLoop, calls=%fused_computation.5 | loop fusion | flops 33552384 | bytes 33570820 | tf_op jit(solution)/shard_map/reduce_sum | solution.py:78
  117.7 1.5 collective-permute-start.14
  119.2 2.7 collective-permute-start.15
  121.9 1.5 collective-permute-start.16
  125.7 13.8 %subtract_reduce_fusion.4 = f32[4096]{0:T(1024)S(1)} fusion(f32[2048,4096]{1,0:T(8,128)} %get-tuple-element.59, f32[2048]{0:T(1024)S(1)} %multiply_subtract_fusion.6), kind=kLoop, calls=%fused_computation.11 | loop fusion | flops 16773120 | bytes 33579008 | tf_op jit(solution)/shard_map/reduce_max | solution.py:83
  139.6 6.3 %copy-done = f32[2048,4096]{1,0:T(8,128)S(1)} copy-done((f32[2048,4096]{1,0:T(8,128)S(1)}, f32[2048,4096]{1,0:T(8,128)}, u32[]{:S(2)}) %copy-start) | copy-done | bytes 33554456
  145.9 7.6 %exponential_reduce_fusion.4 = f32[4096]{0:T(1024)S(1)} fusion(f32[2048,4096]{1,0:T(8,128)S(1)} %copy-done, f32[4096]{0:T(1024)S(1)} %broadcast_divide_fusion.2, f32[2048]{0:T(1024)S(1)} %multiply_subtract_fusion.6, f32[]{:T(128)} %bitcast), kind=kLoop, calls=%fused_computation.4 | loop fusion | flops 33550336 | bytes 33595396 | tf_op jit(solution)/shard_map/reduce_sum | solution.py:84
  154.7 2.7 %collective-permute-start.18 = (f32[2,4096]{1,0:T(2,128)S(1)}, f32[2,4096]{1,0:T(2,128)S(1)}, u32[]{:S(2)}, u32[]{:S(2)}) collective-permute-start(f32[2,4096]{1,0:T(2,128)S(1)} %pad_maximum_fusion.3), channel_id=1, source_target_pairs={{0,16},{8,24},{16,0},{24,8},{32,48},{40,56},{48,32},{56,40},{64,80... | collective-permute-start | bytes 98312 | tf_op jit(solution)/shard_map/ppermute | solution.py:46
  157.4 1.4 collective-permute-start.19
  161.7 2.3 collective-permute-start.21
  163.9 1.7 collective-permute-start.22
  168.0 3.0 %subtract_reduce_fusion.3 = f32[2048]{0:T(1024)S(1)} fusion(f32[2048,4096]{1,0:T(8,128)S(1)} %copy-done, f32[4096]{0:T(1024)S(1)} %bitcast.123), kind=kLoop, calls=%fused_computation.10 | loop fusion | flops 16775168 | bytes 33579008 | tf_op jit(solution)/shard_map/reduce_max | solution.py:77
  171.0 8.0 %exponential_reduce_fusion.3 = f32[2048]{0:T(1024)S(1)} fusion(f32[2048,4096]{1,0:T(8,128)S(1)} %copy-done, f32[2048]{0:T(1024)S(1)} %broadcast_divide_fusion.4, f32[4096]{0:T(1024)S(1)} %bitcast.124, f32[]{:T(128)} %bitcast), kind=kLoop, calls=%fused_computation.3 | loop fusion | flops 33552384 | bytes 33587204 | tf_op jit(solution)/shard_map/reduce_sum | solution.py:78
  180.8 3.8 %collective-permute-start.25 = (f32[2,2048]{1,0:T(2,128)S(1)}, f32[2,2048]{1,0:T(2,128)S(1)}, u32[]{:S(2)}, u32[]{:S(2)}) collective-permute-start(f32[2,2048]{1,0:T(2,128)S(1)} %pad_maximum_fusion.12), channel_id=1, source_target_pairs={{0,4},{1,5},{2,6},{3,7},{4,0},{5,1},{6,2},{7,3},{8,12},{9,13},{10,... | collective-permute-start | bytes 49160 | tf_op jit(solution)/shard_map/ppermute | solution.py:46
  186.5 1.8 collective-permute-done.26
  188.4 4.7 %subtract_reduce_fusion.2 = f32[4096]{0:T(1024)S(1)} fusion(f32[2048,4096]{1,0:T(8,128)S(1)} %copy-done, f32[2048]{0:T(1024)S(1)} %multiply_subtract_fusion.5), kind=kLoop, calls=%fused_computation.9 | loop fusion | flops 16773120 | bytes 33579008 | tf_op jit(solution)/shard_map/reduce_max | solution.py:83
  193.2 7.6 %exponential_reduce_fusion.2 = f32[4096]{0:T(1024)S(1)} fusion(f32[2048,4096]{1,0:T(8,128)S(1)} %copy-done, f32[4096]{0:T(1024)S(1)} %broadcast_divide_fusion.1, f32[2048]{0:T(1024)S(1)} %multiply_subtract_fusion.5, f32[]{:T(128)} %bitcast), kind=kLoop, calls=%fused_computation.2 | loop fusion | flops 33550336 | bytes 33595396 | tf_op jit(solution)/shard_map/reduce_sum | solution.py:84
  200.9 1.7 collective-permute-start.27
  202.6 2.7 collective-permute-start.28
  206.1 2.0 collective-permute-done.28
  209.4 1.5 collective-permute-start.30
  210.9 2.7 collective-permute-start.31
  214.6 1.7 collective-permute-done.31
  217.6 3.0 %subtract_reduce_fusion.1 = f32[2048]{0:T(1024)S(1)} fusion(f32[2048,4096]{1,0:T(8,128)S(1)} %copy-done, f32[4096]{0:T(1024)S(1)} %bitcast.125), kind=kLoop, calls=%fused_computation.8 | loop fusion | flops 16775168 | bytes 33579008 | tf_op jit(solution)/shard_map/reduce_max | solution.py:77
  220.6 8.0 %exponential_reduce_fusion.1 = f32[2048]{0:T(1024)S(1)} fusion(f32[2048,4096]{1,0:T(8,128)S(1)} %copy-done, f32[2048]{0:T(1024)S(1)} %broadcast_divide_fusion.3, f32[4096]{0:T(1024)S(1)} %bitcast.126, f32[]{:T(128)} %bitcast), kind=kLoop, calls=%fused_computation.1 | loop fusion | flops 33552384 | bytes 33587204 | tf_op jit(solution)/shard_map/reduce_sum | solution.py:78
  230.1 2.7 collective-permute-start.35
  232.8 1.5 collective-permute-start.36
  236.6 4.7 %subtract_reduce_fusion = f32[4096]{0:T(1024)S(1)} fusion(f32[2048,4096]{1,0:T(8,128)S(1)} %copy-done, f32[2048]{0:T(1024)S(1)} %multiply_subtract_fusion.4), kind=kLoop, calls=%fused_computation.7 | loop fusion | flops 16773120 | bytes 33579008 | tf_op jit(solution)/shard_map/reduce_max | solution.py:83
  241.4 7.6 %exponential_reduce_fusion = f32[4096]{0:T(1024)S(1)} fusion(f32[2048,4096]{1,0:T(8,128)S(1)} %copy-done, f32[4096]{0:T(1024)S(1)} %broadcast_divide_fusion, f32[2048]{0:T(1024)S(1)} %multiply_subtract_fusion.4, f32[]{:T(128)} %bitcast), kind=kLoop, calls=%fused_computation | loop fusion | flops 33550336 | bytes 33595396 | tf_op jit(solution)/shard_map/reduce_sum | solution.py:84
  249.2 2.7 collective-permute-start.38
  251.8 1.4 collective-permute-start.39
  256.1 2.7 %collective-permute-start.41 = (f32[2,4096]{1,0:T(2,128)S(1)}, f32[2,4096]{1,0:T(2,128)S(1)}, u32[]{:S(2)}, u32[]{:S(2)}) collective-permute-start(f32[2,4096]{1,0:T(2,128)S(1)} %pad_maximum_fusion.8), channel_id=1, source_target_pairs={{0,64},{8,72},{16,80},{24,88},{32,96},{40,104},{48,112},{56,120},{... | collective-permute-start | bytes 98312 | tf_op jit(solution)/shard_map/ppermute | solution.py:46
  (137 shorter events, 42.2 us)
Async XLA Ops:
  7.2 55.9 %all-gather.2.cloned.1.call-start = ((), (), s32[]{:S(2)}) async-start(), calls=%async_computation | async-start | bytes 4038656 | tf_op jit(solution)/shard_map/all_gather | solution.py:111
  9.6 7.4 %collective-permute-start.7 = (f32[24,256]{1,0:T(8,128)S(1)}, f32[24,256]{1,0:T(8,128)S(1)}, u32[]{:S(2)}, u32[]{:S(2)}) collective-permute-start(f32[24,256]{1,0:T(8,128)S(1)} %get-tuple-element.7), channel_id=1, source_target_pairs={{0,8},{8,16},{16,24},{24,0},{32,40},{40,48},{48,56},{56,32},{64,72... | collective-permute-start | bytes 73736 | tf_op jit(solution)/shard_map/ppermute | solution.py:35
  11.3 5.8 %collective-permute-start.8 = (f32[24,256]{1,0:T(8,128)S(1)}, f32[24,256]{1,0:T(8,128)S(1)}, u32[]{:S(2)}, u32[]{:S(2)}) collective-permute-start(f32[24,256]{1,0:T(8,128)S(1)} %get-tuple-element.7), channel_id=1, source_target_pairs={{0,16},{8,24},{16,0},{24,8},{32,48},{40,56},{48,32},{56,40},{64,80... | collective-permute-start | bytes 73736 | tf_op jit(solution)/shard_map/ppermute | solution.py:35
  14.2 3.8 %collective-permute-start.9 = (f32[24,256]{1,0:T(8,128)S(1)}, f32[24,256]{1,0:T(8,128)S(1)}, u32[]{:S(2)}, u32[]{:S(2)}) collective-permute-start(f32[24,256]{1,0:T(8,128)S(1)} %get-tuple-element.7), channel_id=1, source_target_pairs={{0,24},{8,0},{16,8},{24,16},{32,56},{40,32},{48,40},{56,48},{64,88... | collective-permute-start | bytes 73736 | tf_op jit(solution)/shard_map/ppermute | solution.py:35
  15.6 17.1 %collective-permute-start = (f32[256,256]{1,0:T(8,128)}, f32[256,256]{1,0:T(8,128)S(1)}, u32[]{:S(2)}, u32[]{:S(2)}) collective-permute-start(f32[256,256]{1,0:T(8,128)} %param.3), channel_id=1, source_target_pairs={{0,1},{1,2},{2,3},{3,4},{4,5},{5,6},{6,7},{7,0},{8,9},{9,10},{10,1... | collective-permute-start | bytes 786440 | tf_op jit(solution)/shard_map/ppermute | solution.py:35
  15.6 18.7 %collective-permute-start.1 = (f32[256,256]{1,0:T(8,128)}, f32[256,256]{1,0:T(8,128)S(1)}, u32[]{:S(2)}, u32[]{:S(2)}) collective-permute-start(f32[256,256]{1,0:T(8,128)} %param.3), channel_id=1, source_target_pairs={{0,2},{1,3},{2,4},{3,5},{4,6},{5,7},{6,0},{7,1},{8,10},{9,11},{10,... | collective-permute-start | bytes 786440 | tf_op jit(solution)/shard_map/ppermute | solution.py:35
  18.1 8.5 %collective-permute-start.10 = (f32[96,256]{1,0:T(8,128)S(1)}, f32[96,256]{1,0:T(8,128)S(1)}, u32[]{:S(2)}, u32[]{:S(2)}) collective-permute-start(f32[96,256]{1,0:T(8,128)S(1)} %get-tuple-element.11), channel_id=1, source_target_pairs={{0,32},{8,40},{16,48},{24,56},{32,64},{40,72},{48,80},{56,88},{64,... | collective-permute-start | bytes 294920 | tf_op jit(solution)/shard_map/ppermute | solution.py:35
  20.1 10.0 %collective-permute-start.11 = (f32[96,256]{1,0:T(8,128)S(1)}, f32[96,256]{1,0:T(8,128)S(1)}, u32[]{:S(2)}, u32[]{:S(2)}) collective-permute-start(f32[96,256]{1,0:T(8,128)S(1)} %get-tuple-element.11), channel_id=1, source_target_pairs={{0,64},{8,72},{16,80},{24,88},{32,96},{40,104},{48,112},{56,120},{... | collective-permute-start | bytes 294920 | tf_op jit(solution)/shard_map/ppermute | solution.py:35
  23.7 7.8 %collective-permute-start.12 = (f32[96,256]{1,0:T(8,128)S(1)}, f32[96,256]{1,0:T(8,128)S(1)}, u32[]{:S(2)}, u32[]{:S(2)}) collective-permute-start(f32[96,256]{1,0:T(8,128)S(1)} %get-tuple-element.11), channel_id=1, source_target_pairs={{0,96},{8,104},{16,112},{24,120},{32,0},{40,8},{48,16},{56,24},{64... | collective-permute-start | bytes 294920 | tf_op jit(solution)/shard_map/ppermute | solution.py:35
  26.6 10.3 %collective-permute-start.2 = (f32[256,256]{1,0:T(8,128)}, f32[256,256]{1,0:T(8,128)S(1)}, u32[]{:S(2)}, u32[]{:S(2)}) collective-permute-start(f32[256,256]{1,0:T(8,128)} %param.3), channel_id=1, source_target_pairs={{0,3},{1,4},{2,5},{3,6},{4,7},{5,0},{6,1},{7,2},{8,11},{9,12},{10,... | collective-permute-start | bytes 786440 | tf_op jit(solution)/shard_map/ppermute | solution.py:35
  30.1 12.5 %collective-permute-start.3 = (f32[256,256]{1,0:T(8,128)}, f32[256,256]{1,0:T(8,128)S(1)}, u32[]{:S(2)}, u32[]{:S(2)}) collective-permute-start(f32[256,256]{1,0:T(8,128)} %param.3), channel_id=1, source_target_pairs={{0,4},{1,5},{2,6},{3,7},{4,0},{5,1},{6,2},{7,3},{8,12},{9,13},{10,... | collective-permute-start | bytes 786440 | tf_op jit(solution)/shard_map/ppermute | solution.py:35
  31.5 13.8 %collective-permute-start.4 = (f32[256,256]{1,0:T(8,128)}, f32[256,256]{1,0:T(8,128)S(1)}, u32[]{:S(2)}, u32[]{:S(2)}) collective-permute-start(f32[256,256]{1,0:T(8,128)} %param.3), channel_id=1, source_target_pairs={{0,5},{1,6},{2,7},{3,0},{4,1},{5,2},{6,3},{7,4},{8,13},{9,14},{10,... | collective-permute-start | bytes 786440 | tf_op jit(solution)/shard_map/ppermute | solution.py:35
  32.7 18.5 %collective-permute-start.5 = (f32[256,256]{1,0:T(8,128)}, f32[256,256]{1,0:T(8,128)S(1)}, u32[]{:S(2)}, u32[]{:S(2)}) collective-permute-start(f32[256,256]{1,0:T(8,128)} %param.3), channel_id=1, source_target_pairs={{0,6},{1,7},{2,0},{3,1},{4,2},{5,3},{6,4},{7,5},{8,14},{9,15},{10,... | collective-permute-start | bytes 786440 | tf_op jit(solution)/shard_map/ppermute | solution.py:35
  34.3 18.7 %collective-permute-start.6 = (f32[256,256]{1,0:T(8,128)}, f32[256,256]{1,0:T(8,128)S(1)}, u32[]{:S(2)}, u32[]{:S(2)}) collective-permute-start(f32[256,256]{1,0:T(8,128)} %param.3), channel_id=1, source_target_pairs={{0,7},{1,0},{2,1},{3,2},{4,3},{5,4},{6,5},{7,6},{8,15},{9,8},{10,9... | collective-permute-start | bytes 786440 | tf_op jit(solution)/shard_map/ppermute | solution.py:35
  53.3 1.3 copy-start.1
  65.4 1.6 copy-start.2
  116.4 1.3 collective-permute-start.13
  117.7 5.7 %collective-permute-start.14 = (f32[2,2048]{1,0:T(2,128)S(1)}, f32[2,2048]{1,0:T(2,128)S(1)}, u32[]{:S(2)}, u32[]{:S(2)}) collective-permute-start(f32[2,2048]{1,0:T(2,128)S(1)} %pad_maximum_fusion.10), channel_id=1, source_target_pairs={{0,2},{1,3},{2,4},{3,5},{4,6},{5,7},{6,0},{7,1},{8,10},{9,11},{10,... | collective-permute-start | bytes 49160 | tf_op jit(solution)/shard_map/ppermute | solution.py:46
  119.2 5.2 %collective-permute-start.15 = (f32[2,2048]{1,0:T(2,128)S(1)}, f32[2,2048]{1,0:T(2,128)S(1)}, u32[]{:S(2)}, u32[]{:S(2)}) collective-permute-start(f32[2,2048]{1,0:T(2,128)S(1)} %pad_maximum_fusion.10), channel_id=1, source_target_pairs={{0,4},{1,5},{2,6},{3,7},{4,0},{5,1},{6,2},{7,3},{8,12},{9,13},{10,... | collective-permute-start | bytes 49160 | tf_op jit(solution)/shard_map/ppermute | solution.py:46
  121.9 3.7 %collective-permute-start.16 = (f32[2,2048]{1,0:T(2,128)S(1)}, f32[2,2048]{1,0:T(2,128)S(1)}, u32[]{:S(2)}, u32[]{:S(2)}) collective-permute-start(f32[2,2048]{1,0:T(2,128)S(1)} %pad_maximum_fusion.10), channel_id=1, source_target_pairs={{0,6},{1,7},{2,0},{3,1},{4,2},{5,3},{6,4},{7,5},{8,14},{9,15},{10,... | collective-permute-start | bytes 49160 | tf_op jit(solution)/shard_map/ppermute | solution.py:46
  125.7 20.2 %copy-start = (f32[2048,4096]{1,0:T(8,128)S(1)}, f32[2048,4096]{1,0:T(8,128)}, u32[]{:S(2)}) copy-start(f32[2048,4096]{1,0:T(8,128)} %get-tuple-element.59) | copy-start | bytes 100663296
  153.6 5.3 %collective-permute-start.17 = (f32[2,4096]{1,0:T(2,128)S(1)}, f32[2,4096]{1,0:T(2,128)S(1)}, u32[]{:S(2)}, u32[]{:S(2)}) collective-permute-start(f32[2,4096]{1,0:T(2,128)S(1)} %pad_maximum_fusion.3), channel_id=1, source_target_pairs={{0,8},{8,16},{16,24},{24,0},{32,40},{40,48},{48,56},{56,32},{64,72... | collective-permute-start | bytes 98312 | tf_op jit(solution)/shard_map/ppermute | solution.py:46
  154.7 5.4 %collective-permute-start.18 = (f32[2,4096]{1,0:T(2,128)S(1)}, f32[2,4096]{1,0:T(2,128)S(1)}, u32[]{:S(2)}, u32[]{:S(2)}) collective-permute-start(f32[2,4096]{1,0:T(2,128)S(1)} %pad_maximum_fusion.3), channel_id=1, source_target_pairs={{0,16},{8,24},{16,0},{24,8},{32,48},{40,56},{48,32},{56,40},{64,80... | collective-permute-start | bytes 98312 | tf_op jit(solution)/shard_map/ppermute | solution.py:46
  157.4 3.9 %collective-permute-start.19 = (f32[2,4096]{1,0:T(2,128)S(1)}, f32[2,4096]{1,0:T(2,128)S(1)}, u32[]{:S(2)}, u32[]{:S(2)}) collective-permute-start(f32[2,4096]{1,0:T(2,128)S(1)} %pad_maximum_fusion.3), channel_id=1, source_target_pairs={{0,24},{8,0},{16,8},{24,16},{32,56},{40,32},{48,40},{56,48},{64,88... | collective-permute-start | bytes 98312 | tf_op jit(solution)/shard_map/ppermute | solution.py:46
  161.5 5.2 %collective-permute-start.20 = (f32[2,4096]{1,0:T(2,128)S(1)}, f32[2,4096]{1,0:T(2,128)S(1)}, u32[]{:S(2)}, u32[]{:S(2)}) collective-permute-start(f32[2,4096]{1,0:T(2,128)S(1)} %pad_maximum_fusion.4), channel_id=1, source_target_pairs={{0,32},{8,40},{16,48},{24,56},{32,64},{40,72},{48,80},{56,88},{64,... | collective-permute-start | bytes 98312 | tf_op jit(solution)/shard_map/ppermute | solution.py:46
  161.7 5.4 %collective-permute-start.21 = (f32[2,4096]{1,0:T(2,128)S(1)}, f32[2,4096]{1,0:T(2,128)S(1)}, u32[]{:S(2)}, u32[]{:S(2)}) collective-permute-start(f32[2,4096]{1,0:T(2,128)S(1)} %pad_maximum_fusion.4), channel_id=1, source_target_pairs={{0,64},{8,72},{16,80},{24,88},{32,96},{40,104},{48,112},{56,120},{... | collective-permute-start | bytes 98312 | tf_op jit(solution)/shard_map/ppermute | solution.py:46
  163.9 3.9 %collective-permute-start.22 = (f32[2,4096]{1,0:T(2,128)S(1)}, f32[2,4096]{1,0:T(2,128)S(1)}, u32[]{:S(2)}, u32[]{:S(2)}) collective-permute-start(f32[2,4096]{1,0:T(2,128)S(1)} %pad_maximum_fusion.4), channel_id=1, source_target_pairs={{0,96},{8,104},{16,112},{24,120},{32,0},{40,8},{48,16},{56,24},{64... | collective-permute-start | bytes 98312 | tf_op jit(solution)/shard_map/ppermute | solution.py:46
  179.1 1.3 collective-permute-start.23
  180.4 5.0 %collective-permute-start.24 = (f32[2,2048]{1,0:T(2,128)S(1)}, f32[2,2048]{1,0:T(2,128)S(1)}, u32[]{:S(2)}, u32[]{:S(2)}) collective-permute-start(f32[2,2048]{1,0:T(2,128)S(1)} %pad_maximum_fusion.12), channel_id=1, source_target_pairs={{0,2},{1,3},{2,4},{3,5},{4,6},{5,7},{6,0},{7,1},{8,10},{9,11},{10,... | collective-permute-start | bytes 49160 | tf_op jit(solution)/shard_map/ppermute | solution.py:46
  180.8 5.7 %collective-permute-start.25 = (f32[2,2048]{1,0:T(2,128)S(1)}, f32[2,2048]{1,0:T(2,128)S(1)}, u32[]{:S(2)}, u32[]{:S(2)}) collective-permute-start(f32[2,2048]{1,0:T(2,128)S(1)} %pad_maximum_fusion.12), channel_id=1, source_target_pairs={{0,4},{1,5},{2,6},{3,7},{4,0},{5,1},{6,2},{7,3},{8,12},{9,13},{10,... | collective-permute-start | bytes 49160 | tf_op jit(solution)/shard_map/ppermute | solution.py:46
  184.6 3.7 %collective-permute-start.26 = (f32[2,2048]{1,0:T(2,128)S(1)}, f32[2,2048]{1,0:T(2,128)S(1)}, u32[]{:S(2)}, u32[]{:S(2)}) collective-permute-start(f32[2,2048]{1,0:T(2,128)S(1)} %pad_maximum_fusion.12), channel_id=1, source_target_pairs={{0,6},{1,7},{2,0},{3,1},{4,2},{5,3},{6,4},{7,5},{8,14},{9,15},{10,... | collective-permute-start | bytes 49160 | tf_op jit(solution)/shard_map/ppermute | solution.py:46
  200.9 5.2 %collective-permute-start.27 = (f32[2,4096]{1,0:T(2,128)S(1)}, f32[2,4096]{1,0:T(2,128)S(1)}, u32[]{:S(2)}, u32[]{:S(2)}) collective-permute-start(f32[2,4096]{1,0:T(2,128)S(1)} %pad_maximum_fusion.5), channel_id=1, source_target_pairs={{0,8},{8,16},{16,24},{24,0},{32,40},{40,48},{48,56},{56,32},{64,72... | collective-permute-start | bytes 98312 | tf_op jit(solution)/shard_map/ppermute | solution.py:46
  202.6 5.4 %collective-permute-start.28 = (f32[2,4096]{1,0:T(2,128)S(1)}, f32[2,4096]{1,0:T(2,128)S(1)}, u32[]{:S(2)}, u32[]{:S(2)}) collective-permute-start(f32[2,4096]{1,0:T(2,128)S(1)} %pad_maximum_fusion.5), channel_id=1, source_target_pairs={{0,16},{8,24},{16,0},{24,8},{32,48},{40,56},{48,32},{56,40},{64,80... | collective-permute-start | bytes 98312 | tf_op jit(solution)/shard_map/ppermute | solution.py:46
  205.3 3.9 %collective-permute-start.29 = (f32[2,4096]{1,0:T(2,128)S(1)}, f32[2,4096]{1,0:T(2,128)S(1)}, u32[]{:S(2)}, u32[]{:S(2)}) collective-permute-start(f32[2,4096]{1,0:T(2,128)S(1)} %pad_maximum_fusion.5), channel_id=1, source_target_pairs={{0,24},{8,0},{16,8},{24,16},{32,56},{40,32},{48,40},{56,48},{64,88... | collective-permute-start | bytes 98312 | tf_op jit(solution)/shard_map/ppermute | solution.py:46
  209.4 5.2 %collective-permute-start.30 = (f32[2,4096]{1,0:T(2,128)S(1)}, f32[2,4096]{1,0:T(2,128)S(1)}, u32[]{:S(2)}, u32[]{:S(2)}) collective-permute-start(f32[2,4096]{1,0:T(2,128)S(1)} %pad_maximum_fusion.6), channel_id=1, source_target_pairs={{0,32},{8,40},{16,48},{24,56},{32,64},{40,72},{48,80},{56,88},{64,... | collective-permute-start | bytes 98312 | tf_op jit(solution)/shard_map/ppermute | solution.py:46
  210.9 5.4 %collective-permute-start.31 = (f32[2,4096]{1,0:T(2,128)S(1)}, f32[2,4096]{1,0:T(2,128)S(1)}, u32[]{:S(2)}, u32[]{:S(2)}) collective-permute-start(f32[2,4096]{1,0:T(2,128)S(1)} %pad_maximum_fusion.6), channel_id=1, source_target_pairs={{0,64},{8,72},{16,80},{24,88},{32,96},{40,104},{48,112},{56,120},{... | collective-permute-start | bytes 98312 | tf_op jit(solution)/shard_map/ppermute | solution.py:46
  213.6 3.9 %collective-permute-start.32 = (f32[2,4096]{1,0:T(2,128)S(1)}, f32[2,4096]{1,0:T(2,128)S(1)}, u32[]{:S(2)}, u32[]{:S(2)}) collective-permute-start(f32[2,4096]{1,0:T(2,128)S(1)} %pad_maximum_fusion.6), channel_id=1, source_target_pairs={{0,96},{8,104},{16,112},{24,120},{32,0},{40,8},{48,16},{56,24},{64... | collective-permute-start | bytes 98312 | tf_op jit(solution)/shard_map/ppermute | solution.py:46
  228.7 1.3 collective-permute-start.33
  230.0 5.0 %collective-permute-start.34 = (f32[2,2048]{1,0:T(2,128)S(1)}, f32[2,2048]{1,0:T(2,128)S(1)}, u32[]{:S(2)}, u32[]{:S(2)}) collective-permute-start(f32[2,2048]{1,0:T(2,128)S(1)} %pad_maximum_fusion.14), channel_id=1, source_target_pairs={{0,2},{1,3},{2,4},{3,5},{4,6},{5,7},{6,0},{7,1},{8,10},{9,11},{10,... | collective-permute-start | bytes 49160 | tf_op jit(solution)/shard_map/ppermute | solution.py:46
  230.1 5.3 %collective-permute-start.35 = (f32[2,2048]{1,0:T(2,128)S(1)}, f32[2,2048]{1,0:T(2,128)S(1)}, u32[]{:S(2)}, u32[]{:S(2)}) collective-permute-start(f32[2,2048]{1,0:T(2,128)S(1)} %pad_maximum_fusion.14), channel_id=1, source_target_pairs={{0,4},{1,5},{2,6},{3,7},{4,0},{5,1},{6,2},{7,3},{8,12},{9,13},{10,... | collective-permute-start | bytes 49160 | tf_op jit(solution)/shard_map/ppermute | solution.py:46
  232.8 3.7 %collective-permute-start.36 = (f32[2,2048]{1,0:T(2,128)S(1)}, f32[2,2048]{1,0:T(2,128)S(1)}, u32[]{:S(2)}, u32[]{:S(2)}) collective-permute-start(f32[2,2048]{1,0:T(2,128)S(1)} %pad_maximum_fusion.14), channel_id=1, source_target_pairs={{0,6},{1,7},{2,0},{3,1},{4,2},{5,3},{6,4},{7,5},{8,14},{9,15},{10,... | collective-permute-start | bytes 49160 | tf_op jit(solution)/shard_map/ppermute | solution.py:46
  236.6 4.8 %copy-start.3 = (f32[2048]{0:T(1024)}, f32[2048]{0:T(1024)S(1)}, u32[]{:S(2)}) copy-start(f32[2048]{0:T(1024)S(1)} %multiply_subtract_fusion.4) | copy-start | bytes 24580
  249.1 5.2 %collective-permute-start.37 = (f32[2,4096]{1,0:T(2,128)S(1)}, f32[2,4096]{1,0:T(2,128)S(1)}, u32[]{:S(2)}, u32[]{:S(2)}) collective-permute-start(f32[2,4096]{1,0:T(2,128)S(1)} %pad_maximum_fusion.7), channel_id=1, source_target_pairs={{0,8},{8,16},{16,24},{24,0},{32,40},{40,48},{48,56},{56,32},{64,72... | collective-permute-start | bytes 98312 | tf_op jit(solution)/shard_map/ppermute | solution.py:46
  249.2 5.5 %collective-permute-start.38 = (f32[2,4096]{1,0:T(2,128)S(1)}, f32[2,4096]{1,0:T(2,128)S(1)}, u32[]{:S(2)}, u32[]{:S(2)}) collective-permute-start(f32[2,4096]{1,0:T(2,128)S(1)} %pad_maximum_fusion.7), channel_id=1, source_target_pairs={{0,16},{8,24},{16,0},{24,8},{32,48},{40,56},{48,32},{56,40},{64,80... | collective-permute-start | bytes 98312 | tf_op jit(solution)/shard_map/ppermute | solution.py:46
  251.8 3.9 %collective-permute-start.39 = (f32[2,4096]{1,0:T(2,128)S(1)}, f32[2,4096]{1,0:T(2,128)S(1)}, u32[]{:S(2)}, u32[]{:S(2)}) collective-permute-start(f32[2,4096]{1,0:T(2,128)S(1)} %pad_maximum_fusion.7), channel_id=1, source_target_pairs={{0,24},{8,0},{16,8},{24,16},{32,56},{40,32},{48,40},{56,48},{64,88... | collective-permute-start | bytes 98312 | tf_op jit(solution)/shard_map/ppermute | solution.py:46
  256.0 5.2 %collective-permute-start.40 = (f32[2,4096]{1,0:T(2,128)S(1)}, f32[2,4096]{1,0:T(2,128)S(1)}, u32[]{:S(2)}, u32[]{:S(2)}) collective-permute-start(f32[2,4096]{1,0:T(2,128)S(1)} %pad_maximum_fusion.8), channel_id=1, source_target_pairs={{0,32},{8,40},{16,48},{24,56},{32,64},{40,72},{48,80},{56,88},{64,... | collective-permute-start | bytes 98312 | tf_op jit(solution)/shard_map/ppermute | solution.py:46
  256.1 5.5 %collective-permute-start.41 = (f32[2,4096]{1,0:T(2,128)S(1)}, f32[2,4096]{1,0:T(2,128)S(1)}, u32[]{:S(2)}, u32[]{:S(2)}) collective-permute-start(f32[2,4096]{1,0:T(2,128)S(1)} %pad_maximum_fusion.8), channel_id=1, source_target_pairs={{0,64},{8,72},{16,80},{24,88},{32,96},{40,104},{48,112},{56,120},{... | collective-permute-start | bytes 98312 | tf_op jit(solution)/shard_map/ppermute | solution.py:46
  258.8 3.9 %collective-permute-start.42 = (f32[2,4096]{1,0:T(2,128)S(1)}, f32[2,4096]{1,0:T(2,128)S(1)}, u32[]{:S(2)}, u32[]{:S(2)}) collective-permute-start(f32[2,4096]{1,0:T(2,128)S(1)} %pad_maximum_fusion.8), channel_id=1, source_target_pairs={{0,96},{8,104},{16,112},{24,120},{32,0},{40,8},{48,16},{56,24},{64... | collective-permute-start | bytes 98312 | tf_op jit(solution)/shard_map/ppermute | solution.py:46
Sparse Core Ops, SparseCore 0:
  10.1 52.8 all-gather.1

commit v12 on v11

--- a/solution.py
+++ b/solution.py
@@ -106,7 +106,7 @@
     all_passages = passages.shape[0] * row_count * col_count
     query_block = gather_col(queries)
     rows = passages.shape[0]
-    split = rows - (rows * 3) // 32
+    split = rows - (rows * 5) // 32
     passage_block = jnp.concatenate(
         [lax.all_gather(passages[:split], "row", axis=0, tiled=True), gather_row(passages[split:])], axis=0
     )

time: 271 us -> 270 us (level)
    unnamed x27 -> x25, local copies, waits for them, and re-layouts: 12.8 us -> 10.5 us
  transfers between devices with their start and end apart: 44 -> 44, of which waited for: 36 -> 37; matrix products, arithmetic and copies ran while one was open for 1% -> 1% of each run, Pallas kernels for 0% -> 0%
where the time goes in v12:
time: 270 us; the launch traced here: 269 us
  other arithmetic  85.2 us (32%)
  starting transfers between devices  60.7 us (22%)
  waiting for transfers between devices  59.9 us (22%)
  matrix products  34.8 us (13%)
  between operations  15.3 us (6%)
  local copies, waits for them, and re-layouts  13.4 us (5%)
    ppermute x30, starting transfers between devices, combine_over(): lax.ppermute(packed, axis, digit_partners(axis, size, stride, width, k))  40.3 us
    dot_general x1, matrix products, inner_costs(): lax.dot_general(left, right, (((1,), (1,)), ((), ())), precision=lax.Prec...  34.8 us
    reduce_sum x3, other arithmetic, logsum_col(): totals = jnp.sum(jnp.exp(gaps / scale - peak[:, None]), axis=1)  30.6 us
    ppermute x30, waiting for transfers between devices, combine_over(): lax.ppermute(packed, axis, digit_partners(axis, size, stride, width, k))  29.3 us
    ppermute x13, waiting for transfers between devices, exchange(): lax.ppermute(x, axis, digit_partners(axis, size, stride, width, k))  23.6 us
    reduce_max x3, other arithmetic, logsum_row(): peak = jnp.max(gaps, axis=0) / scale  23.2 us
    reduce_sum x3, other arithmetic, logsum_row(): totals = jnp.sum(jnp.exp(gaps / scale - peak[None, :]), axis=0)  22.9 us
    ppermute x13, starting transfers between devices, exchange(): lax.ppermute(x, axis, digit_partners(axis, size, stride, width, k))  20.3 us
  transfers between devices with their start and end apart: 44, of which 37 were waited for; matrix products, arithmetic and copies ran while one was open for 1% of the time, Pallas kernels for 0%

profile of v12, /device:TPU:0, one launch (start us, length us, event | category | flops | bytes accessed | tf_op | source)
XLA Modules:
  0.0 269.4 jit_solution(6732371264932919641)
XLA Ops:
  7.2 1.7 slice.222
  9.7 1.7 collective-permute-start.7
  11.4 2.9 %collective-permute-start.8 = (f32[40,256]{1,0:T(8,128)S(1)}, f32[40,256]{1,0:T(8,128)S(1)}, u32[]{:S(2)}, u32[]{:S(2)}) collective-permute-start(f32[40,256]{1,0:T(8,128)S(1)} %get-tuple-element.7), channel_id=1, source_target_pairs={{0,16},{8,24},{16,0},{24,8},{32,48},{40,56},{48,32},{56,40},{64,80... | collective-permute-start | bytes 122888 | tf_op jit(solution)/shard_map/ppermute | solution.py:35
  15.6 1.5 collective-permute-start.1
  18.4 2.0 collective-permute-start.10
  20.4 3.6 %collective-permute-start.11 = (f32[160,256]{1,0:T(8,128)S(1)}, f32[160,256]{1,0:T(8,128)S(1)}, u32[]{:S(2)}, u32[]{:S(2)}) collective-permute-start(f32[160,256]{1,0:T(8,128)S(1)} %get-tuple-element.9), channel_id=1, source_target_pairs={{0,64},{8,72},{16,80},{24,88},{32,96},{40,104},{48,112},{56,120},{... | collective-permute-start | bytes 491528 | tf_op jit(solution)/shard_map/ppermute | solution.py:35
  25.9 1.9 collective-permute-done.10
  27.8 1.5 collective-permute-start.2
  29.3 5.5 %collective-permute-done.11 = f32[160,256]{1,0:T(8,128)S(1)} collective-permute-done((f32[160,256]{1,0:T(8,128)S(1)}, f32[160,256]{1,0:T(8,128)S(1)}, u32[]{:S(2)}, u32[]{:S(2)}) %collective-permute-start.11) | collective-permute-done | bytes 163872 | tf_op jit(solution)/shard_map/ppermute | solution.py:35
  36.1 1.6 collective-permute-start.4
  39.8 5.0 %collective-permute-done.3 = f32[256,256]{1,0:T(8,128)S(1)} collective-permute-done((f32[256,256]{1,0:T(8,128)}, f32[256,256]{1,0:T(8,128)S(1)}, u32[]{:S(2)}, u32[]{:S(2)}) %collective-permute-start.3) | collective-permute-done | bytes 262176 | tf_op jit(solution)/shard_map/ppermute | solution.py:35
  45.6 7.9 %collective-permute-done.5 = f32[256,256]{1,0:T(8,128)S(1)} collective-permute-done((f32[256,256]{1,0:T(8,128)S(1)}, f32[256,256]{1,0:T(8,128)S(1)}, u32[]{:S(2)}, u32[]{:S(2)}) %collective-permute-start.5) | collective-permute-done | bytes 262176 | tf_op jit(solution)/shard_map/ppermute | solution.py:35
  53.6 2.0 collective-permute-done.6
  56.2 7.0 %all-gather.2.cloned.1.call-done = f32[3456,256]{1,0:T(8,128)} async-done(((f32[216,256]{1,0:T(8,128)}), f32[3456,256]{1,0:T(8,128)}) %all-gather.2.cloned.1.call-update) | async-done | bytes 3538960 | tf_op jit(solution)/shard_map/all_gather | solution.py:111
  63.2 2.2 constant_dynamic-update-slice_fusion
  66.2 34.8 %subtract_reduce_fusion.5 = (f32[2048]{0:T(1024)S(1)}, f32[2048,4096]{1,0:T(8,128)}) fusion(f32[2048,256]{1,0:T(8,128)S(1)} %bitcast_dynamic-update-slice_fusion, f32[4096,256]{1,0:T(8,128)S(1)} %bitcast_dynamic-update-slice_fusion.16, f32[4096]{0:T(1024)S(1)} %multiply_reduce_fusion, f32[2048]{0:T(1024)S(1)} %multiply_reduce_fusion.1), kind=kOutput, calls=%fused_computation.12 | convolution fusion | flops 25811744768 | bytes 39878656 | tf_op jit(solution)/shard_map/dot_general | solution.py:14
  101.0 14.5 %exponential_reduce_fusion.5 = f32[2048]{0:T(1024)S(1)} fusion(f32[2048,4096]{1,0:T(8,128)} %get-tuple-element.59, f32[2048]{0:T(1024)S(1)} %broadcast_divide_fusion.5, f32[]{:T(128)} %bitcast), kind=kLoop, calls=%fused_computation.5 | loop fusion | flops 33552384 | bytes 33570820 | tf_op jit(solution)/shard_map/reduce_sum | solution.py:78
  116.9 1.5 collective-permute-start.14
  118.4 2.7 collective-permute-start.15
  121.1 1.5 collective-permute-start.16
  124.9 13.8 %subtract_reduce_fusion.4 = f32[4096]{0:T(1024)S(1)} fusion(f32[2048,4096]{1,0:T(8,128)} %get-tuple-element.59, f32[2048]{0:T(1024)S(1)} %multiply_subtract_fusion.6), kind=kLoop, calls=%fused_computation.11 | loop fusion | flops 16773120 | bytes 33579008 | tf_op jit(solution)/shard_map/reduce_max | solution.py:83
  138.7 6.3 %copy-done = f32[2048,4096]{1,0:T(8,128)S(1)} copy-done((f32[2048,4096]{1,0:T(8,128)S(1)}, f32[2048,4096]{1,0:T(8,128)}, u32[]{:S(2)}) %copy-start) | copy-done | bytes 33554456
  145.0 7.6 %exponential_reduce_fusion.4 = f32[4096]{0:T(1024)S(1)} fusion(f32[2048,4096]{1,0:T(8,128)S(1)} %copy-done, f32[4096]{0:T(1024)S(1)} %broadcast_divide_fusion.2, f32[2048]{0:T(1024)S(1)} %multiply_subtract_fusion.6, f32[]{:T(128)} %bitcast), kind=kLoop, calls=%fused_computation.4 | loop fusion | flops 33550336 | bytes 33595396 | tf_op jit(solution)/shard_map/reduce_sum | solution.py:84
  153.5 2.7 %collective-permute-start.18 = (f32[2,4096]{1,0:T(2,128)S(1)}, f32[2,4096]{1,0:T(2,128)S(1)}, u32[]{:S(2)}, u32[]{:S(2)}) collective-permute-start(f32[2,4096]{1,0:T(2,128)S(1)} %pad_maximum_fusion.3), channel_id=1, source_target_pairs={{0,16},{8,24},{16,0},{24,8},{32,48},{40,56},{48,32},{56,40},{64,80... | collective-permute-start | bytes 98312 | tf_op jit(solution)/shard_map/ppermute | solution.py:46
  156.2 1.4 collective-permute-start.19
  160.5 2.6 collective-permute-start.21
  163.1 1.4 collective-permute-start.22
  167.2 3.0 %subtract_reduce_fusion.3 = f32[2048]{0:T(1024)S(1)} fusion(f32[2048,4096]{1,0:T(8,128)S(1)} %copy-done, f32[4096]{0:T(1024)S(1)} %bitcast.126), kind=kLoop, calls=%fused_computation.10 | loop fusion | flops 16775168 | bytes 33579008 | tf_op jit(solution)/shard_map/reduce_max | solution.py:77
  170.2 8.0 %exponential_reduce_fusion.3 = f32[2048]{0:T(1024)S(1)} fusion(f32[2048,4096]{1,0:T(8,128)S(1)} %copy-done, f32[2048]{0:T(1024)S(1)} %broadcast_divide_fusion.4, f32[4096]{0:T(1024)S(1)} %bitcast.127, f32[]{:T(128)} %bitcast), kind=kLoop, calls=%fused_computation.3 | loop fusion | flops 33552384 | bytes 33587204 | tf_op jit(solution)/shard_map/reduce_sum | solution.py:78
  180.0 3.8 %collective-permute-start.25 = (f32[2,2048]{1,0:T(2,128)S(1)}, f32[2,2048]{1,0:T(2,128)S(1)}, u32[]{:S(2)}, u32[]{:S(2)}) collective-permute-start(f32[2,2048]{1,0:T(2,128)S(1)} %pad_maximum_fusion.12), channel_id=1, source_target_pairs={{0,4},{1,5},{2,6},{3,7},{4,0},{5,1},{6,2},{7,3},{8,12},{9,13},{10,... | collective-permute-start | bytes 49160 | tf_op jit(solution)/shard_map/ppermute | solution.py:46
  185.7 1.8 collective-permute-done.26
  187.6 4.7 %subtract_reduce_fusion.2 = f32[4096]{0:T(1024)S(1)} fusion(f32[2048,4096]{1,0:T(8,128)S(1)} %copy-done, f32[2048]{0:T(1024)S(1)} %multiply_subtract_fusion.5), kind=kLoop, calls=%fused_computation.9 | loop fusion | flops 16773120 | bytes 33579008 | tf_op jit(solution)/shard_map/reduce_max | solution.py:83
  192.3 7.6 %exponential_reduce_fusion.2 = f32[4096]{0:T(1024)S(1)} fusion(f32[2048,4096]{1,0:T(8,128)S(1)} %copy-done, f32[4096]{0:T(1024)S(1)} %broadcast_divide_fusion.1, f32[2048]{0:T(1024)S(1)} %multiply_subtract_fusion.5, f32[]{:T(128)} %bitcast), kind=kLoop, calls=%fused_computation.2 | loop fusion | flops 33550336 | bytes 33595396 | tf_op jit(solution)/shard_map/reduce_sum | solution.py:84
  200.0 1.4 collective-permute-start.27
  201.5 2.7 %collective-permute-start.28 = (f32[2,4096]{1,0:T(2,128)S(1)}, f32[2,4096]{1,0:T(2,128)S(1)}, u32[]{:S(2)}, u32[]{:S(2)}) collective-permute-start(f32[2,4096]{1,0:T(2,128)S(1)} %pad_maximum_fusion.5), channel_id=1, source_target_pairs={{0,16},{8,24},{16,0},{24,8},{32,48},{40,56},{48,32},{56,40},{64,80... | collective-permute-start | bytes 98312 | tf_op jit(solution)/shard_map/ppermute | solution.py:46
  205.2 1.7 collective-permute-done.28
  208.3 1.4 collective-permute-start.30
  209.7 2.7 collective-permute-start.31
  213.5 1.7 collective-permute-done.31
  216.5 3.0 %subtract_reduce_fusion.1 = f32[2048]{0:T(1024)S(1)} fusion(f32[2048,4096]{1,0:T(8,128)S(1)} %copy-done, f32[4096]{0:T(1024)S(1)} %bitcast.128), kind=kLoop, calls=%fused_computation.8 | loop fusion | flops 16775168 | bytes 33579008 | tf_op jit(solution)/shard_map/reduce_max | solution.py:77
  219.5 8.0 %exponential_reduce_fusion.1 = f32[2048]{0:T(1024)S(1)} fusion(f32[2048,4096]{1,0:T(8,128)S(1)} %copy-done, f32[2048]{0:T(1024)S(1)} %broadcast_divide_fusion.3, f32[4096]{0:T(1024)S(1)} %bitcast.129, f32[]{:T(128)} %bitcast), kind=kLoop, calls=%fused_computation.1 | loop fusion | flops 33552384 | bytes 33587204 | tf_op jit(solution)/shard_map/reduce_sum | solution.py:78
  229.0 2.7 %collective-permute-start.35 = (f32[2,2048]{1,0:T(2,128)S(1)}, f32[2,2048]{1,0:T(2,128)S(1)}, u32[]{:S(2)}, u32[]{:S(2)}) collective-permute-start(f32[2,2048]{1,0:T(2,128)S(1)} %pad_maximum_fusion.14), channel_id=1, source_target_pairs={{0,4},{1,5},{2,6},{3,7},{4,0},{5,1},{6,2},{7,3},{8,12},{9,13},{10,... | collective-permute-start | bytes 49160 | tf_op jit(solution)/shard_map/ppermute | solution.py:46
  231.7 1.5 collective-permute-start.36
  235.5 4.7 %subtract_reduce_fusion = f32[4096]{0:T(1024)S(1)} fusion(f32[2048,4096]{1,0:T(8,128)S(1)} %copy-done, f32[2048]{0:T(1024)S(1)} %multiply_subtract_fusion.4), kind=kLoop, calls=%fused_computation.7 | loop fusion | flops 16773120 | bytes 33579008 | tf_op jit(solution)/shard_map/reduce_max | solution.py:83
  240.2 7.6 %exponential_reduce_fusion = f32[4096]{0:T(1024)S(1)} fusion(f32[2048,4096]{1,0:T(8,128)S(1)} %copy-done, f32[4096]{0:T(1024)S(1)} %broadcast_divide_fusion, f32[2048]{0:T(1024)S(1)} %multiply_subtract_fusion.4, f32[]{:T(128)} %bitcast), kind=kLoop, calls=%fused_computation | loop fusion | flops 33550336 | bytes 33595396 | tf_op jit(solution)/shard_map/reduce_sum | solution.py:84
  248.0 2.7 collective-permute-start.38
  250.7 1.4 collective-permute-start.39
  254.9 2.7 %collective-permute-start.41 = (f32[2,4096]{1,0:T(2,128)S(1)}, f32[2,4096]{1,0:T(2,128)S(1)}, u32[]{:S(2)}, u32[]{:S(2)}) collective-permute-start(f32[2,4096]{1,0:T(2,128)S(1)} %pad_maximum_fusion.8), channel_id=1, source_target_pairs={{0,64},{8,72},{16,80},{24,88},{32,96},{40,104},{48,112},{56,120},{... | collective-permute-start | bytes 98312 | tf_op jit(solution)/shard_map/ppermute | solution.py:46
  (135 shorter events, 40.1 us)
Async XLA Ops:
  7.2 30.6 %copy-start.1 = (f32[256,256]{1,0:T(8,128)S(1)}, f32[256,256]{1,0:T(8,128)}, u32[]{:S(2)}) copy-start(f32[256,256]{1,0:T(8,128)} %param.3) | copy-start | bytes 786436
  7.2 56.0 %all-gather.2.cloned.1.call-start = ((), (), s32[]{:S(2)}) async-start(), calls=%async_computation | async-start | bytes 3760128 | tf_op jit(solution)/shard_map/all_gather | solution.py:111
  9.7 8.1 %collective-permute-start.7 = (f32[40,256]{1,0:T(8,128)S(1)}, f32[40,256]{1,0:T(8,128)S(1)}, u32[]{:S(2)}, u32[]{:S(2)}) collective-permute-start(f32[40,256]{1,0:T(8,128)S(1)} %get-tuple-element.7), channel_id=1, source_target_pairs={{0,8},{8,16},{16,24},{24,0},{32,40},{40,48},{48,56},{56,32},{64,72... | collective-permute-start | bytes 122888 | tf_op jit(solution)/shard_map/ppermute | solution.py:35
  11.4 6.5 %collective-permute-start.8 = (f32[40,256]{1,0:T(8,128)S(1)}, f32[40,256]{1,0:T(8,128)S(1)}, u32[]{:S(2)}, u32[]{:S(2)}) collective-permute-start(f32[40,256]{1,0:T(8,128)S(1)} %get-tuple-element.7), channel_id=1, source_target_pairs={{0,16},{8,24},{16,0},{24,8},{32,48},{40,56},{48,32},{56,40},{64,80... | collective-permute-start | bytes 122888 | tf_op jit(solution)/shard_map/ppermute | solution.py:35
  14.3 4.0 %collective-permute-start.9 = (f32[40,256]{1,0:T(8,128)S(1)}, f32[40,256]{1,0:T(8,128)S(1)}, u32[]{:S(2)}, u32[]{:S(2)}) collective-permute-start(f32[40,256]{1,0:T(8,128)S(1)} %get-tuple-element.7), channel_id=1, source_target_pairs={{0,24},{8,0},{16,8},{24,16},{32,56},{40,32},{48,40},{56,48},{64,88... | collective-permute-start | bytes 122888 | tf_op jit(solution)/shard_map/ppermute | solution.py:35
  15.6 22.1 %collective-permute-start = (f32[256,256]{1,0:T(8,128)}, f32[256,256]{1,0:T(8,128)S(1)}, u32[]{:S(2)}, u32[]{:S(2)}) collective-permute-start(f32[256,256]{1,0:T(8,128)} %param.3), channel_id=1, source_target_pairs={{0,1},{1,2},{2,3},{3,4},{4,5},{5,6},{6,7},{7,0},{8,9},{9,10},{10,1... | collective-permute-start | bytes 786440 | tf_op jit(solution)/shard_map/ppermute | solution.py:35
  15.6 23.4 %collective-permute-start.1 = (f32[256,256]{1,0:T(8,128)}, f32[256,256]{1,0:T(8,128)S(1)}, u32[]{:S(2)}, u32[]{:S(2)}) collective-permute-start(f32[256,256]{1,0:T(8,128)} %param.3), channel_id=1, source_target_pairs={{0,2},{1,3},{2,4},{3,5},{4,6},{5,7},{6,0},{7,1},{8,10},{9,11},{10,... | collective-permute-start | bytes 786440 | tf_op jit(solution)/shard_map/ppermute | solution.py:35
  18.4 9.4 %collective-permute-start.10 = (f32[160,256]{1,0:T(8,128)S(1)}, f32[160,256]{1,0:T(8,128)S(1)}, u32[]{:S(2)}, u32[]{:S(2)}) collective-permute-start(f32[160,256]{1,0:T(8,128)S(1)} %get-tuple-element.9), channel_id=1, source_target_pairs={{0,32},{8,40},{16,48},{24,56},{32,64},{40,72},{48,80},{56,88},{64,... | collective-permute-start | bytes 491528 | tf_op jit(solution)/shard_map/ppermute | solution.py:35
  20.4 14.5 %collective-permute-start.11 = (f32[160,256]{1,0:T(8,128)S(1)}, f32[160,256]{1,0:T(8,128)S(1)}, u32[]{:S(2)}, u32[]{:S(2)}) collective-permute-start(f32[160,256]{1,0:T(8,128)S(1)} %get-tuple-element.9), channel_id=1, source_target_pairs={{0,64},{8,72},{16,80},{24,88},{32,96},{40,104},{48,112},{56,120},{... | collective-permute-start | bytes 491528 | tf_op jit(solution)/shard_map/ppermute | solution.py:35
  23.9 12.1 %collective-permute-start.12 = (f32[160,256]{1,0:T(8,128)S(1)}, f32[160,256]{1,0:T(8,128)S(1)}, u32[]{:S(2)}, u32[]{:S(2)}) collective-permute-start(f32[160,256]{1,0:T(8,128)S(1)} %get-tuple-element.9), channel_id=1, source_target_pairs={{0,96},{8,104},{16,112},{24,120},{32,0},{40,8},{48,16},{56,24},{64... | collective-permute-start | bytes 491528 | tf_op jit(solution)/shard_map/ppermute | solution.py:35
  27.8 12.0 %collective-permute-start.2 = (f32[256,256]{1,0:T(8,128)}, f32[256,256]{1,0:T(8,128)S(1)}, u32[]{:S(2)}, u32[]{:S(2)}) collective-permute-start(f32[256,256]{1,0:T(8,128)} %param.3), channel_id=1, source_target_pairs={{0,3},{1,4},{2,5},{3,6},{4,7},{5,0},{6,1},{7,2},{8,11},{9,12},{10,... | collective-permute-start | bytes 786440 | tf_op jit(solution)/shard_map/ppermute | solution.py:35
  34.8 10.0 %collective-permute-start.3 = (f32[256,256]{1,0:T(8,128)}, f32[256,256]{1,0:T(8,128)S(1)}, u32[]{:S(2)}, u32[]{:S(2)}) collective-permute-start(f32[256,256]{1,0:T(8,128)} %param.3), channel_id=1, source_target_pairs={{0,4},{1,5},{2,6},{3,7},{4,0},{5,1},{6,2},{7,3},{8,12},{9,13},{10,... | collective-permute-start | bytes 786440 | tf_op jit(solution)/shard_map/ppermute | solution.py:35
  36.1 9.5 %collective-permute-start.4 = (f32[256,256]{1,0:T(8,128)}, f32[256,256]{1,0:T(8,128)S(1)}, u32[]{:S(2)}, u32[]{:S(2)}) collective-permute-start(f32[256,256]{1,0:T(8,128)} %param.3), channel_id=1, source_target_pairs={{0,5},{1,6},{2,7},{3,0},{4,1},{5,2},{6,3},{7,4},{8,13},{9,14},{10,... | collective-permute-start | bytes 786440 | tf_op jit(solution)/shard_map/ppermute | solution.py:35
  37.8 15.7 %collective-permute-start.5 = (f32[256,256]{1,0:T(8,128)S(1)}, f32[256,256]{1,0:T(8,128)S(1)}, u32[]{:S(2)}, u32[]{:S(2)}) collective-permute-start(f32[256,256]{1,0:T(8,128)S(1)} %copy-done.1), channel_id=1, source_target_pairs={{0,6},{1,7},{2,0},{3,1},{4,2},{5,3},{6,4},{7,5},{8,14},{9,15},{10,... | collective-permute-start | bytes 786440 | tf_op jit(solution)/shard_map/ppermute | solution.py:35
  39.1 16.5 %collective-permute-start.6 = (f32[256,256]{1,0:T(8,128)S(1)}, f32[256,256]{1,0:T(8,128)S(1)}, u32[]{:S(2)}, u32[]{:S(2)}) collective-permute-start(f32[256,256]{1,0:T(8,128)S(1)} %copy-done.1), channel_id=1, source_target_pairs={{0,7},{1,0},{2,1},{3,2},{4,3},{5,4},{6,5},{7,6},{8,15},{9,8},{10,9... | collective-permute-start | bytes 786440 | tf_op jit(solution)/shard_map/ppermute | solution.py:35
  115.5 1.3 collective-permute-start.13
  116.9 5.7 %collective-permute-start.14 = (f32[2,2048]{1,0:T(2,128)S(1)}, f32[2,2048]{1,0:T(2,128)S(1)}, u32[]{:S(2)}, u32[]{:S(2)}) collective-permute-start(f32[2,2048]{1,0:T(2,128)S(1)} %pad_maximum_fusion.10), channel_id=1, source_target_pairs={{0,2},{1,3},{2,4},{3,5},{4,6},{5,7},{6,0},{7,1},{8,10},{9,11},{10,... | collective-permute-start | bytes 49160 | tf_op jit(solution)/shard_map/ppermute | solution.py:46
  118.4 5.2 %collective-permute-start.15 = (f32[2,2048]{1,0:T(2,128)S(1)}, f32[2,2048]{1,0:T(2,128)S(1)}, u32[]{:S(2)}, u32[]{:S(2)}) collective-permute-start(f32[2,2048]{1,0:T(2,128)S(1)} %pad_maximum_fusion.10), channel_id=1, source_target_pairs={{0,4},{1,5},{2,6},{3,7},{4,0},{5,1},{6,2},{7,3},{8,12},{9,13},{10,... | collective-permute-start | bytes 49160 | tf_op jit(solution)/shard_map/ppermute | solution.py:46
  121.1 3.7 %collective-permute-start.16 = (f32[2,2048]{1,0:T(2,128)S(1)}, f32[2,2048]{1,0:T(2,128)S(1)}, u32[]{:S(2)}, u32[]{:S(2)}) collective-permute-start(f32[2,2048]{1,0:T(2,128)S(1)} %pad_maximum_fusion.10), channel_id=1, source_target_pairs={{0,6},{1,7},{2,0},{3,1},{4,2},{5,3},{6,4},{7,5},{8,14},{9,15},{10,... | collective-permute-start | bytes 49160 | tf_op jit(solution)/shard_map/ppermute | solution.py:46
  124.9 20.2 %copy-start = (f32[2048,4096]{1,0:T(8,128)S(1)}, f32[2048,4096]{1,0:T(8,128)}, u32[]{:S(2)}) copy-start(f32[2048,4096]{1,0:T(8,128)} %get-tuple-element.59) | copy-start | bytes 100663296
  152.7 5.2 %collective-permute-start.17 = (f32[2,4096]{1,0:T(2,128)S(1)}, f32[2,4096]{1,0:T(2,128)S(1)}, u32[]{:S(2)}, u32[]{:S(2)}) collective-permute-start(f32[2,4096]{1,0:T(2,128)S(1)} %pad_maximum_fusion.3), channel_id=1, source_target_pairs={{0,8},{8,16},{16,24},{24,0},{32,40},{40,48},{48,56},{56,32},{64,72... | collective-permute-start | bytes 98312 | tf_op jit(solution)/shard_map/ppermute | solution.py:46
  153.5 5.4 %collective-permute-start.18 = (f32[2,4096]{1,0:T(2,128)S(1)}, f32[2,4096]{1,0:T(2,128)S(1)}, u32[]{:S(2)}, u32[]{:S(2)}) collective-permute-start(f32[2,4096]{1,0:T(2,128)S(1)} %pad_maximum_fusion.3), channel_id=1, source_target_pairs={{0,16},{8,24},{16,0},{24,8},{32,48},{40,56},{48,32},{56,40},{64,80... | collective-permute-start | bytes 98312 | tf_op jit(solution)/shard_map/ppermute | solution.py:46
  156.2 3.9 %collective-permute-start.19 = (f32[2,4096]{1,0:T(2,128)S(1)}, f32[2,4096]{1,0:T(2,128)S(1)}, u32[]{:S(2)}, u32[]{:S(2)}) collective-permute-start(f32[2,4096]{1,0:T(2,128)S(1)} %pad_maximum_fusion.3), channel_id=1, source_target_pairs={{0,24},{8,0},{16,8},{24,16},{32,56},{40,32},{48,40},{56,48},{64,88... | collective-permute-start | bytes 98312 | tf_op jit(solution)/shard_map/ppermute | solution.py:46
  160.3 5.2 %collective-permute-start.20 = (f32[2,4096]{1,0:T(2,128)S(1)}, f32[2,4096]{1,0:T(2,128)S(1)}, u32[]{:S(2)}, u32[]{:S(2)}) collective-permute-start(f32[2,4096]{1,0:T(2,128)S(1)} %pad_maximum_fusion.4), channel_id=1, source_target_pairs={{0,32},{8,40},{16,48},{24,56},{32,64},{40,72},{48,80},{56,88},{64,... | collective-permute-start | bytes 98312 | tf_op jit(solution)/shard_map/ppermute | solution.py:46
  160.5 5.4 %collective-permute-start.21 = (f32[2,4096]{1,0:T(2,128)S(1)}, f32[2,4096]{1,0:T(2,128)S(1)}, u32[]{:S(2)}, u32[]{:S(2)}) collective-permute-start(f32[2,4096]{1,0:T(2,128)S(1)} %pad_maximum_fusion.4), channel_id=1, source_target_pairs={{0,64},{8,72},{16,80},{24,88},{32,96},{40,104},{48,112},{56,120},{... | collective-permute-start | bytes 98312 | tf_op jit(solution)/shard_map/ppermute | solution.py:46
  163.1 3.9 %collective-permute-start.22 = (f32[2,4096]{1,0:T(2,128)S(1)}, f32[2,4096]{1,0:T(2,128)S(1)}, u32[]{:S(2)}, u32[]{:S(2)}) collective-permute-start(f32[2,4096]{1,0:T(2,128)S(1)} %pad_maximum_fusion.4), channel_id=1, source_target_pairs={{0,96},{8,104},{16,112},{24,120},{32,0},{40,8},{48,16},{56,24},{64... | collective-permute-start | bytes 98312 | tf_op jit(solution)/shard_map/ppermute | solution.py:46
  178.2 1.3 collective-permute-start.23
  179.6 5.0 %collective-permute-start.24 = (f32[2,2048]{1,0:T(2,128)S(1)}, f32[2,2048]{1,0:T(2,128)S(1)}, u32[]{:S(2)}, u32[]{:S(2)}) collective-permute-start(f32[2,2048]{1,0:T(2,128)S(1)} %pad_maximum_fusion.12), channel_id=1, source_target_pairs={{0,2},{1,3},{2,4},{3,5},{4,6},{5,7},{6,0},{7,1},{8,10},{9,11},{10,... | collective-permute-start | bytes 49160 | tf_op jit(solution)/shard_map/ppermute | solution.py:46
  180.0 5.7 %collective-permute-start.25 = (f32[2,2048]{1,0:T(2,128)S(1)}, f32[2,2048]{1,0:T(2,128)S(1)}, u32[]{:S(2)}, u32[]{:S(2)}) collective-permute-start(f32[2,2048]{1,0:T(2,128)S(1)} %pad_maximum_fusion.12), channel_id=1, source_target_pairs={{0,4},{1,5},{2,6},{3,7},{4,0},{5,1},{6,2},{7,3},{8,12},{9,13},{10,... | collective-permute-start | bytes 49160 | tf_op jit(solution)/shard_map/ppermute | solution.py:46
  183.8 3.7 %collective-permute-start.26 = (f32[2,2048]{1,0:T(2,128)S(1)}, f32[2,2048]{1,0:T(2,128)S(1)}, u32[]{:S(2)}, u32[]{:S(2)}) collective-permute-start(f32[2,2048]{1,0:T(2,128)S(1)} %pad_maximum_fusion.12), channel_id=1, source_target_pairs={{0,6},{1,7},{2,0},{3,1},{4,2},{5,3},{6,4},{7,5},{8,14},{9,15},{10,... | collective-permute-start | bytes 49160 | tf_op jit(solution)/shard_map/ppermute | solution.py:46
  200.0 5.2 %collective-permute-start.27 = (f32[2,4096]{1,0:T(2,128)S(1)}, f32[2,4096]{1,0:T(2,128)S(1)}, u32[]{:S(2)}, u32[]{:S(2)}) collective-permute-start(f32[2,4096]{1,0:T(2,128)S(1)} %pad_maximum_fusion.5), channel_id=1, source_target_pairs={{0,8},{8,16},{16,24},{24,0},{32,40},{40,48},{48,56},{56,32},{64,72... | collective-permute-start | bytes 98312 | tf_op jit(solution)/shard_map/ppermute | solution.py:46
  201.5 5.4 %collective-permute-start.28 = (f32[2,4096]{1,0:T(2,128)S(1)}, f32[2,4096]{1,0:T(2,128)S(1)}, u32[]{:S(2)}, u32[]{:S(2)}) collective-permute-start(f32[2,4096]{1,0:T(2,128)S(1)} %pad_maximum_fusion.5), channel_id=1, source_target_pairs={{0,16},{8,24},{16,0},{24,8},{32,48},{40,56},{48,32},{56,40},{64,80... | collective-permute-start | bytes 98312 | tf_op jit(solution)/shard_map/ppermute | solution.py:46
  204.2 3.9 %collective-permute-start.29 = (f32[2,4096]{1,0:T(2,128)S(1)}, f32[2,4096]{1,0:T(2,128)S(1)}, u32[]{:S(2)}, u32[]{:S(2)}) collective-permute-start(f32[2,4096]{1,0:T(2,128)S(1)} %pad_maximum_fusion.5), channel_id=1, source_target_pairs={{0,24},{8,0},{16,8},{24,16},{32,56},{40,32},{48,40},{56,48},{64,88... | collective-permute-start | bytes 98312 | tf_op jit(solution)/shard_map/ppermute | solution.py:46
  208.3 5.2 %collective-permute-start.30 = (f32[2,4096]{1,0:T(2,128)S(1)}, f32[2,4096]{1,0:T(2,128)S(1)}, u32[]{:S(2)}, u32[]{:S(2)}) collective-permute-start(f32[2,4096]{1,0:T(2,128)S(1)} %pad_maximum_fusion.6), channel_id=1, source_target_pairs={{0,32},{8,40},{16,48},{24,56},{32,64},{40,72},{48,80},{56,88},{64,... | collective-permute-start | bytes 98312 | tf_op jit(solution)/shard_map/ppermute | solution.py:46
  209.7 5.4 %collective-permute-start.31 = (f32[2,4096]{1,0:T(2,128)S(1)}, f32[2,4096]{1,0:T(2,128)S(1)}, u32[]{:S(2)}, u32[]{:S(2)}) collective-permute-start(f32[2,4096]{1,0:T(2,128)S(1)} %pad_maximum_fusion.6), channel_id=1, source_target_pairs={{0,64},{8,72},{16,80},{24,88},{32,96},{40,104},{48,112},{56,120},{... | collective-permute-start | bytes 98312 | tf_op jit(solution)/shard_map/ppermute | solution.py:46
  212.4 3.9 %collective-permute-start.32 = (f32[2,4096]{1,0:T(2,128)S(1)}, f32[2,4096]{1,0:T(2,128)S(1)}, u32[]{:S(2)}, u32[]{:S(2)}) collective-permute-start(f32[2,4096]{1,0:T(2,128)S(1)} %pad_maximum_fusion.6), channel_id=1, source_target_pairs={{0,96},{8,104},{16,112},{24,120},{32,0},{40,8},{48,16},{56,24},{64... | collective-permute-start | bytes 98312 | tf_op jit(solution)/shard_map/ppermute | solution.py:46
  227.6 1.3 collective-permute-start.33
  228.9 5.0 %collective-permute-start.34 = (f32[2,2048]{1,0:T(2,128)S(1)}, f32[2,2048]{1,0:T(2,128)S(1)}, u32[]{:S(2)}, u32[]{:S(2)}) collective-permute-start(f32[2,2048]{1,0:T(2,128)S(1)} %pad_maximum_fusion.14), channel_id=1, source_target_pairs={{0,2},{1,3},{2,4},{3,5},{4,6},{5,7},{6,0},{7,1},{8,10},{9,11},{10,... | collective-permute-start | bytes 49160 | tf_op jit(solution)/shard_map/ppermute | solution.py:46
  229.0 5.3 %collective-permute-start.35 = (f32[2,2048]{1,0:T(2,128)S(1)}, f32[2,2048]{1,0:T(2,128)S(1)}, u32[]{:S(2)}, u32[]{:S(2)}) collective-permute-start(f32[2,2048]{1,0:T(2,128)S(1)} %pad_maximum_fusion.14), channel_id=1, source_target_pairs={{0,4},{1,5},{2,6},{3,7},{4,0},{5,1},{6,2},{7,3},{8,12},{9,13},{10,... | collective-permute-start | bytes 49160 | tf_op jit(solution)/shard_map/ppermute | solution.py:46
  231.7 3.7 %collective-permute-start.36 = (f32[2,2048]{1,0:T(2,128)S(1)}, f32[2,2048]{1,0:T(2,128)S(1)}, u32[]{:S(2)}, u32[]{:S(2)}) collective-permute-start(f32[2,2048]{1,0:T(2,128)S(1)} %pad_maximum_fusion.14), channel_id=1, source_target_pairs={{0,6},{1,7},{2,0},{3,1},{4,2},{5,3},{6,4},{7,5},{8,14},{9,15},{10,... | collective-permute-start | bytes 49160 | tf_op jit(solution)/shard_map/ppermute | solution.py:46
  235.5 4.8 %copy-start.2 = (f32[2048]{0:T(1024)}, f32[2048]{0:T(1024)S(1)}, u32[]{:S(2)}) copy-start(f32[2048]{0:T(1024)S(1)} %multiply_subtract_fusion.4) | copy-start | bytes 24580
  247.9 5.2 %collective-permute-start.37 = (f32[2,4096]{1,0:T(2,128)S(1)}, f32[2,4096]{1,0:T(2,128)S(1)}, u32[]{:S(2)}, u32[]{:S(2)}) collective-permute-start(f32[2,4096]{1,0:T(2,128)S(1)} %pad_maximum_fusion.7), channel_id=1, source_target_pairs={{0,8},{8,16},{16,24},{24,0},{32,40},{40,48},{48,56},{56,32},{64,72... | collective-permute-start | bytes 98312 | tf_op jit(solution)/shard_map/ppermute | solution.py:46
  248.0 5.5 %collective-permute-start.38 = (f32[2,4096]{1,0:T(2,128)S(1)}, f32[2,4096]{1,0:T(2,128)S(1)}, u32[]{:S(2)}, u32[]{:S(2)}) collective-permute-start(f32[2,4096]{1,0:T(2,128)S(1)} %pad_maximum_fusion.7), channel_id=1, source_target_pairs={{0,16},{8,24},{16,0},{24,8},{32,48},{40,56},{48,32},{56,40},{64,80... | collective-permute-start | bytes 98312 | tf_op jit(solution)/shard_map/ppermute | solution.py:46
  250.7 3.9 %collective-permute-start.39 = (f32[2,4096]{1,0:T(2,128)S(1)}, f32[2,4096]{1,0:T(2,128)S(1)}, u32[]{:S(2)}, u32[]{:S(2)}) collective-permute-start(f32[2,4096]{1,0:T(2,128)S(1)} %pad_maximum_fusion.7), channel_id=1, source_target_pairs={{0,24},{8,0},{16,8},{24,16},{32,56},{40,32},{48,40},{56,48},{64,88... | collective-permute-start | bytes 98312 | tf_op jit(solution)/shard_map/ppermute | solution.py:46
  254.8 5.2 %collective-permute-start.40 = (f32[2,4096]{1,0:T(2,128)S(1)}, f32[2,4096]{1,0:T(2,128)S(1)}, u32[]{:S(2)}, u32[]{:S(2)}) collective-permute-start(f32[2,4096]{1,0:T(2,128)S(1)} %pad_maximum_fusion.8), channel_id=1, source_target_pairs={{0,32},{8,40},{16,48},{24,56},{32,64},{40,72},{48,80},{56,88},{64,... | collective-permute-start | bytes 98312 | tf_op jit(solution)/shard_map/ppermute | solution.py:46
  254.9 5.5 %collective-permute-start.41 = (f32[2,4096]{1,0:T(2,128)S(1)}, f32[2,4096]{1,0:T(2,128)S(1)}, u32[]{:S(2)}, u32[]{:S(2)}) collective-permute-start(f32[2,4096]{1,0:T(2,128)S(1)} %pad_maximum_fusion.8), channel_id=1, source_target_pairs={{0,64},{8,72},{16,80},{24,88},{32,96},{40,104},{48,112},{56,120},{... | collective-permute-start | bytes 98312 | tf_op jit(solution)/shard_map/ppermute | solution.py:46
  257.6 3.9 %collective-permute-start.42 = (f32[2,4096]{1,0:T(2,128)S(1)}, f32[2,4096]{1,0:T(2,128)S(1)}, u32[]{:S(2)}, u32[]{:S(2)}) collective-permute-start(f32[2,4096]{1,0:T(2,128)S(1)} %pad_maximum_fusion.8), channel_id=1, source_target_pairs={{0,96},{8,104},{16,112},{24,120},{32,0},{40,8},{48,16},{56,24},{64... | collective-permute-start | bytes 98312 | tf_op jit(solution)/shard_map/ppermute | solution.py:46
Sparse Core Ops, SparseCore 0:
  10.1 53.0 all-gather.1
